TPU v7x, 256 devices: a whole 4x4x8 slice. The times are simulated.
256 devices in a mesh: fsdp: 32 (over y, x, z_hi), tp: 8 (over z_lo, core).
Axes of the slice: x: 4, y: 4, z: 8 (z_hi: 2, z_lo: 4; z = z_hi * 4 + z_lo), core: 2. Of those that a mesh axis runs over, the one named last changes fastest.
Arguments:
- tokens: bfloat16 [16384, 4096], P(('fsdp', 'tp')), may hold values from -6 to 6
- in_weight: bfloat16 [4096, 3, 4096], P('fsdp', None, 'tp'), may hold values from -0.09375 to 0.09375
- out_weight: bfloat16 [4096, 4096], P('fsdp', 'tp'), may hold values from -0.09375 to 0.09375
- short_taps: float32 [3, 3, 4096], P(None, None, 'tp'), may hold values from -3 to 3
- filter_taps: float32 [128, 4096], P(None, 'tp'), may hold values from -1.2 to 1.2
- decay_rate: float32 [4096], P('tp'), may hold values from 0.00390625 to 0.09375
- doc_lengths: int32 [64], replicated, may hold values from 1 to 2048, 16384 in all
Outputs:
- mixed_out: bfloat16 [16384, 4096], P(('fsdp', 'tp'))
Inputs may be any that keep to these rules, and one draw needn't show every extreme that they name: `doc_lengths`: the documents of the window in order; they sum to 16384.
All inputs are finite; a program needn't handle non-finite values.
Results may differ from a plain program's by a relative error of at most 0.014.
Values may be sent and summed in bfloat16 or wider, within the bound.
No kernel may reach another device: no remote copies, remote signals or barrier semaphores. Data moves between devices by JAX's collectives and lax.ppermute only.
A program may use at most 64 MiB of HBM per device.

v0:
```python
import jax
import jax.numpy as jnp
from jax import lax
from jax.sharding import PartitionSpec as P


def from_behind(value, axis, by):
    length = lax.axis_size(axis)
    pairs = [(i, i + by) for i in range(length) if 0 <= i + by < length]
    return lax.ppermute(value, axis, pairs)


def doc_position(points, lengths):
    starts = jnp.cumsum(lengths) - lengths
    begins = jnp.max(jnp.where(starts[None, :] <= points[:, None], starts[None, :], 0), axis=1)
    return points - begins


def short_filter(extended, short_taps, positions, out_count):
    running = jnp.zeros((out_count,) + extended.shape[1:], jnp.float32)
    for tap_index in range(3):
        window = extended[2 - tap_index : 2 - tap_index + out_count].astype(jnp.float32)
        inside = (positions >= tap_index)[:, None, None]
        running = running + jnp.where(
            inside, short_taps[tap_index][None] * window, jnp.float32(0.0)
        )
    return running


def long_filter(extended, shaped, positions, out_count, tap_count):

    def tap_group(group_index, running):
        for inner in range(16):
            tap_index = group_index * 16 + inner
            window = lax.dynamic_slice_in_dim(extended, tap_count - tap_index, out_count, 0)
            weight_row = lax.dynamic_slice_in_dim(shaped, tap_index, 1, 0)
            inside = (positions >= tap_index)[:, None]
            running = running + jnp.where(
                inside, weight_row * window.astype(jnp.float32), jnp.float32(0.0)
            )
        return running

    zero_sum = jnp.zeros((out_count, shaped.shape[1]), jnp.float32)
    return lax.fori_loop(0, tap_count // 16, tap_group, zero_sum)


def body(tokens, in_weight, out_weight, short_taps, filter_taps, decay_rate, doc_lengths):
    own_rows = tokens.shape[0]
    slab_count = own_rows * lax.axis_size("tp")
    channels = in_weight.shape[2]
    tap_count = filter_taps.shape[0]
    widened = tokens.astype(jnp.float32)
    normed = (
        widened * lax.rsqrt(jnp.mean(widened * widened, axis=1, keepdims=True) + 1e-06)
    ).astype(jnp.bfloat16)
    gathered = lax.all_gather(normed, "tp", axis=0, tiled=True)
    shard_piece = lax.all_gather(in_weight, "fsdp", axis=0, tiled=True)
    count_rows = shard_piece.shape[0]
    flat_piece = shard_piece.reshape(count_rows, 3 * channels)
    projected = jnp.dot(gathered, flat_piece, preferred_element_type=jnp.float32)
    out_full = lax.all_gather(out_weight, "fsdp", axis=0, tiled=True)
    projected = projected.astype(jnp.bfloat16).reshape(slab_count, 3, channels)
    first_row = lax.axis_index("fsdp") * slab_count
    own_points = first_row + jnp.arange(slab_count, dtype=jnp.int32)
    own_position = doc_position(own_points, doc_lengths)
    edge_rows = from_behind(projected[slab_count - 2 :], "fsdp", 1)
    short_all = short_filter(
        jnp.concatenate([edge_rows, projected], 0), short_taps, own_position, slab_count
    )
    kv_product = (short_all[:, 1] * short_all[:, 2]).astype(jnp.bfloat16)
    tail_rows = from_behind(kv_product[slab_count - tap_count :], "fsdp", 1)
    extended = jnp.concatenate([tail_rows, kv_product], 0)
    query = short_all[:, 0]
    shaped = filter_taps * jnp.exp(
        -decay_rate[None, :] * jnp.arange(tap_count, dtype=jnp.float32)[:, None]
    )
    long_mix = long_filter(extended, shaped, own_position, slab_count, tap_count)
    gated_mix = (query * long_mix).astype(jnp.bfloat16)
    summed = lax.psum_scatter(
        lax.dot_general(
            gated_mix, out_full, (((1,), (1,)), ((), ())), preferred_element_type=jnp.float32
        ).astype(jnp.bfloat16),
        "tp",
        scatter_dimension=0,
        tiled=True,
    ).astype(jnp.float32)
    return (widened + summed).astype(jnp.bfloat16)


def solution(mesh):
    in_specs = (
        P(("fsdp", "tp"), None),
        P("fsdp", None, "tp"),
        P("fsdp", "tp"),
        P(None, None, "tp"),
        P(None, "tp"),
        P("tp"),
        P(),
    )
    out_specs = P(("fsdp", "tp"), None)
    return jax.shard_map(body, mesh=mesh, in_specs=in_specs, out_specs=out_specs, check_vma=False)
```

profile of v0, /device:TPU:2, one launch (start us, length us, event | category | flops | bytes accessed | tf_op | source)
XLA Modules:
  0.0 535.3 jit_solution(15529755904550829064)
XLA Ops:
  6.5 0.0 copy-start.6
  6.5 0.0 copy-start.4
  6.5 0.0 copy-start.5
  6.5 0.0 all-gather.4.cloned.1.call-start
  6.6 1.3 fusion.16
  7.9 2.0 fusion.17
  9.9 0.0 all-gather.4.cloned.1.call-update
  9.9 0.0 all-gather.6.cloned.1.call-start
  10.0 1.9 copy.19
  11.9 0.0 all-gather.6.cloned.1.call-update
  11.9 0.0 all-gather.8.cloned.1.call-start
  12.0 0.7 all-gather.8.cloned.1.call-update
  12.7 0.0 reduce-scatter.2.cloned.1.call-start
  12.7 0.0 copy-done.6
  12.8 0.1 copy.18
  12.9 0.1 reduce-window.9
  12.9 0.1 reduce
  13.1 0.1 select_reduce_fusion
  13.2 0.0 copy-done.4
  13.2 0.0 copy-done.5
  13.2 0.0 copy-done.3
  13.2 0.1 exponential_multiply_fusion
  13.3 54.3 %all-gather.4.cloned.1.call-done = bf16[512,4096]{1,0:T(8,128)(2,1)} async-done(((bf16[64,4096]{1,0:T(8,128)(2,1)}), bf16[512,4096]{1,0:T(8,128)(2,1)}) %all-gather.4.cloned.1.call-update) | async-done | bytes 4194320 | tf_op jit(solution)/shard_map/all_gather | solution.py:56
  67.6 279.4 %all-gather.6.cloned.1.call-done = bf16[4096,3,512]{0,2,1:T(8,128)(2,1)} async-done(((bf16[128,3,512]{0,2,1:T(8,128)(2,1)}), bf16[4096,3,512]{0,2,1:T(8,128)(2,1)}) %all-gather.6.cloned.1.call-update) | async-done | bytes 12582928 | tf_op jit(solution)/shard_map/all_gather | solution.py:57
  347.0 10.9 %convolution_convert_fusion.1 = bf16[512,1536]{1,0:T(8,128)(2,1)S(1)} fusion(bf16[512,4096]{1,0:T(8,128)(2,1)} %all-gather.4.cloned.1.call-done, bf16[4096,1536]{0,1:T(8,128)(2,1)} %bitcast.90), kind=kOutput, calls=%fused_computation.50 | convolution fusion | flops 6443237376 | bytes 18350080 | tf_op jit(solution)/shard_map/dot_general | solution.py:60
  357.9 0.0 copy-start.2
  357.9 1.2 copy.24
  359.2 2.2 collective-permute-start
  361.4 0.0 copy-done.2
  361.4 1.7 copy.20
  363.2 19.5 %collective-permute-done = bf16[2,3,512]{0,2,1:T(8,128)(2,1)} collective-permute-done((bf16[2,3,512]{0,2,1:T(8,128)(2,1)}, bf16[2,3,512]{0,2,1:T(8,128)(2,1)}, u32[]{:S(2)}, u32[]{:S(2)}) %collective-permute-start) | collective-permute-done | bytes 6176 | tf_op jit(solution)/shard_map/ppermute | solution.py:10
  382.7 3.9 select_add_fusion.1
  386.6 0.0 copy-start
  386.6 0.2 fusion.19
  386.8 2.1 collective-permute-start.1
  388.9 0.2 fusion.28
  389.1 9.9 %collective-permute-done.1 = bf16[128,512]{0,1:T(8,128)(2,1)S(1)} collective-permute-done((bf16[128,512]{0,1:T(8,128)(2,1)S(1)}, bf16[128,512]{0,1:T(8,128)(2,1)S(1)}, u32[]{:S(2)}, u32[]{:S(2)}) %collective-permute-start.1) | collective-permute-done | bytes 131104 | tf_op jit(solution)/shard_map/ppermute | solution.py:10
  398.9 0.0 copy-done
  398.9 0.1 pad_maximum_fusion.1
  399.0 0.3 copy.22
  399.3 51.9 %while.17 = (s32[]{:T(128)}, f32[512,512]{1,0:T(8,128)S(1)}, s32[512]{0:T(512)S(1)}, f32[128,512]{1,0:T(8,128)S(1)}, bf16[640,512]{1,0:T(8,128)(2,1)S(1)}, /*ind...) while((s32[]{:T(128)}, f32[512,512]{1,0:T(8,128)S(1)}, ...), condition=%wide.region_4.5_spmd.clone, body=%wide.region_3.4_spmd.clone.sunk | while | flops 17047684 | bytes 10604503 | solution.py:44
  399.4 0.1 constant_dynamic-slice_fusion.17
  399.7 6.1 %fusion.30 = f32[512,512]{1,0:T(8,128)S(1)} fusion(f32[512,512]{1,0:T(8,128)S(1)} %get-tuple-element.425, bf16[640,512]{1,0:T(8,128)(2,1)S(1)} %get-tuple-element.467, s32[]{:T(128)S(6)} %select_n.679, f32[512]{0:T(512)S(1)} %bitcast.74, s32[]{:T(128)S(6)} %select_n.696, f32[512]{0:T(512)S(1)} %bitcast.75, s32[]{:T(128)S(6)} %select_n.697, ...), kind=kLoop, calls=%fused_computation.15.clone.1 | loop fusion | flops 17039360 | bytes 10526785 | tf_op jit(solution)/shard_map/while/body/eval_jaxpr/add | solution.py:38
  405.9 0.1 constant_dynamic-slice_fusion.17
  406.2 6.1 %fusion.30 = f32[512,512]{1,0:T(8,128)S(1)} fusion(f32[512,512]{1,0:T(8,128)S(1)} %get-tuple-element.425, bf16[640,512]{1,0:T(8,128)(2,1)S(1)} %get-tuple-element.467, s32[]{:T(128)S(6)} %select_n.679, f32[512]{0:T(512)S(1)} %bitcast.74, s32[]{:T(128)S(6)} %select_n.696, f32[512]{0:T(512)S(1)} %bitcast.75, s32[]{:T(128)S(6)} %select_n.697, ...), kind=kLoop, calls=%fused_computation.15.clone.1 | loop fusion | flops 17039360 | bytes 10526785 | tf_op jit(solution)/shard_map/while/body/eval_jaxpr/add | solution.py:38
  412.4 0.1 constant_dynamic-slice_fusion.17
  412.7 6.1 %fusion.30 = f32[512,512]{1,0:T(8,128)S(1)} fusion(f32[512,512]{1,0:T(8,128)S(1)} %get-tuple-element.425, bf16[640,512]{1,0:T(8,128)(2,1)S(1)} %get-tuple-element.467, s32[]{:T(128)S(6)} %select_n.679, f32[512]{0:T(512)S(1)} %bitcast.74, s32[]{:T(128)S(6)} %select_n.696, f32[512]{0:T(512)S(1)} %bitcast.75, s32[]{:T(128)S(6)} %select_n.697, ...), kind=kLoop, calls=%fused_computation.15.clone.1 | loop fusion | flops 17039360 | bytes 10526785 | tf_op jit(solution)/shard_map/while/body/eval_jaxpr/add | solution.py:38
  418.9 0.1 constant_dynamic-slice_fusion.17
  419.2 6.1 %fusion.30 = f32[512,512]{1,0:T(8,128)S(1)} fusion(f32[512,512]{1,0:T(8,128)S(1)} %get-tuple-element.425, bf16[640,512]{1,0:T(8,128)(2,1)S(1)} %get-tuple-element.467, s32[]{:T(128)S(6)} %select_n.679, f32[512]{0:T(512)S(1)} %bitcast.74, s32[]{:T(128)S(6)} %select_n.696, f32[512]{0:T(512)S(1)} %bitcast.75, s32[]{:T(128)S(6)} %select_n.697, ...), kind=kLoop, calls=%fused_computation.15.clone.1 | loop fusion | flops 17039360 | bytes 10526785 | tf_op jit(solution)/shard_map/while/body/eval_jaxpr/add | solution.py:38
  425.4 0.1 constant_dynamic-slice_fusion.17
  425.6 6.1 %fusion.30 = f32[512,512]{1,0:T(8,128)S(1)} fusion(f32[512,512]{1,0:T(8,128)S(1)} %get-tuple-element.425, bf16[640,512]{1,0:T(8,128)(2,1)S(1)} %get-tuple-element.467, s32[]{:T(128)S(6)} %select_n.679, f32[512]{0:T(512)S(1)} %bitcast.74, s32[]{:T(128)S(6)} %select_n.696, f32[512]{0:T(512)S(1)} %bitcast.75, s32[]{:T(128)S(6)} %select_n.697, ...), kind=kLoop, calls=%fused_computation.15.clone.1 | loop fusion | flops 17039360 | bytes 10526785 | tf_op jit(solution)/shard_map/while/body/eval_jaxpr/add | solution.py:38
  431.8 0.1 constant_dynamic-slice_fusion.17
  432.1 6.1 %fusion.30 = f32[512,512]{1,0:T(8,128)S(1)} fusion(f32[512,512]{1,0:T(8,128)S(1)} %get-tuple-element.425, bf16[640,512]{1,0:T(8,128)(2,1)S(1)} %get-tuple-element.467, s32[]{:T(128)S(6)} %select_n.679, f32[512]{0:T(512)S(1)} %bitcast.74, s32[]{:T(128)S(6)} %select_n.696, f32[512]{0:T(512)S(1)} %bitcast.75, s32[]{:T(128)S(6)} %select_n.697, ...), kind=kLoop, calls=%fused_computation.15.clone.1 | loop fusion | flops 17039360 | bytes 10526785 | tf_op jit(solution)/shard_map/while/body/eval_jaxpr/add | solution.py:38
  438.3 0.1 constant_dynamic-slice_fusion.17
  438.6 6.1 %fusion.30 = f32[512,512]{1,0:T(8,128)S(1)} fusion(f32[512,512]{1,0:T(8,128)S(1)} %get-tuple-element.425, bf16[640,512]{1,0:T(8,128)(2,1)S(1)} %get-tuple-element.467, s32[]{:T(128)S(6)} %select_n.679, f32[512]{0:T(512)S(1)} %bitcast.74, s32[]{:T(128)S(6)} %select_n.696, f32[512]{0:T(512)S(1)} %bitcast.75, s32[]{:T(128)S(6)} %select_n.697, ...), kind=kLoop, calls=%fused_computation.15.clone.1 | loop fusion | flops 17039360 | bytes 10526785 | tf_op jit(solution)/shard_map/while/body/eval_jaxpr/add | solution.py:38
  444.8 0.1 constant_dynamic-slice_fusion.17
  445.1 6.1 %fusion.30 = f32[512,512]{1,0:T(8,128)S(1)} fusion(f32[512,512]{1,0:T(8,128)S(1)} %get-tuple-element.425, bf16[640,512]{1,0:T(8,128)(2,1)S(1)} %get-tuple-element.467, s32[]{:T(128)S(6)} %select_n.679, f32[512]{0:T(512)S(1)} %bitcast.74, s32[]{:T(128)S(6)} %select_n.696, f32[512]{0:T(512)S(1)} %bitcast.75, s32[]{:T(128)S(6)} %select_n.697, ...), kind=kLoop, calls=%fused_computation.15.clone.1 | loop fusion | flops 17039360 | bytes 10526785 | tf_op jit(solution)/shard_map/while/body/eval_jaxpr/add | solution.py:38
  451.2 0.3 copy.23
  451.5 17.6 %all-gather.8.cloned.1.call-done = bf16[4096,512]{1,0:T(8,128)(2,1)} async-done(((bf16[128,512]{1,0:T(8,128)(2,1)}), bf16[4096,512]{1,0:T(8,128)(2,1)}) %all-gather.8.cloned.1.call-update) | async-done | bytes 4194320 | tf_op jit(solution)/shard_map/all_gather | solution.py:61
  469.2 6.9 %convolution_convert_fusion = bf16[512,4096]{1,0:T(8,128)(2,1)} fusion(bf16[4096,512]{1,0:T(8,128)(2,1)} %all-gather.8.cloned.1.call-done, f32[512,512]{0,1:T(8,128)S(1)} %copy.23, f32[512,3,512]{0,2,1:T(8,128)} %copy-done), kind=kOutput, calls=%fused_computation.48 | convolution fusion | flops 2150105088 | bytes 10485760 | tf_op jit(solution)/shard_map/dot_general | solution.py:80
  476.1 0.0 reduce-scatter.2.cloned.1.call-update
  476.1 50.6 %reduce-scatter.2.cloned.1.call-done = bf16[64,4096]{1,0:T(8,128)(2,1)} async-done(((bf16[512,4096]{1,0:T(8,128)(2,1)}), bf16[64,4096]{1,0:T(8,128)(2,1)}) %reduce-scatter.2.cloned.1.call-update) | async-done | bytes 524304 | tf_op jit(solution)/shard_map/reduce_scatter | solution.py:79
  526.8 0.0 copy-done.1
  526.8 2.0 fusion.18
  (20 shorter events, 0.4 us)
Async XLA Ops:
  6.5 6.2 %copy-start.6 = (s32[64]{0:T(128)S(1)}, s32[64]{0:T(128)}, u32[]{:S(2)}) copy-start(s32[64]{0:T(128)} %param.15) | copy-start | bytes 772
  6.5 6.7 %copy-start.4 = (f32[3,3,512]{2,1,0:T(4,128)S(1)}, f32[3,3,512]{2,1,0:T(4,128)}, u32[]{:S(2)}) copy-start(f32[3,3,512]{2,1,0:T(4,128)} %param.12) | copy-start | bytes 55300
  6.5 6.7 %copy-start.5 = (f32[512]{0:T(512)S(1)}, f32[512]{0:T(512)}, u32[]{:S(2)}) copy-start(f32[512]{0:T(512)} %param.14) | copy-start | bytes 6148
  6.5 6.7 %copy-start.3 = (f32[128,512]{1,0:T(8,128)S(1)}, f32[128,512]{1,0:T(8,128)}, u32[]{:S(2)}) copy-start(f32[128,512]{1,0:T(8,128)} %param.13) | copy-start | bytes 786436
  6.5 61.0 %all-gather.4.cloned.1.call-start = ((), (), s32[]{:S(2)}) async-start(), calls=%async_computation.1 | async-start | bytes 4718592 | tf_op jit(solution)/shard_map/all_gather | solution.py:56
  9.9 337.0 %all-gather.6.cloned.1.call-start = ((), (), s32[]{:S(2)}) async-start(), calls=%async_computation.2 | async-start | bytes 12976128 | tf_op jit(solution)/shard_map/all_gather | solution.py:57
  11.9 457.2 %all-gather.8.cloned.1.call-start = ((), (), s32[]{:S(2)}) async-start(), calls=%async_computation.3 | async-start | bytes 4325376 | tf_op jit(solution)/shard_map/all_gather | solution.py:61
  12.7 514.1 %reduce-scatter.2.cloned.1.call-start = ((), (), s32[]{:S(2)}) async-start(), calls=%async_computation.4 | async-start | bytes 4718592 | tf_op jit(solution)/shard_map/reduce_scatter | solution.py:79
  357.9 3.5 copy-start.2
  359.2 23.5 %collective-permute-start = (bf16[2,3,512]{0,2,1:T(8,128)(2,1)}, bf16[2,3,512]{0,2,1:T(8,128)(2,1)}, u32[]{:S(2)}, u32[]{:S(2)}) collective-permute-start(bf16[2,3,512]{0,2,1:T(8,128)(2,1)} %bitcast.5), channel_id=1, source_target_pairs={{0,8},{8,16},{16,24},{24,32},{32,40},{40,48},{48,56},{56,64},{64,7... | collective-permute-start | bytes 18440 | tf_op jit(solution)/shard_map/ppermute | solution.py:10
  386.6 12.4 %copy-start = (f32[512,3,512]{0,2,1:T(8,128)}, f32[512,3,512]{0,2,1:T(8,128)S(1)}, u32[]{:S(2)}) copy-start(f32[512,3,512]{0,2,1:T(8,128)S(1)} %select_add_fusion.1) | copy-start | bytes 9437188
  386.8 12.2 %collective-permute-start.1 = (bf16[128,512]{0,1:T(8,128)(2,1)S(1)}, bf16[128,512]{0,1:T(8,128)(2,1)S(1)}, u32[]{:S(2)}, u32[]{:S(2)}) collective-permute-start(bf16[128,512]{0,1:T(8,128)(2,1)S(1)} %slice_bitcast_fusion.1), channel_id=1, source_target_pairs={{0,8},{8,16},{16,24},{24,32},{32,40},{40,48},{48,56},{56,64},{64,7... | collective-permute-start | bytes 393224 | tf_op jit(solution)/shard_map/ppermute | solution.py:10
  476.1 50.6 %copy-start.1 = (bf16[64,4096]{1,0:T(8,128)(2,1)S(1)}, bf16[64,4096]{1,0:T(8,128)(2,1)}, u32[]{:S(2)}) copy-start(bf16[64,4096]{1,0:T(8,128)(2,1)} %param.9) | copy-start | bytes 1572868
Sparse Core Ops, SparseCore 0:
  10.1 57.4 all-gather.3
  70.8 276.1 all-gather.5
  350.4 118.7 all-gather.7
  476.3 50.4 reduce-scatter.1
where the time goes:
time: 536 us; the launch traced here: 535 us
  waiting for transfers between devices  432 us (81%)
  other arithmetic  58.9 us (11%)
  matrix products  17.9 us (3%)
  between operations  13.4 us (2%)
  local copies, waits for them, and re-layouts  6.33 us (1%)
    all_gather x1, waiting for transfers between devices, body(): shard_piece = lax.all_gather(in_weight, 'fsdp', axis=0, tiled=True)  279 us
    all_gather x1, waiting for transfers between devices, body(): gathered = lax.all_gather(normed, 'tp', axis=0, tiled=True)  54.3 us
    reduce_scatter x1, waiting for transfers between devices, body(): lax.psum_scatter(lax.dot_general(gated_mix, out_full, (((1,), (1,)), ((),...  50.6 us
    add x8, other arithmetic, tap_group(): running + jnp.where(inside, weight_row * window.astype(jnp.float32), jnp....  48.6 us
    ppermute x2, waiting for transfers between devices, from_behind(): return lax.ppermute(value, axis, pairs)  29.4 us
    all_gather x1, waiting for transfers between devices, body(): out_full = lax.all_gather(out_weight, 'fsdp', axis=0, tiled=True)  17.6 us
    dot_general x1, matrix products, body(): jnp.dot(gathered, flat_piece, preferred_element_type=jnp.float32)  10.9 us
  transfers between devices with their start and end apart: 6, of which 6 were waited for; matrix products, arithmetic and copies ran while one was open for 13% of the time, Pallas kernels for 0%

commit v1 on v0

v1 whole, which is shorter than its diff:
```python
import jax
import jax.numpy as jnp
from jax import lax
from jax.sharding import Mesh
from jax.sharding import PartitionSpec as P

COL = ("zh", "zl", "c")


def doc_position(points, lengths):
    starts = jnp.cumsum(lengths) - lengths
    begins = jnp.max(jnp.where(starts[None, :] <= points[:, None], starts[None, :], 0), axis=1)
    return points - begins


def short_filter(extended, short_taps, positions, out_count):
    running = jnp.zeros((out_count,) + extended.shape[1:], jnp.float32)
    for tap_index in range(3):
        window = extended[2 - tap_index : 2 - tap_index + out_count].astype(jnp.float32)
        inside = (positions >= tap_index)[:, None, None]
        running = running + jnp.where(
            inside, short_taps[tap_index][None] * window, jnp.float32(0.0)
        )
    return running


def long_filter(extended, shaped, positions, out_count, tap_count):

    def tap_group(group_index, running):
        for inner in range(16):
            tap_index = group_index * 16 + inner
            window = lax.dynamic_slice_in_dim(extended, tap_count - tap_index, out_count, 0)
            weight_row = lax.dynamic_slice_in_dim(shaped, tap_index, 1, 0)
            inside = (positions >= tap_index)[:, None]
            running = running + jnp.where(
                inside, weight_row * window.astype(jnp.float32), jnp.float32(0.0)
            )
        return running

    zero_sum = jnp.zeros((out_count, shaped.shape[1]), jnp.float32)
    return lax.fori_loop(0, tap_count // 16, tap_group, zero_sum)


def swap_half(piece, zh, axis):
    width = piece.shape[axis] // 2
    lo = lax.slice_in_dim(piece, 0, width, axis=axis)
    hi = lax.slice_in_dim(piece, width, 2 * width, axis=axis)
    keep = jnp.where(zh == 0, lo, hi)
    give = jnp.where(zh == 0, hi, lo)
    got = lax.ppermute(give, "zh", [(0, 1), (1, 0)])
    first = jnp.where(zh == 0, keep, got)
    second = jnp.where(zh == 0, got, keep)
    return jnp.concatenate([first, second], 0)


def body(tokens, in_weight, out_weight, short_taps, filter_taps, decay_rate, doc_lengths):
    zh = lax.axis_index("zh")
    col_size = lax.axis_size("zh") * lax.axis_size("zl") * lax.axis_size("c")
    own_rows = tokens.shape[0]
    col_rows = own_rows * col_size
    half = in_weight.shape[2] // 2
    tap_count = filter_taps.shape[0]

    widened = tokens.astype(jnp.float32)
    normed = (
        widened * lax.rsqrt(jnp.mean(widened * widened, axis=1, keepdims=True) + 1e-06)
    ).astype(jnp.bfloat16)
    gathered = lax.all_gather(normed, COL, axis=0, tiled=True)

    in_piece = swap_half(in_weight, zh, 2)
    in_full = lax.all_gather(in_piece, "p", axis=0, tiled=True)
    out_piece = swap_half(out_weight, zh, 1)
    out_full = lax.all_gather(out_piece, "p", axis=0, tiled=True)

    flat_in = in_full.reshape(in_full.shape[0], 3 * half)
    projected = jnp.dot(gathered, flat_in, preferred_element_type=jnp.float32)
    projected = projected.astype(jnp.bfloat16).reshape(col_rows, 3, half)

    first_row = lax.axis_index("p") * col_rows
    own_points = first_row + jnp.arange(col_rows, dtype=jnp.int32)
    own_position = doc_position(own_points, doc_lengths)

    columns = lax.axis_size("p")
    ahead = [(i, i + 1) for i in range(columns - 1)]
    my_taps = lax.dynamic_slice_in_dim(short_taps, zh * half, half, 2)
    my_filter = lax.dynamic_slice_in_dim(filter_taps, zh * half, half, 1)
    my_decay = lax.dynamic_slice_in_dim(decay_rate, zh * half, half, 0)

    edge_rows = lax.ppermute(projected[col_rows - 2 :], "p", ahead)
    short_all = short_filter(
        jnp.concatenate([edge_rows, projected], 0), my_taps, own_position, col_rows
    )
    kv_product = (short_all[:, 1] * short_all[:, 2]).astype(jnp.bfloat16)
    tail_rows = lax.ppermute(kv_product[col_rows - tap_count :], "p", ahead)
    extended = jnp.concatenate([tail_rows, kv_product], 0)
    query = short_all[:, 0]
    shaped = my_filter * jnp.exp(
        -my_decay[None, :] * jnp.arange(tap_count, dtype=jnp.float32)[:, None]
    )
    long_mix = long_filter(extended, shaped, own_position, col_rows, tap_count)
    gated_mix = (query * long_mix).astype(jnp.bfloat16)
    summed = lax.psum_scatter(
        lax.dot_general(
            gated_mix, out_full, (((1,), (1,)), ((), ())), preferred_element_type=jnp.float32
        ).astype(jnp.bfloat16),
        COL,
        scatter_dimension=0,
        tiled=True,
    ).astype(jnp.float32)
    return (widened + summed).astype(jnp.bfloat16)


def solution(mesh):
    fsdp, tp = mesh.shape["fsdp"], mesh.shape["tp"]
    grid = mesh.devices.reshape(fsdp // 2, 2, tp // 2, 2)
    fine = Mesh(grid, ("p", "zh", "zl", "c"))
    rows = ("p", "zh", "zl", "c")
    chan = ("zl", "c")
    in_specs = (
        P(rows, None),
        P(("p", "zh"), None, chan),
        P(("p", "zh"), chan),
        P(None, None, chan),
        P(None, chan),
        P(chan),
        P(),
    )
    out_specs = P(rows, None)
    return jax.shard_map(body, mesh=fine, in_specs=in_specs, out_specs=out_specs, check_vma=False)
```

time: 536 us -> 329 us (0.61)
  waiting for transfers between devices: 432 us -> 205 us
  starting transfers between devices: 4.5 us -> 23.5 us
    all_gather x3, waiting for transfers between devices: 351 us -> 121 us  [the longest x1 63.8 us: body(): in_full = lax.all_gather(in_piece, 'p', axis=0, tiled=True)]
    reduce_scatter x1, waiting for transfers between devices: 50.6 us -> 71.4 us  [body(): lax.psum_scatter(lax.dot_general(gated_mix, out_full, (((1,), (1,)), ((),...]
    ppermute x2 -> x4, starting transfers between devices: 4.35 us -> 23.4 us  [the longest x2 16.4 us: swap_half(): got = lax.ppermute(give, 'zh', [(0, 1), (1, 0)])]
    ppermute x2 -> x4, waiting for transfers between devices: 29.4 us -> 12.6 us  [the longest x2 6.86 us: swap_half(): got = lax.ppermute(give, 'zh', [(0, 1), (1, 0)])]
  transfers between devices with their start and end apart: 6 -> 8, of which waited for: 6 -> 7; matrix products, arithmetic and copies ran while one was open for 13% -> 18% of each run, Pallas kernels for 0% -> 0%
where the time goes in v1:
time: 329 us; the launch traced here: 328 us
  waiting for transfers between devices  205 us (62%)
  other arithmetic  59.4 us (18%)
  starting transfers between devices  23.5 us (7%)
  matrix products  18.6 us (6%)
  between operations  13.4 us (4%)
  local copies, waits for them, and re-layouts  5.96 us (2%)
    reduce_scatter x1, waiting for transfers between devices, body(): lax.psum_scatter(lax.dot_general(gated_mix, out_full, (((1,), (1,)), ((),...  71.4 us
    all_gather x1, waiting for transfers between devices, body(): in_full = lax.all_gather(in_piece, 'p', axis=0, tiled=True)  63.8 us
    all_gather x1, waiting for transfers between devices, body(): gathered = lax.all_gather(normed, COL, axis=0, tiled=True)  57.4 us
    add x8, other arithmetic, tap_group(): running + jnp.where(inside, weight_row * window.astype(jnp.float32), jnp....  51.3 us
    ppermute x2, starting transfers between devices, swap_half(): got = lax.ppermute(give, 'zh', [(0, 1), (1, 0)])  16.4 us
    dot_general x1, matrix products, body(): projected = jnp.dot(gathered, flat_in, preferred_element_type=jnp.float32)  11 us
    dot_general x1, matrix products, body(): lax.dot_general(gated_mix, out_full, (((1,), (1,)), ((), ())), preferred_...  7.58 us
    ppermute x2, waiting for transfers between devices, swap_half(): got = lax.ppermute(give, 'zh', [(0, 1), (1, 0)])  6.86 us
  transfers between devices with their start and end apart: 8, of which 7 were waited for; matrix products, arithmetic and copies ran while one was open for 18% of the time, Pallas kernels for 0%

profile of v1, /device:TPU:2, one launch (start us, length us, event | category | flops | bytes accessed | tf_op | source)
XLA Modules:
  0.0 328.4 jit_solution(9179054055207928626)
XLA Ops:
  6.5 1.1 fusion.25
  7.7 0.0 copy-start.8
  7.7 0.0 copy-start.5
  7.7 0.0 copy-start.6
  7.7 0.2 copy.27
  7.9 0.2 copy.28
  8.1 7.3 %collective-permute-start = (bf16[128,3,256]{0,2,1:T(8,128)(2,1)S(1)}, bf16[128,3,256]{0,2,1:T(8,128)(2,1)S(1)}, u32[]{:S(2)}, u32[]{:S(2)}) collective-permute-start(bf16[128,3,256]{0,2,1:T(8,128)(2,1)S(1)} %broadcast_select_fusion.2), channel_id=1, source_target_pairs={{0,8},{8,0},{1,9},{9,1},{2,10},{10,2},{3,11},{11,3},{4,12},{12,4},... | collective-permute-start | bytes 589832 | tf_op jit(solution)/shard_map/ppermute | solution.py:50
  15.3 5.0 %collective-permute-done = bf16[128,3,256]{0,2,1:T(8,128)(2,1)S(1)} collective-permute-done((bf16[128,3,256]{0,2,1:T(8,128)(2,1)S(1)}, bf16[128,3,256]{0,2,1:T(8,128)(2,1)S(1)}, u32[]{:S(2)}, u32[]{:S(2)}) %collective-permute-start) | collective-permute-done | bytes 196640 | tf_op jit(solution)/shard_map/ppermute | solution.py:50
  20.4 0.8 pad_maximum_fusion.2
  21.2 0.0 all-gather.6.cloned.1.call-update
  21.2 0.0 all-gather.4.cloned.1.call-start
  21.3 0.0 copy-done.1
  21.3 0.2 fusion.16
  21.5 1.0 fusion.17
  22.4 0.0 all-gather.4.cloned.1.call-update
  22.5 0.0 all-gather.8.cloned.1.call-start
  22.5 9.2 %collective-permute-start.3 = (bf16[128,256]{1,0:T(8,128)(2,1)S(1)}, bf16[128,256]{1,0:T(8,128)(2,1)S(1)}, u32[]{:S(2)}, u32[]{:S(2)}) collective-permute-start(bf16[128,256]{1,0:T(8,128)(2,1)S(1)} %broadcast_select_fusion.6), channel_id=1, source_target_pairs={{0,8},{8,0},{1,9},{9,1},{2,10},{10,2},{3,11},{11,3},{4,12},{12,4},... | collective-permute-start | bytes 196616 | tf_op jit(solution)/shard_map/ppermute | solution.py:50
  31.7 0.1 copy.19
  31.8 0.1 reduce-window.9
  31.9 0.1 reduce
  32.0 0.1 dynamic-slice_negate_fusion
  32.1 0.1 select_reduce_fusion
  32.4 1.9 collective-permute-done.3
  34.2 63.8 %all-gather.6.cloned.1.call-done = bf16[4096,3,256]{0,2,1:T(8,128)(2,1)} async-done(((bf16[256,3,256]{0,2,1:T(8,128)(2,1)}), bf16[4096,3,256]{0,2,1:T(8,128)(2,1)}) %all-gather.6.cloned.1.call-update) | async-done | bytes 6291472 | tf_op jit(solution)/shard_map/all_gather | solution.py:71
  98.1 57.4 %all-gather.4.cloned.1.call-done = bf16[1024,4096]{1,0:T(8,128)(2,1)} async-done(((bf16[64,4096]{1,0:T(8,128)(2,1)}), bf16[1024,4096]{1,0:T(8,128)(2,1)}) %all-gather.4.cloned.1.call-update) | async-done | bytes 8388624 | tf_op jit(solution)/shard_map/all_gather | solution.py:68
  155.5 11.0 %convolution_convert_fusion.1 = bf16[1024,768]{1,0:T(8,128)(2,1)S(1)} fusion(bf16[1024,4096]{1,0:T(8,128)(2,1)} %all-gather.4.cloned.1.call-done, bf16[4096,768]{0,1:T(8,128)(2,1)} %bitcast.91), kind=kOutput, calls=%fused_computation.52 | convolution fusion | flops 6443237376 | bytes 16252928 | tf_op jit(solution)/shard_map/dot_general | solution.py:76
  166.5 1.2 copy-done.3
  167.7 0.2 copy.26
  167.9 3.4 %collective-permute-start.1 = (bf16[2,3,256]{0,2,1:T(8,128)(2,1)S(1)}, bf16[2,3,256]{0,2,1:T(8,128)(2,1)S(1)}, u32[]{:S(2)}, u32[]{:S(2)}) collective-permute-start(bf16[2,3,256]{0,2,1:T(8,128)(2,1)S(1)} %bitcast.73), channel_id=1, source_target_pairs={{0,16},{16,32},{32,48},{48,64},{64,80},{80,96},{96,112},{112,128},... | collective-permute-start | bytes 9224 | tf_op jit(solution)/shard_map/ppermute | solution.py:89
  171.2 0.7 pad_maximum_fusion.3
  171.9 0.0 all-gather.8.cloned.1.call-update
  171.9 0.0 reduce-scatter.2.cloned.1.call-start
  172.0 1.7 copy.22
  173.7 3.1 collective-permute-done.1
  176.8 2.3 select_add_fusion.1
  179.1 0.1 fusion.19
  179.2 3.6 %collective-permute-start.2 = (bf16[128,256]{0,1:T(8,128)(2,1)S(1)}, bf16[128,256]{0,1:T(8,128)(2,1)S(1)}, u32[]{:S(2)}, u32[]{:S(2)}) collective-permute-start(bf16[128,256]{0,1:T(8,128)(2,1)S(1)} %slice_bitcast_fusion.1), channel_id=1, source_target_pairs={{0,16},{16,32},{32,48},{48,64},{64,80},{80,96},{96,112},{112,128},... | collective-permute-start | bytes 196616 | tf_op jit(solution)/shard_map/ppermute | solution.py:94
  182.8 0.1 fusion.29
  182.9 2.7 collective-permute-done.2
  185.6 0.1 pad_maximum_fusion.1
  185.7 0.2 copy.24
  186.0 54.6 %while.17 = (s32[]{:T(128)}, f32[1024,256]{1,0:T(8,128)S(1)}, s32[1024]{0:T(1024)S(1)}, f32[128,256]{1,0:T(8,128)S(1)}, bf16[1152,256]{1,0:T(8,128)(2,1)S(1)}, /...) while((s32[]{:T(128)}, f32[1024,256]{1,0:T(8,128)S(1)}, ...), condition=%wide.region_4.5_spmd.clone, body=%wide.region_3.4_spmd.clone.sunk | while | flops 17055876 | bytes 10573783 | solution.py:41
  186.1 0.1 constant_dynamic-slice_fusion.17
  186.3 6.4 %fusion.31 = f32[1024,256]{1,0:T(8,128)S(1)} fusion(f32[1024,256]{1,0:T(8,128)S(1)} %get-tuple-element.431, bf16[1152,256]{1,0:T(8,128)(2,1)S(1)} %get-tuple-element.473, s32[]{:T(128)S(6)} %select_n.767, f32[256]{0:T(256)S(1)} %bitcast.75, s32[]{:T(128)S(6)} %select_n.784, f32[256]{0:T(256)S(1)} %bitcast.76, s32[]{:T(128)S(6)} %select_n.785, ...), kind=kLoop, calls=%fused_computation.15.clone.1 | loop fusion | flops 17039360 | bytes 10518593 | tf_op jit(solution)/shard_map/while/body/eval_jaxpr/add | solution.py:35
  192.9 0.1 constant_dynamic-slice_fusion.17
  193.2 6.4 %fusion.31 = f32[1024,256]{1,0:T(8,128)S(1)} fusion(f32[1024,256]{1,0:T(8,128)S(1)} %get-tuple-element.431, bf16[1152,256]{1,0:T(8,128)(2,1)S(1)} %get-tuple-element.473, s32[]{:T(128)S(6)} %select_n.767, f32[256]{0:T(256)S(1)} %bitcast.75, s32[]{:T(128)S(6)} %select_n.784, f32[256]{0:T(256)S(1)} %bitcast.76, s32[]{:T(128)S(6)} %select_n.785, ...), kind=kLoop, calls=%fused_computation.15.clone.1 | loop fusion | flops 17039360 | bytes 10518593 | tf_op jit(solution)/shard_map/while/body/eval_jaxpr/add | solution.py:35
  199.7 0.1 constant_dynamic-slice_fusion.17
  200.0 6.4 %fusion.31 = f32[1024,256]{1,0:T(8,128)S(1)} fusion(f32[1024,256]{1,0:T(8,128)S(1)} %get-tuple-element.431, bf16[1152,256]{1,0:T(8,128)(2,1)S(1)} %get-tuple-element.473, s32[]{:T(128)S(6)} %select_n.767, f32[256]{0:T(256)S(1)} %bitcast.75, s32[]{:T(128)S(6)} %select_n.784, f32[256]{0:T(256)S(1)} %bitcast.76, s32[]{:T(128)S(6)} %select_n.785, ...), kind=kLoop, calls=%fused_computation.15.clone.1 | loop fusion | flops 17039360 | bytes 10518593 | tf_op jit(solution)/shard_map/while/body/eval_jaxpr/add | solution.py:35
  206.6 0.1 constant_dynamic-slice_fusion.17
  206.8 6.4 %fusion.31 = f32[1024,256]{1,0:T(8,128)S(1)} fusion(f32[1024,256]{1,0:T(8,128)S(1)} %get-tuple-element.431, bf16[1152,256]{1,0:T(8,128)(2,1)S(1)} %get-tuple-element.473, s32[]{:T(128)S(6)} %select_n.767, f32[256]{0:T(256)S(1)} %bitcast.75, s32[]{:T(128)S(6)} %select_n.784, f32[256]{0:T(256)S(1)} %bitcast.76, s32[]{:T(128)S(6)} %select_n.785, ...), kind=kLoop, calls=%fused_computation.15.clone.1 | loop fusion | flops 17039360 | bytes 10518593 | tf_op jit(solution)/shard_map/while/body/eval_jaxpr/add | solution.py:35
  213.4 0.1 constant_dynamic-slice_fusion.17
  213.7 6.4 %fusion.31 = f32[1024,256]{1,0:T(8,128)S(1)} fusion(f32[1024,256]{1,0:T(8,128)S(1)} %get-tuple-element.431, bf16[1152,256]{1,0:T(8,128)(2,1)S(1)} %get-tuple-element.473, s32[]{:T(128)S(6)} %select_n.767, f32[256]{0:T(256)S(1)} %bitcast.75, s32[]{:T(128)S(6)} %select_n.784, f32[256]{0:T(256)S(1)} %bitcast.76, s32[]{:T(128)S(6)} %select_n.785, ...), kind=kLoop, calls=%fused_computation.15.clone.1 | loop fusion | flops 17039360 | bytes 10518593 | tf_op jit(solution)/shard_map/while/body/eval_jaxpr/add | solution.py:35
  220.2 0.1 constant_dynamic-slice_fusion.17
  220.5 6.4 %fusion.31 = f32[1024,256]{1,0:T(8,128)S(1)} fusion(f32[1024,256]{1,0:T(8,128)S(1)} %get-tuple-element.431, bf16[1152,256]{1,0:T(8,128)(2,1)S(1)} %get-tuple-element.473, s32[]{:T(128)S(6)} %select_n.767, f32[256]{0:T(256)S(1)} %bitcast.75, s32[]{:T(128)S(6)} %select_n.784, f32[256]{0:T(256)S(1)} %bitcast.76, s32[]{:T(128)S(6)} %select_n.785, ...), kind=kLoop, calls=%fused_computation.15.clone.1 | loop fusion | flops 17039360 | bytes 10518593 | tf_op jit(solution)/shard_map/while/body/eval_jaxpr/add | solution.py:35
  227.0 0.1 constant_dynamic-slice_fusion.17
  227.3 6.4 %fusion.31 = f32[1024,256]{1,0:T(8,128)S(1)} fusion(f32[1024,256]{1,0:T(8,128)S(1)} %get-tuple-element.431, bf16[1152,256]{1,0:T(8,128)(2,1)S(1)} %get-tuple-element.473, s32[]{:T(128)S(6)} %select_n.767, f32[256]{0:T(256)S(1)} %bitcast.75, s32[]{:T(128)S(6)} %select_n.784, f32[256]{0:T(256)S(1)} %bitcast.76, s32[]{:T(128)S(6)} %select_n.785, ...), kind=kLoop, calls=%fused_computation.15.clone.1 | loop fusion | flops 17039360 | bytes 10518593 | tf_op jit(solution)/shard_map/while/body/eval_jaxpr/add | solution.py:35
  233.9 0.1 constant_dynamic-slice_fusion.17
  234.2 6.4 %fusion.31 = f32[1024,256]{1,0:T(8,128)S(1)} fusion(f32[1024,256]{1,0:T(8,128)S(1)} %get-tuple-element.431, bf16[1152,256]{1,0:T(8,128)(2,1)S(1)} %get-tuple-element.473, s32[]{:T(128)S(6)} %select_n.767, f32[256]{0:T(256)S(1)} %bitcast.75, s32[]{:T(128)S(6)} %select_n.784, f32[256]{0:T(256)S(1)} %bitcast.76, s32[]{:T(128)S(6)} %select_n.785, ...), kind=kLoop, calls=%fused_computation.15.clone.1 | loop fusion | flops 17039360 | bytes 10518593 | tf_op jit(solution)/shard_map/while/body/eval_jaxpr/add | solution.py:35
  240.6 0.3 copy.25
  240.9 0.0 all-gather.8.cloned.1.call-done
  240.9 7.6 %convolution_convert_fusion = bf16[1024,4096]{1,0:T(8,128)(2,1)} fusion(bf16[4096,256]{1,0:T(8,128)(2,1)} %all-gather.8.cloned.1.call-done, f32[1024,256]{0,1:T(8,128)S(1)} %copy.25, f32[1024,3,256]{0,2,1:T(8,128)} %copy-done), kind=kOutput, calls=%fused_computation.48 | convolution fusion | flops 2152202240 | bytes 12582912 | tf_op jit(solution)/shard_map/dot_general | solution.py:103
  248.5 0.0 reduce-scatter.2.cloned.1.call-update
  248.5 71.4 %reduce-scatter.2.cloned.1.call-done = bf16[64,4096]{1,0:T(8,128)(2,1)} async-done(((bf16[1024,4096]{1,0:T(8,128)(2,1)}), bf16[64,4096]{1,0:T(8,128)(2,1)}) %reduce-scatter.2.cloned.1.call-update) | async-done | bytes 524304 | tf_op jit(solution)/shard_map/reduce_scatter | solution.py:102
  319.9 2.0 fusion.18
  (36 shorter events, 0.6 us)
Async XLA Ops:
  6.5 14.7 %copy-start.1 = (bf16[64,4096]{1,0:T(8,128)(2,1)S(1)}, bf16[64,4096]{1,0:T(8,128)(2,1)}, u32[]{:S(2)}) copy-start(bf16[64,4096]{1,0:T(8,128)(2,1)} %param.9) | copy-start | bytes 1572868
  6.5 91.5 %all-gather.6.cloned.1.call-start = ((), (), s32[]{:S(2)}) async-start(), calls=%async_computation.2 | async-start | bytes 6684672 | tf_op jit(solution)/shard_map/all_gather | solution.py:71
  6.5 16.0 %copy-start.4 = (bf16[128,512]{1,0:T(8,128)(2,1)S(1)}, bf16[128,512]{1,0:T(8,128)(2,1)}, u32[]{:S(2)}) copy-start(bf16[128,512]{1,0:T(8,128)(2,1)} %param.11) | copy-start | bytes 393220
  6.5 25.2 %copy-start.7 = (s32[64]{0:T(128)S(1)}, s32[64]{0:T(128)}, u32[]{:S(2)}) copy-start(s32[64]{0:T(128)} %param.15) | copy-start | bytes 772
  7.7 24.4 %copy-start.8 = (f32[512]{0:T(512)S(1)}, f32[512]{0:T(512)}, u32[]{:S(2)}) copy-start(f32[512]{0:T(512)} %param.14) | copy-start | bytes 6148
  7.7 24.6 %copy-start.5 = (f32[128,512]{1,0:T(8,128)S(1)}, f32[128,512]{1,0:T(8,128)}, u32[]{:S(2)}) copy-start(f32[128,512]{1,0:T(8,128)} %param.13) | copy-start | bytes 786436
  7.7 24.6 %copy-start.6 = (f32[3,3,512]{2,1,0:T(4,128)S(1)}, f32[3,3,512]{2,1,0:T(4,128)}, u32[]{:S(2)}) copy-start(f32[3,3,512]{2,1,0:T(4,128)} %param.12) | copy-start | bytes 55300
  8.1 12.3 %collective-permute-start = (bf16[128,3,256]{0,2,1:T(8,128)(2,1)S(1)}, bf16[128,3,256]{0,2,1:T(8,128)(2,1)S(1)}, u32[]{:S(2)}, u32[]{:S(2)}) collective-permute-start(bf16[128,3,256]{0,2,1:T(8,128)(2,1)S(1)} %broadcast_select_fusion.2), channel_id=1, source_target_pairs={{0,8},{8,0},{1,9},{9,1},{2,10},{10,2},{3,11},{11,3},{4,12},{12,4},... | collective-permute-start | bytes 589832 | tf_op jit(solution)/shard_map/ppermute | solution.py:50
  21.2 134.3 %all-gather.4.cloned.1.call-start = ((), (), s32[]{:S(2)}) async-start(), calls=%async_computation.1 | async-start | bytes 8912896 | tf_op jit(solution)/shard_map/all_gather | solution.py:68
  22.5 218.5 %all-gather.8.cloned.1.call-start = ((), (), s32[]{:S(2)}) async-start(), calls=%async_computation.3 | async-start | bytes 2228224 | tf_op jit(solution)/shard_map/all_gather | solution.py:73
  22.5 11.7 %collective-permute-start.3 = (bf16[128,256]{1,0:T(8,128)(2,1)S(1)}, bf16[128,256]{1,0:T(8,128)(2,1)S(1)}, u32[]{:S(2)}, u32[]{:S(2)}) collective-permute-start(bf16[128,256]{1,0:T(8,128)(2,1)S(1)} %broadcast_select_fusion.6), channel_id=1, source_target_pairs={{0,8},{8,0},{1,9},{9,1},{2,10},{10,2},{3,11},{11,3},{4,12},{12,4},... | collective-permute-start | bytes 196616 | tf_op jit(solution)/shard_map/ppermute | solution.py:50
  166.5 1.2 copy-start.3
  167.9 8.9 %collective-permute-start.1 = (bf16[2,3,256]{0,2,1:T(8,128)(2,1)S(1)}, bf16[2,3,256]{0,2,1:T(8,128)(2,1)S(1)}, u32[]{:S(2)}, u32[]{:S(2)}) collective-permute-start(bf16[2,3,256]{0,2,1:T(8,128)(2,1)S(1)} %bitcast.73), channel_id=1, source_target_pairs={{0,16},{16,32},{32,48},{48,64},{64,80},{80,96},{96,112},{112,128},... | collective-permute-start | bytes 9224 | tf_op jit(solution)/shard_map/ppermute | solution.py:89
  171.9 148.0 %reduce-scatter.2.cloned.1.call-start = ((), (), s32[]{:S(2)}) async-start(), calls=%async_computation.4 | async-start | bytes 8912896 | tf_op jit(solution)/shard_map/reduce_scatter | solution.py:102
  179.1 6.6 %copy-start = (f32[1024,3,256]{0,2,1:T(8,128)}, f32[1024,3,256]{0,2,1:T(8,128)S(1)}, u32[]{:S(2)}) copy-start(f32[1024,3,256]{0,2,1:T(8,128)S(1)} %select_add_fusion.1) | copy-start | bytes 9437188
  179.2 6.4 %collective-permute-start.2 = (bf16[128,256]{0,1:T(8,128)(2,1)S(1)}, bf16[128,256]{0,1:T(8,128)(2,1)S(1)}, u32[]{:S(2)}, u32[]{:S(2)}) collective-permute-start(bf16[128,256]{0,1:T(8,128)(2,1)S(1)} %slice_bitcast_fusion.1), channel_id=1, source_target_pairs={{0,16},{16,32},{32,48},{48,64},{64,80},{80,96},{96,112},{112,128},... | collective-permute-start | bytes 196616 | tf_op jit(solution)/shard_map/ppermute | solution.py:94
  248.5 71.4 %copy-start.2 = (bf16[64,4096]{1,0:T(8,128)(2,1)S(1)}, bf16[64,4096]{1,0:T(8,128)(2,1)}, u32[]{:S(2)}) copy-start(bf16[64,4096]{1,0:T(8,128)(2,1)} %param.9) | copy-start | bytes 1572868
Sparse Core Ops, SparseCore 0:
  21.3 76.6 all-gather.5
  99.9 55.5 all-gather.3
  172.1 47.8 all-gather.7
  248.7 71.2 reduce-scatter.1

commit v2 on v1

--- a/solution.py
+++ b/solution.py
@@ -53,6 +53,25 @@
     return jnp.concatenate([first, second], 0)
 
 
+def z_ring_gather(block):
+    nz = lax.axis_size("zh") * lax.axis_size("zl")
+    z = lax.axis_index("zh") * lax.axis_size("zl") + lax.axis_index("zl")
+    right = [(i, (i + 1) % nz) for i in range(nz)]
+    left = [(i, (i - 1) % nz) for i in range(nz)]
+    by_offset = {0: block}
+    going_right, going_left = block, block
+    for step in range(1, nz // 2 + 1):
+        going_right = lax.ppermute(going_right, ("zh", "zl"), right)
+        by_offset[-step] = going_right
+        if step < nz - step:
+            going_left = lax.ppermute(going_left, ("zh", "zl"), left)
+            by_offset[step] = going_left
+    lowest = -(nz // 2)
+    relative = jnp.stack([by_offset[lowest + i] for i in range(nz)], 0)
+    pick = (jnp.arange(nz, dtype=jnp.int32) - z - lowest) % nz
+    return jnp.take(relative, pick, axis=0)
+
+
 def body(tokens, in_weight, out_weight, short_taps, filter_taps, decay_rate, doc_lengths):
     zh = lax.axis_index("zh")
     col_size = lax.axis_size("zh") * lax.axis_size("zl") * lax.axis_size("c")
@@ -65,7 +84,7 @@
     normed = (
         widened * lax.rsqrt(jnp.mean(widened * widened, axis=1, keepdims=True) + 1e-06)
     ).astype(jnp.bfloat16)
-    gathered = lax.all_gather(normed, COL, axis=0, tiled=True)
+    gathered = z_ring_gather(normed)
 
     in_piece = swap_half(in_weight, zh, 2)
     in_full = lax.all_gather(in_piece, "p", axis=0, tiled=True)
@@ -73,8 +92,20 @@
     out_full = lax.all_gather(out_piece, "p", axis=0, tiled=True)
 
     flat_in = in_full.reshape(in_full.shape[0], 3 * half)
-    projected = jnp.dot(gathered, flat_in, preferred_element_type=jnp.float32)
-    projected = projected.astype(jnp.bfloat16).reshape(col_rows, 3, half)
+    nz = gathered.shape[0]
+
+    def project(rows):
+        flat = rows.reshape(nz * own_rows, rows.shape[2])
+        out = jnp.dot(flat, flat_in, preferred_element_type=jnp.float32)
+        return out.astype(jnp.bfloat16).reshape(nz, own_rows, 3 * half)
+
+    partner_rows = lax.ppermute(gathered, "c", [(0, 1), (1, 0)])
+    from_mine = project(gathered)
+    from_partner = project(partner_rows)
+    core = lax.axis_index("c")
+    first = jnp.where(core == 0, from_mine, from_partner)
+    second = jnp.where(core == 0, from_partner, from_mine)
+    projected = jnp.stack([first, second], 1).reshape(col_rows, 3, half)
 
     first_row = lax.axis_index("p") * col_rows
     own_points = first_row + jnp.arange(col_rows, dtype=jnp.int32)

time: 329 us -> 327 us (level)
  waiting for transfers between devices: 205 us -> 164 us
  local copies, waits for them, and re-layouts: 5.96 us -> 27.4 us
  other arithmetic: 59.4 us -> 75.7 us
    all_gather x1 -> x0, waiting for transfers between devices: 57.4 us -> none  [body(): gathered = lax.all_gather(normed, COL, axis=0, tiled=True)]
    ppermute x0 -> x8, waiting for transfers between devices: none -> 46.5 us  [the longest x4 45.3 us: z_ring_gather(): going_right = lax.ppermute(going_right, ('zh', 'zl'), right)]
    all_gather x1, waiting for transfers between devices: 63.8 us -> 34.9 us  [body(): in_full = lax.all_gather(in_piece, 'p', axis=0, tiled=True)]
    ppermute x0 -> x8, starting transfers between devices: none -> 9.82 us  [the longest x3 7.89 us: z_ring_gather(): going_left = lax.ppermute(going_left, ('zh', 'zl'), left)]
    unnamed x21 -> x35, local copies, waits for them, and re-layouts: 1.78 us -> 10.9 us
    ppermute x2, starting transfers between devices: 16.4 us -> 8.51 us  [swap_half(): got = lax.ppermute(give, 'zh', [(0, 1), (1, 0)])]
    reshape x0 -> x1, local copies, waits for them, and re-layouts: none -> 5.27 us  [body(): projected = jnp.stack([first, second], 1).reshape(col_rows, 3, half)]
    gather x0 -> x1, local copies, waits for them, and re-layouts: none -> 5.11 us  [z_ring_gather(): return jnp.take(relative, pick, axis=0)]
  transfers between devices with their start and end apart: 8 -> 15, of which waited for: 7 -> 10; matrix products, arithmetic and copies ran while one was open for 18% -> 30% of each run, Pallas kernels for 0% -> 0%
where the time goes in v2:
time: 327 us; the launch traced here: 326 us
  waiting for transfers between devices  164 us (50%)
  other arithmetic  75.7 us (23%)
  local copies, waits for them, and re-layouts  27.4 us (8%)
  starting transfers between devices  23.1 us (7%)
  matrix products  20.6 us (6%)
  between operations  13.4 us (4%)
    reduce_scatter x1, waiting for transfers between devices, body(): lax.psum_scatter(lax.dot_general(gated_mix, out_full, (((1,), (1,)), ((),...  73.6 us
    add x8, other arithmetic, tap_group(): running + jnp.where(inside, weight_row * window.astype(jnp.float32), jnp....  51.3 us
    ppermute x4, waiting for transfers between devices, z_ring_gather(): going_right = lax.ppermute(going_right, ('zh', 'zl'), right)  45.3 us
    all_gather x1, waiting for transfers between devices, body(): in_full = lax.all_gather(in_piece, 'p', axis=0, tiled=True)  34.9 us
    dot_general x2, matrix products, project(): out = jnp.dot(flat, flat_in, preferred_element_type=jnp.float32)  13.3 us
    unnamed x35, local copies, waits for them, and re-layouts  10.9 us
    ppermute x2, starting transfers between devices, swap_half(): got = lax.ppermute(give, 'zh', [(0, 1), (1, 0)])  8.51 us
    ppermute x3, starting transfers between devices, z_ring_gather(): going_left = lax.ppermute(going_left, ('zh', 'zl'), left)  7.89 us
  transfers between devices with their start and end apart: 15, of which 10 were waited for; matrix products, arithmetic and copies ran while one was open for 30% of the time, Pallas kernels for 0%

profile of v2, /device:TPU:2, one launch (start us, length us, event | category | flops | bytes accessed | tf_op | source)
XLA Modules:
  0.0 326.3 jit_solution(14039087296554838327)
XLA Ops:
  6.5 1.2 fusion.15
  7.8 2.0 fusion.16
  9.8 1.9 collective-permute-start
  11.7 16.1 %collective-permute-done = bf16[64,4096]{1,0:T(8,128)(2,1)S(1)} collective-permute-done((bf16[64,4096]{1,0:T(8,128)(2,1)}, bf16[64,4096]{1,0:T(8,128)(2,1)S(1)}, u32[]{:S(2)}, u32[]{:S(2)}) %collective-permute-start) | collective-permute-done | bytes 524320 | tf_op jit(solution)/shard_map/ppermute | solution.py:64
  27.8 3.2 collective-permute-start.4
  31.0 11.1 %collective-permute-done.1 = bf16[64,4096]{1,0:T(8,128)(2,1)S(1)} collective-permute-done((bf16[64,4096]{1,0:T(8,128)(2,1)S(1)}, bf16[64,4096]{1,0:T(8,128)(2,1)S(1)}, u32[]{:S(2)}, u32[]{:S(2)}) %collective-permute-start.1) | collective-permute-done | bytes 524320 | tf_op jit(solution)/shard_map/ppermute | solution.py:64
  42.1 1.0 fusion.27
  43.1 0.2 copy.33
  43.3 0.2 copy.34
  43.5 4.1 %collective-permute-start.7 = (bf16[128,3,256]{0,2,1:T(8,128)(2,1)S(1)}, bf16[128,3,256]{0,2,1:T(8,128)(2,1)S(1)}, u32[]{:S(2)}, u32[]{:S(2)}) collective-permute-start(bf16[128,3,256]{0,2,1:T(8,128)(2,1)S(1)} %broadcast_select_fusion.5), channel_id=1, source_target_pairs={{0,8},{8,0},{1,9},{9,1},{2,10},{10,2},{3,11},{11,3},{4,12},{12,4},... | collective-permute-start | bytes 589832 | tf_op jit(solution)/shard_map/ppermute | solution.py:50
  47.6 3.3 %collective-permute-start.5 = (bf16[64,4096]{1,0:T(8,128)(2,1)S(1)}, bf16[64,4096]{1,0:T(8,128)(2,1)}, u32[]{:S(2)}, u32[]{:S(2)}) collective-permute-start(bf16[64,4096]{1,0:T(8,128)(2,1)S(1)} %collective-permute-done.4), channel_id=1, source_target_pairs={{0,14},{2,0},{4,2},{6,4},{8,6},{10,8},{12,10},{14,12},{1,15},{3,1}... | collective-permute-start | bytes 1572872 | tf_op jit(solution)/shard_map/ppermute | solution.py:67
  50.9 12.3 %collective-permute-done.2 = bf16[64,4096]{1,0:T(8,128)(2,1)} collective-permute-done((bf16[64,4096]{1,0:T(8,128)(2,1)S(1)}, bf16[64,4096]{1,0:T(8,128)(2,1)}, u32[]{:S(2)}, u32[]{:S(2)}) %collective-permute-start.2) | collective-permute-done | bytes 524320 | tf_op jit(solution)/shard_map/ppermute | solution.py:64
  63.3 3.9 %collective-permute-done.7 = bf16[128,3,256]{0,2,1:T(8,128)(2,1)S(1)} collective-permute-done((bf16[128,3,256]{0,2,1:T(8,128)(2,1)S(1)}, bf16[128,3,256]{0,2,1:T(8,128)(2,1)S(1)}, u32[]{:S(2)}, u32[]{:S(2)}) %collective-permute-start.7) | collective-permute-done | bytes 196640 | tf_op jit(solution)/shard_map/ppermute | solution.py:50
  67.3 0.8 pad_maximum_fusion.2
  68.1 1.4 collective-permute-start.6
  69.5 5.8 %collective-permute-done.3 = bf16[64,4096]{1,0:T(8,128)(2,1)} collective-permute-done((bf16[64,4096]{1,0:T(8,128)(2,1)}, bf16[64,4096]{1,0:T(8,128)(2,1)}, u32[]{:S(2)}, u32[]{:S(2)}) %collective-permute-start.3) | collective-permute-done | bytes 524320 | tf_op jit(solution)/shard_map/ppermute | solution.py:64
  75.3 1.9 bitcast_dynamic-update-slice_fusion.7
  77.2 1.9 bitcast_dynamic-update-slice_fusion.6
  79.1 0.8 bitcast_dynamic-update-slice_fusion.5
  79.9 0.9 bitcast_dynamic-update-slice_fusion.4
  80.8 1.0 bitcast_dynamic-update-slice_fusion.3
  81.8 0.8 bitcast_dynamic-update-slice_fusion.2
  82.7 1.9 bitcast_dynamic-update-slice_fusion.1
  84.5 0.9 bitcast_dynamic-update-slice_fusion
  85.4 5.1 %gather_fusion = bf16[8,64,4096]{2,1,0:T(8,128)(2,1)} fusion(bf16[8,64,4096]{2,1,0:T(8,128)(2,1)} %bitcast_dynamic-update-slice_fusion, s32[1024]{0:T(1024)S(1)} %pad_clamp_fusion), kind=kCustom, calls=%fused_computation | custom fusion | bytes 8388640 | tf_op jit(solution)/shard_map/jit(_take)/gather | solution.py:72
  90.5 4.8 %broadcast_select_fusion = bf16[8,64,4096]{2,1,0:T(8,128)(2,1)} fusion(bf16[8,64,4096]{2,1,0:T(8,128)(2,1)} %gather_fusion, pred[8]{0:T(512)(128)(4,1)S(1)} %compare_and_fusion), kind=kLoop, calls=%fused_computation.51 | loop fusion | flops 2097152 | bytes 8388616 | tf_op jit(solution)/shard_map/jit(_take)/select_n | solution.py:72
  95.3 4.4 %collective-permute-start.11 = (bf16[128,256]{1,0:T(8,128)(2,1)S(1)}, bf16[128,256]{1,0:T(8,128)(2,1)S(1)}, u32[]{:S(2)}, u32[]{:S(2)}) collective-permute-start(bf16[128,256]{1,0:T(8,128)(2,1)S(1)} %broadcast_select_fusion.9), channel_id=1, source_target_pairs={{0,8},{8,0},{1,9},{9,1},{2,10},{10,2},{3,11},{11,3},{4,12},{12,4},... | collective-permute-start | bytes 196616 | tf_op jit(solution)/shard_map/ppermute | solution.py:50
  99.7 0.1 copy.25
  99.8 0.1 reduce-window.9
  99.9 0.1 reduce
  100.1 0.1 select_reduce_fusion
  100.3 0.6 broadcast_compare_fusion.18
  100.9 0.6 broadcast_compare_fusion.17
  101.5 1.3 collective-permute-done.8
  102.8 34.9 %all-gather.3.cloned.1.call-done = bf16[4096,3,256]{0,2,1:T(8,128)(2,1)} async-done(((bf16[256,3,256]{0,2,1:T(8,128)(2,1)}), bf16[4096,3,256]{0,2,1:T(8,128)(2,1)}) %all-gather.3.cloned.1.call-update) | async-done | bytes 6291472 | tf_op jit(solution)/shard_map/all_gather | solution.py:90
  137.7 7.6 %convolution_convert_fusion.1 = bf16[512,768]{1,0:T(8,128)(2,1)S(1)} fusion(bf16[512,4096]{1,0:T(8,128)(2,1)} %bitcast.13, bf16[4096,768]{0,1:T(8,128)(2,1)} %bitcast.121), kind=kOutput, calls=%fused_computation.56 | convolution fusion | flops 3221618688 | bytes 11272192 | tf_op jit(solution)/shard_map/dot_general | solution.py:99
  145.4 5.7 %broadcast_select_fusion.2 = (bf16[512,768]{1,0:T(8,128)(2,1)S(1)}, bf16[512,768]{1,0:T(8,128)(2,1)S(1)}) fusion(bf16[512,768]{1,0:T(8,128)(2,1)S(1)} %convolution_convert_fusion.1, pred[]{:T(512)S(6)} %eq.6, bf16[512,4096]{1,0:T(8,128)(2,1)} %bitcast.11, bf16[4096,768]{0,1:T(8,128)(2,1)S(1)} %bitcast.122), kind=kOutput, calls=%fused_computation.66 | convolution fusion | flops 3222405120 | bytes 12845057 | tf_op jit(solution)/shard_map/dot_general | solution.py:99
  151.1 1.3 pad_maximum_fusion
  152.3 5.3 %reshape.301 = bf16[1024,3,256]{2,1,0:T(4,128)(2,1)} reshape(bf16[8,2,64,768]{3,2,1,0:T(8,128)(2,1)} %pad_maximum_fusion) | data formatting | bytes 3145728 | tf_op jit(solution)/shard_map/reshape | solution.py:108
  157.6 0.8 slice.62
  158.4 2.2 collective-permute-start.9
  160.6 3.3 %collective-permute-done.9 = bf16[2,3,256]{2,1,0:T(4,128)(2,1)S(1)} collective-permute-done((bf16[2,3,256]{2,1,0:T(4,128)(2,1)S(1)}, bf16[2,3,256]{2,1,0:T(4,128)(2,1)S(1)}, u32[]{:S(2)}, u32[]{:S(2)}) %collective-permute-start.9) | collective-permute-done | bytes 3104 | tf_op jit(solution)/shard_map/ppermute | solution.py:120
  163.9 2.4 constant_dynamic-update-slice_fusion
  166.4 6.3 %select_add_fusion.1 = f32[1024,3,256]{2,1,0:T(4,128)S(1)} fusion(bf16[1024,3,256]{2,1,0:T(4,128)(2,1)S(1)} %copy-done, bf16[1026,3,256]{2,1,0:T(4,128)(2,1)S(1)} %constant_dynamic-update-slice_fusion, f32[3,256]{1,0:T(4,128)S(1)} %get-tuple-element.287, f32[3,256]{1,0:T(4,128)S(1)} %get-tuple-element.286, f32[3,256]{1,0:T(4,128)S(1)} %get-tuple-element.285, ...), kind=kLoop, calls=%fused_computation.50 | loop fusion | flops 8650752 | bytes 7876608 | tf_op jit(solution)/shard_map/add | solution.py:21
  172.8 2.2 fusion.26
  174.9 1.0 copy-done.2
  175.9 0.1 slice.68
  176.1 2.3 collective-permute-start.10
  178.4 0.7 pad_maximum_fusion.3
  179.0 0.3 reduce-scatter.2.cloned.1.call-start
  179.3 1.3 copy.39
  180.6 1.6 collective-permute-done.10
  182.3 54.6 %while.17 = (s32[]{:T(128)}, f32[1024,256]{1,0:T(8,128)S(1)}, s32[1024]{0:T(1024)S(1)}, f32[128,256]{1,0:T(8,128)S(1)}, bf16[1152,256]{1,0:T(8,128)(2,1)S(1)}, /...) while((s32[]{:T(128)}, f32[1024,256]{1,0:T(8,128)S(1)}, ...), condition=%wide.region_4.5_spmd.clone, body=%wide.region_3.4_spmd.clone.sunk | while | flops 17055876 | bytes 10573783 | solution.py:41
  182.7 6.4 %fusion.34 = f32[1024,256]{1,0:T(8,128)S(1)} fusion(f32[1024,256]{1,0:T(8,128)S(1)} %get-tuple-element.425, bf16[1152,256]{1,0:T(8,128)(2,1)S(1)} %get-tuple-element.467, s32[]{:T(128)S(6)} %select_n.879, f32[256]{0:T(256)S(1)} %bitcast.104, s32[]{:T(128)S(6)} %select_n.896, f32[256]{0:T(256)S(1)} %bitcast.105, s32[]{:T(128)S(6)} %select_n.897, ...), kind=kLoop, calls=%fused_computation.16.clone.1 | loop fusion | flops 17039360 | bytes 10518593 | tf_op jit(solution)/shard_map/while/body/eval_jaxpr/add | solution.py:35
  189.5 6.4 %fusion.34 = f32[1024,256]{1,0:T(8,128)S(1)} fusion(f32[1024,256]{1,0:T(8,128)S(1)} %get-tuple-element.425, bf16[1152,256]{1,0:T(8,128)(2,1)S(1)} %get-tuple-element.467, s32[]{:T(128)S(6)} %select_n.879, f32[256]{0:T(256)S(1)} %bitcast.104, s32[]{:T(128)S(6)} %select_n.896, f32[256]{0:T(256)S(1)} %bitcast.105, s32[]{:T(128)S(6)} %select_n.897, ...), kind=kLoop, calls=%fused_computation.16.clone.1 | loop fusion | flops 17039360 | bytes 10518593 | tf_op jit(solution)/shard_map/while/body/eval_jaxpr/add | solution.py:35
  196.3 6.4 %fusion.34 = f32[1024,256]{1,0:T(8,128)S(1)} fusion(f32[1024,256]{1,0:T(8,128)S(1)} %get-tuple-element.425, bf16[1152,256]{1,0:T(8,128)(2,1)S(1)} %get-tuple-element.467, s32[]{:T(128)S(6)} %select_n.879, f32[256]{0:T(256)S(1)} %bitcast.104, s32[]{:T(128)S(6)} %select_n.896, f32[256]{0:T(256)S(1)} %bitcast.105, s32[]{:T(128)S(6)} %select_n.897, ...), kind=kLoop, calls=%fused_computation.16.clone.1 | loop fusion | flops 17039360 | bytes 10518593 | tf_op jit(solution)/shard_map/while/body/eval_jaxpr/add | solution.py:35
  203.2 6.4 %fusion.34 = f32[1024,256]{1,0:T(8,128)S(1)} fusion(f32[1024,256]{1,0:T(8,128)S(1)} %get-tuple-element.425, bf16[1152,256]{1,0:T(8,128)(2,1)S(1)} %get-tuple-element.467, s32[]{:T(128)S(6)} %select_n.879, f32[256]{0:T(256)S(1)} %bitcast.104, s32[]{:T(128)S(6)} %select_n.896, f32[256]{0:T(256)S(1)} %bitcast.105, s32[]{:T(128)S(6)} %select_n.897, ...), kind=kLoop, calls=%fused_computation.16.clone.1 | loop fusion | flops 17039360 | bytes 10518593 | tf_op jit(solution)/shard_map/while/body/eval_jaxpr/add | solution.py:35
  210.0 6.4 %fusion.34 = f32[1024,256]{1,0:T(8,128)S(1)} fusion(f32[1024,256]{1,0:T(8,128)S(1)} %get-tuple-element.425, bf16[1152,256]{1,0:T(8,128)(2,1)S(1)} %get-tuple-element.467, s32[]{:T(128)S(6)} %select_n.879, f32[256]{0:T(256)S(1)} %bitcast.104, s32[]{:T(128)S(6)} %select_n.896, f32[256]{0:T(256)S(1)} %bitcast.105, s32[]{:T(128)S(6)} %select_n.897, ...), kind=kLoop, calls=%fused_computation.16.clone.1 | loop fusion | flops 17039360 | bytes 10518593 | tf_op jit(solution)/shard_map/while/body/eval_jaxpr/add | solution.py:35
  216.8 6.4 %fusion.34 = f32[1024,256]{1,0:T(8,128)S(1)} fusion(f32[1024,256]{1,0:T(8,128)S(1)} %get-tuple-element.425, bf16[1152,256]{1,0:T(8,128)(2,1)S(1)} %get-tuple-element.467, s32[]{:T(128)S(6)} %select_n.879, f32[256]{0:T(256)S(1)} %bitcast.104, s32[]{:T(128)S(6)} %select_n.896, f32[256]{0:T(256)S(1)} %bitcast.105, s32[]{:T(128)S(6)} %select_n.897, ...), kind=kLoop, calls=%fused_computation.16.clone.1 | loop fusion | flops 17039360 | bytes 10518593 | tf_op jit(solution)/shard_map/while/body/eval_jaxpr/add | solution.py:35
  223.6 6.4 %fusion.34 = f32[1024,256]{1,0:T(8,128)S(1)} fusion(f32[1024,256]{1,0:T(8,128)S(1)} %get-tuple-element.425, bf16[1152,256]{1,0:T(8,128)(2,1)S(1)} %get-tuple-element.467, s32[]{:T(128)S(6)} %select_n.879, f32[256]{0:T(256)S(1)} %bitcast.104, s32[]{:T(128)S(6)} %select_n.896, f32[256]{0:T(256)S(1)} %bitcast.105, s32[]{:T(128)S(6)} %select_n.897, ...), kind=kLoop, calls=%fused_computation.16.clone.1 | loop fusion | flops 17039360 | bytes 10518593 | tf_op jit(solution)/shard_map/while/body/eval_jaxpr/add | solution.py:35
  230.5 6.4 %fusion.34 = f32[1024,256]{1,0:T(8,128)S(1)} fusion(f32[1024,256]{1,0:T(8,128)S(1)} %get-tuple-element.425, bf16[1152,256]{1,0:T(8,128)(2,1)S(1)} %get-tuple-element.467, s32[]{:T(128)S(6)} %select_n.879, f32[256]{0:T(256)S(1)} %bitcast.104, s32[]{:T(128)S(6)} %select_n.896, f32[256]{0:T(256)S(1)} %bitcast.105, s32[]{:T(128)S(6)} %select_n.897, ...), kind=kLoop, calls=%fused_computation.16.clone.1 | loop fusion | flops 17039360 | bytes 10518593 | tf_op jit(solution)/shard_map/while/body/eval_jaxpr/add | solution.py:35
  236.9 7.3 %convolution_convert_fusion = bf16[1024,4096]{1,0:T(8,128)(2,1)} fusion(bf16[4096,256]{1,0:T(8,128)(2,1)} %all-gather.5.cloned.1.call-done, f32[1024,256]{1,0:T(8,128)S(1)} %get-tuple-element.212, f32[1024,1,256]{2,1,0:T(1,128)S(1)} %get-tuple-element.275), kind=kOutput, calls=%fused_computation.49 | convolution fusion | flops 2152202240 | bytes 12582912 | tf_op jit(solution)/shard_map/dot_general | solution.py:134
  244.2 73.6 %reduce-scatter.2.cloned.1.call-done = bf16[64,4096]{1,0:T(8,128)(2,1)} async-done(((bf16[1024,4096]{1,0:T(8,128)(2,1)}), bf16[64,4096]{1,0:T(8,128)(2,1)}) %reduce-scatter.2.cloned.1.call-update) | async-done | bytes 524304 | tf_op jit(solution)/shard_map/reduce_scatter | solution.py:133
  317.8 2.0 fusion.17
  (70 shorter events, 1.5 us)
Async XLA Ops:
  6.5 131.2 %all-gather.3.cloned.1.call-start = ((), (), s32[]{:S(2)}) async-start(), calls=%async_computation.1 | async-start | bytes 6684672 | tf_op jit(solution)/shard_map/all_gather | solution.py:90
  9.8 18.0 %collective-permute-start = (bf16[64,4096]{1,0:T(8,128)(2,1)}, bf16[64,4096]{1,0:T(8,128)(2,1)S(1)}, u32[]{:S(2)}, u32[]{:S(2)}) collective-permute-start(bf16[64,4096]{1,0:T(8,128)(2,1)} %fusion.16), channel_id=1, source_target_pairs={{0,2},{2,4},{4,6},{6,8},{8,10},{10,12},{12,14},{14,0},{1,3},{3,5},... | collective-permute-start | bytes 1572872 | tf_op jit(solution)/shard_map/ppermute | solution.py:64
  27.8 14.3 %collective-permute-start.1 = (bf16[64,4096]{1,0:T(8,128)(2,1)S(1)}, bf16[64,4096]{1,0:T(8,128)(2,1)S(1)}, u32[]{:S(2)}, u32[]{:S(2)}) collective-permute-start(bf16[64,4096]{1,0:T(8,128)(2,1)S(1)} %collective-permute-done), channel_id=1, source_target_pairs={{0,2},{2,4},{4,6},{6,8},{8,10},{10,12},{12,14},{14,0},{1,3},{3,5},... | collective-permute-start | bytes 1572872 | tf_op jit(solution)/shard_map/ppermute | solution.py:64
  27.8 19.8 %collective-permute-start.4 = (bf16[64,4096]{1,0:T(8,128)(2,1)}, bf16[64,4096]{1,0:T(8,128)(2,1)S(1)}, u32[]{:S(2)}, u32[]{:S(2)}) collective-permute-start(bf16[64,4096]{1,0:T(8,128)(2,1)} %fusion.16), channel_id=1, source_target_pairs={{0,14},{2,0},{4,2},{6,4},{8,6},{10,8},{12,10},{14,12},{1,15},{3,1}... | collective-permute-start | bytes 1572872 | tf_op jit(solution)/shard_map/ppermute | solution.py:67
  31.0 49.8 %copy-start.1 = (bf16[64,4096]{1,0:T(8,128)(2,1)S(1)}, bf16[64,4096]{1,0:T(8,128)(2,1)}, u32[]{:S(2)}) copy-start(bf16[64,4096]{1,0:T(8,128)(2,1)} %param.9) | copy-start | bytes 1572868
  42.1 21.2 %collective-permute-start.2 = (bf16[64,4096]{1,0:T(8,128)(2,1)S(1)}, bf16[64,4096]{1,0:T(8,128)(2,1)}, u32[]{:S(2)}, u32[]{:S(2)}) collective-permute-start(bf16[64,4096]{1,0:T(8,128)(2,1)S(1)} %collective-permute-done.1), channel_id=1, source_target_pairs={{0,2},{2,4},{4,6},{6,8},{8,10},{10,12},{12,14},{14,0},{1,3},{3,5},... | collective-permute-start | bytes 1572872 | tf_op jit(solution)/shard_map/ppermute | solution.py:64
  43.5 23.7 %collective-permute-start.7 = (bf16[128,3,256]{0,2,1:T(8,128)(2,1)S(1)}, bf16[128,3,256]{0,2,1:T(8,128)(2,1)S(1)}, u32[]{:S(2)}, u32[]{:S(2)}) collective-permute-start(bf16[128,3,256]{0,2,1:T(8,128)(2,1)S(1)} %broadcast_select_fusion.5), channel_id=1, source_target_pairs={{0,8},{8,0},{1,9},{9,1},{2,10},{10,2},{3,11},{11,3},{4,12},{12,4},... | collective-permute-start | bytes 589832 | tf_op jit(solution)/shard_map/ppermute | solution.py:50
  47.6 20.5 %collective-permute-start.5 = (bf16[64,4096]{1,0:T(8,128)(2,1)S(1)}, bf16[64,4096]{1,0:T(8,128)(2,1)}, u32[]{:S(2)}, u32[]{:S(2)}) collective-permute-start(bf16[64,4096]{1,0:T(8,128)(2,1)S(1)} %collective-permute-done.4), channel_id=1, source_target_pairs={{0,14},{2,0},{4,2},{6,4},{8,6},{10,8},{12,10},{14,12},{1,15},{3,1}... | collective-permute-start | bytes 1572872 | tf_op jit(solution)/shard_map/ppermute | solution.py:67
  63.3 12.0 %collective-permute-start.3 = (bf16[64,4096]{1,0:T(8,128)(2,1)}, bf16[64,4096]{1,0:T(8,128)(2,1)}, u32[]{:S(2)}, u32[]{:S(2)}) collective-permute-start(bf16[64,4096]{1,0:T(8,128)(2,1)} %collective-permute-done.2), channel_id=1, source_target_pairs={{0,2},{2,4},{4,6},{6,8},{8,10},{10,12},{12,14},{14,0},{1,3},{3,5},... | collective-permute-start | bytes 1572872 | tf_op jit(solution)/shard_map/ppermute | solution.py:64
  68.1 168.8 %all-gather.5.cloned.1.call-start = ((), (), s32[]{:S(2)}) async-start(), calls=%async_computation.2 | async-start | bytes 2228224 | tf_op jit(solution)/shard_map/all_gather | solution.py:92
  68.1 16.4 %collective-permute-start.6 = (bf16[64,4096]{1,0:T(8,128)(2,1)}, bf16[64,4096]{1,0:T(8,128)(2,1)S(1)}, u32[]{:S(2)}, u32[]{:S(2)}) collective-permute-start(bf16[64,4096]{1,0:T(8,128)(2,1)} %collective-permute-done.5), channel_id=1, source_target_pairs={{0,14},{2,0},{4,2},{6,4},{8,6},{10,8},{12,10},{14,12},{1,15},{3,1}... | collective-permute-start | bytes 1572872 | tf_op jit(solution)/shard_map/ppermute | solution.py:67
  90.5 4.8 %copy-start.3 = (bf16[128,512]{1,0:T(8,128)(2,1)S(1)}, bf16[128,512]{1,0:T(8,128)(2,1)}, u32[]{:S(2)}) copy-start(bf16[128,512]{1,0:T(8,128)(2,1)} %param.11) | copy-start | bytes 393220
  90.5 9.2 %copy-start.9 = (s32[64]{0:T(128)S(1)}, s32[64]{0:T(128)}, u32[]{:S(2)}) copy-start(s32[64]{0:T(128)} %param.15) | copy-start | bytes 772
  90.5 9.5 %copy-start.10 = (f32[512]{0:T(512)S(1)}, f32[512]{0:T(512)}, u32[]{:S(2)}) copy-start(f32[512]{0:T(512)} %param.14) | copy-start | bytes 6148
  90.5 9.6 %copy-start.5 = (f32[3,3,512]{2,1,0:T(4,128)S(1)}, f32[3,3,512]{2,1,0:T(4,128)}, u32[]{:S(2)}) copy-start(f32[3,3,512]{2,1,0:T(4,128)} %param.12) | copy-start | bytes 55300
  90.5 11.0 %copy-start.4 = (f32[128,512]{1,0:T(8,128)S(1)}, f32[128,512]{1,0:T(8,128)}, u32[]{:S(2)}) copy-start(f32[128,512]{1,0:T(8,128)} %param.13) | copy-start | bytes 786436
  95.3 7.5 %collective-permute-start.8 = (bf16[8,64,4096]{2,1,0:T(8,128)(2,1)}, bf16[8,64,4096]{2,1,0:T(8,128)(2,1)}, u32[]{:S(2)}, u32[]{:S(2)}) collective-permute-start(bf16[8,64,4096]{2,1,0:T(8,128)(2,1)} %broadcast_select_fusion), channel_id=1, source_target_pairs={{0,1},{1,0},{2,3},{3,2},{4,5},{5,4},{6,7},{7,6},{8,9},{9,8},{10,11... | collective-permute-start | bytes 12582920 | tf_op jit(solution)/shard_map/ppermute | solution.py:102
  95.3 65.3 %collective-permute-start.11 = (bf16[128,256]{1,0:T(8,128)(2,1)S(1)}, bf16[128,256]{1,0:T(8,128)(2,1)S(1)}, u32[]{:S(2)}, u32[]{:S(2)}) collective-permute-start(bf16[128,256]{1,0:T(8,128)(2,1)S(1)} %broadcast_select_fusion.9), channel_id=1, source_target_pairs={{0,8},{8,0},{1,9},{9,1},{2,10},{10,2},{3,11},{11,3},{4,12},{12,4},... | collective-permute-start | bytes 196616 | tf_op jit(solution)/shard_map/ppermute | solution.py:50
  137.7 7.7 %copy-start.11 = (bf16[4096,3,256]{0,2,1:T(8,128)(2,1)S(1)}, bf16[4096,3,256]{0,2,1:T(8,128)(2,1)}, u32[]{:S(2)}) copy-start(bf16[4096,3,256]{0,2,1:T(8,128)(2,1)} %all-gather.3.cloned.1.call-done) | copy-start | bytes 18874372
  152.3 14.0 %copy-start.6 = (pred[1024]{0:T(1024)(128)(4,1)S(1)}, pred[1024]{0:T(1024)(128)(4,1)}, u32[]{:S(2)}) copy-start(pred[1024]{0:T(1024)(128)(4,1)} %get-tuple-element.241) | copy-start | bytes 3076
  152.3 14.0 %copy-start.7 = (pred[1024]{0:T(1024)(128)(4,1)S(1)}, pred[1024]{0:T(1024)(128)(4,1)}, u32[]{:S(2)}) copy-start(pred[1024]{0:T(1024)(128)(4,1)} %get-tuple-element.288) | copy-start | bytes 3076
  152.3 14.1 %copy-start.8 = (pred[1024]{0:T(1024)(128)(4,1)S(1)}, pred[1024]{0:T(1024)(128)(4,1)}, u32[]{:S(2)}) copy-start(pred[1024]{0:T(1024)(128)(4,1)} %get-tuple-element.289) | copy-start | bytes 3076
  157.6 8.8 %copy-start = (bf16[1024,3,256]{2,1,0:T(4,128)(2,1)S(1)}, bf16[1024,3,256]{2,1,0:T(4,128)(2,1)}, u32[]{:S(2)}) copy-start(bf16[1024,3,256]{2,1,0:T(4,128)(2,1)} %reshape.301) | copy-start | bytes 4718596
  158.4 5.5 %collective-permute-start.9 = (bf16[2,3,256]{2,1,0:T(4,128)(2,1)S(1)}, bf16[2,3,256]{2,1,0:T(4,128)(2,1)S(1)}, u32[]{:S(2)}, u32[]{:S(2)}) collective-permute-start(bf16[2,3,256]{2,1,0:T(4,128)(2,1)S(1)} %slice.62), channel_id=1, source_target_pairs={{0,16},{16,32},{32,48},{48,64},{64,80},{80,96},{96,112},{112,128},... | collective-permute-start | bytes 9224 | tf_op jit(solution)/shard_map/ppermute | solution.py:120
  174.9 1.0 copy-start.2
  176.1 6.2 %collective-permute-start.10 = (bf16[128,256]{1,0:T(8,128)(2,1)S(1)}, bf16[128,256]{1,0:T(8,128)(2,1)S(1)}, u32[]{:S(2)}, u32[]{:S(2)}) collective-permute-start(bf16[128,256]{1,0:T(8,128)(2,1)S(1)} %bitcast.119), channel_id=1, source_target_pairs={{0,16},{16,32},{32,48},{48,64},{64,80},{80,96},{96,112},{112,128},... | collective-permute-start | bytes 196616 | tf_op jit(solution)/shard_map/ppermute | solution.py:125
  179.0 138.7 %reduce-scatter.2.cloned.1.call-start = ((), (), s32[]{:S(2)}) async-start(), calls=%async_computation.3 | async-start | bytes 8912896 | tf_op jit(solution)/shard_map/reduce_scatter | solution.py:133
Sparse Core Ops, SparseCore 0:
  68.2 69.4 all-gather.2
  179.2 53.4 all-gather.4
  244.3 73.4 reduce-scatter.1

commit v3 on v2

--- a/solution.py
+++ b/solution.py
@@ -3,8 +3,6 @@
 from jax import lax
 from jax.sharding import Mesh
 from jax.sharding import PartitionSpec as P
-
-COL = ("zh", "zl", "c")
 
 
 def doc_position(points, lengths):
@@ -72,7 +70,7 @@
     return jnp.take(relative, pick, axis=0)
 
 
-def body(tokens, in_weight, out_weight, short_taps, filter_taps, decay_rate, doc_lengths):
+def block_body(tokens, in_weight, out_weight, short_taps, filter_taps, decay_rate, doc_lengths):
     zh = lax.axis_index("zh")
     col_size = lax.axis_size("zh") * lax.axis_size("zl") * lax.axis_size("c")
     own_rows = tokens.shape[0]
@@ -84,10 +82,10 @@
     normed = (
         widened * lax.rsqrt(jnp.mean(widened * widened, axis=1, keepdims=True) + 1e-06)
     ).astype(jnp.bfloat16)
+    in_piece = swap_half(in_weight, zh, 2)
+    in_full = lax.all_gather(in_piece, "p", axis=0, tiled=True)
     gathered = z_ring_gather(normed)
 
-    in_piece = swap_half(in_weight, zh, 2)
-    in_full = lax.all_gather(in_piece, "p", axis=0, tiled=True)
     out_piece = swap_half(out_weight, zh, 1)
     out_full = lax.all_gather(out_piece, "p", axis=0, tiled=True)
 
@@ -130,11 +128,20 @@
     )
     long_mix = long_filter(extended, shaped, own_position, col_rows, tap_count)
     gated_mix = (query * long_mix).astype(jnp.bfloat16)
+    core = lax.axis_index("c")
+    swap = [(0, 1), (1, 0)]
+    by_core = gated_mix.reshape(nz, 2, own_rows, half)
+    mine_rows = lax.dynamic_index_in_dim(by_core, core, 1, keepdims=False)
+    other_rows = lax.dynamic_index_in_dim(by_core, 1 - core, 1, keepdims=False)
+    partner_cols = lax.ppermute(other_rows, "c", swap)
+    partner_out = lax.ppermute(out_full, "c", swap)
+    lhs = jnp.concatenate([mine_rows, partner_cols], 2).reshape(nz * own_rows, 2 * half)
+    rhs = jnp.concatenate([out_full, partner_out], 1)
     summed = lax.psum_scatter(
         lax.dot_general(
-            gated_mix, out_full, (((1,), (1,)), ((), ())), preferred_element_type=jnp.float32
+            lhs, rhs, (((1,), (1,)), ((), ())), preferred_element_type=jnp.float32
         ).astype(jnp.bfloat16),
-        COL,
+        ("zh", "zl"),
         scatter_dimension=0,
         tiled=True,
     ).astype(jnp.float32)
@@ -157,4 +164,4 @@
         P(),
     )
     out_specs = P(rows, None)
-    return jax.shard_map(body, mesh=fine, in_specs=in_specs, out_specs=out_specs, check_vma=False)
+    return jax.shard_map(block_body, mesh=fine, in_specs=in_specs, out_specs=out_specs, check_vma=False)

time: 327 us -> 321 us (0.982)
  waiting for transfers between devices: 164 us -> 160 us
  local copies, waits for them, and re-layouts: 27.4 us -> 23.8 us
    reduce_scatter x1, waiting for transfers between devices: 73.6 us -> 55.5 us  [block_body(): lax.psum_scatter(lax.dot_general(lhs, rhs, (((1,), (1,)), ((), ())), pref...]
    all_gather x2, waiting for transfers between devices: 35 us -> 47.1 us  [the longest x1 33 us: block_body(): in_full = lax.all_gather(in_piece, 'p', axis=0, tiled=True)]
    ppermute x2, waiting for transfers between devices: 3.92 us -> 7.72 us  [swap_half(): got = lax.ppermute(give, 'zh', [(0, 1), (1, 0)])]
    unnamed x35 -> x25, local copies, waits for them, and re-layouts: 10.9 us -> 9.88 us
  transfers between devices with their start and end apart: 15 -> 17, of which waited for: 10 -> 11; matrix products, arithmetic and copies ran while one was open for 30% -> 34% of each run, Pallas kernels for 0% -> 0%
where the time goes in v3:
time: 321 us; the launch traced here: 320 us
  waiting for transfers between devices  160 us (50%)
  other arithmetic  76.8 us (24%)
  local copies, waits for them, and re-layouts  23.8 us (7%)
  starting transfers between devices  23.5 us (7%)
  matrix products  19.9 us (6%)
  between operations  13.4 us (4%)
    reduce_scatter x1, waiting for transfers between devices, block_body(): lax.psum_scatter(lax.dot_general(lhs, rhs, (((1,), (1,)), ((), ())), pref...  55.5 us
    add x8, other arithmetic, tap_group(): running + jnp.where(inside, weight_row * window.astype(jnp.float32), jnp....  51.3 us
    ppermute x4, waiting for transfers between devices, z_ring_gather(): going_right = lax.ppermute(going_right, ('zh', 'zl'), right)  45.3 us
    all_gather x1, waiting for transfers between devices, block_body(): in_full = lax.all_gather(in_piece, 'p', axis=0, tiled=True)  33 us
    all_gather x1, waiting for transfers between devices, block_body(): out_full = lax.all_gather(out_piece, 'p', axis=0, tiled=True)  14.2 us
    dot_general x2, matrix products, project(): out = jnp.dot(flat, flat_in, preferred_element_type=jnp.float32)  13.3 us
    unnamed x25, local copies, waits for them, and re-layouts  9.88 us
    ppermute x2, starting transfers between devices, swap_half(): got = lax.ppermute(give, 'zh', [(0, 1), (1, 0)])  8.33 us
  transfers between devices with their start and end apart: 17, of which 11 were waited for; matrix products, arithmetic and copies ran while one was open for 34% of the time, Pallas kernels for 0%

profile of v3, /device:TPU:2, one launch (start us, length us, event | category | flops | bytes accessed | tf_op | source)
XLA Modules:
  0.0 319.6 jit_solution(17780111102204796389)
XLA Ops:
  6.5 1.2 fusion.18
  7.8 2.0 fusion.19
  9.8 1.9 collective-permute-start
  11.7 16.1 %collective-permute-done = bf16[64,4096]{1,0:T(8,128)(2,1)S(1)} collective-permute-done((bf16[64,4096]{1,0:T(8,128)(2,1)}, bf16[64,4096]{1,0:T(8,128)(2,1)S(1)}, u32[]{:S(2)}, u32[]{:S(2)}) %collective-permute-start) | collective-permute-done | bytes 524320 | tf_op jit(solution)/shard_map/ppermute | solution.py:62
  27.8 3.2 %collective-permute-start.4 = (bf16[64,4096]{1,0:T(8,128)(2,1)}, bf16[64,4096]{1,0:T(8,128)(2,1)S(1)}, u32[]{:S(2)}, u32[]{:S(2)}) collective-permute-start(bf16[64,4096]{1,0:T(8,128)(2,1)} %fusion.19), channel_id=1, source_target_pairs={{0,14},{2,0},{4,2},{6,4},{8,6},{10,8},{12,10},{14,12},{1,15},{3,1}... | collective-permute-start | bytes 1572872 | tf_op jit(solution)/shard_map/ppermute | solution.py:65
  31.0 11.1 %collective-permute-done.1 = bf16[64,4096]{1,0:T(8,128)(2,1)S(1)} collective-permute-done((bf16[64,4096]{1,0:T(8,128)(2,1)S(1)}, bf16[64,4096]{1,0:T(8,128)(2,1)S(1)}, u32[]{:S(2)}, u32[]{:S(2)}) %collective-permute-start.1) | collective-permute-done | bytes 524320 | tf_op jit(solution)/shard_map/ppermute | solution.py:62
  42.1 1.0 fusion.33
  43.1 0.2 copy.33
  43.3 0.2 copy.34
  43.5 4.1 %collective-permute-start.7 = (bf16[128,3,256]{0,2,1:T(8,128)(2,1)S(1)}, bf16[128,3,256]{0,2,1:T(8,128)(2,1)S(1)}, u32[]{:S(2)}, u32[]{:S(2)}) collective-permute-start(bf16[128,3,256]{0,2,1:T(8,128)(2,1)S(1)} %broadcast_select_fusion.5), channel_id=1, source_target_pairs={{0,8},{8,0},{1,9},{9,1},{2,10},{10,2},{3,11},{11,3},{4,12},{12,4},... | collective-permute-start | bytes 589832 | tf_op jit(solution)/shard_map/ppermute | solution.py:48
  47.6 3.3 %collective-permute-start.5 = (bf16[64,4096]{1,0:T(8,128)(2,1)S(1)}, bf16[64,4096]{1,0:T(8,128)(2,1)}, u32[]{:S(2)}, u32[]{:S(2)}) collective-permute-start(bf16[64,4096]{1,0:T(8,128)(2,1)S(1)} %collective-permute-done.4), channel_id=1, source_target_pairs={{0,14},{2,0},{4,2},{6,4},{8,6},{10,8},{12,10},{14,12},{1,15},{3,1}... | collective-permute-start | bytes 1572872 | tf_op jit(solution)/shard_map/ppermute | solution.py:65
  50.9 12.3 %collective-permute-done.2 = bf16[64,4096]{1,0:T(8,128)(2,1)} collective-permute-done((bf16[64,4096]{1,0:T(8,128)(2,1)S(1)}, bf16[64,4096]{1,0:T(8,128)(2,1)}, u32[]{:S(2)}, u32[]{:S(2)}) %collective-permute-start.2) | collective-permute-done | bytes 524320 | tf_op jit(solution)/shard_map/ppermute | solution.py:62
  63.3 3.9 %collective-permute-done.7 = bf16[128,3,256]{0,2,1:T(8,128)(2,1)S(1)} collective-permute-done((bf16[128,3,256]{0,2,1:T(8,128)(2,1)S(1)}, bf16[128,3,256]{0,2,1:T(8,128)(2,1)S(1)}, u32[]{:S(2)}, u32[]{:S(2)}) %collective-permute-start.7) | collective-permute-done | bytes 196640 | tf_op jit(solution)/shard_map/ppermute | solution.py:48
  67.3 0.8 pad_maximum_fusion.2
  68.1 1.4 collective-permute-start.6
  69.5 5.8 %collective-permute-done.3 = bf16[64,4096]{1,0:T(8,128)(2,1)} collective-permute-done((bf16[64,4096]{1,0:T(8,128)(2,1)}, bf16[64,4096]{1,0:T(8,128)(2,1)}, u32[]{:S(2)}, u32[]{:S(2)}) %collective-permute-start.3) | collective-permute-done | bytes 524320 | tf_op jit(solution)/shard_map/ppermute | solution.py:62
  75.3 1.9 bitcast_dynamic-update-slice_fusion.7
  77.2 1.9 bitcast_dynamic-update-slice_fusion.6
  79.1 0.8 bitcast_dynamic-update-slice_fusion.5
  79.9 0.9 bitcast_dynamic-update-slice_fusion.4
  80.8 1.0 bitcast_dynamic-update-slice_fusion.3
  81.8 0.8 bitcast_dynamic-update-slice_fusion.2
  82.6 1.9 bitcast_dynamic-update-slice_fusion.1
  84.5 0.9 bitcast_dynamic-update-slice_fusion
  85.4 5.1 %gather_fusion = bf16[8,64,4096]{2,1,0:T(8,128)(2,1)} fusion(bf16[8,64,4096]{2,1,0:T(8,128)(2,1)} %bitcast_dynamic-update-slice_fusion, s32[1024]{0:T(1024)S(1)} %pad_clamp_fusion), kind=kCustom, calls=%fused_computation | custom fusion | bytes 8388640 | tf_op jit(solution)/shard_map/jit(_take)/gather | solution.py:70
  90.5 4.8 %broadcast_select_fusion = bf16[8,64,4096]{2,1,0:T(8,128)(2,1)} fusion(bf16[8,64,4096]{2,1,0:T(8,128)(2,1)} %gather_fusion, pred[8]{0:T(512)(128)(4,1)S(1)} %compare_and_fusion), kind=kLoop, calls=%fused_computation.54 | loop fusion | flops 2097152 | bytes 8388616 | tf_op jit(solution)/shard_map/jit(_take)/select_n | solution.py:70
  95.3 4.2 %collective-permute-start.12 = (bf16[128,256]{1,0:T(8,128)(2,1)S(1)}, bf16[128,256]{1,0:T(8,128)(2,1)S(1)}, u32[]{:S(2)}, u32[]{:S(2)}) collective-permute-start(bf16[128,256]{1,0:T(8,128)(2,1)S(1)} %broadcast_select_fusion.9), channel_id=1, source_target_pairs={{0,8},{8,0},{1,9},{9,1},{2,10},{10,2},{3,11},{11,3},{4,12},{12,4},... | collective-permute-start | bytes 196616 | tf_op jit(solution)/shard_map/ppermute | solution.py:48
  99.5 0.1 copy.25
  99.6 0.1 reduce-window.9
  99.7 0.1 reduce
  99.8 0.1 select_reduce_fusion
  100.0 3.8 %collective-permute-done.12 = bf16[128,256]{1,0:T(8,128)(2,1)S(1)} collective-permute-done((bf16[128,256]{1,0:T(8,128)(2,1)S(1)}, bf16[128,256]{1,0:T(8,128)(2,1)S(1)}, u32[]{:S(2)}, u32[]{:S(2)}) %collective-permute-start.12) | collective-permute-done | bytes 65568 | tf_op jit(solution)/shard_map/ppermute | solution.py:48
  103.8 0.7 pad_maximum_fusion.3
  104.5 0.2 reduce-scatter.2.cloned.1.call-start
  104.8 33.0 %all-gather.3.cloned.1.call-done = bf16[4096,3,256]{0,2,1:T(8,128)(2,1)} async-done(((bf16[256,3,256]{0,2,1:T(8,128)(2,1)}), bf16[4096,3,256]{0,2,1:T(8,128)(2,1)}) %all-gather.3.cloned.1.call-update) | async-done | bytes 6291472 | tf_op jit(solution)/shard_map/all_gather | solution.py:86
  137.7 7.6 %convolution_convert_fusion.1 = bf16[512,768]{1,0:T(8,128)(2,1)S(1)} fusion(bf16[512,4096]{1,0:T(8,128)(2,1)} %bitcast.13, bf16[4096,768]{0,1:T(8,128)(2,1)} %bitcast.126), kind=kOutput, calls=%fused_computation.59 | convolution fusion | flops 3221618688 | bytes 11272192 | tf_op jit(solution)/shard_map/dot_general | solution.py:97
  145.4 5.7 %broadcast_select_fusion.2 = (bf16[512,768]{1,0:T(8,128)(2,1)S(1)}, bf16[512,768]{1,0:T(8,128)(2,1)S(1)}) fusion(bf16[512,768]{1,0:T(8,128)(2,1)S(1)} %convolution_convert_fusion.1, pred[]{:T(512)S(6)} %eq.6, bf16[512,4096]{1,0:T(8,128)(2,1)} %bitcast.11, bf16[4096,768]{0,1:T(8,128)(2,1)S(1)} %bitcast.127), kind=kOutput, calls=%fused_computation.69 | convolution fusion | flops 3222405120 | bytes 12845057 | tf_op jit(solution)/shard_map/dot_general | solution.py:97
  151.1 1.3 pad_maximum_fusion
  152.4 4.2 %reshape.308 = bf16[1024,3,256]{2,1,0:T(4,128)(2,1)S(1)} reshape(bf16[8,2,64,768]{3,2,1,0:T(8,128)(2,1)} %pad_maximum_fusion) | data formatting | bytes 3145728 | tf_op jit(solution)/shard_map/reshape | solution.py:106
  156.6 2.2 collective-permute-start.9
  158.8 3.2 %collective-permute-done.9 = bf16[2,3,256]{2,1,0:T(4,128)(2,1)S(1)} collective-permute-done((bf16[2,3,256]{2,1,0:T(4,128)(2,1)S(1)}, bf16[2,3,256]{2,1,0:T(4,128)(2,1)S(1)}, u32[]{:S(2)}, u32[]{:S(2)}) %collective-permute-start.9) | collective-permute-done | bytes 3104 | tf_op jit(solution)/shard_map/ppermute | solution.py:118
  162.1 0.8 constant_dynamic-update-slice_fusion
  162.9 6.3 %select_add_fusion.1 = f32[1024,3,256]{2,1,0:T(4,128)S(1)} fusion(bf16[1024,3,256]{2,1,0:T(4,128)(2,1)S(1)} %reshape.308, bf16[1026,3,256]{2,1,0:T(4,128)(2,1)S(1)} %constant_dynamic-update-slice_fusion, f32[3,256]{1,0:T(4,128)S(1)} %get-tuple-element.289, f32[3,256]{1,0:T(4,128)S(1)} %get-tuple-element.288, f32[3,256]{1,0:T(4,128)S(1)} %get-tuple-element.287, ...), kind=kLoop, calls=%fused_computation.53 | loop fusion | flops 8650752 | bytes 7876608 | tf_op jit(solution)/shard_map/add | solution.py:19
  169.3 3.1 fusion.32
  172.4 1.0 slice.68
  173.4 2.3 collective-permute-start.10
  175.8 14.2 %all-gather.5.cloned.1.call-done = bf16[4096,256]{1,0:T(8,128)(2,1)} async-done(((bf16[256,256]{1,0:T(8,128)(2,1)}), bf16[4096,256]{1,0:T(8,128)(2,1)}) %all-gather.5.cloned.1.call-update) | async-done | bytes 2097168 | tf_op jit(solution)/shard_map/all_gather | solution.py:90
  190.0 1.3 copy.38
  191.3 54.6 %while.17 = (s32[]{:T(128)}, f32[1024,256]{1,0:T(8,128)S(1)}, s32[1024]{0:T(1024)S(1)}, f32[128,256]{1,0:T(8,128)S(1)}, bf16[1152,256]{1,0:T(8,128)(2,1)S(1)}, /...) while((s32[]{:T(128)}, f32[1024,256]{1,0:T(8,128)S(1)}, ...), condition=%wide.region_4.5_spmd.clone, body=%wide.region_3.4_spmd.clone.sunk | while | flops 17055876 | bytes 10573783 | solution.py:39
  191.7 6.4 %fusion.39 = f32[1024,256]{1,0:T(8,128)S(1)} fusion(f32[1024,256]{1,0:T(8,128)S(1)} %get-tuple-element.427, bf16[1152,256]{1,0:T(8,128)(2,1)S(1)} %get-tuple-element.469, s32[]{:T(128)S(6)} %select_n.888, f32[256]{0:T(256)S(1)} %bitcast.109, s32[]{:T(128)S(6)} %select_n.905, f32[256]{0:T(256)S(1)} %bitcast.110, s32[]{:T(128)S(6)} %select_n.906, ...), kind=kLoop, calls=%fused_computation.16.clone.1 | loop fusion | flops 17039360 | bytes 10518593 | tf_op jit(solution)/shard_map/while/body/eval_jaxpr/add | solution.py:33
  198.6 6.4 %fusion.39 = f32[1024,256]{1,0:T(8,128)S(1)} fusion(f32[1024,256]{1,0:T(8,128)S(1)} %get-tuple-element.427, bf16[1152,256]{1,0:T(8,128)(2,1)S(1)} %get-tuple-element.469, s32[]{:T(128)S(6)} %select_n.888, f32[256]{0:T(256)S(1)} %bitcast.109, s32[]{:T(128)S(6)} %select_n.905, f32[256]{0:T(256)S(1)} %bitcast.110, s32[]{:T(128)S(6)} %select_n.906, ...), kind=kLoop, calls=%fused_computation.16.clone.1 | loop fusion | flops 17039360 | bytes 10518593 | tf_op jit(solution)/shard_map/while/body/eval_jaxpr/add | solution.py:33
  205.4 6.4 %fusion.39 = f32[1024,256]{1,0:T(8,128)S(1)} fusion(f32[1024,256]{1,0:T(8,128)S(1)} %get-tuple-element.427, bf16[1152,256]{1,0:T(8,128)(2,1)S(1)} %get-tuple-element.469, s32[]{:T(128)S(6)} %select_n.888, f32[256]{0:T(256)S(1)} %bitcast.109, s32[]{:T(128)S(6)} %select_n.905, f32[256]{0:T(256)S(1)} %bitcast.110, s32[]{:T(128)S(6)} %select_n.906, ...), kind=kLoop, calls=%fused_computation.16.clone.1 | loop fusion | flops 17039360 | bytes 10518593 | tf_op jit(solution)/shard_map/while/body/eval_jaxpr/add | solution.py:33
  211.9 0.1 constant_dynamic-slice_fusion.18
  212.2 6.4 %fusion.39 = f32[1024,256]{1,0:T(8,128)S(1)} fusion(f32[1024,256]{1,0:T(8,128)S(1)} %get-tuple-element.427, bf16[1152,256]{1,0:T(8,128)(2,1)S(1)} %get-tuple-element.469, s32[]{:T(128)S(6)} %select_n.888, f32[256]{0:T(256)S(1)} %bitcast.109, s32[]{:T(128)S(6)} %select_n.905, f32[256]{0:T(256)S(1)} %bitcast.110, s32[]{:T(128)S(6)} %select_n.906, ...), kind=kLoop, calls=%fused_computation.16.clone.1 | loop fusion | flops 17039360 | bytes 10518593 | tf_op jit(solution)/shard_map/while/body/eval_jaxpr/add | solution.py:33
  219.0 6.4 %fusion.39 = f32[1024,256]{1,0:T(8,128)S(1)} fusion(f32[1024,256]{1,0:T(8,128)S(1)} %get-tuple-element.427, bf16[1152,256]{1,0:T(8,128)(2,1)S(1)} %get-tuple-element.469, s32[]{:T(128)S(6)} %select_n.888, f32[256]{0:T(256)S(1)} %bitcast.109, s32[]{:T(128)S(6)} %select_n.905, f32[256]{0:T(256)S(1)} %bitcast.110, s32[]{:T(128)S(6)} %select_n.906, ...), kind=kLoop, calls=%fused_computation.16.clone.1 | loop fusion | flops 17039360 | bytes 10518593 | tf_op jit(solution)/shard_map/while/body/eval_jaxpr/add | solution.py:33
  225.9 6.4 %fusion.39 = f32[1024,256]{1,0:T(8,128)S(1)} fusion(f32[1024,256]{1,0:T(8,128)S(1)} %get-tuple-element.427, bf16[1152,256]{1,0:T(8,128)(2,1)S(1)} %get-tuple-element.469, s32[]{:T(128)S(6)} %select_n.888, f32[256]{0:T(256)S(1)} %bitcast.109, s32[]{:T(128)S(6)} %select_n.905, f32[256]{0:T(256)S(1)} %bitcast.110, s32[]{:T(128)S(6)} %select_n.906, ...), kind=kLoop, calls=%fused_computation.16.clone.1 | loop fusion | flops 17039360 | bytes 10518593 | tf_op jit(solution)/shard_map/while/body/eval_jaxpr/add | solution.py:33
  232.7 6.4 %fusion.39 = f32[1024,256]{1,0:T(8,128)S(1)} fusion(f32[1024,256]{1,0:T(8,128)S(1)} %get-tuple-element.427, bf16[1152,256]{1,0:T(8,128)(2,1)S(1)} %get-tuple-element.469, s32[]{:T(128)S(6)} %select_n.888, f32[256]{0:T(256)S(1)} %bitcast.109, s32[]{:T(128)S(6)} %select_n.905, f32[256]{0:T(256)S(1)} %bitcast.110, s32[]{:T(128)S(6)} %select_n.906, ...), kind=kLoop, calls=%fused_computation.16.clone.1 | loop fusion | flops 17039360 | bytes 10518593 | tf_op jit(solution)/shard_map/while/body/eval_jaxpr/add | solution.py:33
  239.5 6.4 %fusion.39 = f32[1024,256]{1,0:T(8,128)S(1)} fusion(f32[1024,256]{1,0:T(8,128)S(1)} %get-tuple-element.427, bf16[1152,256]{1,0:T(8,128)(2,1)S(1)} %get-tuple-element.469, s32[]{:T(128)S(6)} %select_n.888, f32[256]{0:T(256)S(1)} %bitcast.109, s32[]{:T(128)S(6)} %select_n.905, f32[256]{0:T(256)S(1)} %bitcast.110, s32[]{:T(128)S(6)} %select_n.906, ...), kind=kLoop, calls=%fused_computation.16.clone.1 | loop fusion | flops 17039360 | bytes 10518593 | tf_op jit(solution)/shard_map/while/body/eval_jaxpr/add | solution.py:33
  245.9 1.3 fusion.22
  247.3 0.6 collective-permute-start.11
  247.9 1.2 collective-permute-done.11
  249.1 6.6 %convolution_convert_fusion = bf16[512,4096]{1,0:T(8,128)(2,1)} fusion(bf16[4096,256]{1,0:T(8,128)(2,1)} %collective-permute-done.13, bf16[4096,256]{1,0:T(8,128)(2,1)} %all-gather.5.cloned.1.call-done, bf16[512,256]{1,0:T(8,128)(2,1)S(1)} %bitcast.128, bf16[512,256]{1,0:T(8,128)(2,1)S(1)} %bitcast.107), kind=kOutput, calls=%fused_computation.49 | convolution fusion | flops 2159017984 | bytes 8912896 | tf_op jit(solution)/shard_map/dot_general | solution.py:141
  255.7 55.5 %reduce-scatter.2.cloned.1.call-done = bf16[64,4096]{1,0:T(8,128)(2,1)} async-done(((bf16[512,4096]{1,0:T(8,128)(2,1)}), bf16[64,4096]{1,0:T(8,128)(2,1)}) %reduce-scatter.2.cloned.1.call-update) | async-done | bytes 524304 | tf_op jit(solution)/shard_map/reduce_scatter | solution.py:140
  311.1 2.0 fusion.20
  (66 shorter events, 1.5 us)
Async XLA Ops:
  6.5 131.2 %all-gather.3.cloned.1.call-start = ((), (), s32[]{:S(2)}) async-start(), calls=%async_computation.1 | async-start | bytes 6684672 | tf_op jit(solution)/shard_map/all_gather | solution.py:86
  9.8 18.0 %collective-permute-start = (bf16[64,4096]{1,0:T(8,128)(2,1)}, bf16[64,4096]{1,0:T(8,128)(2,1)S(1)}, u32[]{:S(2)}, u32[]{:S(2)}) collective-permute-start(bf16[64,4096]{1,0:T(8,128)(2,1)} %fusion.19), channel_id=1, source_target_pairs={{0,2},{2,4},{4,6},{6,8},{8,10},{10,12},{12,14},{14,0},{1,3},{3,5},... | collective-permute-start | bytes 1572872 | tf_op jit(solution)/shard_map/ppermute | solution.py:62
  27.8 14.3 %collective-permute-start.1 = (bf16[64,4096]{1,0:T(8,128)(2,1)S(1)}, bf16[64,4096]{1,0:T(8,128)(2,1)S(1)}, u32[]{:S(2)}, u32[]{:S(2)}) collective-permute-start(bf16[64,4096]{1,0:T(8,128)(2,1)S(1)} %collective-permute-done), channel_id=1, source_target_pairs={{0,2},{2,4},{4,6},{6,8},{8,10},{10,12},{12,14},{14,0},{1,3},{3,5},... | collective-permute-start | bytes 1572872 | tf_op jit(solution)/shard_map/ppermute | solution.py:62
  27.8 19.8 %collective-permute-start.4 = (bf16[64,4096]{1,0:T(8,128)(2,1)}, bf16[64,4096]{1,0:T(8,128)(2,1)S(1)}, u32[]{:S(2)}, u32[]{:S(2)}) collective-permute-start(bf16[64,4096]{1,0:T(8,128)(2,1)} %fusion.19), channel_id=1, source_target_pairs={{0,14},{2,0},{4,2},{6,4},{8,6},{10,8},{12,10},{14,12},{1,15},{3,1}... | collective-permute-start | bytes 1572872 | tf_op jit(solution)/shard_map/ppermute | solution.py:65
  31.0 49.8 %copy-start = (bf16[64,4096]{1,0:T(8,128)(2,1)S(1)}, bf16[64,4096]{1,0:T(8,128)(2,1)}, u32[]{:S(2)}) copy-start(bf16[64,4096]{1,0:T(8,128)(2,1)} %param.9) | copy-start | bytes 1572868
  42.1 21.2 %collective-permute-start.2 = (bf16[64,4096]{1,0:T(8,128)(2,1)S(1)}, bf16[64,4096]{1,0:T(8,128)(2,1)}, u32[]{:S(2)}, u32[]{:S(2)}) collective-permute-start(bf16[64,4096]{1,0:T(8,128)(2,1)S(1)} %collective-permute-done.1), channel_id=1, source_target_pairs={{0,2},{2,4},{4,6},{6,8},{8,10},{10,12},{12,14},{14,0},{1,3},{3,5},... | collective-permute-start | bytes 1572872 | tf_op jit(solution)/shard_map/ppermute | solution.py:62
  43.5 23.7 %collective-permute-start.7 = (bf16[128,3,256]{0,2,1:T(8,128)(2,1)S(1)}, bf16[128,3,256]{0,2,1:T(8,128)(2,1)S(1)}, u32[]{:S(2)}, u32[]{:S(2)}) collective-permute-start(bf16[128,3,256]{0,2,1:T(8,128)(2,1)S(1)} %broadcast_select_fusion.5), channel_id=1, source_target_pairs={{0,8},{8,0},{1,9},{9,1},{2,10},{10,2},{3,11},{11,3},{4,12},{12,4},... | collective-permute-start | bytes 589832 | tf_op jit(solution)/shard_map/ppermute | solution.py:48
  47.6 20.5 %collective-permute-start.5 = (bf16[64,4096]{1,0:T(8,128)(2,1)S(1)}, bf16[64,4096]{1,0:T(8,128)(2,1)}, u32[]{:S(2)}, u32[]{:S(2)}) collective-permute-start(bf16[64,4096]{1,0:T(8,128)(2,1)S(1)} %collective-permute-done.4), channel_id=1, source_target_pairs={{0,14},{2,0},{4,2},{6,4},{8,6},{10,8},{12,10},{14,12},{1,15},{3,1}... | collective-permute-start | bytes 1572872 | tf_op jit(solution)/shard_map/ppermute | solution.py:65
  63.3 12.0 %collective-permute-start.3 = (bf16[64,4096]{1,0:T(8,128)(2,1)}, bf16[64,4096]{1,0:T(8,128)(2,1)}, u32[]{:S(2)}, u32[]{:S(2)}) collective-permute-start(bf16[64,4096]{1,0:T(8,128)(2,1)} %collective-permute-done.2), channel_id=1, source_target_pairs={{0,2},{2,4},{4,6},{6,8},{8,10},{10,12},{12,14},{14,0},{1,3},{3,5},... | collective-permute-start | bytes 1572872 | tf_op jit(solution)/shard_map/ppermute | solution.py:62
  68.1 121.9 %all-gather.5.cloned.1.call-start = ((), (), s32[]{:S(2)}) async-start(), calls=%async_computation.2 | async-start | bytes 2228224 | tf_op jit(solution)/shard_map/all_gather | solution.py:90
  68.1 16.4 %collective-permute-start.6 = (bf16[64,4096]{1,0:T(8,128)(2,1)}, bf16[64,4096]{1,0:T(8,128)(2,1)S(1)}, u32[]{:S(2)}, u32[]{:S(2)}) collective-permute-start(bf16[64,4096]{1,0:T(8,128)(2,1)} %collective-permute-done.5), channel_id=1, source_target_pairs={{0,14},{2,0},{4,2},{6,4},{8,6},{10,8},{12,10},{14,12},{1,15},{3,1}... | collective-permute-start | bytes 1572872 | tf_op jit(solution)/shard_map/ppermute | solution.py:65
  90.5 4.8 %copy-start.1 = (bf16[128,512]{1,0:T(8,128)(2,1)S(1)}, bf16[128,512]{1,0:T(8,128)(2,1)}, u32[]{:S(2)}) copy-start(bf16[128,512]{1,0:T(8,128)(2,1)} %param.11) | copy-start | bytes 393220
  90.5 9.0 %copy-start.4 = (s32[64]{0:T(128)S(1)}, s32[64]{0:T(128)}, u32[]{:S(2)}) copy-start(s32[64]{0:T(128)} %param.15) | copy-start | bytes 772
  90.5 9.5 %copy-start.3 = (f32[3,3,512]{2,1,0:T(4,128)S(1)}, f32[3,3,512]{2,1,0:T(4,128)}, u32[]{:S(2)}) copy-start(f32[3,3,512]{2,1,0:T(4,128)} %param.12) | copy-start | bytes 55300
  95.3 9.5 %collective-permute-start.8 = (bf16[8,64,4096]{2,1,0:T(8,128)(2,1)}, bf16[8,64,4096]{2,1,0:T(8,128)(2,1)}, u32[]{:S(2)}, u32[]{:S(2)}) collective-permute-start(bf16[8,64,4096]{2,1,0:T(8,128)(2,1)} %broadcast_select_fusion), channel_id=1, source_target_pairs={{0,1},{1,0},{2,3},{3,2},{4,5},{5,4},{6,7},{7,6},{8,9},{9,8},{10,11... | collective-permute-start | bytes 12582920 | tf_op jit(solution)/shard_map/ppermute | solution.py:100
  95.3 8.5 %collective-permute-start.12 = (bf16[128,256]{1,0:T(8,128)(2,1)S(1)}, bf16[128,256]{1,0:T(8,128)(2,1)S(1)}, u32[]{:S(2)}, u32[]{:S(2)}) collective-permute-start(bf16[128,256]{1,0:T(8,128)(2,1)S(1)} %broadcast_select_fusion.9), channel_id=1, source_target_pairs={{0,8},{8,0},{1,9},{9,1},{2,10},{10,2},{3,11},{11,3},{4,12},{12,4},... | collective-permute-start | bytes 196616 | tf_op jit(solution)/shard_map/ppermute | solution.py:48
  104.5 206.6 %reduce-scatter.2.cloned.1.call-start = ((), (), s32[]{:S(2)}) async-start(), calls=%async_computation.3 | async-start | bytes 4718592 | tf_op jit(solution)/shard_map/reduce_scatter | solution.py:140
  137.7 7.7 %copy-start.6 = (bf16[4096,3,256]{0,2,1:T(8,128)(2,1)S(1)}, bf16[4096,3,256]{0,2,1:T(8,128)(2,1)}, u32[]{:S(2)}) copy-start(bf16[4096,3,256]{0,2,1:T(8,128)(2,1)} %all-gather.3.cloned.1.call-done) | copy-start | bytes 18874372
  151.0 7.7 %copy-start.5 = (f32[512]{0:T(512)S(1)}, f32[512]{0:T(512)}, u32[]{:S(2)}) copy-start(f32[512]{0:T(512)} %param.14) | copy-start | bytes 6148
  156.6 5.5 %collective-permute-start.9 = (bf16[2,3,256]{2,1,0:T(4,128)(2,1)S(1)}, bf16[2,3,256]{2,1,0:T(4,128)(2,1)S(1)}, u32[]{:S(2)}, u32[]{:S(2)}) collective-permute-start(bf16[2,3,256]{2,1,0:T(4,128)(2,1)S(1)} %slice.62), channel_id=1, source_target_pairs={{0,16},{16,32},{32,48},{48,64},{64,80},{80,96},{96,112},{112,128},... | collective-permute-start | bytes 9224 | tf_op jit(solution)/shard_map/ppermute | solution.py:118
  169.3 6.4 %copy-start.2 = (f32[128,512]{1,0:T(8,128)S(1)}, f32[128,512]{1,0:T(8,128)}, u32[]{:S(2)}) copy-start(f32[128,512]{1,0:T(8,128)} %param.13) | copy-start | bytes 786436
  173.4 17.8 %collective-permute-start.10 = (bf16[128,256]{1,0:T(8,128)(2,1)S(1)}, bf16[128,256]{1,0:T(8,128)(2,1)S(1)}, u32[]{:S(2)}, u32[]{:S(2)}) collective-permute-start(bf16[128,256]{1,0:T(8,128)(2,1)S(1)} %bitcast.124), channel_id=1, source_target_pairs={{0,16},{16,32},{32,48},{48,64},{64,80},{80,96},{96,112},{112,128},... | collective-permute-start | bytes 196616 | tf_op jit(solution)/shard_map/ppermute | solution.py:123
  189.9 58.0 %collective-permute-start.13 = (bf16[4096,256]{1,0:T(8,128)(2,1)}, bf16[4096,256]{1,0:T(8,128)(2,1)}, u32[]{:S(2)}, u32[]{:S(2)}) collective-permute-start(bf16[4096,256]{1,0:T(8,128)(2,1)} %all-gather.5.cloned.1.call-done), channel_id=1, source_target_pairs={{0,1},{1,0},{2,3},{3,2},{4,5},{5,4},{6,7},{7,6},{8,9},{9,8},{10,11... | collective-permute-start | bytes 6291464 | tf_op jit(solution)/shard_map/ppermute | solution.py:137
  247.3 1.8 collective-permute-start.11
Sparse Core Ops, SparseCore 0:
  68.2 69.4 all-gather.2
  140.1 49.7 all-gather.4
  255.8 55.2 reduce-scatter.1

commit v4 on v3

--- a/solution.py
+++ b/solution.py
@@ -86,8 +86,10 @@
     in_full = lax.all_gather(in_piece, "p", axis=0, tiled=True)
     gathered = z_ring_gather(normed)
 
-    out_piece = swap_half(out_weight, zh, 1)
+    chip_out = jnp.stack([out_weight, lax.ppermute(out_weight, "c", [(0, 1), (1, 0)])], 1)
+    out_piece = swap_half(chip_out, zh, 2)
     out_full = lax.all_gather(out_piece, "p", axis=0, tiled=True)
+    out_full = out_full.reshape(out_full.shape[0], 2 * half)
 
     flat_in = in_full.reshape(in_full.shape[0], 3 * half)
     nz = gathered.shape[0]
@@ -128,15 +130,15 @@
     )
     long_mix = long_filter(extended, shaped, own_position, col_rows, tap_count)
     gated_mix = (query * long_mix).astype(jnp.bfloat16)
+    gated_mix, out_full = lax.optimization_barrier((gated_mix, out_full))
     core = lax.axis_index("c")
     swap = [(0, 1), (1, 0)]
     by_core = gated_mix.reshape(nz, 2, own_rows, half)
     mine_rows = lax.dynamic_index_in_dim(by_core, core, 1, keepdims=False)
     other_rows = lax.dynamic_index_in_dim(by_core, 1 - core, 1, keepdims=False)
     partner_cols = lax.ppermute(other_rows, "c", swap)
-    partner_out = lax.ppermute(out_full, "c", swap)
     lhs = jnp.concatenate([mine_rows, partner_cols], 2).reshape(nz * own_rows, 2 * half)
-    rhs = jnp.concatenate([out_full, partner_out], 1)
+    rhs = out_full
     summed = lax.psum_scatter(
         lax.dot_general(
             lhs, rhs, (((1,), (1,)), ((), ())), preferred_element_type=jnp.float32

time: 321 us -> 318 us (level)
  waiting for transfers between devices: 160 us -> 156 us
    all_gather x1, waiting for transfers between devices: 14.2 us -> 7.45 us  [block_body(): out_full = lax.all_gather(out_piece, 'p', axis=0, tiled=True)]
    ppermute x1, waiting for transfers between devices: 0.01 us -> 6.16 us  [block_body(): lax.ppermute(out_weight, 'c', [(0, 1), (1, 0)])]
    ppermute x2, waiting for transfers between devices: 7.72 us -> 3.92 us  [swap_half(): got = lax.ppermute(give, 'zh', [(0, 1), (1, 0)])]
    unnamed x25 -> x30, local copies, waits for them, and re-layouts: 9.88 us -> 8.78 us
  transfers between devices with their start and end apart: 17 -> 17, of which waited for: 11 -> 12; matrix products, arithmetic and copies ran while one was open for 34% -> 31% of each run, Pallas kernels for 0% -> 0%
where the time goes in v4:
time: 318 us; the launch traced here: 316 us
  waiting for transfers between devices  156 us (49%)
  other arithmetic  75.6 us (24%)
  local copies, waits for them, and re-layouts  25.3 us (8%)
  starting transfers between devices  23.5 us (7%)
  matrix products  19.9 us (6%)
  between operations  13.4 us (4%)
    reduce_scatter x1, waiting for transfers between devices, block_body(): lax.psum_scatter(lax.dot_general(lhs, rhs, (((1,), (1,)), ((), ())), pref...  55.2 us
    add x8, other arithmetic, tap_group(): running + jnp.where(inside, weight_row * window.astype(jnp.float32), jnp....  51.5 us
    ppermute x4, waiting for transfers between devices, z_ring_gather(): going_right = lax.ppermute(going_right, ('zh', 'zl'), right)  45.3 us
    all_gather x1, waiting for transfers between devices, block_body(): in_full = lax.all_gather(in_piece, 'p', axis=0, tiled=True)  30.4 us
    dot_general x2, matrix products, project(): out = jnp.dot(flat, flat_in, preferred_element_type=jnp.float32)  13.3 us
    unnamed x30, local copies, waits for them, and re-layouts  8.78 us
    ppermute x2, starting transfers between devices, swap_half(): got = lax.ppermute(give, 'zh', [(0, 1), (1, 0)])  8.51 us
    ppermute x3, starting transfers between devices, z_ring_gather(): going_left = lax.ppermute(going_left, ('zh', 'zl'), left)  7.89 us
  transfers between devices with their start and end apart: 17, of which 12 were waited for; matrix products, arithmetic and copies ran while one was open for 31% of the time, Pallas kernels for 0%

profile of v4, /device:TPU:2, one launch (start us, length us, event | category | flops | bytes accessed | tf_op | source)
XLA Modules:
  0.0 316.3 jit_solution(991063668058641662)
XLA Ops:
  6.5 1.2 fusion.15
  7.8 2.0 fusion.16
  9.8 1.9 collective-permute-start
  11.7 16.1 %collective-permute-done = bf16[64,4096]{1,0:T(8,128)(2,1)S(1)} collective-permute-done((bf16[64,4096]{1,0:T(8,128)(2,1)}, bf16[64,4096]{1,0:T(8,128)(2,1)S(1)}, u32[]{:S(2)}, u32[]{:S(2)}) %collective-permute-start) | collective-permute-done | bytes 524320 | tf_op jit(solution)/shard_map/ppermute | solution.py:62
  27.8 3.2 %collective-permute-start.4 = (bf16[64,4096]{1,0:T(8,128)(2,1)}, bf16[64,4096]{1,0:T(8,128)(2,1)S(1)}, u32[]{:S(2)}, u32[]{:S(2)}) collective-permute-start(bf16[64,4096]{1,0:T(8,128)(2,1)} %fusion.16), channel_id=1, source_target_pairs={{0,14},{2,0},{4,2},{6,4},{8,6},{10,8},{12,10},{14,12},{1,15},{3,1}... | collective-permute-start | bytes 1572872 | tf_op jit(solution)/shard_map/ppermute | solution.py:65
  31.0 11.1 %collective-permute-done.1 = bf16[64,4096]{1,0:T(8,128)(2,1)S(1)} collective-permute-done((bf16[64,4096]{1,0:T(8,128)(2,1)S(1)}, bf16[64,4096]{1,0:T(8,128)(2,1)S(1)}, u32[]{:S(2)}, u32[]{:S(2)}) %collective-permute-start.1) | collective-permute-done | bytes 524320 | tf_op jit(solution)/shard_map/ppermute | solution.py:62
  42.1 1.0 fusion.31
  43.1 0.2 copy.42
  43.3 0.2 copy.41
  43.5 4.1 %collective-permute-start.7 = (bf16[128,3,256]{0,2,1:T(8,128)(2,1)S(1)}, bf16[128,3,256]{0,2,1:T(8,128)(2,1)S(1)}, u32[]{:S(2)}, u32[]{:S(2)}) collective-permute-start(bf16[128,3,256]{0,2,1:T(8,128)(2,1)S(1)} %broadcast_select_fusion.5), channel_id=1, source_target_pairs={{0,8},{8,0},{1,9},{9,1},{2,10},{10,2},{3,11},{11,3},{4,12},{12,4},... | collective-permute-start | bytes 589832 | tf_op jit(solution)/shard_map/ppermute | solution.py:48
  47.6 3.3 %collective-permute-start.5 = (bf16[64,4096]{1,0:T(8,128)(2,1)S(1)}, bf16[64,4096]{1,0:T(8,128)(2,1)}, u32[]{:S(2)}, u32[]{:S(2)}) collective-permute-start(bf16[64,4096]{1,0:T(8,128)(2,1)S(1)} %collective-permute-done.4), channel_id=1, source_target_pairs={{0,14},{2,0},{4,2},{6,4},{8,6},{10,8},{12,10},{14,12},{1,15},{3,1}... | collective-permute-start | bytes 1572872 | tf_op jit(solution)/shard_map/ppermute | solution.py:65
  50.9 12.3 %collective-permute-done.2 = bf16[64,4096]{1,0:T(8,128)(2,1)} collective-permute-done((bf16[64,4096]{1,0:T(8,128)(2,1)S(1)}, bf16[64,4096]{1,0:T(8,128)(2,1)}, u32[]{:S(2)}, u32[]{:S(2)}) %collective-permute-start.2) | collective-permute-done | bytes 524320 | tf_op jit(solution)/shard_map/ppermute | solution.py:62
  63.3 3.9 %collective-permute-done.7 = bf16[128,3,256]{0,2,1:T(8,128)(2,1)S(1)} collective-permute-done((bf16[128,3,256]{0,2,1:T(8,128)(2,1)S(1)}, bf16[128,3,256]{0,2,1:T(8,128)(2,1)S(1)}, u32[]{:S(2)}, u32[]{:S(2)}) %collective-permute-start.7) | collective-permute-done | bytes 196640 | tf_op jit(solution)/shard_map/ppermute | solution.py:48
  67.3 0.8 pad_maximum_fusion.2
  68.1 1.4 collective-permute-start.6
  69.5 5.8 %collective-permute-done.3 = bf16[64,4096]{1,0:T(8,128)(2,1)} collective-permute-done((bf16[64,4096]{1,0:T(8,128)(2,1)}, bf16[64,4096]{1,0:T(8,128)(2,1)}, u32[]{:S(2)}, u32[]{:S(2)}) %collective-permute-start.3) | collective-permute-done | bytes 524320 | tf_op jit(solution)/shard_map/ppermute | solution.py:62
  75.3 1.9 bitcast_dynamic-update-slice_fusion.7
  77.2 1.9 bitcast_dynamic-update-slice_fusion.6
  79.1 0.8 bitcast_dynamic-update-slice_fusion.5
  79.9 0.9 bitcast_dynamic-update-slice_fusion.4
  80.8 1.0 bitcast_dynamic-update-slice_fusion.3
  81.8 0.8 bitcast_dynamic-update-slice_fusion.2
  82.7 1.9 bitcast_dynamic-update-slice_fusion.1
  84.5 0.9 bitcast_dynamic-update-slice_fusion
  85.4 5.1 %gather_fusion = bf16[8,64,4096]{2,1,0:T(8,128)(2,1)} fusion(bf16[8,64,4096]{2,1,0:T(8,128)(2,1)} %bitcast_dynamic-update-slice_fusion, s32[1024]{0:T(1024)S(1)} %pad_clamp_fusion), kind=kCustom, calls=%fused_computation | custom fusion | bytes 8388640 | tf_op jit(solution)/shard_map/jit(_take)/gather | solution.py:70
  90.5 4.8 %broadcast_select_fusion = bf16[8,64,4096]{2,1,0:T(8,128)(2,1)} fusion(bf16[8,64,4096]{2,1,0:T(8,128)(2,1)} %gather_fusion, pred[8]{0:T(512)(128)(4,1)S(1)} %compare_and_fusion), kind=kLoop, calls=%fused_computation.51 | loop fusion | flops 2097152 | bytes 8388616 | tf_op jit(solution)/shard_map/jit(_take)/select_n | solution.py:70
  95.3 0.1 copy.36
  95.4 0.6 collective-permute-start.11
  96.0 0.1 copy.31
  96.1 0.1 reduce-window.9
  96.2 0.1 reduce
  96.4 0.1 select_reduce_fusion
  96.7 6.2 %collective-permute-done.11 = bf16[128,512]{0,1:T(8,128)(2,1)S(1)} collective-permute-done((bf16[128,512]{0,1:T(8,128)(2,1)S(1)}, bf16[128,512]{0,1:T(8,128)(2,1)S(1)}, u32[]{:S(2)}, u32[]{:S(2)}) %collective-permute-start.11) | collective-permute-done | bytes 131104 | tf_op jit(solution)/shard_map/ppermute | solution.py:89
  102.9 4.4 %collective-permute-start.12 = (bf16[128,2,256]{0,2,1:T(8,128)(2,1)S(1)}, bf16[128,2,256]{0,2,1:T(8,128)(2,1)S(1)}, u32[]{:S(2)}, u32[]{:S(2)}) collective-permute-start(bf16[128,2,256]{0,2,1:T(8,128)(2,1)S(1)} %broadcast_select_fusion.9), channel_id=1, source_target_pairs={{0,8},{8,0},{1,9},{9,1},{2,10},{10,2},{3,11},{11,3},{4,12},{12,4},... | collective-permute-start | bytes 393224 | tf_op jit(solution)/shard_map/ppermute | solution.py:48
  107.3 30.4 %all-gather.3.cloned.1.call-done = bf16[4096,3,256]{0,2,1:T(8,128)(2,1)} async-done(((bf16[256,3,256]{0,2,1:T(8,128)(2,1)}), bf16[4096,3,256]{0,2,1:T(8,128)(2,1)}) %all-gather.3.cloned.1.call-update) | async-done | bytes 6291472 | tf_op jit(solution)/shard_map/all_gather | solution.py:86
  137.7 7.6 %convolution_convert_fusion.1 = bf16[512,768]{1,0:T(8,128)(2,1)S(1)} fusion(bf16[512,4096]{1,0:T(8,128)(2,1)} %bitcast.13, bf16[4096,768]{0,1:T(8,128)(2,1)} %bitcast.134), kind=kOutput, calls=%fused_computation.56 | convolution fusion | flops 3221618688 | bytes 11272192 | tf_op jit(solution)/shard_map/dot_general | solution.py:99
  145.4 5.7 %broadcast_select_fusion.2 = (bf16[512,768]{1,0:T(8,128)(2,1)S(1)}, bf16[512,768]{1,0:T(8,128)(2,1)S(1)}) fusion(bf16[512,768]{1,0:T(8,128)(2,1)S(1)} %convolution_convert_fusion.1, pred[]{:T(512)S(6)} %eq.6, bf16[512,4096]{1,0:T(8,128)(2,1)} %bitcast.11, bf16[4096,768]{0,1:T(8,128)(2,1)S(1)} %bitcast.135), kind=kOutput, calls=%fused_computation.66 | convolution fusion | flops 3222405120 | bytes 12845057 | tf_op jit(solution)/shard_map/dot_general | solution.py:99
  151.0 1.3 pad_maximum_fusion
  152.3 5.3 %reshape.311 = bf16[1024,3,256]{2,1,0:T(4,128)(2,1)} reshape(bf16[8,2,64,768]{3,2,1,0:T(8,128)(2,1)} %pad_maximum_fusion) | data formatting | bytes 3145728 | tf_op jit(solution)/shard_map/reshape | solution.py:108
  157.6 0.8 slice.62
  158.4 2.2 collective-permute-start.9
  160.7 3.2 %collective-permute-done.9 = bf16[2,3,256]{2,1,0:T(4,128)(2,1)S(1)} collective-permute-done((bf16[2,3,256]{2,1,0:T(4,128)(2,1)S(1)}, bf16[2,3,256]{2,1,0:T(4,128)(2,1)S(1)}, u32[]{:S(2)}, u32[]{:S(2)}) %collective-permute-start.9) | collective-permute-done | bytes 3104 | tf_op jit(solution)/shard_map/ppermute | solution.py:120
  163.9 2.4 constant_dynamic-update-slice_fusion
  166.4 6.3 %select_add_fusion.1 = f32[1024,3,256]{2,1,0:T(4,128)S(1)} fusion(bf16[1024,3,256]{2,1,0:T(4,128)(2,1)S(1)} %copy-done, bf16[1026,3,256]{2,1,0:T(4,128)(2,1)S(1)} %constant_dynamic-update-slice_fusion, f32[3,256]{1,0:T(4,128)S(1)} %get-tuple-element.293, f32[3,256]{1,0:T(4,128)S(1)} %get-tuple-element.292, f32[3,256]{1,0:T(4,128)S(1)} %get-tuple-element.291, ...), kind=kLoop, calls=%fused_computation.50 | loop fusion | flops 8650752 | bytes 7876608 | tf_op jit(solution)/shard_map/add | solution.py:19
  172.7 2.9 fusion.30
  175.6 0.1 slice.68
  175.7 2.3 collective-permute-start.10
  178.0 0.7 pad_maximum_fusion.3
  178.9 3.0 collective-permute-done.10
  182.0 54.7 %while.17 = (s32[]{:T(128)}, f32[1024,256]{1,0:T(8,128)S(1)}, s32[1024]{0:T(1024)S(1)}, f32[128,256]{1,0:T(8,128)S(1)}, bf16[1152,256]{1,0:T(8,128)(2,1)S(1)}, /...) while((s32[]{:T(128)}, f32[1024,256]{1,0:T(8,128)S(1)}, ...), condition=%wide.region_4.5_spmd.clone, body=%wide.region_3.4_spmd.clone.sunk | while | flops 17055876 | bytes 10573791 | solution.py:39
  182.4 6.4 %fusion.38 = f32[1024,256]{1,0:T(8,128)S(1)} fusion(f32[1024,256]{1,0:T(8,128)S(1)} %get-tuple-element.431, bf16[1152,256]{1,0:T(8,128)(2,1)S(1)} %get-tuple-element.473, s32[]{:T(128)S(6)} %select_n.888, f32[256]{0:T(256)S(1)} %bitcast.117, s32[]{:T(128)S(6)} %select_n.905, f32[256]{0:T(256)S(1)} %bitcast.118, s32[]{:T(128)S(6)} %select_n.906, ...), kind=kLoop, calls=%fused_computation.16.clone.1 | loop fusion | flops 17039360 | bytes 10518593 | tf_op jit(solution)/shard_map/while/body/eval_jaxpr/add | solution.py:33
  189.2 6.4 %fusion.38 = f32[1024,256]{1,0:T(8,128)S(1)} fusion(f32[1024,256]{1,0:T(8,128)S(1)} %get-tuple-element.431, bf16[1152,256]{1,0:T(8,128)(2,1)S(1)} %get-tuple-element.473, s32[]{:T(128)S(6)} %select_n.888, f32[256]{0:T(256)S(1)} %bitcast.117, s32[]{:T(128)S(6)} %select_n.905, f32[256]{0:T(256)S(1)} %bitcast.118, s32[]{:T(128)S(6)} %select_n.906, ...), kind=kLoop, calls=%fused_computation.16.clone.1 | loop fusion | flops 17039360 | bytes 10518593 | tf_op jit(solution)/shard_map/while/body/eval_jaxpr/add | solution.py:33
  196.0 6.4 %fusion.38 = f32[1024,256]{1,0:T(8,128)S(1)} fusion(f32[1024,256]{1,0:T(8,128)S(1)} %get-tuple-element.431, bf16[1152,256]{1,0:T(8,128)(2,1)S(1)} %get-tuple-element.473, s32[]{:T(128)S(6)} %select_n.888, f32[256]{0:T(256)S(1)} %bitcast.117, s32[]{:T(128)S(6)} %select_n.905, f32[256]{0:T(256)S(1)} %bitcast.118, s32[]{:T(128)S(6)} %select_n.906, ...), kind=kLoop, calls=%fused_computation.16.clone.1 | loop fusion | flops 17039360 | bytes 10518593 | tf_op jit(solution)/shard_map/while/body/eval_jaxpr/add | solution.py:33
  202.9 6.4 %fusion.38 = f32[1024,256]{1,0:T(8,128)S(1)} fusion(f32[1024,256]{1,0:T(8,128)S(1)} %get-tuple-element.431, bf16[1152,256]{1,0:T(8,128)(2,1)S(1)} %get-tuple-element.473, s32[]{:T(128)S(6)} %select_n.888, f32[256]{0:T(256)S(1)} %bitcast.117, s32[]{:T(128)S(6)} %select_n.905, f32[256]{0:T(256)S(1)} %bitcast.118, s32[]{:T(128)S(6)} %select_n.906, ...), kind=kLoop, calls=%fused_computation.16.clone.1 | loop fusion | flops 17039360 | bytes 10518593 | tf_op jit(solution)/shard_map/while/body/eval_jaxpr/add | solution.py:33
  209.7 6.4 %fusion.38 = f32[1024,256]{1,0:T(8,128)S(1)} fusion(f32[1024,256]{1,0:T(8,128)S(1)} %get-tuple-element.431, bf16[1152,256]{1,0:T(8,128)(2,1)S(1)} %get-tuple-element.473, s32[]{:T(128)S(6)} %select_n.888, f32[256]{0:T(256)S(1)} %bitcast.117, s32[]{:T(128)S(6)} %select_n.905, f32[256]{0:T(256)S(1)} %bitcast.118, s32[]{:T(128)S(6)} %select_n.906, ...), kind=kLoop, calls=%fused_computation.16.clone.1 | loop fusion | flops 17039360 | bytes 10518593 | tf_op jit(solution)/shard_map/while/body/eval_jaxpr/add | solution.py:33
  216.6 6.4 %fusion.38 = f32[1024,256]{1,0:T(8,128)S(1)} fusion(f32[1024,256]{1,0:T(8,128)S(1)} %get-tuple-element.431, bf16[1152,256]{1,0:T(8,128)(2,1)S(1)} %get-tuple-element.473, s32[]{:T(128)S(6)} %select_n.888, f32[256]{0:T(256)S(1)} %bitcast.117, s32[]{:T(128)S(6)} %select_n.905, f32[256]{0:T(256)S(1)} %bitcast.118, s32[]{:T(128)S(6)} %select_n.906, ...), kind=kLoop, calls=%fused_computation.16.clone.1 | loop fusion | flops 17039360 | bytes 10518593 | tf_op jit(solution)/shard_map/while/body/eval_jaxpr/add | solution.py:33
  223.4 6.4 %fusion.38 = f32[1024,256]{1,0:T(8,128)S(1)} fusion(f32[1024,256]{1,0:T(8,128)S(1)} %get-tuple-element.431, bf16[1152,256]{1,0:T(8,128)(2,1)S(1)} %get-tuple-element.473, s32[]{:T(128)S(6)} %select_n.888, f32[256]{0:T(256)S(1)} %bitcast.117, s32[]{:T(128)S(6)} %select_n.905, f32[256]{0:T(256)S(1)} %bitcast.118, s32[]{:T(128)S(6)} %select_n.906, ...), kind=kLoop, calls=%fused_computation.16.clone.1 | loop fusion | flops 17039360 | bytes 10518593 | tf_op jit(solution)/shard_map/while/body/eval_jaxpr/add | solution.py:33
  230.3 6.4 %fusion.38 = f32[1024,256]{1,0:T(8,128)S(1)} fusion(f32[1024,256]{1,0:T(8,128)S(1)} %get-tuple-element.431, bf16[1152,256]{1,0:T(8,128)(2,1)S(1)} %get-tuple-element.473, s32[]{:T(128)S(6)} %select_n.888, f32[256]{0:T(256)S(1)} %bitcast.117, s32[]{:T(128)S(6)} %select_n.905, f32[256]{0:T(256)S(1)} %bitcast.118, s32[]{:T(128)S(6)} %select_n.906, ...), kind=kLoop, calls=%fused_computation.16.clone.1 | loop fusion | flops 17039360 | bytes 10518593 | tf_op jit(solution)/shard_map/while/body/eval_jaxpr/add | solution.py:33
  236.7 0.2 fusion.19
  236.9 7.5 %all-gather.5.cloned.1.call-done = bf16[4096,2,256]{0,2,1:T(8,128)(2,1)} async-done(((bf16[256,2,256]{0,2,1:T(8,128)(2,1)}), bf16[4096,2,256]{0,2,1:T(8,128)(2,1)}) %all-gather.5.cloned.1.call-update) | async-done | bytes 4194320 | tf_op jit(solution)/shard_map/all_gather | solution.py:91
  244.5 1.5 collective-permute-done.13
  246.0 6.6 %convolution_convert_fusion = bf16[512,4096]{1,0:T(8,128)(2,1)} fusion(bf16[4096,512]{0,1:T(8,128)(2,1)} %bitcast.136, bf16[512,256]{1,0:T(8,128)(2,1)S(1)} %bitcast.137, bf16[512,256]{1,0:T(8,128)(2,1)S(1)} %bitcast.115), kind=kOutput, calls=%fused_computation.49 | convolution fusion | flops 2150629376 | bytes 8912896 | tf_op jit(solution)/shard_map/dot_general | solution.py:143
  252.6 55.2 %reduce-scatter.2.cloned.1.call-done = bf16[64,4096]{1,0:T(8,128)(2,1)} async-done(((bf16[512,4096]{1,0:T(8,128)(2,1)}), bf16[64,4096]{1,0:T(8,128)(2,1)}) %reduce-scatter.2.cloned.1.call-update) | async-done | bytes 524304 | tf_op jit(solution)/shard_map/reduce_scatter | solution.py:142
  307.8 2.0 fusion.17
  (71 shorter events, 1.9 us)
Async XLA Ops:
  6.5 131.2 %all-gather.3.cloned.1.call-start = ((), (), s32[]{:S(2)}) async-start(), calls=%async_computation.1 | async-start | bytes 6684672 | tf_op jit(solution)/shard_map/all_gather | solution.py:86
  9.8 18.0 %collective-permute-start = (bf16[64,4096]{1,0:T(8,128)(2,1)}, bf16[64,4096]{1,0:T(8,128)(2,1)S(1)}, u32[]{:S(2)}, u32[]{:S(2)}) collective-permute-start(bf16[64,4096]{1,0:T(8,128)(2,1)} %fusion.16), channel_id=1, source_target_pairs={{0,2},{2,4},{4,6},{6,8},{8,10},{10,12},{12,14},{14,0},{1,3},{3,5},... | collective-permute-start | bytes 1572872 | tf_op jit(solution)/shard_map/ppermute | solution.py:62
  27.8 14.3 %collective-permute-start.1 = (bf16[64,4096]{1,0:T(8,128)(2,1)S(1)}, bf16[64,4096]{1,0:T(8,128)(2,1)S(1)}, u32[]{:S(2)}, u32[]{:S(2)}) collective-permute-start(bf16[64,4096]{1,0:T(8,128)(2,1)S(1)} %collective-permute-done), channel_id=1, source_target_pairs={{0,2},{2,4},{4,6},{6,8},{8,10},{10,12},{12,14},{14,0},{1,3},{3,5},... | collective-permute-start | bytes 1572872 | tf_op jit(solution)/shard_map/ppermute | solution.py:62
  27.8 19.8 %collective-permute-start.4 = (bf16[64,4096]{1,0:T(8,128)(2,1)}, bf16[64,4096]{1,0:T(8,128)(2,1)S(1)}, u32[]{:S(2)}, u32[]{:S(2)}) collective-permute-start(bf16[64,4096]{1,0:T(8,128)(2,1)} %fusion.16), channel_id=1, source_target_pairs={{0,14},{2,0},{4,2},{6,4},{8,6},{10,8},{12,10},{14,12},{1,15},{3,1}... | collective-permute-start | bytes 1572872 | tf_op jit(solution)/shard_map/ppermute | solution.py:65
  31.0 49.8 %copy-start.1 = (bf16[64,4096]{1,0:T(8,128)(2,1)S(1)}, bf16[64,4096]{1,0:T(8,128)(2,1)}, u32[]{:S(2)}) copy-start(bf16[64,4096]{1,0:T(8,128)(2,1)} %param.9) | copy-start | bytes 1572868
  42.1 21.2 %collective-permute-start.2 = (bf16[64,4096]{1,0:T(8,128)(2,1)S(1)}, bf16[64,4096]{1,0:T(8,128)(2,1)}, u32[]{:S(2)}, u32[]{:S(2)}) collective-permute-start(bf16[64,4096]{1,0:T(8,128)(2,1)S(1)} %collective-permute-done.1), channel_id=1, source_target_pairs={{0,2},{2,4},{4,6},{6,8},{8,10},{10,12},{12,14},{14,0},{1,3},{3,5},... | collective-permute-start | bytes 1572872 | tf_op jit(solution)/shard_map/ppermute | solution.py:62
  43.5 23.7 %collective-permute-start.7 = (bf16[128,3,256]{0,2,1:T(8,128)(2,1)S(1)}, bf16[128,3,256]{0,2,1:T(8,128)(2,1)S(1)}, u32[]{:S(2)}, u32[]{:S(2)}) collective-permute-start(bf16[128,3,256]{0,2,1:T(8,128)(2,1)S(1)} %broadcast_select_fusion.5), channel_id=1, source_target_pairs={{0,8},{8,0},{1,9},{9,1},{2,10},{10,2},{3,11},{11,3},{4,12},{12,4},... | collective-permute-start | bytes 589832 | tf_op jit(solution)/shard_map/ppermute | solution.py:48
  47.6 20.5 %collective-permute-start.5 = (bf16[64,4096]{1,0:T(8,128)(2,1)S(1)}, bf16[64,4096]{1,0:T(8,128)(2,1)}, u32[]{:S(2)}, u32[]{:S(2)}) collective-permute-start(bf16[64,4096]{1,0:T(8,128)(2,1)S(1)} %collective-permute-done.4), channel_id=1, source_target_pairs={{0,14},{2,0},{4,2},{6,4},{8,6},{10,8},{12,10},{14,12},{1,15},{3,1}... | collective-permute-start | bytes 1572872 | tf_op jit(solution)/shard_map/ppermute | solution.py:65
  63.3 12.0 %collective-permute-start.3 = (bf16[64,4096]{1,0:T(8,128)(2,1)}, bf16[64,4096]{1,0:T(8,128)(2,1)}, u32[]{:S(2)}, u32[]{:S(2)}) collective-permute-start(bf16[64,4096]{1,0:T(8,128)(2,1)} %collective-permute-done.2), channel_id=1, source_target_pairs={{0,2},{2,4},{4,6},{6,8},{8,10},{10,12},{12,14},{14,0},{1,3},{3,5},... | collective-permute-start | bytes 1572872 | tf_op jit(solution)/shard_map/ppermute | solution.py:62
  68.1 176.2 %all-gather.5.cloned.1.call-start = ((), (), s32[]{:S(2)}) async-start(), calls=%async_computation.2 | async-start | bytes 4456448 | tf_op jit(solution)/shard_map/all_gather | solution.py:91
  68.1 16.4 %collective-permute-start.6 = (bf16[64,4096]{1,0:T(8,128)(2,1)}, bf16[64,4096]{1,0:T(8,128)(2,1)S(1)}, u32[]{:S(2)}, u32[]{:S(2)}) collective-permute-start(bf16[64,4096]{1,0:T(8,128)(2,1)} %collective-permute-done.5), channel_id=1, source_target_pairs={{0,14},{2,0},{4,2},{6,4},{8,6},{10,8},{12,10},{14,12},{1,15},{3,1}... | collective-permute-start | bytes 1572872 | tf_op jit(solution)/shard_map/ppermute | solution.py:65
  90.5 4.8 %copy-start.3 = (bf16[128,512]{1,0:T(8,128)(2,1)S(1)}, bf16[128,512]{1,0:T(8,128)(2,1)}, u32[]{:S(2)}) copy-start(bf16[128,512]{1,0:T(8,128)(2,1)} %param.11) | copy-start | bytes 393220
  90.5 5.5 %copy-start.6 = (s32[64]{0:T(128)S(1)}, s32[64]{0:T(128)}, u32[]{:S(2)}) copy-start(s32[64]{0:T(128)} %param.15) | copy-start | bytes 772
  90.5 5.8 %copy-start.7 = (f32[512]{0:T(512)S(1)}, f32[512]{0:T(512)}, u32[]{:S(2)}) copy-start(f32[512]{0:T(512)} %param.14) | copy-start | bytes 6148
  90.5 6.1 %copy-start.4 = (f32[128,512]{1,0:T(8,128)S(1)}, f32[128,512]{1,0:T(8,128)}, u32[]{:S(2)}) copy-start(f32[128,512]{1,0:T(8,128)} %param.13) | copy-start | bytes 786436
  90.5 6.1 %copy-start.5 = (f32[3,3,512]{2,1,0:T(4,128)S(1)}, f32[3,3,512]{2,1,0:T(4,128)}, u32[]{:S(2)}) copy-start(f32[3,3,512]{2,1,0:T(4,128)} %param.12) | copy-start | bytes 55300
  95.3 12.0 %collective-permute-start.8 = (bf16[8,64,4096]{2,1,0:T(8,128)(2,1)}, bf16[8,64,4096]{2,1,0:T(8,128)(2,1)}, u32[]{:S(2)}, u32[]{:S(2)}) collective-permute-start(bf16[8,64,4096]{2,1,0:T(8,128)(2,1)} %broadcast_select_fusion), channel_id=1, source_target_pairs={{0,1},{1,0},{2,3},{3,2},{4,5},{5,4},{6,7},{7,6},{8,9},{9,8},{10,11... | collective-permute-start | bytes 12582920 | tf_op jit(solution)/shard_map/ppermute | solution.py:102
  95.4 7.4 %collective-permute-start.11 = (bf16[128,512]{0,1:T(8,128)(2,1)S(1)}, bf16[128,512]{0,1:T(8,128)(2,1)S(1)}, u32[]{:S(2)}, u32[]{:S(2)}) collective-permute-start(bf16[128,512]{0,1:T(8,128)(2,1)S(1)} %copy.36), channel_id=1, source_target_pairs={{0,1},{1,0},{2,3},{3,2},{4,5},{5,4},{6,7},{7,6},{8,9},{9,8},{10,11... | collective-permute-start | bytes 393224 | tf_op jit(solution)/shard_map/ppermute | solution.py:89
  102.9 57.7 %collective-permute-start.12 = (bf16[128,2,256]{0,2,1:T(8,128)(2,1)S(1)}, bf16[128,2,256]{0,2,1:T(8,128)(2,1)S(1)}, u32[]{:S(2)}, u32[]{:S(2)}) collective-permute-start(bf16[128,2,256]{0,2,1:T(8,128)(2,1)S(1)} %broadcast_select_fusion.9), channel_id=1, source_target_pairs={{0,8},{8,0},{1,9},{9,1},{2,10},{10,2},{3,11},{11,3},{4,12},{12,4},... | collective-permute-start | bytes 393224 | tf_op jit(solution)/shard_map/ppermute | solution.py:48
  137.7 7.7 %copy-start.8 = (bf16[4096,3,256]{0,2,1:T(8,128)(2,1)S(1)}, bf16[4096,3,256]{0,2,1:T(8,128)(2,1)}, u32[]{:S(2)}) copy-start(bf16[4096,3,256]{0,2,1:T(8,128)(2,1)} %all-gather.3.cloned.1.call-done) | copy-start | bytes 18874372
  157.6 8.8 %copy-start = (bf16[1024,3,256]{2,1,0:T(4,128)(2,1)S(1)}, bf16[1024,3,256]{2,1,0:T(4,128)(2,1)}, u32[]{:S(2)}) copy-start(bf16[1024,3,256]{2,1,0:T(4,128)(2,1)} %reshape.311) | copy-start | bytes 4718596
  158.4 5.5 %collective-permute-start.9 = (bf16[2,3,256]{2,1,0:T(4,128)(2,1)S(1)}, bf16[2,3,256]{2,1,0:T(4,128)(2,1)S(1)}, u32[]{:S(2)}, u32[]{:S(2)}) collective-permute-start(bf16[2,3,256]{2,1,0:T(4,128)(2,1)S(1)} %slice.62), channel_id=1, source_target_pairs={{0,16},{16,32},{32,48},{48,64},{64,80},{80,96},{96,112},{112,128},... | collective-permute-start | bytes 9224 | tf_op jit(solution)/shard_map/ppermute | solution.py:120
  175.7 6.2 %collective-permute-start.10 = (bf16[128,256]{1,0:T(8,128)(2,1)S(1)}, bf16[128,256]{1,0:T(8,128)(2,1)S(1)}, u32[]{:S(2)}, u32[]{:S(2)}) collective-permute-start(bf16[128,256]{1,0:T(8,128)(2,1)S(1)} %bitcast.132), channel_id=1, source_target_pairs={{0,16},{16,32},{32,48},{48,64},{64,80},{80,96},{96,112},{112,128},... | collective-permute-start | bytes 196616 | tf_op jit(solution)/shard_map/ppermute | solution.py:125
  178.8 129.0 %reduce-scatter.2.cloned.1.call-start = ((), (), s32[]{:S(2)}) async-start(), calls=%async_computation.3 | async-start | bytes 4718592 | tf_op jit(solution)/shard_map/reduce_scatter | solution.py:142
  181.9 54.8 %copy-start.2 = (f32[1024,1,256]{2,1,0:T(1,128)S(1)}, f32[1024,1,256]{2,1,0:T(1,128)}, u32[]{:S(2)}) copy-start(f32[1024,1,256]{2,1,0:T(1,128)} %get-tuple-element.279) | copy-start | bytes 3145732
  244.4 1.6 collective-permute-start.13
Sparse Core Ops, SparseCore 0:
  68.2 69.4 all-gather.2
  178.9 65.3 all-gather.4
  252.7 55.0 reduce-scatter.1

commit v5 on v4

--- a/solution.py
+++ b/solution.py
@@ -15,7 +15,7 @@
     running = jnp.zeros((out_count,) + extended.shape[1:], jnp.float32)
     for tap_index in range(3):
         window = extended[2 - tap_index : 2 - tap_index + out_count].astype(jnp.float32)
-        inside = (positions >= tap_index)[:, None, None]
+        inside = (positions >= tap_index)[:, None]
         running = running + jnp.where(
             inside, short_taps[tap_index][None] * window, jnp.float32(0.0)
         )
@@ -105,7 +105,7 @@
     core = lax.axis_index("c")
     first = jnp.where(core == 0, from_mine, from_partner)
     second = jnp.where(core == 0, from_partner, from_mine)
-    projected = jnp.stack([first, second], 1).reshape(col_rows, 3, half)
+    projected = jnp.stack([first, second], 1).reshape(col_rows, 3 * half)
 
     first_row = lax.axis_index("p") * col_rows
     own_points = first_row + jnp.arange(col_rows, dtype=jnp.int32)
@@ -113,7 +113,7 @@
 
     columns = lax.axis_size("p")
     ahead = [(i, i + 1) for i in range(columns - 1)]
-    my_taps = lax.dynamic_slice_in_dim(short_taps, zh * half, half, 2)
+    my_taps = lax.dynamic_slice_in_dim(short_taps, zh * half, half, 2).reshape(3, 3 * half)
     my_filter = lax.dynamic_slice_in_dim(filter_taps, zh * half, half, 1)
     my_decay = lax.dynamic_slice_in_dim(decay_rate, zh * half, half, 0)
 
@@ -121,10 +121,10 @@
     short_all = short_filter(
         jnp.concatenate([edge_rows, projected], 0), my_taps, own_position, col_rows
     )
-    kv_product = (short_all[:, 1] * short_all[:, 2]).astype(jnp.bfloat16)
+    kv_product = (short_all[:, half : 2 * half] * short_all[:, 2 * half :]).astype(jnp.bfloat16)
     tail_rows = lax.ppermute(kv_product[col_rows - tap_count :], "p", ahead)
     extended = jnp.concatenate([tail_rows, kv_product], 0)
-    query = short_all[:, 0]
+    query = short_all[:, :half]
     shaped = my_filter * jnp.exp(
         -my_decay[None, :] * jnp.arange(tap_count, dtype=jnp.float32)[:, None]
     )

time: 318 us -> 302 us (0.950)
  other arithmetic: 75.6 us -> 68.4 us
  local copies, waits for them, and re-layouts: 25.3 us -> 18.4 us
    reshape x1 -> x0, local copies, waits for them, and re-layouts: 5.27 us -> none  [block_body(): projected = jnp.stack([first, second], 1).reshape(col_rows, 3, half)]
    add x1, other arithmetic: 6.31 us -> 1.88 us  [short_filter(): running + jnp.where(inside, short_taps[tap_index][None] * window, jnp.flo...]
    unnamed x30 -> x25, local copies, waits for them, and re-layouts: 8.78 us -> 10.3 us
  transfers between devices with their start and end apart: 17 -> 17, of which waited for: 12 -> 12; matrix products, arithmetic and copies ran while one was open for 31% -> 30% of each run, Pallas kernels for 0% -> 0%
where the time goes in v5:
time: 302 us; the launch traced here: 301 us
  waiting for transfers between devices  155 us (51%)
  other arithmetic  68.4 us (23%)
  starting transfers between devices  23.5 us (8%)
  matrix products  19.9 us (7%)
  local copies, waits for them, and re-layouts  18.4 us (6%)
  between operations  13.4 us (4%)
    reduce_scatter x1, waiting for transfers between devices, block_body(): lax.psum_scatter(lax.dot_general(lhs, rhs, (((1,), (1,)), ((), ())), pref...  55.2 us
    add x8, other arithmetic, tap_group(): running + jnp.where(inside, weight_row * window.astype(jnp.float32), jnp....  51.4 us
    ppermute x4, waiting for transfers between devices, z_ring_gather(): going_right = lax.ppermute(going_right, ('zh', 'zl'), right)  45.3 us
    all_gather x1, waiting for transfers between devices, block_body(): in_full = lax.all_gather(in_piece, 'p', axis=0, tiled=True)  30.4 us
    dot_general x2, matrix products, project(): out = jnp.dot(flat, flat_in, preferred_element_type=jnp.float32)  13.3 us
    unnamed x25, local copies, waits for them, and re-layouts  10.3 us
    ppermute x2, starting transfers between devices, swap_half(): got = lax.ppermute(give, 'zh', [(0, 1), (1, 0)])  8.51 us
    ppermute x3, starting transfers between devices, z_ring_gather(): going_left = lax.ppermute(going_left, ('zh', 'zl'), left)  7.89 us
  transfers between devices with their start and end apart: 17, of which 12 were waited for; matrix products, arithmetic and copies ran while one was open for 30% of the time, Pallas kernels for 0%

profile of v5, /device:TPU:2, one launch (start us, length us, event | category | flops | bytes accessed | tf_op | source)
XLA Modules:
  0.0 301.1 jit_solution(8688722172114003612)
XLA Ops:
  6.5 1.2 fusion.16
  7.8 2.0 fusion.17
  9.8 1.9 collective-permute-start
  11.7 16.1 %collective-permute-done = bf16[64,4096]{1,0:T(8,128)(2,1)S(1)} collective-permute-done((bf16[64,4096]{1,0:T(8,128)(2,1)}, bf16[64,4096]{1,0:T(8,128)(2,1)S(1)}, u32[]{:S(2)}, u32[]{:S(2)}) %collective-permute-start) | collective-permute-done | bytes 524320 | tf_op jit(solution)/shard_map/ppermute | solution.py:62
  27.8 3.2 %collective-permute-start.4 = (bf16[64,4096]{1,0:T(8,128)(2,1)}, bf16[64,4096]{1,0:T(8,128)(2,1)S(1)}, u32[]{:S(2)}, u32[]{:S(2)}) collective-permute-start(bf16[64,4096]{1,0:T(8,128)(2,1)} %fusion.17), channel_id=1, source_target_pairs={{0,14},{2,0},{4,2},{6,4},{8,6},{10,8},{12,10},{14,12},{1,15},{3,1}... | collective-permute-start | bytes 1572872 | tf_op jit(solution)/shard_map/ppermute | solution.py:65
  31.0 11.1 %collective-permute-done.1 = bf16[64,4096]{1,0:T(8,128)(2,1)S(1)} collective-permute-done((bf16[64,4096]{1,0:T(8,128)(2,1)S(1)}, bf16[64,4096]{1,0:T(8,128)(2,1)S(1)}, u32[]{:S(2)}, u32[]{:S(2)}) %collective-permute-start.1) | collective-permute-done | bytes 524320 | tf_op jit(solution)/shard_map/ppermute | solution.py:62
  42.1 1.0 fusion.31
  43.1 0.2 copy.23
  43.3 0.2 copy.22
  43.5 4.1 %collective-permute-start.7 = (bf16[128,3,256]{0,2,1:T(8,128)(2,1)S(1)}, bf16[128,3,256]{0,2,1:T(8,128)(2,1)S(1)}, u32[]{:S(2)}, u32[]{:S(2)}) collective-permute-start(bf16[128,3,256]{0,2,1:T(8,128)(2,1)S(1)} %broadcast_select_fusion.5), channel_id=1, source_target_pairs={{0,8},{8,0},{1,9},{9,1},{2,10},{10,2},{3,11},{11,3},{4,12},{12,4},... | collective-permute-start | bytes 589832 | tf_op jit(solution)/shard_map/ppermute | solution.py:48
  47.6 3.3 %collective-permute-start.5 = (bf16[64,4096]{1,0:T(8,128)(2,1)S(1)}, bf16[64,4096]{1,0:T(8,128)(2,1)}, u32[]{:S(2)}, u32[]{:S(2)}) collective-permute-start(bf16[64,4096]{1,0:T(8,128)(2,1)S(1)} %collective-permute-done.4), channel_id=1, source_target_pairs={{0,14},{2,0},{4,2},{6,4},{8,6},{10,8},{12,10},{14,12},{1,15},{3,1}... | collective-permute-start | bytes 1572872 | tf_op jit(solution)/shard_map/ppermute | solution.py:65
  50.9 12.3 %collective-permute-done.2 = bf16[64,4096]{1,0:T(8,128)(2,1)} collective-permute-done((bf16[64,4096]{1,0:T(8,128)(2,1)S(1)}, bf16[64,4096]{1,0:T(8,128)(2,1)}, u32[]{:S(2)}, u32[]{:S(2)}) %collective-permute-start.2) | collective-permute-done | bytes 524320 | tf_op jit(solution)/shard_map/ppermute | solution.py:62
  63.3 3.9 %collective-permute-done.7 = bf16[128,3,256]{0,2,1:T(8,128)(2,1)S(1)} collective-permute-done((bf16[128,3,256]{0,2,1:T(8,128)(2,1)S(1)}, bf16[128,3,256]{0,2,1:T(8,128)(2,1)S(1)}, u32[]{:S(2)}, u32[]{:S(2)}) %collective-permute-start.7) | collective-permute-done | bytes 196640 | tf_op jit(solution)/shard_map/ppermute | solution.py:48
  67.3 0.8 pad_maximum_fusion.3
  68.1 1.4 collective-permute-start.6
  69.5 5.8 %collective-permute-done.3 = bf16[64,4096]{1,0:T(8,128)(2,1)} collective-permute-done((bf16[64,4096]{1,0:T(8,128)(2,1)}, bf16[64,4096]{1,0:T(8,128)(2,1)}, u32[]{:S(2)}, u32[]{:S(2)}) %collective-permute-start.3) | collective-permute-done | bytes 524320 | tf_op jit(solution)/shard_map/ppermute | solution.py:62
  75.3 1.9 bitcast_dynamic-update-slice_fusion.7
  77.2 1.9 bitcast_dynamic-update-slice_fusion.6
  79.1 0.8 bitcast_dynamic-update-slice_fusion.5
  79.9 0.9 bitcast_dynamic-update-slice_fusion.4
  80.8 1.0 bitcast_dynamic-update-slice_fusion.3
  81.8 0.8 bitcast_dynamic-update-slice_fusion.2
  82.6 1.9 bitcast_dynamic-update-slice_fusion.1
  84.5 0.9 bitcast_dynamic-update-slice_fusion
  85.4 5.1 %gather_fusion = bf16[8,64,4096]{2,1,0:T(8,128)(2,1)} fusion(bf16[8,64,4096]{2,1,0:T(8,128)(2,1)} %bitcast_dynamic-update-slice_fusion, s32[1024]{0:T(1024)S(1)} %pad_clamp_fusion), kind=kCustom, calls=%fused_computation | custom fusion | bytes 8388640 | tf_op jit(solution)/shard_map/jit(_take)/gather | solution.py:70
  90.5 4.8 %broadcast_select_fusion = bf16[8,64,4096]{2,1,0:T(8,128)(2,1)} fusion(bf16[8,64,4096]{2,1,0:T(8,128)(2,1)} %gather_fusion, pred[8]{0:T(512)(128)(4,1)S(1)} %compare_and_fusion), kind=kLoop, calls=%fused_computation.50 | loop fusion | flops 2097152 | bytes 8388616 | tf_op jit(solution)/shard_map/jit(_take)/select_n | solution.py:70
  95.3 0.1 copy.20
  95.4 0.6 collective-permute-start.11
  96.0 0.1 copy.16
  96.1 0.1 reduce-window.9
  96.2 0.1 reduce
  96.5 0.1 select_reduce_fusion
  96.7 6.1 %collective-permute-done.11 = bf16[128,512]{0,1:T(8,128)(2,1)S(1)} collective-permute-done((bf16[128,512]{0,1:T(8,128)(2,1)S(1)}, bf16[128,512]{0,1:T(8,128)(2,1)S(1)}, u32[]{:S(2)}, u32[]{:S(2)}) %collective-permute-start.11) | collective-permute-done | bytes 131104 | tf_op jit(solution)/shard_map/ppermute | solution.py:89
  102.9 4.4 %collective-permute-start.12 = (bf16[128,2,256]{0,2,1:T(8,128)(2,1)S(1)}, bf16[128,2,256]{0,2,1:T(8,128)(2,1)S(1)}, u32[]{:S(2)}, u32[]{:S(2)}) collective-permute-start(bf16[128,2,256]{0,2,1:T(8,128)(2,1)S(1)} %broadcast_select_fusion.9), channel_id=1, source_target_pairs={{0,8},{8,0},{1,9},{9,1},{2,10},{10,2},{3,11},{11,3},{4,12},{12,4},... | collective-permute-start | bytes 393224 | tf_op jit(solution)/shard_map/ppermute | solution.py:48
  107.3 30.4 %all-gather.3.cloned.1.call-done = bf16[4096,3,256]{0,2,1:T(8,128)(2,1)} async-done(((bf16[256,3,256]{0,2,1:T(8,128)(2,1)}), bf16[4096,3,256]{0,2,1:T(8,128)(2,1)}) %all-gather.3.cloned.1.call-update) | async-done | bytes 6291472 | tf_op jit(solution)/shard_map/all_gather | solution.py:86
  137.7 7.6 %convolution_convert_fusion.1 = bf16[512,768]{1,0:T(8,128)(2,1)S(1)} fusion(bf16[512,4096]{1,0:T(8,128)(2,1)} %bitcast.12, bf16[4096,768]{0,1:T(8,128)(2,1)} %bitcast.113), kind=kOutput, calls=%fused_computation.60 | convolution fusion | flops 3221618688 | bytes 11272192 | tf_op jit(solution)/shard_map/dot_general | solution.py:99
  145.4 5.7 %broadcast_select_fusion.2 = (bf16[512,768]{1,0:T(8,128)(2,1)S(1)}, bf16[512,768]{1,0:T(8,128)(2,1)S(1)}) fusion(bf16[512,768]{1,0:T(8,128)(2,1)S(1)} %convolution_convert_fusion.1, pred[]{:T(512)S(6)} %eq.6, bf16[512,4096]{1,0:T(8,128)(2,1)} %bitcast.10, bf16[4096,768]{0,1:T(8,128)(2,1)S(1)} %bitcast.114), kind=kOutput, calls=%fused_computation.70 | convolution fusion | flops 3222405120 | bytes 12845057 | tf_op jit(solution)/shard_map/dot_general | solution.py:99
  151.1 0.1 pad_maximum_fusion.1
  151.2 0.1 copy.19
  151.4 2.2 collective-permute-start.9
  153.6 3.2 %collective-permute-done.9 = bf16[2,768]{1,0:T(2,128)(2,1)S(1)} collective-permute-done((bf16[2,768]{1,0:T(2,128)(2,1)S(1)}, bf16[2,768]{1,0:T(2,128)(2,1)S(1)}, u32[]{:S(2)}, u32[]{:S(2)}) %collective-permute-start.9) | collective-permute-done | bytes 3104 | tf_op jit(solution)/shard_map/ppermute | solution.py:120
  156.9 1.9 select_add_fusion.1
  158.8 1.7 copy-done
  160.4 0.1 fusion.19
  160.5 2.3 collective-permute-start.10
  162.8 0.7 pad_maximum_fusion.4
  163.6 3.1 %collective-permute-done.10 = bf16[128,256]{1,0:T(8,128)(2,1)S(1)} collective-permute-done((bf16[128,256]{1,0:T(8,128)(2,1)S(1)}, bf16[128,256]{1,0:T(8,128)(2,1)S(1)}, u32[]{:S(2)}, u32[]{:S(2)}) %collective-permute-start.10) | collective-permute-done | bytes 65568 | tf_op jit(solution)/shard_map/ppermute | solution.py:125
  166.7 54.6 %while.17 = (s32[]{:T(128)}, f32[1024,256]{1,0:T(8,128)S(1)}, s32[1024]{0:T(1024)S(1)}, f32[128,256]{1,0:T(8,128)S(1)}, bf16[1152,256]{1,0:T(8,128)(2,1)S(1)}, /...) while((s32[]{:T(128)}, f32[1024,256]{1,0:T(8,128)S(1)}, ...), condition=%wide.region_4.5_spmd.clone, body=%wide.region_3.4_spmd.clone.sunk | while | flops 17055876 | bytes 10573791 | solution.py:39
  167.1 6.4 %fusion.38 = f32[1024,256]{1,0:T(8,128)S(1)} fusion(f32[1024,256]{1,0:T(8,128)S(1)} %get-tuple-element.429, bf16[1152,256]{1,0:T(8,128)(2,1)S(1)} %get-tuple-element.471, s32[]{:T(128)S(6)} %select_n.888, f32[256]{0:T(256)S(1)} %bitcast.97, s32[]{:T(128)S(6)} %select_n.905, f32[256]{0:T(256)S(1)} %bitcast.98, s32[]{:T(128)S(6)} %select_n.906, ...), kind=kLoop, calls=%fused_computation.16.clone.1 | loop fusion | flops 17039360 | bytes 10518593 | tf_op jit(solution)/shard_map/while/body/eval_jaxpr/add | solution.py:33
  173.7 0.1 constant_dynamic-slice_fusion.21
  174.0 6.4 %fusion.38 = f32[1024,256]{1,0:T(8,128)S(1)} fusion(f32[1024,256]{1,0:T(8,128)S(1)} %get-tuple-element.429, bf16[1152,256]{1,0:T(8,128)(2,1)S(1)} %get-tuple-element.471, s32[]{:T(128)S(6)} %select_n.888, f32[256]{0:T(256)S(1)} %bitcast.97, s32[]{:T(128)S(6)} %select_n.905, f32[256]{0:T(256)S(1)} %bitcast.98, s32[]{:T(128)S(6)} %select_n.906, ...), kind=kLoop, calls=%fused_computation.16.clone.1 | loop fusion | flops 17039360 | bytes 10518593 | tf_op jit(solution)/shard_map/while/body/eval_jaxpr/add | solution.py:33
  180.8 6.4 %fusion.38 = f32[1024,256]{1,0:T(8,128)S(1)} fusion(f32[1024,256]{1,0:T(8,128)S(1)} %get-tuple-element.429, bf16[1152,256]{1,0:T(8,128)(2,1)S(1)} %get-tuple-element.471, s32[]{:T(128)S(6)} %select_n.888, f32[256]{0:T(256)S(1)} %bitcast.97, s32[]{:T(128)S(6)} %select_n.905, f32[256]{0:T(256)S(1)} %bitcast.98, s32[]{:T(128)S(6)} %select_n.906, ...), kind=kLoop, calls=%fused_computation.16.clone.1 | loop fusion | flops 17039360 | bytes 10518593 | tf_op jit(solution)/shard_map/while/body/eval_jaxpr/add | solution.py:33
  187.6 6.4 %fusion.38 = f32[1024,256]{1,0:T(8,128)S(1)} fusion(f32[1024,256]{1,0:T(8,128)S(1)} %get-tuple-element.429, bf16[1152,256]{1,0:T(8,128)(2,1)S(1)} %get-tuple-element.471, s32[]{:T(128)S(6)} %select_n.888, f32[256]{0:T(256)S(1)} %bitcast.97, s32[]{:T(128)S(6)} %select_n.905, f32[256]{0:T(256)S(1)} %bitcast.98, s32[]{:T(128)S(6)} %select_n.906, ...), kind=kLoop, calls=%fused_computation.16.clone.1 | loop fusion | flops 17039360 | bytes 10518593 | tf_op jit(solution)/shard_map/while/body/eval_jaxpr/add | solution.py:33
  194.5 6.4 %fusion.38 = f32[1024,256]{1,0:T(8,128)S(1)} fusion(f32[1024,256]{1,0:T(8,128)S(1)} %get-tuple-element.429, bf16[1152,256]{1,0:T(8,128)(2,1)S(1)} %get-tuple-element.471, s32[]{:T(128)S(6)} %select_n.888, f32[256]{0:T(256)S(1)} %bitcast.97, s32[]{:T(128)S(6)} %select_n.905, f32[256]{0:T(256)S(1)} %bitcast.98, s32[]{:T(128)S(6)} %select_n.906, ...), kind=kLoop, calls=%fused_computation.16.clone.1 | loop fusion | flops 17039360 | bytes 10518593 | tf_op jit(solution)/shard_map/while/body/eval_jaxpr/add | solution.py:33
  201.3 6.4 %fusion.38 = f32[1024,256]{1,0:T(8,128)S(1)} fusion(f32[1024,256]{1,0:T(8,128)S(1)} %get-tuple-element.429, bf16[1152,256]{1,0:T(8,128)(2,1)S(1)} %get-tuple-element.471, s32[]{:T(128)S(6)} %select_n.888, f32[256]{0:T(256)S(1)} %bitcast.97, s32[]{:T(128)S(6)} %select_n.905, f32[256]{0:T(256)S(1)} %bitcast.98, s32[]{:T(128)S(6)} %select_n.906, ...), kind=kLoop, calls=%fused_computation.16.clone.1 | loop fusion | flops 17039360 | bytes 10518593 | tf_op jit(solution)/shard_map/while/body/eval_jaxpr/add | solution.py:33
  208.1 6.4 %fusion.38 = f32[1024,256]{1,0:T(8,128)S(1)} fusion(f32[1024,256]{1,0:T(8,128)S(1)} %get-tuple-element.429, bf16[1152,256]{1,0:T(8,128)(2,1)S(1)} %get-tuple-element.471, s32[]{:T(128)S(6)} %select_n.888, f32[256]{0:T(256)S(1)} %bitcast.97, s32[]{:T(128)S(6)} %select_n.905, f32[256]{0:T(256)S(1)} %bitcast.98, s32[]{:T(128)S(6)} %select_n.906, ...), kind=kLoop, calls=%fused_computation.16.clone.1 | loop fusion | flops 17039360 | bytes 10518593 | tf_op jit(solution)/shard_map/while/body/eval_jaxpr/add | solution.py:33
  215.0 6.4 %fusion.38 = f32[1024,256]{1,0:T(8,128)S(1)} fusion(f32[1024,256]{1,0:T(8,128)S(1)} %get-tuple-element.429, bf16[1152,256]{1,0:T(8,128)(2,1)S(1)} %get-tuple-element.471, s32[]{:T(128)S(6)} %select_n.888, f32[256]{0:T(256)S(1)} %bitcast.97, s32[]{:T(128)S(6)} %select_n.905, f32[256]{0:T(256)S(1)} %bitcast.98, s32[]{:T(128)S(6)} %select_n.906, ...), kind=kLoop, calls=%fused_computation.16.clone.1 | loop fusion | flops 17039360 | bytes 10518593 | tf_op jit(solution)/shard_map/while/body/eval_jaxpr/add | solution.py:33
  221.4 1.4 fusion.20
  222.8 6.4 %all-gather.5.cloned.1.call-done = bf16[4096,2,256]{0,2,1:T(8,128)(2,1)} async-done(((bf16[256,2,256]{0,2,1:T(8,128)(2,1)}), bf16[4096,2,256]{0,2,1:T(8,128)(2,1)}) %all-gather.5.cloned.1.call-update) | async-done | bytes 4194320 | tf_op jit(solution)/shard_map/all_gather | solution.py:91
  229.2 0.1 collective-permute-start.13
  229.3 1.5 collective-permute-done.13
  230.8 6.6 %convolution_convert_fusion = bf16[512,4096]{1,0:T(8,128)(2,1)} fusion(bf16[4096,512]{0,1:T(8,128)(2,1)} %bitcast.115, bf16[512,256]{1,0:T(8,128)(2,1)S(1)} %bitcast.116, bf16[512,256]{1,0:T(8,128)(2,1)S(1)} %bitcast.95), kind=kOutput, calls=%fused_computation.49 | convolution fusion | flops 2150629376 | bytes 8912896 | tf_op jit(solution)/shard_map/dot_general | solution.py:143
  237.4 55.2 %reduce-scatter.2.cloned.1.call-done = bf16[64,4096]{1,0:T(8,128)(2,1)} async-done(((bf16[512,4096]{1,0:T(8,128)(2,1)}), bf16[64,4096]{1,0:T(8,128)(2,1)}) %reduce-scatter.2.cloned.1.call-update) | async-done | bytes 524304 | tf_op jit(solution)/shard_map/reduce_scatter | solution.py:142
  292.6 2.0 fusion.18
  (68 shorter events, 1.6 us)
Async XLA Ops:
  6.5 131.2 %all-gather.3.cloned.1.call-start = ((), (), s32[]{:S(2)}) async-start(), calls=%async_computation.1 | async-start | bytes 6684672 | tf_op jit(solution)/shard_map/all_gather | solution.py:86
  9.8 18.0 %collective-permute-start = (bf16[64,4096]{1,0:T(8,128)(2,1)}, bf16[64,4096]{1,0:T(8,128)(2,1)S(1)}, u32[]{:S(2)}, u32[]{:S(2)}) collective-permute-start(bf16[64,4096]{1,0:T(8,128)(2,1)} %fusion.17), channel_id=1, source_target_pairs={{0,2},{2,4},{4,6},{6,8},{8,10},{10,12},{12,14},{14,0},{1,3},{3,5},... | collective-permute-start | bytes 1572872 | tf_op jit(solution)/shard_map/ppermute | solution.py:62
  27.8 14.3 %collective-permute-start.1 = (bf16[64,4096]{1,0:T(8,128)(2,1)S(1)}, bf16[64,4096]{1,0:T(8,128)(2,1)S(1)}, u32[]{:S(2)}, u32[]{:S(2)}) collective-permute-start(bf16[64,4096]{1,0:T(8,128)(2,1)S(1)} %collective-permute-done), channel_id=1, source_target_pairs={{0,2},{2,4},{4,6},{6,8},{8,10},{10,12},{12,14},{14,0},{1,3},{3,5},... | collective-permute-start | bytes 1572872 | tf_op jit(solution)/shard_map/ppermute | solution.py:62
  27.8 19.8 %collective-permute-start.4 = (bf16[64,4096]{1,0:T(8,128)(2,1)}, bf16[64,4096]{1,0:T(8,128)(2,1)S(1)}, u32[]{:S(2)}, u32[]{:S(2)}) collective-permute-start(bf16[64,4096]{1,0:T(8,128)(2,1)} %fusion.17), channel_id=1, source_target_pairs={{0,14},{2,0},{4,2},{6,4},{8,6},{10,8},{12,10},{14,12},{1,15},{3,1}... | collective-permute-start | bytes 1572872 | tf_op jit(solution)/shard_map/ppermute | solution.py:65
  31.0 49.8 %copy-start.1 = (bf16[64,4096]{1,0:T(8,128)(2,1)S(1)}, bf16[64,4096]{1,0:T(8,128)(2,1)}, u32[]{:S(2)}) copy-start(bf16[64,4096]{1,0:T(8,128)(2,1)} %param.9) | copy-start | bytes 1572868
  42.1 21.2 %collective-permute-start.2 = (bf16[64,4096]{1,0:T(8,128)(2,1)S(1)}, bf16[64,4096]{1,0:T(8,128)(2,1)}, u32[]{:S(2)}, u32[]{:S(2)}) collective-permute-start(bf16[64,4096]{1,0:T(8,128)(2,1)S(1)} %collective-permute-done.1), channel_id=1, source_target_pairs={{0,2},{2,4},{4,6},{6,8},{8,10},{10,12},{12,14},{14,0},{1,3},{3,5},... | collective-permute-start | bytes 1572872 | tf_op jit(solution)/shard_map/ppermute | solution.py:62
  43.5 23.7 %collective-permute-start.7 = (bf16[128,3,256]{0,2,1:T(8,128)(2,1)S(1)}, bf16[128,3,256]{0,2,1:T(8,128)(2,1)S(1)}, u32[]{:S(2)}, u32[]{:S(2)}) collective-permute-start(bf16[128,3,256]{0,2,1:T(8,128)(2,1)S(1)} %broadcast_select_fusion.5), channel_id=1, source_target_pairs={{0,8},{8,0},{1,9},{9,1},{2,10},{10,2},{3,11},{11,3},{4,12},{12,4},... | collective-permute-start | bytes 589832 | tf_op jit(solution)/shard_map/ppermute | solution.py:48
  47.6 20.5 %collective-permute-start.5 = (bf16[64,4096]{1,0:T(8,128)(2,1)S(1)}, bf16[64,4096]{1,0:T(8,128)(2,1)}, u32[]{:S(2)}, u32[]{:S(2)}) collective-permute-start(bf16[64,4096]{1,0:T(8,128)(2,1)S(1)} %collective-permute-done.4), channel_id=1, source_target_pairs={{0,14},{2,0},{4,2},{6,4},{8,6},{10,8},{12,10},{14,12},{1,15},{3,1}... | collective-permute-start | bytes 1572872 | tf_op jit(solution)/shard_map/ppermute | solution.py:65
  63.3 12.0 %collective-permute-start.3 = (bf16[64,4096]{1,0:T(8,128)(2,1)}, bf16[64,4096]{1,0:T(8,128)(2,1)}, u32[]{:S(2)}, u32[]{:S(2)}) collective-permute-start(bf16[64,4096]{1,0:T(8,128)(2,1)} %collective-permute-done.2), channel_id=1, source_target_pairs={{0,2},{2,4},{4,6},{6,8},{8,10},{10,12},{12,14},{14,0},{1,3},{3,5},... | collective-permute-start | bytes 1572872 | tf_op jit(solution)/shard_map/ppermute | solution.py:62
  68.1 161.1 %all-gather.5.cloned.1.call-start = ((), (), s32[]{:S(2)}) async-start(), calls=%async_computation.2 | async-start | bytes 4456448 | tf_op jit(solution)/shard_map/all_gather | solution.py:91
  68.1 16.4 %collective-permute-start.6 = (bf16[64,4096]{1,0:T(8,128)(2,1)}, bf16[64,4096]{1,0:T(8,128)(2,1)S(1)}, u32[]{:S(2)}, u32[]{:S(2)}) collective-permute-start(bf16[64,4096]{1,0:T(8,128)(2,1)} %collective-permute-done.5), channel_id=1, source_target_pairs={{0,14},{2,0},{4,2},{6,4},{8,6},{10,8},{12,10},{14,12},{1,15},{3,1}... | collective-permute-start | bytes 1572872 | tf_op jit(solution)/shard_map/ppermute | solution.py:65
  90.5 4.8 %copy-start.2 = (bf16[128,512]{1,0:T(8,128)(2,1)S(1)}, bf16[128,512]{1,0:T(8,128)(2,1)}, u32[]{:S(2)}) copy-start(bf16[128,512]{1,0:T(8,128)(2,1)} %param.11) | copy-start | bytes 393220
  90.5 5.5 %copy-start.5 = (s32[64]{0:T(128)S(1)}, s32[64]{0:T(128)}, u32[]{:S(2)}) copy-start(s32[64]{0:T(128)} %param.15) | copy-start | bytes 772
  90.5 5.8 %copy-start.4 = (f32[3,3,512]{2,1,0:T(4,128)S(1)}, f32[3,3,512]{2,1,0:T(4,128)}, u32[]{:S(2)}) copy-start(f32[3,3,512]{2,1,0:T(4,128)} %param.12) | copy-start | bytes 55300
  90.5 5.9 %copy-start.6 = (f32[512]{0:T(512)S(1)}, f32[512]{0:T(512)}, u32[]{:S(2)}) copy-start(f32[512]{0:T(512)} %param.14) | copy-start | bytes 6148
  90.5 6.1 %copy-start.3 = (f32[128,512]{1,0:T(8,128)S(1)}, f32[128,512]{1,0:T(8,128)}, u32[]{:S(2)}) copy-start(f32[128,512]{1,0:T(8,128)} %param.13) | copy-start | bytes 786436
  95.3 12.0 %collective-permute-start.8 = (bf16[8,64,4096]{2,1,0:T(8,128)(2,1)}, bf16[8,64,4096]{2,1,0:T(8,128)(2,1)}, u32[]{:S(2)}, u32[]{:S(2)}) collective-permute-start(bf16[8,64,4096]{2,1,0:T(8,128)(2,1)} %broadcast_select_fusion), channel_id=1, source_target_pairs={{0,1},{1,0},{2,3},{3,2},{4,5},{5,4},{6,7},{7,6},{8,9},{9,8},{10,11... | collective-permute-start | bytes 12582920 | tf_op jit(solution)/shard_map/ppermute | solution.py:102
  95.4 7.4 %collective-permute-start.11 = (bf16[128,512]{0,1:T(8,128)(2,1)S(1)}, bf16[128,512]{0,1:T(8,128)(2,1)S(1)}, u32[]{:S(2)}, u32[]{:S(2)}) collective-permute-start(bf16[128,512]{0,1:T(8,128)(2,1)S(1)} %copy.20), channel_id=1, source_target_pairs={{0,1},{1,0},{2,3},{3,2},{4,5},{5,4},{6,7},{7,6},{8,9},{9,8},{10,11... | collective-permute-start | bytes 393224 | tf_op jit(solution)/shard_map/ppermute | solution.py:89
  102.9 50.7 %collective-permute-start.12 = (bf16[128,2,256]{0,2,1:T(8,128)(2,1)S(1)}, bf16[128,2,256]{0,2,1:T(8,128)(2,1)S(1)}, u32[]{:S(2)}, u32[]{:S(2)}) collective-permute-start(bf16[128,2,256]{0,2,1:T(8,128)(2,1)S(1)} %broadcast_select_fusion.9), channel_id=1, source_target_pairs={{0,8},{8,0},{1,9},{9,1},{2,10},{10,2},{3,11},{11,3},{4,12},{12,4},... | collective-permute-start | bytes 393224 | tf_op jit(solution)/shard_map/ppermute | solution.py:48
  137.7 7.7 %copy-start.7 = (bf16[4096,3,256]{0,2,1:T(8,128)(2,1)S(1)}, bf16[4096,3,256]{0,2,1:T(8,128)(2,1)}, u32[]{:S(2)}) copy-start(bf16[4096,3,256]{0,2,1:T(8,128)(2,1)} %all-gather.3.cloned.1.call-done) | copy-start | bytes 18874372
  151.4 5.5 %collective-permute-start.9 = (bf16[2,768]{1,0:T(2,128)(2,1)S(1)}, bf16[2,768]{1,0:T(2,128)(2,1)S(1)}, u32[]{:S(2)}, u32[]{:S(2)}) collective-permute-start(bf16[2,768]{1,0:T(2,128)(2,1)S(1)} %slice.61), channel_id=1, source_target_pairs={{0,16},{16,32},{32,48},{48,64},{64,80},{80,96},{96,112},{112,128},... | collective-permute-start | bytes 9224 | tf_op jit(solution)/shard_map/ppermute | solution.py:120
  158.7 1.7 copy-start
  160.5 6.2 %collective-permute-start.10 = (bf16[128,256]{1,0:T(8,128)(2,1)S(1)}, bf16[128,256]{1,0:T(8,128)(2,1)S(1)}, u32[]{:S(2)}, u32[]{:S(2)}) collective-permute-start(bf16[128,256]{1,0:T(8,128)(2,1)S(1)} %slice.67), channel_id=1, source_target_pairs={{0,16},{16,32},{32,48},{48,64},{64,80},{80,96},{96,112},{112,128},... | collective-permute-start | bytes 196616 | tf_op jit(solution)/shard_map/ppermute | solution.py:125
  163.6 129.0 %reduce-scatter.2.cloned.1.call-start = ((), (), s32[]{:S(2)}) async-start(), calls=%async_computation.3 | async-start | bytes 4718592 | tf_op jit(solution)/shard_map/reduce_scatter | solution.py:142
  229.2 1.6 collective-permute-start.13
Sparse Core Ops, SparseCore 0:
  68.2 69.4 all-gather.2
  163.7 65.3 all-gather.4
  237.5 55.0 reduce-scatter.1

commit v6 on v5

--- a/solution.py
+++ b/solution.py
@@ -22,20 +22,26 @@
     return running
 
 
-def long_filter(extended, shaped, positions, out_count, tap_count):
+def long_filter(extended, shaped, positions, blocks, part, parts, tap_count):
+    out_count = positions.shape[0]
+    block_rows = out_count // blocks
+    sub = block_rows // parts
+    pick = slice(part * sub, (part + 1) * sub)
+    where_in = positions.reshape(blocks, block_rows)[:, pick]
 
     def tap_group(group_index, running):
         for inner in range(16):
             tap_index = group_index * 16 + inner
             window = lax.dynamic_slice_in_dim(extended, tap_count - tap_index, out_count, 0)
+            window = window.reshape(blocks, block_rows, window.shape[1])[:, pick]
             weight_row = lax.dynamic_slice_in_dim(shaped, tap_index, 1, 0)
-            inside = (positions >= tap_index)[:, None]
+            inside = (where_in >= tap_index)[:, :, None]
             running = running + jnp.where(
-                inside, weight_row * window.astype(jnp.float32), jnp.float32(0.0)
+                inside, weight_row[None] * window.astype(jnp.float32), jnp.float32(0.0)
             )
         return running
 
-    zero_sum = jnp.zeros((out_count, shaped.shape[1]), jnp.float32)
+    zero_sum = jnp.zeros((blocks, sub, shaped.shape[1]), jnp.float32)
     return lax.fori_loop(0, tap_count // 16, tap_group, zero_sum)
 
 
@@ -128,25 +134,30 @@
     shaped = my_filter * jnp.exp(
         -my_decay[None, :] * jnp.arange(tap_count, dtype=jnp.float32)[:, None]
     )
-    long_mix = long_filter(extended, shaped, own_position, col_rows, tap_count)
-    gated_mix = (query * long_mix).astype(jnp.bfloat16)
-    gated_mix, out_full = lax.optimization_barrier((gated_mix, out_full))
     core = lax.axis_index("c")
     swap = [(0, 1), (1, 0)]
-    by_core = gated_mix.reshape(nz, 2, own_rows, half)
-    mine_rows = lax.dynamic_index_in_dim(by_core, core, 1, keepdims=False)
-    other_rows = lax.dynamic_index_in_dim(by_core, 1 - core, 1, keepdims=False)
-    partner_cols = lax.ppermute(other_rows, "c", swap)
-    lhs = jnp.concatenate([mine_rows, partner_cols], 2).reshape(nz * own_rows, 2 * half)
-    rhs = out_full
-    summed = lax.psum_scatter(
-        lax.dot_general(
-            lhs, rhs, (((1,), (1,)), ((), ())), preferred_element_type=jnp.float32
-        ).astype(jnp.bfloat16),
-        ("zh", "zl"),
-        scatter_dimension=0,
-        tiled=True,
-    ).astype(jnp.float32)
+    blocks = col_rows // own_rows
+    parts = 2
+    sub = own_rows // parts
+    query_blocks = query.reshape(blocks, own_rows, half)
+    pieces = []
+    for part in range(parts):
+        long_mix = long_filter(extended, shaped, own_position, blocks, part, parts, tap_count)
+        gated_mix = (query_blocks[:, part * sub : (part + 1) * sub] * long_mix).astype(jnp.bfloat16)
+        if part == 0:
+            gated_mix, out_full = lax.optimization_barrier((gated_mix, out_full))
+        by_core = gated_mix.reshape(nz, 2, sub, half)
+        mine_rows = lax.dynamic_index_in_dim(by_core, core, 1, keepdims=False)
+        other_rows = lax.dynamic_index_in_dim(by_core, 1 - core, 1, keepdims=False)
+        partner_cols = lax.ppermute(other_rows, "c", swap)
+        lhs = jnp.concatenate([mine_rows, partner_cols], 2).reshape(nz * sub, 2 * half)
+        partial = lax.dot_general(
+            lhs, out_full, (((1,), (1,)), ((), ())), preferred_element_type=jnp.float32
+        ).astype(jnp.bfloat16)
+        if part + 1 < parts:
+            extended, partial = lax.optimization_barrier((extended, partial))
+        pieces.append(lax.psum_scatter(partial, ("zh", "zl"), scatter_dimension=0, tiled=True))
+    summed = jnp.concatenate(pieces, 0).astype(jnp.float32)
     return (widened + summed).astype(jnp.bfloat16)
 
 

time: 302 us -> 379 us (1.25)
  local copies, waits for them, and re-layouts: 18.4 us -> 78.2 us
  other arithmetic: 68.4 us -> 96.6 us
  waiting for transfers between devices: 155 us -> 141 us
    dynamic_slice x0 -> x16, local copies, waits for them, and re-layouts: none -> 62.7 us  [tap_group(): lax.dynamic_slice_in_dim(extended, tap_count - tap_index, out_count, 0)]
    add x8 -> x16, other arithmetic: 51.4 us -> 76.9 us  [tap_group(): running + jnp.where(inside, weight_row[None] * window.astype(jnp.float32)...]
    reduce_scatter x1 -> x2, waiting for transfers between devices: 55.2 us -> 45.4 us  [block_body(): lax.psum_scatter(partial, ('zh', 'zl'), scatter_dimension=0, tiled=True)]
    all_gather x1, waiting for transfers between devices: 6.37 us -> 0.02 us  [block_body(): out_full = lax.all_gather(out_piece, 'p', axis=0, tiled=True)]
    dot_general x1 -> x2, matrix products: 6.56 us -> 9.75 us  [block_body(): lax.dot_general(lhs, out_full, (((1,), (1,)), ((), ())), preferred_elemen...]
  transfers between devices with their start and end apart: 17 -> 19, of which waited for: 12 -> 12; matrix products, arithmetic and copies ran while one was open for 30% -> 49% of each run, Pallas kernels for 0% -> 0%
where the time goes in v6:
time: 379 us; the launch traced here: 377 us
  waiting for transfers between devices  141 us (37%)
  other arithmetic  96.6 us (25%)
  local copies, waits for them, and re-layouts  78.2 us (21%)
  starting transfers between devices  23.7 us (6%)
  matrix products  23 us (6%)
  between operations  13.4 us (4%)
    add x16, other arithmetic, tap_group(): running + jnp.where(inside, weight_row[None] * window.astype(jnp.float32)...  76.9 us
    dynamic_slice x16, local copies, waits for them, and re-layouts, tap_group(): lax.dynamic_slice_in_dim(extended, tap_count - tap_index, out_count, 0)  62.7 us
    reduce_scatter x2, waiting for transfers between devices, block_body(): lax.psum_scatter(partial, ('zh', 'zl'), scatter_dimension=0, tiled=True)  45.4 us
    ppermute x4, waiting for transfers between devices, z_ring_gather(): going_right = lax.ppermute(going_right, ('zh', 'zl'), right)  45.2 us
    all_gather x1, waiting for transfers between devices, block_body(): in_full = lax.all_gather(in_piece, 'p', axis=0, tiled=True)  31.8 us
    dot_general x2, matrix products, project(): out = jnp.dot(flat, flat_in, preferred_element_type=jnp.float32)  13.3 us
    dot_general x2, matrix products, block_body(): lax.dot_general(lhs, out_full, (((1,), (1,)), ((), ())), preferred_elemen...  9.75 us
    ppermute x2, starting transfers between devices, swap_half(): got = lax.ppermute(give, 'zh', [(0, 1), (1, 0)])  8.25 us
  transfers between devices with their start and end apart: 19, of which 12 were waited for; matrix products, arithmetic and copies ran while one was open for 49% of the time, Pallas kernels for 0%

profile of v6, /device:TPU:2, one launch (start us, length us, event | category | flops | bytes accessed | tf_op | source)
XLA Modules:
  0.0 376.9 jit_solution(10775387247490315577)
XLA Ops:
  7.8 2.0 fusion.32
  9.8 1.9 collective-permute-start
  11.7 16.1 %collective-permute-done = bf16[64,4096]{1,0:T(8,128)(2,1)S(1)} collective-permute-done((bf16[64,4096]{1,0:T(8,128)(2,1)}, bf16[64,4096]{1,0:T(8,128)(2,1)S(1)}, u32[]{:S(2)}, u32[]{:S(2)}) %collective-permute-start) | collective-permute-done | bytes 524320 | tf_op jit(solution)/shard_map/ppermute | solution.py:68
  27.8 3.2 collective-permute-start.4
  31.0 11.1 %collective-permute-done.1 = bf16[64,4096]{1,0:T(8,128)(2,1)S(1)} collective-permute-done((bf16[64,4096]{1,0:T(8,128)(2,1)S(1)}, bf16[64,4096]{1,0:T(8,128)(2,1)S(1)}, u32[]{:S(2)}, u32[]{:S(2)}) %collective-permute-start.1) | collective-permute-done | bytes 524320 | tf_op jit(solution)/shard_map/ppermute | solution.py:68
  43.5 4.1 %collective-permute-start.7 = (bf16[128,3,256]{0,2,1:T(8,128)(2,1)S(1)}, bf16[128,3,256]{0,2,1:T(8,128)(2,1)S(1)}, u32[]{:S(2)}, u32[]{:S(2)}) collective-permute-start(bf16[128,3,256]{0,2,1:T(8,128)(2,1)S(1)} %broadcast_select_fusion.5), channel_id=1, source_target_pairs={{0,8},{8,0},{1,9},{9,1},{2,10},{10,2},{3,11},{11,3},{4,12},{12,4},... | collective-permute-start | bytes 589832 | tf_op jit(solution)/shard_map/ppermute | solution.py:54
  47.6 3.3 collective-permute-start.5
  50.9 12.2 %collective-permute-done.2 = bf16[64,4096]{1,0:T(8,128)(2,1)S(1)} collective-permute-done((bf16[64,4096]{1,0:T(8,128)(2,1)S(1)}, bf16[64,4096]{1,0:T(8,128)(2,1)S(1)}, u32[]{:S(2)}, u32[]{:S(2)}) %collective-permute-start.2) | collective-permute-done | bytes 524320 | tf_op jit(solution)/shard_map/ppermute | solution.py:68
  63.2 4.1 %collective-permute-done.7 = bf16[128,3,256]{0,2,1:T(8,128)(2,1)S(1)} collective-permute-done((bf16[128,3,256]{0,2,1:T(8,128)(2,1)S(1)}, bf16[128,3,256]{0,2,1:T(8,128)(2,1)S(1)}, u32[]{:S(2)}, u32[]{:S(2)}) %collective-permute-start.7) | collective-permute-done | bytes 196640 | tf_op jit(solution)/shard_map/ppermute | solution.py:54
  69.5 5.8 %collective-permute-done.3 = bf16[64,4096]{1,0:T(8,128)(2,1)} collective-permute-done((bf16[64,4096]{1,0:T(8,128)(2,1)S(1)}, bf16[64,4096]{1,0:T(8,128)(2,1)}, u32[]{:S(2)}, u32[]{:S(2)}) %collective-permute-start.3) | collective-permute-done | bytes 524320 | tf_op jit(solution)/shard_map/ppermute | solution.py:68
  75.3 1.9 bitcast_dynamic-update-slice_fusion.7
  81.6 1.9 bitcast_dynamic-update-slice_fusion.1
  84.3 5.1 %gather_fusion = bf16[8,64,4096]{2,1,0:T(8,128)(2,1)} fusion(bf16[8,64,4096]{2,1,0:T(8,128)(2,1)} %bitcast_dynamic-update-slice_fusion, s32[1024]{0:T(1024)S(1)} %pad_clamp_fusion), kind=kCustom, calls=%fused_computation | custom fusion | bytes 8388640 | tf_op jit(solution)/shard_map/jit(_take)/gather | solution.py:76
  89.4 4.8 %broadcast_select_fusion = bf16[8,64,4096]{2,1,0:T(8,128)(2,1)} fusion(bf16[8,64,4096]{2,1,0:T(8,128)(2,1)} %gather_fusion, pred[8]{0:T(512)(128)(4,1)S(1)} %compare_and_fusion), kind=kLoop, calls=%fused_computation.131 | loop fusion | flops 2097152 | bytes 8388616 | tf_op jit(solution)/shard_map/jit(_take)/select_n | solution.py:76
  95.7 6.0 %collective-permute-done.11 = bf16[128,512]{0,1:T(8,128)(2,1)S(1)} collective-permute-done((bf16[128,512]{0,1:T(8,128)(2,1)S(1)}, bf16[128,512]{0,1:T(8,128)(2,1)S(1)}, u32[]{:S(2)}, u32[]{:S(2)}) %collective-permute-start.11) | collective-permute-done | bytes 131104 | tf_op jit(solution)/shard_map/ppermute | solution.py:95
  101.8 4.2 %collective-permute-start.12 = (bf16[128,2,256]{0,2,1:T(8,128)(2,1)S(1)}, bf16[128,2,256]{0,2,1:T(8,128)(2,1)S(1)}, u32[]{:S(2)}, u32[]{:S(2)}) collective-permute-start(bf16[128,2,256]{0,2,1:T(8,128)(2,1)S(1)} %broadcast_select_fusion.9), channel_id=1, source_target_pairs={{0,8},{8,0},{1,9},{9,1},{2,10},{10,2},{3,11},{11,3},{4,12},{12,4},... | collective-permute-start | bytes 393224 | tf_op jit(solution)/shard_map/ppermute | solution.py:54
  105.9 31.8 %all-gather.3.cloned.1.call-done = bf16[4096,3,256]{0,2,1:T(8,128)(2,1)} async-done(((bf16[256,3,256]{0,2,1:T(8,128)(2,1)}), bf16[4096,3,256]{0,2,1:T(8,128)(2,1)}) %all-gather.3.cloned.1.call-update) | async-done | bytes 6291472 | tf_op jit(solution)/shard_map/all_gather | solution.py:92
  137.8 7.6 %convolution_convert_fusion.2 = bf16[512,768]{1,0:T(8,128)(2,1)S(1)} fusion(bf16[512,4096]{1,0:T(8,128)(2,1)} %bitcast.12, bf16[4096,768]{0,1:T(8,128)(2,1)} %bitcast.316), kind=kOutput, calls=%fused_computation.141 | convolution fusion | flops 3221618688 | bytes 11272192 | tf_op jit(solution)/shard_map/dot_general | solution.py:105
  145.4 5.7 %broadcast_select_fusion.2 = (bf16[512,768]{1,0:T(8,128)(2,1)S(1)}, bf16[512,768]{1,0:T(8,128)(2,1)S(1)}) fusion(bf16[512,768]{1,0:T(8,128)(2,1)S(1)} %convolution_convert_fusion.2, pred[]{:T(512)S(6)} %eq.6, bf16[512,4096]{1,0:T(8,128)(2,1)} %bitcast.10, bf16[4096,768]{0,1:T(8,128)(2,1)S(1)} %bitcast.317), kind=kOutput, calls=%fused_computation.149 | convolution fusion | flops 3222405120 | bytes 12845057 | tf_op jit(solution)/shard_map/dot_general | solution.py:105
  151.4 2.2 collective-permute-start.9
  153.7 3.2 collective-permute-done.9
  156.9 1.9 select_add_fusion.2
  159.9 2.3 collective-permute-start.10
  163.0 3.1 collective-permute-done.10
  166.1 70.8 %while.34 = (s32[]{:T(128)}, f32[16,32,256]{2,1,0:T(8,128)}, s32[16,32]{1,0:T(8,128)S(1)}, f32[128,256]{1,0:T(8,128)S(1)}, bf16[1152,256]{1,0:T(8,128)(2,1)S(1)}...) while((s32[]{:T(128)}, f32[16,32,256]{2,1,0:T(8,128)}, ...), condition=%wide.region_4.5_spmd.clone, body=%wide.region_3.4_spmd.clone.sunk | while | flops 8528003 | bytes 22089652 | solution.py:45
  166.2 4.0 %constant_dynamic-slice_fusion.73 = (bf16[1024,256]{1,0:T(8,128)(2,1)S(1)}, bf16[1024,256]{1,0:T(8,128)(2,1)S(1)}, bf16[1024,256]{1,0:T(8,128)(2,1)S(1)}, bf16[1...) fusion(bf16[1152,256]{1,0:T(8,128)(2,1)S(1)} %get-tuple-element, ...), kind=kLoop, calls=%fused_computation.47.clone.1 | loop fusion | bytes 16777280 | tf_op jit(solution)/shard_map/while/body/eval_jaxpr/dynamic_slice | solution.py:35
  170.3 4.7 %fusion.61 = f32[16,32,256]{2,1,0:T(8,128)} fusion(f32[16,32,256]{2,1,0:T(8,128)} %get-tuple-element.897, bf16[16,64,256]{2,1,0:T(8,128)(2,1)S(1)} %bitcast.238, bf16[16,64,256]{2,1,0:T(8,128)(2,1)S(1)} %bitcast.239, bf16[16,64,256]{2,1,0:T(8,128)(2,1)S(1)} %bitcast.240, bf16[16,64,256]{2,1,0:T(8,128)(2,1)S(1)} %bitcast.241, ...), kind=kLoop, calls=%fused_computation.16.clone.1 | loop fusion | flops 8519680 | bytes 5267457 | tf_op jit(solution)/shard_map/while/body/eval_jaxpr/add | solution.py:39
  175.0 3.9 %constant_dynamic-slice_fusion.73 = (bf16[1024,256]{1,0:T(8,128)(2,1)S(1)}, bf16[1024,256]{1,0:T(8,128)(2,1)S(1)}, bf16[1024,256]{1,0:T(8,128)(2,1)S(1)}, bf16[1...) fusion(bf16[1152,256]{1,0:T(8,128)(2,1)S(1)} %get-tuple-element, ...), kind=kLoop, calls=%fused_computation.47.clone.1 | loop fusion | bytes 16777280 | tf_op jit(solution)/shard_map/while/body/eval_jaxpr/dynamic_slice | solution.py:35
  179.0 4.8 %fusion.61 = f32[16,32,256]{2,1,0:T(8,128)} fusion(f32[16,32,256]{2,1,0:T(8,128)} %get-tuple-element.897, bf16[16,64,256]{2,1,0:T(8,128)(2,1)S(1)} %bitcast.238, bf16[16,64,256]{2,1,0:T(8,128)(2,1)S(1)} %bitcast.239, bf16[16,64,256]{2,1,0:T(8,128)(2,1)S(1)} %bitcast.240, bf16[16,64,256]{2,1,0:T(8,128)(2,1)S(1)} %bitcast.241, ...), kind=kLoop, calls=%fused_computation.16.clone.1 | loop fusion | flops 8519680 | bytes 5267457 | tf_op jit(solution)/shard_map/while/body/eval_jaxpr/add | solution.py:39
  183.8 4.0 %constant_dynamic-slice_fusion.73 = (bf16[1024,256]{1,0:T(8,128)(2,1)S(1)}, bf16[1024,256]{1,0:T(8,128)(2,1)S(1)}, bf16[1024,256]{1,0:T(8,128)(2,1)S(1)}, bf16[1...) fusion(bf16[1152,256]{1,0:T(8,128)(2,1)S(1)} %get-tuple-element, ...), kind=kLoop, calls=%fused_computation.47.clone.1 | loop fusion | bytes 16777280 | tf_op jit(solution)/shard_map/while/body/eval_jaxpr/dynamic_slice | solution.py:35
  187.9 4.8 %fusion.61 = f32[16,32,256]{2,1,0:T(8,128)} fusion(f32[16,32,256]{2,1,0:T(8,128)} %get-tuple-element.897, bf16[16,64,256]{2,1,0:T(8,128)(2,1)S(1)} %bitcast.238, bf16[16,64,256]{2,1,0:T(8,128)(2,1)S(1)} %bitcast.239, bf16[16,64,256]{2,1,0:T(8,128)(2,1)S(1)} %bitcast.240, bf16[16,64,256]{2,1,0:T(8,128)(2,1)S(1)} %bitcast.241, ...), kind=kLoop, calls=%fused_computation.16.clone.1 | loop fusion | flops 8519680 | bytes 5267457 | tf_op jit(solution)/shard_map/while/body/eval_jaxpr/add | solution.py:39
  192.7 3.9 %constant_dynamic-slice_fusion.73 = (bf16[1024,256]{1,0:T(8,128)(2,1)S(1)}, bf16[1024,256]{1,0:T(8,128)(2,1)S(1)}, bf16[1024,256]{1,0:T(8,128)(2,1)S(1)}, bf16[1...) fusion(bf16[1152,256]{1,0:T(8,128)(2,1)S(1)} %get-tuple-element, ...), kind=kLoop, calls=%fused_computation.47.clone.1 | loop fusion | bytes 16777280 | tf_op jit(solution)/shard_map/while/body/eval_jaxpr/dynamic_slice | solution.py:35
  196.7 4.8 %fusion.61 = f32[16,32,256]{2,1,0:T(8,128)} fusion(f32[16,32,256]{2,1,0:T(8,128)} %get-tuple-element.897, bf16[16,64,256]{2,1,0:T(8,128)(2,1)S(1)} %bitcast.238, bf16[16,64,256]{2,1,0:T(8,128)(2,1)S(1)} %bitcast.239, bf16[16,64,256]{2,1,0:T(8,128)(2,1)S(1)} %bitcast.240, bf16[16,64,256]{2,1,0:T(8,128)(2,1)S(1)} %bitcast.241, ...), kind=kLoop, calls=%fused_computation.16.clone.1 | loop fusion | flops 8519680 | bytes 5267457 | tf_op jit(solution)/shard_map/while/body/eval_jaxpr/add | solution.py:39
  201.5 4.0 %constant_dynamic-slice_fusion.73 = (bf16[1024,256]{1,0:T(8,128)(2,1)S(1)}, bf16[1024,256]{1,0:T(8,128)(2,1)S(1)}, bf16[1024,256]{1,0:T(8,128)(2,1)S(1)}, bf16[1...) fusion(bf16[1152,256]{1,0:T(8,128)(2,1)S(1)} %get-tuple-element, ...), kind=kLoop, calls=%fused_computation.47.clone.1 | loop fusion | bytes 16777280 | tf_op jit(solution)/shard_map/while/body/eval_jaxpr/dynamic_slice | solution.py:35
  205.6 4.8 %fusion.61 = f32[16,32,256]{2,1,0:T(8,128)} fusion(f32[16,32,256]{2,1,0:T(8,128)} %get-tuple-element.897, bf16[16,64,256]{2,1,0:T(8,128)(2,1)S(1)} %bitcast.238, bf16[16,64,256]{2,1,0:T(8,128)(2,1)S(1)} %bitcast.239, bf16[16,64,256]{2,1,0:T(8,128)(2,1)S(1)} %bitcast.240, bf16[16,64,256]{2,1,0:T(8,128)(2,1)S(1)} %bitcast.241, ...), kind=kLoop, calls=%fused_computation.16.clone.1 | loop fusion | flops 8519680 | bytes 5267457 | tf_op jit(solution)/shard_map/while/body/eval_jaxpr/add | solution.py:39
  210.4 3.9 %constant_dynamic-slice_fusion.73 = (bf16[1024,256]{1,0:T(8,128)(2,1)S(1)}, bf16[1024,256]{1,0:T(8,128)(2,1)S(1)}, bf16[1024,256]{1,0:T(8,128)(2,1)S(1)}, bf16[1...) fusion(bf16[1152,256]{1,0:T(8,128)(2,1)S(1)} %get-tuple-element, ...), kind=kLoop, calls=%fused_computation.47.clone.1 | loop fusion | bytes 16777280 | tf_op jit(solution)/shard_map/while/body/eval_jaxpr/dynamic_slice | solution.py:35
  214.4 4.9 %fusion.61 = f32[16,32,256]{2,1,0:T(8,128)} fusion(f32[16,32,256]{2,1,0:T(8,128)} %get-tuple-element.897, bf16[16,64,256]{2,1,0:T(8,128)(2,1)S(1)} %bitcast.238, bf16[16,64,256]{2,1,0:T(8,128)(2,1)S(1)} %bitcast.239, bf16[16,64,256]{2,1,0:T(8,128)(2,1)S(1)} %bitcast.240, bf16[16,64,256]{2,1,0:T(8,128)(2,1)S(1)} %bitcast.241, ...), kind=kLoop, calls=%fused_computation.16.clone.1 | loop fusion | flops 8519680 | bytes 5267457 | tf_op jit(solution)/shard_map/while/body/eval_jaxpr/add | solution.py:39
  219.2 4.0 %constant_dynamic-slice_fusion.73 = (bf16[1024,256]{1,0:T(8,128)(2,1)S(1)}, bf16[1024,256]{1,0:T(8,128)(2,1)S(1)}, bf16[1024,256]{1,0:T(8,128)(2,1)S(1)}, bf16[1...) fusion(bf16[1152,256]{1,0:T(8,128)(2,1)S(1)} %get-tuple-element, ...), kind=kLoop, calls=%fused_computation.47.clone.1 | loop fusion | bytes 16777280 | tf_op jit(solution)/shard_map/while/body/eval_jaxpr/dynamic_slice | solution.py:35
  223.3 4.8 %fusion.61 = f32[16,32,256]{2,1,0:T(8,128)} fusion(f32[16,32,256]{2,1,0:T(8,128)} %get-tuple-element.897, bf16[16,64,256]{2,1,0:T(8,128)(2,1)S(1)} %bitcast.238, bf16[16,64,256]{2,1,0:T(8,128)(2,1)S(1)} %bitcast.239, bf16[16,64,256]{2,1,0:T(8,128)(2,1)S(1)} %bitcast.240, bf16[16,64,256]{2,1,0:T(8,128)(2,1)S(1)} %bitcast.241, ...), kind=kLoop, calls=%fused_computation.16.clone.1 | loop fusion | flops 8519680 | bytes 5267457 | tf_op jit(solution)/shard_map/while/body/eval_jaxpr/add | solution.py:39
  228.1 3.9 %constant_dynamic-slice_fusion.73 = (bf16[1024,256]{1,0:T(8,128)(2,1)S(1)}, bf16[1024,256]{1,0:T(8,128)(2,1)S(1)}, bf16[1024,256]{1,0:T(8,128)(2,1)S(1)}, bf16[1...) fusion(bf16[1152,256]{1,0:T(8,128)(2,1)S(1)} %get-tuple-element, ...), kind=kLoop, calls=%fused_computation.47.clone.1 | loop fusion | bytes 16777280 | tf_op jit(solution)/shard_map/while/body/eval_jaxpr/dynamic_slice | solution.py:35
  232.1 4.8 %fusion.61 = f32[16,32,256]{2,1,0:T(8,128)} fusion(f32[16,32,256]{2,1,0:T(8,128)} %get-tuple-element.897, bf16[16,64,256]{2,1,0:T(8,128)(2,1)S(1)} %bitcast.238, bf16[16,64,256]{2,1,0:T(8,128)(2,1)S(1)} %bitcast.239, bf16[16,64,256]{2,1,0:T(8,128)(2,1)S(1)} %bitcast.240, bf16[16,64,256]{2,1,0:T(8,128)(2,1)S(1)} %bitcast.241, ...), kind=kLoop, calls=%fused_computation.16.clone.1 | loop fusion | flops 8519680 | bytes 5267457 | tf_op jit(solution)/shard_map/while/body/eval_jaxpr/add | solution.py:39
  238.5 1.3 collective-permute-done.13
  239.9 4.8 %convolution_convert_fusion.1 = bf16[256,4096]{1,0:T(8,128)(2,1)} fusion(bf16[4096,512]{0,1:T(8,128)(2,1)} %bitcast.318, bf16[256,256]{1,0:T(8,128)(2,1)S(1)} %bitcast.320, bf16[256,256]{1,0:T(8,128)(2,1)S(1)} %bitcast.282), kind=kOutput, calls=%fused_computation.130 | convolution fusion | flops 1075314688 | bytes 6553600 | tf_op jit(solution)/shard_map/dot_general | solution.py:154
  244.8 70.6 %while.35 = (s32[]{:T(128)}, f32[16,32,256]{2,1,0:T(8,128)}, s32[16,32]{1,0:T(8,128)S(1)}, f32[128,256]{1,0:T(8,128)S(1)}, bf16[1152,256]{1,0:T(8,128)(2,1)S(1)}...) while((s32[]{:T(128)}, f32[16,32,256]{2,1,0:T(8,128)}, ...), condition=%wide.region_7.8_spmd.clone, body=%wide.region_6.7_spmd.clone.sunk | while | flops 8528003 | bytes 22089652 | solution.py:45
  244.9 4.0 %constant_dynamic-slice_fusion.75 = (bf16[1024,256]{1,0:T(8,128)(2,1)S(1)}, bf16[1024,256]{1,0:T(8,128)(2,1)S(1)}, bf16[1024,256]{1,0:T(8,128)(2,1)S(1)}, bf16[1...) fusion(bf16[1152,256]{1,0:T(8,128)(2,1)S(1)} %get-tuple-element, ...), kind=kLoop, calls=%fused_computation.111.clone.1 | loop fusion | bytes 16777280 | tf_op jit(solution)/shard_map/while/body/eval_jaxpr/dynamic_slice | solution.py:35
  248.9 4.7 %fusion.62 = f32[16,32,256]{2,1,0:T(8,128)} fusion(f32[16,32,256]{2,1,0:T(8,128)} %get-tuple-element.1014, bf16[16,64,256]{2,1,0:T(8,128)(2,1)S(1)} %bitcast.254, bf16[16,64,256]{2,1,0:T(8,128)(2,1)S(1)} %bitcast.255, bf16[16,64,256]{2,1,0:T(8,128)(2,1)S(1)} %bitcast.256, bf16[16,64,256]{2,1,0:T(8,128)(2,1)S(1)} %bitcast.257, ...), kind=kLoop, calls=%fused_computation.80.clone.1 | loop fusion | flops 8519680 | bytes 5267457 | tf_op jit(solution)/shard_map/while/body/eval_jaxpr/add | solution.py:39
  253.7 3.8 %constant_dynamic-slice_fusion.75 = (bf16[1024,256]{1,0:T(8,128)(2,1)S(1)}, bf16[1024,256]{1,0:T(8,128)(2,1)S(1)}, bf16[1024,256]{1,0:T(8,128)(2,1)S(1)}, bf16[1...) fusion(bf16[1152,256]{1,0:T(8,128)(2,1)S(1)} %get-tuple-element, ...), kind=kLoop, calls=%fused_computation.111.clone.1 | loop fusion | bytes 16777280 | tf_op jit(solution)/shard_map/while/body/eval_jaxpr/dynamic_slice | solution.py:35
  257.6 4.8 %fusion.62 = f32[16,32,256]{2,1,0:T(8,128)} fusion(f32[16,32,256]{2,1,0:T(8,128)} %get-tuple-element.1014, bf16[16,64,256]{2,1,0:T(8,128)(2,1)S(1)} %bitcast.254, bf16[16,64,256]{2,1,0:T(8,128)(2,1)S(1)} %bitcast.255, bf16[16,64,256]{2,1,0:T(8,128)(2,1)S(1)} %bitcast.256, bf16[16,64,256]{2,1,0:T(8,128)(2,1)S(1)} %bitcast.257, ...), kind=kLoop, calls=%fused_computation.80.clone.1 | loop fusion | flops 8519680 | bytes 5267457 | tf_op jit(solution)/shard_map/while/body/eval_jaxpr/add | solution.py:39
  262.4 4.0 %constant_dynamic-slice_fusion.75 = (bf16[1024,256]{1,0:T(8,128)(2,1)S(1)}, bf16[1024,256]{1,0:T(8,128)(2,1)S(1)}, bf16[1024,256]{1,0:T(8,128)(2,1)S(1)}, bf16[1...) fusion(bf16[1152,256]{1,0:T(8,128)(2,1)S(1)} %get-tuple-element, ...), kind=kLoop, calls=%fused_computation.111.clone.1 | loop fusion | bytes 16777280 | tf_op jit(solution)/shard_map/while/body/eval_jaxpr/dynamic_slice | solution.py:35
  266.5 4.8 %fusion.62 = f32[16,32,256]{2,1,0:T(8,128)} fusion(f32[16,32,256]{2,1,0:T(8,128)} %get-tuple-element.1014, bf16[16,64,256]{2,1,0:T(8,128)(2,1)S(1)} %bitcast.254, bf16[16,64,256]{2,1,0:T(8,128)(2,1)S(1)} %bitcast.255, bf16[16,64,256]{2,1,0:T(8,128)(2,1)S(1)} %bitcast.256, bf16[16,64,256]{2,1,0:T(8,128)(2,1)S(1)} %bitcast.257, ...), kind=kLoop, calls=%fused_computation.80.clone.1 | loop fusion | flops 8519680 | bytes 5267457 | tf_op jit(solution)/shard_map/while/body/eval_jaxpr/add | solution.py:39
  271.3 3.9 %constant_dynamic-slice_fusion.75 = (bf16[1024,256]{1,0:T(8,128)(2,1)S(1)}, bf16[1024,256]{1,0:T(8,128)(2,1)S(1)}, bf16[1024,256]{1,0:T(8,128)(2,1)S(1)}, bf16[1...) fusion(bf16[1152,256]{1,0:T(8,128)(2,1)S(1)} %get-tuple-element, ...), kind=kLoop, calls=%fused_computation.111.clone.1 | loop fusion | bytes 16777280 | tf_op jit(solution)/shard_map/while/body/eval_jaxpr/dynamic_slice | solution.py:35
  275.3 4.8 %fusion.62 = f32[16,32,256]{2,1,0:T(8,128)} fusion(f32[16,32,256]{2,1,0:T(8,128)} %get-tuple-element.1014, bf16[16,64,256]{2,1,0:T(8,128)(2,1)S(1)} %bitcast.254, bf16[16,64,256]{2,1,0:T(8,128)(2,1)S(1)} %bitcast.255, bf16[16,64,256]{2,1,0:T(8,128)(2,1)S(1)} %bitcast.256, bf16[16,64,256]{2,1,0:T(8,128)(2,1)S(1)} %bitcast.257, ...), kind=kLoop, calls=%fused_computation.80.clone.1 | loop fusion | flops 8519680 | bytes 5267457 | tf_op jit(solution)/shard_map/while/body/eval_jaxpr/add | solution.py:39
  280.1 4.0 %constant_dynamic-slice_fusion.75 = (bf16[1024,256]{1,0:T(8,128)(2,1)S(1)}, bf16[1024,256]{1,0:T(8,128)(2,1)S(1)}, bf16[1024,256]{1,0:T(8,128)(2,1)S(1)}, bf16[1...) fusion(bf16[1152,256]{1,0:T(8,128)(2,1)S(1)} %get-tuple-element, ...), kind=kLoop, calls=%fused_computation.111.clone.1 | loop fusion | bytes 16777280 | tf_op jit(solution)/shard_map/while/body/eval_jaxpr/dynamic_slice | solution.py:35
  284.2 4.8 %fusion.62 = f32[16,32,256]{2,1,0:T(8,128)} fusion(f32[16,32,256]{2,1,0:T(8,128)} %get-tuple-element.1014, bf16[16,64,256]{2,1,0:T(8,128)(2,1)S(1)} %bitcast.254, bf16[16,64,256]{2,1,0:T(8,128)(2,1)S(1)} %bitcast.255, bf16[16,64,256]{2,1,0:T(8,128)(2,1)S(1)} %bitcast.256, bf16[16,64,256]{2,1,0:T(8,128)(2,1)S(1)} %bitcast.257, ...), kind=kLoop, calls=%fused_computation.80.clone.1 | loop fusion | flops 8519680 | bytes 5267457 | tf_op jit(solution)/shard_map/while/body/eval_jaxpr/add | solution.py:39
  289.0 3.8 %constant_dynamic-slice_fusion.75 = (bf16[1024,256]{1,0:T(8,128)(2,1)S(1)}, bf16[1024,256]{1,0:T(8,128)(2,1)S(1)}, bf16[1024,256]{1,0:T(8,128)(2,1)S(1)}, bf16[1...) fusion(bf16[1152,256]{1,0:T(8,128)(2,1)S(1)} %get-tuple-element, ...), kind=kLoop, calls=%fused_computation.111.clone.1 | loop fusion | bytes 16777280 | tf_op jit(solution)/shard_map/while/body/eval_jaxpr/dynamic_slice | solution.py:35
  293.0 4.8 %fusion.62 = f32[16,32,256]{2,1,0:T(8,128)} fusion(f32[16,32,256]{2,1,0:T(8,128)} %get-tuple-element.1014, bf16[16,64,256]{2,1,0:T(8,128)(2,1)S(1)} %bitcast.254, bf16[16,64,256]{2,1,0:T(8,128)(2,1)S(1)} %bitcast.255, bf16[16,64,256]{2,1,0:T(8,128)(2,1)S(1)} %bitcast.256, bf16[16,64,256]{2,1,0:T(8,128)(2,1)S(1)} %bitcast.257, ...), kind=kLoop, calls=%fused_computation.80.clone.1 | loop fusion | flops 8519680 | bytes 5267457 | tf_op jit(solution)/shard_map/while/body/eval_jaxpr/add | solution.py:39
  297.8 3.9 %constant_dynamic-slice_fusion.75 = (bf16[1024,256]{1,0:T(8,128)(2,1)S(1)}, bf16[1024,256]{1,0:T(8,128)(2,1)S(1)}, bf16[1024,256]{1,0:T(8,128)(2,1)S(1)}, bf16[1...) fusion(bf16[1152,256]{1,0:T(8,128)(2,1)S(1)} %get-tuple-element, ...), kind=kLoop, calls=%fused_computation.111.clone.1 | loop fusion | bytes 16777280 | tf_op jit(solution)/shard_map/while/body/eval_jaxpr/dynamic_slice | solution.py:35
  301.8 4.8 %fusion.62 = f32[16,32,256]{2,1,0:T(8,128)} fusion(f32[16,32,256]{2,1,0:T(8,128)} %get-tuple-element.1014, bf16[16,64,256]{2,1,0:T(8,128)(2,1)S(1)} %bitcast.254, bf16[16,64,256]{2,1,0:T(8,128)(2,1)S(1)} %bitcast.255, bf16[16,64,256]{2,1,0:T(8,128)(2,1)S(1)} %bitcast.256, bf16[16,64,256]{2,1,0:T(8,128)(2,1)S(1)} %bitcast.257, ...), kind=kLoop, calls=%fused_computation.80.clone.1 | loop fusion | flops 8519680 | bytes 5267457 | tf_op jit(solution)/shard_map/while/body/eval_jaxpr/add | solution.py:39
  306.6 3.8 %constant_dynamic-slice_fusion.75 = (bf16[1024,256]{1,0:T(8,128)(2,1)S(1)}, bf16[1024,256]{1,0:T(8,128)(2,1)S(1)}, bf16[1024,256]{1,0:T(8,128)(2,1)S(1)}, bf16[1...) fusion(bf16[1152,256]{1,0:T(8,128)(2,1)S(1)} %get-tuple-element, ...), kind=kLoop, calls=%fused_computation.111.clone.1 | loop fusion | bytes 16777280 | tf_op jit(solution)/shard_map/while/body/eval_jaxpr/dynamic_slice | solution.py:35
  310.6 4.8 %fusion.62 = f32[16,32,256]{2,1,0:T(8,128)} fusion(f32[16,32,256]{2,1,0:T(8,128)} %get-tuple-element.1014, bf16[16,64,256]{2,1,0:T(8,128)(2,1)S(1)} %bitcast.254, bf16[16,64,256]{2,1,0:T(8,128)(2,1)S(1)} %bitcast.255, bf16[16,64,256]{2,1,0:T(8,128)(2,1)S(1)} %bitcast.256, bf16[16,64,256]{2,1,0:T(8,128)(2,1)S(1)} %bitcast.257, ...), kind=kLoop, calls=%fused_computation.80.clone.1 | loop fusion | flops 8519680 | bytes 5267457 | tf_op jit(solution)/shard_map/while/body/eval_jaxpr/add | solution.py:39
  315.4 1.3 fusion.35
  318.1 4.9 %convolution_convert_fusion = bf16[256,4096]{1,0:T(8,128)(2,1)} fusion(bf16[4096,512]{0,1:T(8,128)(2,1)} %bitcast.319, bf16[256,256]{1,0:T(8,128)(2,1)S(1)} %bitcast.321, bf16[256,256]{1,0:T(8,128)(2,1)S(1)} %bitcast.281), kind=kOutput, calls=%fused_computation.129 | convolution fusion | flops 1075314688 | bytes 6553600 | tf_op jit(solution)/shard_map/dot_general | solution.py:154
  323.1 45.4 %reduce-scatter.5.cloned.1.call-done = bf16[32,4096]{1,0:T(8,128)(2,1)} async-done(((bf16[256,4096]{1,0:T(8,128)(2,1)}), bf16[32,4096]{1,0:T(8,128)(2,1)}) %reduce-scatter.5.cloned.1.call-update) | async-done | bytes 262160 | tf_op jit(solution)/shard_map/reduce_scatter | solution.py:159
  368.4 1.9 fusion.33
  (120 shorter events, 18.3 us)
Async XLA Ops:
  6.5 131.2 %all-gather.3.cloned.1.call-start = ((), (), s32[]{:S(2)}) async-start(), calls=%async_computation.2 | async-start | bytes 6684672 | tf_op jit(solution)/shard_map/all_gather | solution.py:92
  9.8 18.0 %collective-permute-start = (bf16[64,4096]{1,0:T(8,128)(2,1)}, bf16[64,4096]{1,0:T(8,128)(2,1)S(1)}, u32[]{:S(2)}, u32[]{:S(2)}) collective-permute-start(bf16[64,4096]{1,0:T(8,128)(2,1)} %fusion.32), channel_id=1, source_target_pairs={{0,2},{2,4},{4,6},{6,8},{8,10},{10,12},{12,14},{14,0},{1,3},{3,5},... | collective-permute-start | bytes 1572872 | tf_op jit(solution)/shard_map/ppermute | solution.py:68
  27.8 14.3 %collective-permute-start.1 = (bf16[64,4096]{1,0:T(8,128)(2,1)S(1)}, bf16[64,4096]{1,0:T(8,128)(2,1)S(1)}, u32[]{:S(2)}, u32[]{:S(2)}) collective-permute-start(bf16[64,4096]{1,0:T(8,128)(2,1)S(1)} %collective-permute-done), channel_id=1, source_target_pairs={{0,2},{2,4},{4,6},{6,8},{8,10},{10,12},{12,14},{14,0},{1,3},{3,5},... | collective-permute-start | bytes 1572872 | tf_op jit(solution)/shard_map/ppermute | solution.py:68
  27.8 19.8 %collective-permute-start.4 = (bf16[64,4096]{1,0:T(8,128)(2,1)}, bf16[64,4096]{1,0:T(8,128)(2,1)S(1)}, u32[]{:S(2)}, u32[]{:S(2)}) collective-permute-start(bf16[64,4096]{1,0:T(8,128)(2,1)} %fusion.32), channel_id=1, source_target_pairs={{0,14},{2,0},{4,2},{6,4},{8,6},{10,8},{12,10},{14,12},{1,15},{3,1}... | collective-permute-start | bytes 1572872 | tf_op jit(solution)/shard_map/ppermute | solution.py:71
  31.0 48.7 %copy-start = (bf16[64,4096]{1,0:T(8,128)(2,1)S(1)}, bf16[64,4096]{1,0:T(8,128)(2,1)}, u32[]{:S(2)}) copy-start(bf16[64,4096]{1,0:T(8,128)(2,1)} %param.11) | copy-start | bytes 1572868
  42.1 21.1 %collective-permute-start.2 = (bf16[64,4096]{1,0:T(8,128)(2,1)S(1)}, bf16[64,4096]{1,0:T(8,128)(2,1)S(1)}, u32[]{:S(2)}, u32[]{:S(2)}) collective-permute-start(bf16[64,4096]{1,0:T(8,128)(2,1)S(1)} %collective-permute-done.1), channel_id=1, source_target_pairs={{0,2},{2,4},{4,6},{6,8},{8,10},{10,12},{12,14},{14,0},{1,3},{3,5},... | collective-permute-start | bytes 1572872 | tf_op jit(solution)/shard_map/ppermute | solution.py:68
  43.5 23.8 %collective-permute-start.7 = (bf16[128,3,256]{0,2,1:T(8,128)(2,1)S(1)}, bf16[128,3,256]{0,2,1:T(8,128)(2,1)S(1)}, u32[]{:S(2)}, u32[]{:S(2)}) collective-permute-start(bf16[128,3,256]{0,2,1:T(8,128)(2,1)S(1)} %broadcast_select_fusion.5), channel_id=1, source_target_pairs={{0,8},{8,0},{1,9},{9,1},{2,10},{10,2},{3,11},{11,3},{4,12},{12,4},... | collective-permute-start | bytes 589832 | tf_op jit(solution)/shard_map/ppermute | solution.py:54
  47.6 20.6 %collective-permute-start.5 = (bf16[64,4096]{1,0:T(8,128)(2,1)S(1)}, bf16[64,4096]{1,0:T(8,128)(2,1)}, u32[]{:S(2)}, u32[]{:S(2)}) collective-permute-start(bf16[64,4096]{1,0:T(8,128)(2,1)S(1)} %collective-permute-done.4), channel_id=1, source_target_pairs={{0,14},{2,0},{4,2},{6,4},{8,6},{10,8},{12,10},{14,12},{1,15},{3,1}... | collective-permute-start | bytes 1572872 | tf_op jit(solution)/shard_map/ppermute | solution.py:71
  63.2 12.1 %collective-permute-start.3 = (bf16[64,4096]{1,0:T(8,128)(2,1)S(1)}, bf16[64,4096]{1,0:T(8,128)(2,1)}, u32[]{:S(2)}, u32[]{:S(2)}) collective-permute-start(bf16[64,4096]{1,0:T(8,128)(2,1)S(1)} %collective-permute-done.2), channel_id=1, source_target_pairs={{0,2},{2,4},{4,6},{6,8},{8,10},{10,12},{12,14},{14,0},{1,3},{3,5},... | collective-permute-start | bytes 1572872 | tf_op jit(solution)/shard_map/ppermute | solution.py:68
  68.2 170.0 %all-gather.5.cloned.1.call-start = ((), (), s32[]{:S(2)}) async-start(), calls=%async_computation.3 | async-start | bytes 4456448 | tf_op jit(solution)/shard_map/all_gather | solution.py:97
  68.2 15.2 %collective-permute-start.6 = (bf16[64,4096]{1,0:T(8,128)(2,1)}, bf16[64,4096]{1,0:T(8,128)(2,1)S(1)}, u32[]{:S(2)}, u32[]{:S(2)}) collective-permute-start(bf16[64,4096]{1,0:T(8,128)(2,1)} %collective-permute-done.5), channel_id=1, source_target_pairs={{0,14},{2,0},{4,2},{6,4},{8,6},{10,8},{12,10},{14,12},{1,15},{3,1}... | collective-permute-start | bytes 1572872 | tf_op jit(solution)/shard_map/ppermute | solution.py:71
  89.3 4.9 %copy-start.2 = (bf16[128,512]{1,0:T(8,128)(2,1)S(1)}, bf16[128,512]{1,0:T(8,128)(2,1)}, u32[]{:S(2)}) copy-start(bf16[128,512]{1,0:T(8,128)(2,1)} %param.13) | copy-start | bytes 393220
  89.3 5.6 %copy-start.4 = (f32[3,3,512]{2,1,0:T(4,128)S(1)}, f32[3,3,512]{2,1,0:T(4,128)}, u32[]{:S(2)}) copy-start(f32[3,3,512]{2,1,0:T(4,128)} %param.14) | copy-start | bytes 55300
  89.3 5.6 %copy-start.5 = (s32[64]{0:T(128)S(1)}, s32[64]{0:T(128)}, u32[]{:S(2)}) copy-start(s32[64]{0:T(128)} %param.17) | copy-start | bytes 772
  89.3 6.1 %copy-start.6 = (f32[512]{0:T(512)S(1)}, f32[512]{0:T(512)}, u32[]{:S(2)}) copy-start(f32[512]{0:T(512)} %param.16) | copy-start | bytes 6148
  89.3 6.3 %copy-start.3 = (f32[128,512]{1,0:T(8,128)S(1)}, f32[128,512]{1,0:T(8,128)}, u32[]{:S(2)}) copy-start(f32[128,512]{1,0:T(8,128)} %param.15) | copy-start | bytes 786436
  94.2 11.8 %collective-permute-start.8 = (bf16[8,64,4096]{2,1,0:T(8,128)(2,1)}, bf16[8,64,4096]{2,1,0:T(8,128)(2,1)}, u32[]{:S(2)}, u32[]{:S(2)}) collective-permute-start(bf16[8,64,4096]{2,1,0:T(8,128)(2,1)} %broadcast_select_fusion), channel_id=1, source_target_pairs={{0,1},{1,0},{2,3},{3,2},{4,5},{5,4},{6,7},{7,6},{8,9},{9,8},{10,11... | collective-permute-start | bytes 12582920 | tf_op jit(solution)/shard_map/ppermute | solution.py:108
  94.3 7.4 %collective-permute-start.11 = (bf16[128,512]{0,1:T(8,128)(2,1)S(1)}, bf16[128,512]{0,1:T(8,128)(2,1)S(1)}, u32[]{:S(2)}, u32[]{:S(2)}) collective-permute-start(bf16[128,512]{0,1:T(8,128)(2,1)S(1)} %copy.20), channel_id=1, source_target_pairs={{0,1},{1,0},{2,3},{3,2},{4,5},{5,4},{6,7},{7,6},{8,9},{9,8},{10,11... | collective-permute-start | bytes 393224 | tf_op jit(solution)/shard_map/ppermute | solution.py:95
  101.8 51.8 %collective-permute-start.12 = (bf16[128,2,256]{0,2,1:T(8,128)(2,1)S(1)}, bf16[128,2,256]{0,2,1:T(8,128)(2,1)S(1)}, u32[]{:S(2)}, u32[]{:S(2)}) collective-permute-start(bf16[128,2,256]{0,2,1:T(8,128)(2,1)S(1)} %broadcast_select_fusion.9), channel_id=1, source_target_pairs={{0,8},{8,0},{1,9},{9,1},{2,10},{10,2},{3,11},{11,3},{4,12},{12,4},... | collective-permute-start | bytes 393224 | tf_op jit(solution)/shard_map/ppermute | solution.py:54
  137.8 7.6 %copy-start.7 = (bf16[4096,3,256]{0,2,1:T(8,128)(2,1)S(1)}, bf16[4096,3,256]{0,2,1:T(8,128)(2,1)}, u32[]{:S(2)}) copy-start(bf16[4096,3,256]{0,2,1:T(8,128)(2,1)} %all-gather.3.cloned.1.call-done) | copy-start | bytes 18874372
  151.4 5.5 %collective-permute-start.9 = (bf16[2,768]{1,0:T(2,128)(2,1)S(1)}, bf16[2,768]{1,0:T(2,128)(2,1)S(1)}, u32[]{:S(2)}, u32[]{:S(2)}) collective-permute-start(bf16[2,768]{1,0:T(2,128)(2,1)S(1)} %slice.493), channel_id=1, source_target_pairs={{0,16},{16,32},{32,48},{48,64},{64,80},{80,96},{96,112},{112,128},... | collective-permute-start | bytes 9224 | tf_op jit(solution)/shard_map/ppermute | solution.py:126
  159.9 6.1 %collective-permute-start.10 = (bf16[128,256]{1,0:T(8,128)(2,1)S(1)}, bf16[128,256]{1,0:T(8,128)(2,1)S(1)}, u32[]{:S(2)}, u32[]{:S(2)}) collective-permute-start(bf16[128,256]{1,0:T(8,128)(2,1)S(1)} %slice.498), channel_id=1, source_target_pairs={{0,16},{16,32},{32,48},{48,64},{64,80},{80,96},{96,112},{112,128},... | collective-permute-start | bytes 196616 | tf_op jit(solution)/shard_map/ppermute | solution.py:131
  162.9 160.2 %reduce-scatter.3.cloned.1.call-start = ((), (), s32[]{:S(2)}) async-start(), calls=%async_computation.4 | async-start | bytes 2359296 | tf_op jit(solution)/shard_map/reduce_scatter | solution.py:159
  238.2 1.7 collective-permute-start.13
  244.7 123.7 %reduce-scatter.5.cloned.1.call-start = ((), (), s32[]{:S(2)}) async-start(), calls=%async_computation.5 | async-start | bytes 2359296 | tf_op jit(solution)/shard_map/reduce_scatter | solution.py:159
  316.7 1.4 collective-permute-start.14
  318.1 50.4 %copy-start.1 = (bf16[64,4096]{1,0:T(8,128)(2,1)S(1)}, bf16[64,4096]{1,0:T(8,128)(2,1)}, u32[]{:S(2)}) copy-start(bf16[64,4096]{1,0:T(8,128)(2,1)} %param.11) | copy-start | bytes 1572868
Sparse Core Ops, SparseCore 0:
  68.3 69.4 all-gather.2
  163.0 65.3 all-gather.4
  244.8 45.5 reduce-scatter.2
  323.2 45.2 reduce-scatter.4

commit v7 on v5

--- a/solution.py
+++ b/solution.py
@@ -67,7 +67,7 @@
     lowest = -(nz // 2)
     relative = jnp.stack([by_offset[lowest + i] for i in range(nz)], 0)
     pick = (jnp.arange(nz, dtype=jnp.int32) - z - lowest) % nz
-    return jnp.take(relative, pick, axis=0)
+    return relative, pick
 
 
 def block_body(tokens, in_weight, out_weight, short_taps, filter_taps, decay_rate, doc_lengths):
@@ -84,7 +84,7 @@
     ).astype(jnp.bfloat16)
     in_piece = swap_half(in_weight, zh, 2)
     in_full = lax.all_gather(in_piece, "p", axis=0, tiled=True)
-    gathered = z_ring_gather(normed)
+    gathered, pick = z_ring_gather(normed)
 
     chip_out = jnp.stack([out_weight, lax.ppermute(out_weight, "c", [(0, 1), (1, 0)])], 1)
     out_piece = swap_half(chip_out, zh, 2)
@@ -103,9 +103,10 @@
     from_mine = project(gathered)
     from_partner = project(partner_rows)
     core = lax.axis_index("c")
-    first = jnp.where(core == 0, from_mine, from_partner)
-    second = jnp.where(core == 0, from_partner, from_mine)
-    projected = jnp.stack([first, second], 1).reshape(col_rows, 3 * half)
+    both = jnp.concatenate([from_mine, from_partner], 0)
+    from_core = jnp.array([[0, 1]], jnp.int32) != core
+    order = (from_core.astype(jnp.int32) * nz + pick[:, None]).reshape(2 * nz)
+    projected = jnp.take(both, order, axis=0).reshape(col_rows, 3 * half)
 
     first_row = lax.axis_index("p") * col_rows
     own_points = first_row + jnp.arange(col_rows, dtype=jnp.int32)

time: 302 us -> 305 us (level)
  waiting for transfers between devices: 155 us -> 164 us
  local copies, waits for them, and re-layouts: 18.4 us -> 13.9 us
    all_gather x1, waiting for transfers between devices: 30.4 us -> 42.2 us  [block_body(): in_full = lax.all_gather(in_piece, 'p', axis=0, tiled=True)]
    gather x1, local copies, waits for them, and re-layouts: 5.12 us -> 1.97 us  [block_body(): projected = jnp.take(both, order, axis=0).reshape(col_rows, 3 * half)]
    select_n x2 -> x3, other arithmetic: 4.78 us -> 1.65 us  [the longest x2 1.64 us: block_body(): projected = jnp.take(both, order, axis=0).reshape(col_rows, 3 * half)]
    unnamed x25 -> x33, local copies, waits for them, and re-layouts: 10.3 us -> 8.25 us
  transfers between devices with their start and end apart: 17 -> 17, of which waited for: 12 -> 12; matrix products, arithmetic and copies ran while one was open for 30% -> 29% of each run, Pallas kernels for 0% -> 0%
where the time goes in v7:
time: 305 us; the launch traced here: 304 us
  waiting for transfers between devices  164 us (54%)
  other arithmetic  67.8 us (22%)
  starting transfers between devices  22.8 us (7%)
  matrix products  19.9 us (7%)
  local copies, waits for them, and re-layouts  13.9 us (5%)
  between operations  13.4 us (4%)
    reduce_scatter x1, waiting for transfers between devices, block_body(): lax.psum_scatter(lax.dot_general(lhs, rhs, (((1,), (1,)), ((), ())), pref...  55.2 us
    add x8, other arithmetic, tap_group(): running + jnp.where(inside, weight_row * window.astype(jnp.float32), jnp....  51.4 us
    ppermute x4, waiting for transfers between devices, z_ring_gather(): going_right = lax.ppermute(going_right, ('zh', 'zl'), right)  45.2 us
    all_gather x1, waiting for transfers between devices, block_body(): in_full = lax.all_gather(in_piece, 'p', axis=0, tiled=True)  42.2 us
    dot_general x2, matrix products, project(): out = jnp.dot(flat, flat_in, preferred_element_type=jnp.float32)  13.3 us
    unnamed x33, local copies, waits for them, and re-layouts  8.25 us
    ppermute x2, starting transfers between devices, swap_half(): got = lax.ppermute(give, 'zh', [(0, 1), (1, 0)])  8.04 us
    ppermute x3, starting transfers between devices, z_ring_gather(): going_left = lax.ppermute(going_left, ('zh', 'zl'), left)  7.6 us
  transfers between devices with their start and end apart: 17, of which 12 were waited for; matrix products, arithmetic and copies ran while one was open for 29% of the time, Pallas kernels for 0%

profile of v7, /device:TPU:2, one launch (start us, length us, event | category | flops | bytes accessed | tf_op | source)
XLA Modules:
  0.0 303.7 jit_solution(14571584001966191552)
XLA Ops:
  6.5 1.2 fusion.16
  7.8 1.2 fusion.17
  9.0 2.0 collective-permute-start
  11.0 15.9 %collective-permute-done = bf16[64,4096]{1,0:T(8,128)(2,1)S(1)} collective-permute-done((bf16[64,4096]{1,0:T(8,128)(2,1)S(1)}, bf16[64,4096]{1,0:T(8,128)(2,1)S(1)}, u32[]{:S(2)}, u32[]{:S(2)}) %collective-permute-start) | collective-permute-done | bytes 524320 | tf_op jit(solution)/shard_map/ppermute | solution.py:62
  26.9 3.2 %collective-permute-start.4 = (bf16[64,4096]{1,0:T(8,128)(2,1)S(1)}, bf16[64,4096]{1,0:T(8,128)(2,1)S(1)}, u32[]{:S(2)}, u32[]{:S(2)}) collective-permute-start(bf16[64,4096]{1,0:T(8,128)(2,1)S(1)} %fusion.17), channel_id=1, source_target_pairs={{0,14},{2,0},{4,2},{6,4},{8,6},{10,8},{12,10},{14,12},{1,15},{3,1}... | collective-permute-start | bytes 1572872 | tf_op jit(solution)/shard_map/ppermute | solution.py:65
  30.1 11.1 %collective-permute-done.1 = bf16[64,4096]{1,0:T(8,128)(2,1)S(1)} collective-permute-done((bf16[64,4096]{1,0:T(8,128)(2,1)S(1)}, bf16[64,4096]{1,0:T(8,128)(2,1)S(1)}, u32[]{:S(2)}, u32[]{:S(2)}) %collective-permute-start.1) | collective-permute-done | bytes 524320 | tf_op jit(solution)/shard_map/ppermute | solution.py:62
  41.2 1.0 fusion.31
  42.2 0.2 copy.21
  42.4 0.2 copy.20
  42.6 4.1 %collective-permute-start.7 = (bf16[128,3,256]{0,2,1:T(8,128)(2,1)S(1)}, bf16[128,3,256]{0,2,1:T(8,128)(2,1)S(1)}, u32[]{:S(2)}, u32[]{:S(2)}) collective-permute-start(bf16[128,3,256]{0,2,1:T(8,128)(2,1)S(1)} %broadcast_select_fusion.2), channel_id=1, source_target_pairs={{0,8},{8,0},{1,9},{9,1},{2,10},{10,2},{3,11},{11,3},{4,12},{12,4},... | collective-permute-start | bytes 589832 | tf_op jit(solution)/shard_map/ppermute | solution.py:48
  46.7 3.2 %collective-permute-start.5 = (bf16[64,4096]{1,0:T(8,128)(2,1)S(1)}, bf16[64,4096]{1,0:T(8,128)(2,1)S(1)}, u32[]{:S(2)}, u32[]{:S(2)}) collective-permute-start(bf16[64,4096]{1,0:T(8,128)(2,1)S(1)} %collective-permute-done.4), channel_id=1, source_target_pairs={{0,14},{2,0},{4,2},{6,4},{8,6},{10,8},{12,10},{14,12},{1,15},{3,1}... | collective-permute-start | bytes 1572872 | tf_op jit(solution)/shard_map/ppermute | solution.py:65
  49.9 12.3 %collective-permute-done.2 = bf16[64,4096]{1,0:T(8,128)(2,1)S(1)} collective-permute-done((bf16[64,4096]{1,0:T(8,128)(2,1)S(1)}, bf16[64,4096]{1,0:T(8,128)(2,1)S(1)}, u32[]{:S(2)}, u32[]{:S(2)}) %collective-permute-start.2) | collective-permute-done | bytes 524320 | tf_op jit(solution)/shard_map/ppermute | solution.py:62
  62.3 4.1 %collective-permute-done.7 = bf16[128,3,256]{0,2,1:T(8,128)(2,1)S(1)} collective-permute-done((bf16[128,3,256]{0,2,1:T(8,128)(2,1)S(1)}, bf16[128,3,256]{0,2,1:T(8,128)(2,1)S(1)}, u32[]{:S(2)}, u32[]{:S(2)}) %collective-permute-start.7) | collective-permute-done | bytes 196640 | tf_op jit(solution)/shard_map/ppermute | solution.py:48
  66.4 0.8 pad_maximum_fusion.3
  67.3 1.1 collective-permute-start.6
  68.4 5.9 %collective-permute-done.3 = bf16[64,4096]{1,0:T(8,128)(2,1)} collective-permute-done((bf16[64,4096]{1,0:T(8,128)(2,1)S(1)}, bf16[64,4096]{1,0:T(8,128)(2,1)}, u32[]{:S(2)}, u32[]{:S(2)}) %collective-permute-start.3) | collective-permute-done | bytes 524320 | tf_op jit(solution)/shard_map/ppermute | solution.py:62
  74.4 1.9 bitcast_dynamic-update-slice_fusion.7
  76.3 0.8 bitcast_dynamic-update-slice_fusion.6
  77.1 0.9 bitcast_dynamic-update-slice_fusion.5
  78.0 0.9 bitcast_dynamic-update-slice_fusion.4
  78.8 1.0 bitcast_dynamic-update-slice_fusion.3
  79.9 0.8 bitcast_dynamic-update-slice_fusion.2
  80.7 0.8 bitcast_dynamic-update-slice_fusion.1
  81.5 0.9 bitcast_dynamic-update-slice_fusion
  82.4 0.1 copy.18
  82.5 0.6 collective-permute-start.11
  83.6 0.1 reduce
  83.8 0.1 select_reduce_fusion
  83.9 0.5 broadcast_compare_fusion.18
  84.5 0.6 broadcast_compare_fusion.17
  85.2 0.7 broadcast_in_dim.462
  85.9 0.6 pad_clamp_fusion
  86.5 3.4 %collective-permute-done.11 = bf16[128,512]{0,1:T(8,128)(2,1)S(1)} collective-permute-done((bf16[128,512]{0,1:T(8,128)(2,1)S(1)}, bf16[128,512]{0,1:T(8,128)(2,1)S(1)}, u32[]{:S(2)}, u32[]{:S(2)}) %collective-permute-start.11) | collective-permute-done | bytes 131104 | tf_op jit(solution)/shard_map/ppermute | solution.py:89
  89.9 0.7 broadcast_select_fusion.6
  90.6 4.0 %collective-permute-start.12 = (bf16[128,2,256]{0,2,1:T(8,128)(2,1)}, bf16[128,2,256]{0,2,1:T(8,128)(2,1)}, u32[]{:S(2)}, u32[]{:S(2)}) collective-permute-start(bf16[128,2,256]{0,2,1:T(8,128)(2,1)} %broadcast_select_fusion.6), channel_id=1, source_target_pairs={{0,8},{8,0},{1,9},{9,1},{2,10},{10,2},{3,11},{11,3},{4,12},{12,4},... | collective-permute-start | bytes 393224 | tf_op jit(solution)/shard_map/ppermute | solution.py:48
  94.6 42.2 %all-gather.3.cloned.1.call-done = bf16[4096,3,256]{0,2,1:T(8,128)(2,1)} async-done(((bf16[256,3,256]{0,2,1:T(8,128)(2,1)}), bf16[4096,3,256]{0,2,1:T(8,128)(2,1)}) %all-gather.3.cloned.1.call-update) | async-done | bytes 6291472 | tf_op jit(solution)/shard_map/all_gather | solution.py:86
  136.8 7.6 %convolution_convert_fusion.1 = bf16[512,768]{1,0:T(8,128)(2,1)S(1)} fusion(bf16[512,4096]{1,0:T(8,128)(2,1)} %bitcast.13, bf16[4096,768]{0,1:T(8,128)(2,1)} %bitcast.114), kind=kOutput, calls=%fused_computation.60 | convolution fusion | flops 3221618688 | bytes 11272192 | tf_op jit(solution)/shard_map/dot_general | solution.py:99
  144.5 5.7 %convolution_convert_fusion.2 = bf16[512,768]{1,0:T(8,128)(2,1)S(1)} fusion(bf16[512,4096]{1,0:T(8,128)(2,1)} %bitcast.10, bf16[4096,768]{0,1:T(8,128)(2,1)S(1)} %bitcast.115), kind=kOutput, calls=%fused_computation.61 | convolution fusion | flops 3221618688 | bytes 11272192 | tf_op jit(solution)/shard_map/dot_general | solution.py:99
  150.1 0.1 pad_maximum_fusion.1
  150.3 2.0 gather_fusion
  152.3 1.6 bitcast_select_fusion
  153.9 2.2 collective-permute-start.9
  156.1 1.0 broadcast_select_fusion.5
  157.1 2.3 collective-permute-done.9
  159.4 1.9 select_add_fusion.1
  161.3 1.7 copy-done
  163.1 2.2 collective-permute-start.10
  165.4 0.7 pad_maximum_fusion.4
  166.2 3.1 %collective-permute-done.10 = bf16[128,256]{1,0:T(8,128)(2,1)S(1)} collective-permute-done((bf16[128,256]{1,0:T(8,128)(2,1)S(1)}, bf16[128,256]{1,0:T(8,128)(2,1)S(1)}, u32[]{:S(2)}, u32[]{:S(2)}) %collective-permute-start.10) | collective-permute-done | bytes 65568 | tf_op jit(solution)/shard_map/ppermute | solution.py:126
  169.3 54.6 %while.17 = (s32[]{:T(128)}, f32[1024,256]{1,0:T(8,128)S(1)}, s32[1024]{0:T(1024)S(1)}, f32[128,256]{1,0:T(8,128)S(1)}, bf16[1152,256]{1,0:T(8,128)(2,1)S(1)}, /...) while((s32[]{:T(128)}, f32[1024,256]{1,0:T(8,128)S(1)}, ...), condition=%wide.region_4.5_spmd.clone, body=%wide.region_3.4_spmd.clone.sunk | while | flops 17055876 | bytes 10573791 | solution.py:39
  169.7 6.4 %fusion.38 = f32[1024,256]{1,0:T(8,128)S(1)} fusion(f32[1024,256]{1,0:T(8,128)S(1)} %get-tuple-element.427, bf16[1152,256]{1,0:T(8,128)(2,1)S(1)} %get-tuple-element.469, s32[]{:T(128)S(6)} %select_n.820, f32[256]{0:T(256)S(1)} %bitcast.98, s32[]{:T(128)S(6)} %select_n.837, f32[256]{0:T(256)S(1)} %bitcast.99, s32[]{:T(128)S(6)} %select_n.838, ...), kind=kLoop, calls=%fused_computation.16.clone.1 | loop fusion | flops 17039360 | bytes 10518593 | tf_op jit(solution)/shard_map/while/body/eval_jaxpr/add | solution.py:33
  176.6 6.4 %fusion.38 = f32[1024,256]{1,0:T(8,128)S(1)} fusion(f32[1024,256]{1,0:T(8,128)S(1)} %get-tuple-element.427, bf16[1152,256]{1,0:T(8,128)(2,1)S(1)} %get-tuple-element.469, s32[]{:T(128)S(6)} %select_n.820, f32[256]{0:T(256)S(1)} %bitcast.98, s32[]{:T(128)S(6)} %select_n.837, f32[256]{0:T(256)S(1)} %bitcast.99, s32[]{:T(128)S(6)} %select_n.838, ...), kind=kLoop, calls=%fused_computation.16.clone.1 | loop fusion | flops 17039360 | bytes 10518593 | tf_op jit(solution)/shard_map/while/body/eval_jaxpr/add | solution.py:33
  183.4 6.4 %fusion.38 = f32[1024,256]{1,0:T(8,128)S(1)} fusion(f32[1024,256]{1,0:T(8,128)S(1)} %get-tuple-element.427, bf16[1152,256]{1,0:T(8,128)(2,1)S(1)} %get-tuple-element.469, s32[]{:T(128)S(6)} %select_n.820, f32[256]{0:T(256)S(1)} %bitcast.98, s32[]{:T(128)S(6)} %select_n.837, f32[256]{0:T(256)S(1)} %bitcast.99, s32[]{:T(128)S(6)} %select_n.838, ...), kind=kLoop, calls=%fused_computation.16.clone.1 | loop fusion | flops 17039360 | bytes 10518593 | tf_op jit(solution)/shard_map/while/body/eval_jaxpr/add | solution.py:33
  190.2 6.4 %fusion.38 = f32[1024,256]{1,0:T(8,128)S(1)} fusion(f32[1024,256]{1,0:T(8,128)S(1)} %get-tuple-element.427, bf16[1152,256]{1,0:T(8,128)(2,1)S(1)} %get-tuple-element.469, s32[]{:T(128)S(6)} %select_n.820, f32[256]{0:T(256)S(1)} %bitcast.98, s32[]{:T(128)S(6)} %select_n.837, f32[256]{0:T(256)S(1)} %bitcast.99, s32[]{:T(128)S(6)} %select_n.838, ...), kind=kLoop, calls=%fused_computation.16.clone.1 | loop fusion | flops 17039360 | bytes 10518593 | tf_op jit(solution)/shard_map/while/body/eval_jaxpr/add | solution.py:33
  197.0 6.4 %fusion.38 = f32[1024,256]{1,0:T(8,128)S(1)} fusion(f32[1024,256]{1,0:T(8,128)S(1)} %get-tuple-element.427, bf16[1152,256]{1,0:T(8,128)(2,1)S(1)} %get-tuple-element.469, s32[]{:T(128)S(6)} %select_n.820, f32[256]{0:T(256)S(1)} %bitcast.98, s32[]{:T(128)S(6)} %select_n.837, f32[256]{0:T(256)S(1)} %bitcast.99, s32[]{:T(128)S(6)} %select_n.838, ...), kind=kLoop, calls=%fused_computation.16.clone.1 | loop fusion | flops 17039360 | bytes 10518593 | tf_op jit(solution)/shard_map/while/body/eval_jaxpr/add | solution.py:33
  203.9 6.4 %fusion.38 = f32[1024,256]{1,0:T(8,128)S(1)} fusion(f32[1024,256]{1,0:T(8,128)S(1)} %get-tuple-element.427, bf16[1152,256]{1,0:T(8,128)(2,1)S(1)} %get-tuple-element.469, s32[]{:T(128)S(6)} %select_n.820, f32[256]{0:T(256)S(1)} %bitcast.98, s32[]{:T(128)S(6)} %select_n.837, f32[256]{0:T(256)S(1)} %bitcast.99, s32[]{:T(128)S(6)} %select_n.838, ...), kind=kLoop, calls=%fused_computation.16.clone.1 | loop fusion | flops 17039360 | bytes 10518593 | tf_op jit(solution)/shard_map/while/body/eval_jaxpr/add | solution.py:33
  210.7 6.4 %fusion.38 = f32[1024,256]{1,0:T(8,128)S(1)} fusion(f32[1024,256]{1,0:T(8,128)S(1)} %get-tuple-element.427, bf16[1152,256]{1,0:T(8,128)(2,1)S(1)} %get-tuple-element.469, s32[]{:T(128)S(6)} %select_n.820, f32[256]{0:T(256)S(1)} %bitcast.98, s32[]{:T(128)S(6)} %select_n.837, f32[256]{0:T(256)S(1)} %bitcast.99, s32[]{:T(128)S(6)} %select_n.838, ...), kind=kLoop, calls=%fused_computation.16.clone.1 | loop fusion | flops 17039360 | bytes 10518593 | tf_op jit(solution)/shard_map/while/body/eval_jaxpr/add | solution.py:33
  217.5 6.4 %fusion.38 = f32[1024,256]{1,0:T(8,128)S(1)} fusion(f32[1024,256]{1,0:T(8,128)S(1)} %get-tuple-element.427, bf16[1152,256]{1,0:T(8,128)(2,1)S(1)} %get-tuple-element.469, s32[]{:T(128)S(6)} %select_n.820, f32[256]{0:T(256)S(1)} %bitcast.98, s32[]{:T(128)S(6)} %select_n.837, f32[256]{0:T(256)S(1)} %bitcast.99, s32[]{:T(128)S(6)} %select_n.838, ...), kind=kLoop, calls=%fused_computation.16.clone.1 | loop fusion | flops 17039360 | bytes 10518593 | tf_op jit(solution)/shard_map/while/body/eval_jaxpr/add | solution.py:33
  224.0 1.4 fusion.20
  225.3 6.4 %all-gather.5.cloned.1.call-done = bf16[4096,2,256]{0,2,1:T(8,128)(2,1)} async-done(((bf16[256,2,256]{0,2,1:T(8,128)(2,1)}), bf16[4096,2,256]{0,2,1:T(8,128)(2,1)}) %all-gather.5.cloned.1.call-update) | async-done | bytes 4194320 | tf_op jit(solution)/shard_map/all_gather | solution.py:91
  231.9 1.5 collective-permute-done.13
  233.4 6.6 %convolution_convert_fusion = bf16[512,4096]{1,0:T(8,128)(2,1)} fusion(bf16[4096,512]{0,1:T(8,128)(2,1)} %bitcast.116, bf16[512,256]{1,0:T(8,128)(2,1)S(1)} %bitcast.117, bf16[512,256]{1,0:T(8,128)(2,1)S(1)} %bitcast.96), kind=kOutput, calls=%fused_computation.49 | convolution fusion | flops 2150629376 | bytes 8912896 | tf_op jit(solution)/shard_map/dot_general | solution.py:144
  240.0 55.2 %reduce-scatter.2.cloned.1.call-done = bf16[64,4096]{1,0:T(8,128)(2,1)} async-done(((bf16[512,4096]{1,0:T(8,128)(2,1)}), bf16[64,4096]{1,0:T(8,128)(2,1)}) %reduce-scatter.2.cloned.1.call-update) | async-done | bytes 524304 | tf_op jit(solution)/shard_map/reduce_scatter | solution.py:143
  295.2 2.0 fusion.18
  (82 shorter events, 2.3 us)
Async XLA Ops:
  6.5 130.3 %all-gather.3.cloned.1.call-start = ((), (), s32[]{:S(2)}) async-start(), calls=%async_computation.1 | async-start | bytes 6684672 | tf_op jit(solution)/shard_map/all_gather | solution.py:86
  9.0 17.9 %collective-permute-start = (bf16[64,4096]{1,0:T(8,128)(2,1)S(1)}, bf16[64,4096]{1,0:T(8,128)(2,1)S(1)}, u32[]{:S(2)}, u32[]{:S(2)}) collective-permute-start(bf16[64,4096]{1,0:T(8,128)(2,1)S(1)} %fusion.17), channel_id=1, source_target_pairs={{0,2},{2,4},{4,6},{6,8},{8,10},{10,12},{12,14},{14,0},{1,3},{3,5},... | collective-permute-start | bytes 1572872 | tf_op jit(solution)/shard_map/ppermute | solution.py:62
  26.9 14.3 %collective-permute-start.1 = (bf16[64,4096]{1,0:T(8,128)(2,1)S(1)}, bf16[64,4096]{1,0:T(8,128)(2,1)S(1)}, u32[]{:S(2)}, u32[]{:S(2)}) collective-permute-start(bf16[64,4096]{1,0:T(8,128)(2,1)S(1)} %collective-permute-done), channel_id=1, source_target_pairs={{0,2},{2,4},{4,6},{6,8},{8,10},{10,12},{12,14},{14,0},{1,3},{3,5},... | collective-permute-start | bytes 1572872 | tf_op jit(solution)/shard_map/ppermute | solution.py:62
  26.9 19.8 %collective-permute-start.4 = (bf16[64,4096]{1,0:T(8,128)(2,1)S(1)}, bf16[64,4096]{1,0:T(8,128)(2,1)S(1)}, u32[]{:S(2)}, u32[]{:S(2)}) collective-permute-start(bf16[64,4096]{1,0:T(8,128)(2,1)S(1)} %fusion.17), channel_id=1, source_target_pairs={{0,14},{2,0},{4,2},{6,4},{8,6},{10,8},{12,10},{14,12},{1,15},{3,1}... | collective-permute-start | bytes 1572872 | tf_op jit(solution)/shard_map/ppermute | solution.py:65
  41.2 21.1 %collective-permute-start.2 = (bf16[64,4096]{1,0:T(8,128)(2,1)S(1)}, bf16[64,4096]{1,0:T(8,128)(2,1)S(1)}, u32[]{:S(2)}, u32[]{:S(2)}) collective-permute-start(bf16[64,4096]{1,0:T(8,128)(2,1)S(1)} %collective-permute-done.1), channel_id=1, source_target_pairs={{0,2},{2,4},{4,6},{6,8},{8,10},{10,12},{12,14},{14,0},{1,3},{3,5},... | collective-permute-start | bytes 1572872 | tf_op jit(solution)/shard_map/ppermute | solution.py:62
  42.6 36.3 %copy-start.1 = (bf16[64,4096]{1,0:T(8,128)(2,1)S(1)}, bf16[64,4096]{1,0:T(8,128)(2,1)}, u32[]{:S(2)}) copy-start(bf16[64,4096]{1,0:T(8,128)(2,1)} %param.10) | copy-start | bytes 1572868
  42.6 23.8 %collective-permute-start.7 = (bf16[128,3,256]{0,2,1:T(8,128)(2,1)S(1)}, bf16[128,3,256]{0,2,1:T(8,128)(2,1)S(1)}, u32[]{:S(2)}, u32[]{:S(2)}) collective-permute-start(bf16[128,3,256]{0,2,1:T(8,128)(2,1)S(1)} %broadcast_select_fusion.2), channel_id=1, source_target_pairs={{0,8},{8,0},{1,9},{9,1},{2,10},{10,2},{3,11},{11,3},{4,12},{12,4},... | collective-permute-start | bytes 589832 | tf_op jit(solution)/shard_map/ppermute | solution.py:48
  46.7 20.6 %collective-permute-start.5 = (bf16[64,4096]{1,0:T(8,128)(2,1)S(1)}, bf16[64,4096]{1,0:T(8,128)(2,1)S(1)}, u32[]{:S(2)}, u32[]{:S(2)}) collective-permute-start(bf16[64,4096]{1,0:T(8,128)(2,1)S(1)} %collective-permute-done.4), channel_id=1, source_target_pairs={{0,14},{2,0},{4,2},{6,4},{8,6},{10,8},{12,10},{14,12},{1,15},{3,1}... | collective-permute-start | bytes 1572872 | tf_op jit(solution)/shard_map/ppermute | solution.py:65
  62.3 12.1 %collective-permute-start.3 = (bf16[64,4096]{1,0:T(8,128)(2,1)S(1)}, bf16[64,4096]{1,0:T(8,128)(2,1)}, u32[]{:S(2)}, u32[]{:S(2)}) collective-permute-start(bf16[64,4096]{1,0:T(8,128)(2,1)S(1)} %collective-permute-done.2), channel_id=1, source_target_pairs={{0,2},{2,4},{4,6},{6,8},{8,10},{10,12},{12,14},{14,0},{1,3},{3,5},... | collective-permute-start | bytes 1572872 | tf_op jit(solution)/shard_map/ppermute | solution.py:62
  67.2 164.5 %all-gather.5.cloned.1.call-start = ((), (), s32[]{:S(2)}) async-start(), calls=%async_computation.2 | async-start | bytes 4456448 | tf_op jit(solution)/shard_map/all_gather | solution.py:91
  67.3 14.2 %collective-permute-start.6 = (bf16[64,4096]{1,0:T(8,128)(2,1)S(1)}, bf16[64,4096]{1,0:T(8,128)(2,1)S(1)}, u32[]{:S(2)}, u32[]{:S(2)}) collective-permute-start(bf16[64,4096]{1,0:T(8,128)(2,1)S(1)} %collective-permute-done.5), channel_id=1, source_target_pairs={{0,14},{2,0},{4,2},{6,4},{8,6},{10,8},{12,10},{14,12},{1,15},{3,1}... | collective-permute-start | bytes 1572872 | tf_op jit(solution)/shard_map/ppermute | solution.py:65
  77.1 5.3 %copy-start.2 = (bf16[128,512]{1,0:T(8,128)(2,1)S(1)}, bf16[128,512]{1,0:T(8,128)(2,1)}, u32[]{:S(2)}) copy-start(bf16[128,512]{1,0:T(8,128)(2,1)} %param.12) | copy-start | bytes 393220
  77.1 6.0 %copy-start.11 = (s32[1,2]{1,0:T(1,128)S(1)}, s32[1,2]{1,0:T(1,128)}, u32[]{:S(2)}) copy-start(s32[1,2]{1,0:T(1,128)} %constant.353.clone) | copy-start | bytes 28
  77.1 6.3 %copy-start.8 = (s32[64]{0:T(128)S(1)}, s32[64]{0:T(128)}, u32[]{:S(2)}) copy-start(s32[64]{0:T(128)} %param.16) | copy-start | bytes 772
  77.1 6.6 %copy-start.9 = (f32[512]{0:T(512)S(1)}, f32[512]{0:T(512)}, u32[]{:S(2)}) copy-start(f32[512]{0:T(512)} %param.15) | copy-start | bytes 6148
  77.1 7.9 %copy-start.3 = (f32[128,512]{1,0:T(8,128)S(1)}, f32[128,512]{1,0:T(8,128)}, u32[]{:S(2)}) copy-start(f32[128,512]{1,0:T(8,128)} %param.14) | copy-start | bytes 786436
  78.0 7.1 %copy-start.4 = (f32[3,3,512]{2,1,0:T(4,128)S(1)}, f32[3,3,512]{2,1,0:T(4,128)}, u32[]{:S(2)}) copy-start(f32[3,3,512]{2,1,0:T(4,128)} %param.13) | copy-start | bytes 55300
  82.4 12.2 %collective-permute-start.8 = (bf16[8,64,4096]{2,1,0:T(8,128)(2,1)}, bf16[8,64,4096]{2,1,0:T(8,128)(2,1)}, u32[]{:S(2)}, u32[]{:S(2)}) collective-permute-start(bf16[8,64,4096]{2,1,0:T(8,128)(2,1)} %bitcast_dynamic-update-slice_fusion), channel_id=1, source_target_pairs={{0,1},{1,0},{2,3},{3,2},{4,5},{5,4},{6,7},{7,6},{8,9},{9,8},{10,11... | collective-permute-start | bytes 12582920 | tf_op jit(solution)/shard_map/ppermute | solution.py:102
  82.5 7.4 %collective-permute-start.11 = (bf16[128,512]{0,1:T(8,128)(2,1)S(1)}, bf16[128,512]{0,1:T(8,128)(2,1)S(1)}, u32[]{:S(2)}, u32[]{:S(2)}) collective-permute-start(bf16[128,512]{0,1:T(8,128)(2,1)S(1)} %copy.18), channel_id=1, source_target_pairs={{0,1},{1,0},{2,3},{3,2},{4,5},{5,4},{6,7},{7,6},{8,9},{9,8},{10,11... | collective-permute-start | bytes 393224 | tf_op jit(solution)/shard_map/ppermute | solution.py:89
  90.6 65.5 %collective-permute-start.12 = (bf16[128,2,256]{0,2,1:T(8,128)(2,1)}, bf16[128,2,256]{0,2,1:T(8,128)(2,1)}, u32[]{:S(2)}, u32[]{:S(2)}) collective-permute-start(bf16[128,2,256]{0,2,1:T(8,128)(2,1)} %broadcast_select_fusion.6), channel_id=1, source_target_pairs={{0,8},{8,0},{1,9},{9,1},{2,10},{10,2},{3,11},{11,3},{4,12},{12,4},... | collective-permute-start | bytes 393224 | tf_op jit(solution)/shard_map/ppermute | solution.py:48
  136.8 7.7 %copy-start.10 = (bf16[4096,3,256]{0,2,1:T(8,128)(2,1)S(1)}, bf16[4096,3,256]{0,2,1:T(8,128)(2,1)}, u32[]{:S(2)}) copy-start(bf16[4096,3,256]{0,2,1:T(8,128)(2,1)} %all-gather.3.cloned.1.call-done) | copy-start | bytes 18874372
  152.2 7.2 %copy-start.5 = (pred[1024]{0:T(1024)(128)(4,1)S(1)}, pred[1024]{0:T(1024)(128)(4,1)}, u32[]{:S(2)}) copy-start(pred[1024]{0:T(1024)(128)(4,1)} %get-tuple-element.245) | copy-start | bytes 3076
  152.2 7.2 %copy-start.6 = (pred[1024]{0:T(1024)(128)(4,1)S(1)}, pred[1024]{0:T(1024)(128)(4,1)}, u32[]{:S(2)}) copy-start(pred[1024]{0:T(1024)(128)(4,1)} %get-tuple-element.290) | copy-start | bytes 3076
  152.3 7.2 %copy-start.7 = (pred[1024]{0:T(1024)(128)(4,1)S(1)}, pred[1024]{0:T(1024)(128)(4,1)}, u32[]{:S(2)}) copy-start(pred[1024]{0:T(1024)(128)(4,1)} %get-tuple-element.291) | copy-start | bytes 3076
  153.9 5.5 %collective-permute-start.9 = (bf16[2,768]{1,0:T(2,128)(2,1)S(1)}, bf16[2,768]{1,0:T(2,128)(2,1)S(1)}, u32[]{:S(2)}, u32[]{:S(2)}) collective-permute-start(bf16[2,768]{1,0:T(2,128)(2,1)S(1)} %slice.61), channel_id=1, source_target_pairs={{0,16},{16,32},{32,48},{48,64},{64,80},{80,96},{96,112},{112,128},... | collective-permute-start | bytes 9224 | tf_op jit(solution)/shard_map/ppermute | solution.py:121
  161.3 1.7 copy-start
  163.1 6.2 %collective-permute-start.10 = (bf16[128,256]{1,0:T(8,128)(2,1)S(1)}, bf16[128,256]{1,0:T(8,128)(2,1)S(1)}, u32[]{:S(2)}, u32[]{:S(2)}) collective-permute-start(bf16[128,256]{1,0:T(8,128)(2,1)S(1)} %slice.67), channel_id=1, source_target_pairs={{0,16},{16,32},{32,48},{48,64},{64,80},{80,96},{96,112},{112,128},... | collective-permute-start | bytes 196616 | tf_op jit(solution)/shard_map/ppermute | solution.py:126
  166.1 129.0 %reduce-scatter.2.cloned.1.call-start = ((), (), s32[]{:S(2)}) async-start(), calls=%async_computation.3 | async-start | bytes 4718592 | tf_op jit(solution)/shard_map/reduce_scatter | solution.py:143
  231.8 1.6 collective-permute-start.13
Sparse Core Ops, SparseCore 0:
  67.4 69.3 all-gather.2
  166.3 65.4 all-gather.4
  240.1 55.0 reduce-scatter.1

commit v8 on v7

--- a/solution.py
+++ b/solution.py
@@ -109,8 +109,10 @@
     projected = jnp.take(both, order, axis=0).reshape(col_rows, 3 * half)
 
     first_row = lax.axis_index("p") * col_rows
-    own_points = first_row + jnp.arange(col_rows, dtype=jnp.int32)
-    own_position = doc_position(own_points, doc_lengths)
+    wide_rows = tap_count + col_rows
+    wide_points = first_row - tap_count + jnp.arange(wide_rows, dtype=jnp.int32)
+    wide_position = doc_position(wide_points, doc_lengths)
+    own_position = wide_position[tap_count:]
 
     columns = lax.axis_size("p")
     ahead = [(i, i + 1) for i in range(columns - 1)]
@@ -118,14 +120,12 @@
     my_filter = lax.dynamic_slice_in_dim(filter_taps, zh * half, half, 1)
     my_decay = lax.dynamic_slice_in_dim(decay_rate, zh * half, half, 0)
 
-    edge_rows = lax.ppermute(projected[col_rows - 2 :], "p", ahead)
+    before = lax.ppermute(projected[col_rows - tap_count - 2 :], "p", ahead)
     short_all = short_filter(
-        jnp.concatenate([edge_rows, projected], 0), my_taps, own_position, col_rows
+        jnp.concatenate([before, projected], 0), my_taps, wide_position, wide_rows
     )
-    kv_product = (short_all[:, half : 2 * half] * short_all[:, 2 * half :]).astype(jnp.bfloat16)
-    tail_rows = lax.ppermute(kv_product[col_rows - tap_count :], "p", ahead)
-    extended = jnp.concatenate([tail_rows, kv_product], 0)
-    query = short_all[:, :half]
+    extended = (short_all[:, half : 2 * half] * short_all[:, 2 * half :]).astype(jnp.bfloat16)
+    query = short_all[tap_count:, :half]
     shaped = my_filter * jnp.exp(
         -my_decay[None, :] * jnp.arange(tap_count, dtype=jnp.float32)[:, None]
     )

time: 305 us -> 304 us (level)
  waiting for transfers between devices: 164 us -> 158 us
  local copies, waits for them, and re-layouts: 13.9 us -> 18 us
    all_gather x1, waiting for transfers between devices: 6.37 us -> 0.02 us  [block_body(): out_full = lax.all_gather(out_piece, 'p', axis=0, tiled=True)]
    add x1, other arithmetic: 1.92 us -> 5.52 us  [short_filter(): running + jnp.where(inside, short_taps[tap_index][None] * window, jnp.flo...]
    unnamed x33 -> x29, local copies, waits for them, and re-layouts: 8.25 us -> 11.6 us
  transfers between devices with their start and end apart: 17 -> 16, of which waited for: 12 -> 10; matrix products, arithmetic and copies ran while one was open for 29% -> 31% of each run, Pallas kernels for 0% -> 0%
where the time goes in v8:
time: 304 us; the launch traced here: 302 us
  waiting for transfers between devices  158 us (52%)
  other arithmetic  70.1 us (23%)
  starting transfers between devices  21.1 us (7%)
  matrix products  19.9 us (7%)
  local copies, waits for them, and re-layouts  18 us (6%)
  between operations  13.5 us (4%)
    reduce_scatter x1, waiting for transfers between devices, block_body(): lax.psum_scatter(lax.dot_general(lhs, rhs, (((1,), (1,)), ((), ())), pref...  56.1 us
    add x8, other arithmetic, tap_group(): running + jnp.where(inside, weight_row * window.astype(jnp.float32), jnp....  51.4 us
    ppermute x4, waiting for transfers between devices, z_ring_gather(): going_right = lax.ppermute(going_right, ('zh', 'zl'), right)  45.4 us
    all_gather x1, waiting for transfers between devices, block_body(): in_full = lax.all_gather(in_piece, 'p', axis=0, tiled=True)  40.3 us
    dot_general x2, matrix products, project(): out = jnp.dot(flat, flat_in, preferred_element_type=jnp.float32)  13.3 us
    unnamed x29, local copies, waits for them, and re-layouts  11.6 us
    ppermute x2, starting transfers between devices, swap_half(): got = lax.ppermute(give, 'zh', [(0, 1), (1, 0)])  8.46 us
    ppermute x3, starting transfers between devices, z_ring_gather(): going_left = lax.ppermute(going_left, ('zh', 'zl'), left)  7.8 us
  transfers between devices with their start and end apart: 16, of which 10 were waited for; matrix products, arithmetic and copies ran while one was open for 31% of the time, Pallas kernels for 0%

profile of v8, /device:TPU:2, one launch (start us, length us, event | category | flops | bytes accessed | tf_op | source)
XLA Modules:
  0.0 302.4 jit_solution(6356546394815572456)
XLA Ops:
  6.5 1.2 fusion.18
  7.8 2.0 fusion.19
  9.8 1.9 collective-permute-start
  11.7 16.1 %collective-permute-done = bf16[64,4096]{1,0:T(8,128)(2,1)S(1)} collective-permute-done((bf16[64,4096]{1,0:T(8,128)(2,1)}, bf16[64,4096]{1,0:T(8,128)(2,1)S(1)}, u32[]{:S(2)}, u32[]{:S(2)}) %collective-permute-start) | collective-permute-done | bytes 524320 | tf_op jit(solution)/shard_map/ppermute | solution.py:62
  27.8 3.2 %collective-permute-start.4 = (bf16[64,4096]{1,0:T(8,128)(2,1)}, bf16[64,4096]{1,0:T(8,128)(2,1)S(1)}, u32[]{:S(2)}, u32[]{:S(2)}) collective-permute-start(bf16[64,4096]{1,0:T(8,128)(2,1)} %fusion.19), channel_id=1, source_target_pairs={{0,14},{2,0},{4,2},{6,4},{8,6},{10,8},{12,10},{14,12},{1,15},{3,1}... | collective-permute-start | bytes 1572872 | tf_op jit(solution)/shard_map/ppermute | solution.py:65
  31.0 11.1 %collective-permute-done.1 = bf16[64,4096]{1,0:T(8,128)(2,1)S(1)} collective-permute-done((bf16[64,4096]{1,0:T(8,128)(2,1)S(1)}, bf16[64,4096]{1,0:T(8,128)(2,1)S(1)}, u32[]{:S(2)}, u32[]{:S(2)}) %collective-permute-start.1) | collective-permute-done | bytes 524320 | tf_op jit(solution)/shard_map/ppermute | solution.py:62
  42.1 1.0 fusion.32
  43.1 0.2 copy.21
  43.3 0.2 copy.20
  43.5 4.1 %collective-permute-start.7 = (bf16[128,3,256]{0,2,1:T(8,128)(2,1)S(1)}, bf16[128,3,256]{0,2,1:T(8,128)(2,1)S(1)}, u32[]{:S(2)}, u32[]{:S(2)}) collective-permute-start(bf16[128,3,256]{0,2,1:T(8,128)(2,1)S(1)} %broadcast_select_fusion.2), channel_id=1, source_target_pairs={{0,8},{8,0},{1,9},{9,1},{2,10},{10,2},{3,11},{11,3},{4,12},{12,4},... | collective-permute-start | bytes 589832 | tf_op jit(solution)/shard_map/ppermute | solution.py:48
  47.6 3.2 %collective-permute-start.5 = (bf16[64,4096]{1,0:T(8,128)(2,1)S(1)}, bf16[64,4096]{1,0:T(8,128)(2,1)}, u32[]{:S(2)}, u32[]{:S(2)}) collective-permute-start(bf16[64,4096]{1,0:T(8,128)(2,1)S(1)} %collective-permute-done.4), channel_id=1, source_target_pairs={{0,14},{2,0},{4,2},{6,4},{8,6},{10,8},{12,10},{14,12},{1,15},{3,1}... | collective-permute-start | bytes 1572872 | tf_op jit(solution)/shard_map/ppermute | solution.py:65
  50.9 12.4 %collective-permute-done.2 = bf16[64,4096]{1,0:T(8,128)(2,1)} collective-permute-done((bf16[64,4096]{1,0:T(8,128)(2,1)S(1)}, bf16[64,4096]{1,0:T(8,128)(2,1)}, u32[]{:S(2)}, u32[]{:S(2)}) %collective-permute-start.2) | collective-permute-done | bytes 524320 | tf_op jit(solution)/shard_map/ppermute | solution.py:62
  63.3 4.0 %collective-permute-done.7 = bf16[128,3,256]{0,2,1:T(8,128)(2,1)S(1)} collective-permute-done((bf16[128,3,256]{0,2,1:T(8,128)(2,1)S(1)}, bf16[128,3,256]{0,2,1:T(8,128)(2,1)S(1)}, u32[]{:S(2)}, u32[]{:S(2)}) %collective-permute-start.7) | collective-permute-done | bytes 196640 | tf_op jit(solution)/shard_map/ppermute | solution.py:48
  67.3 0.8 pad_maximum_fusion.2
  68.1 1.3 collective-permute-start.6
  69.5 5.8 %collective-permute-done.3 = bf16[64,4096]{1,0:T(8,128)(2,1)} collective-permute-done((bf16[64,4096]{1,0:T(8,128)(2,1)}, bf16[64,4096]{1,0:T(8,128)(2,1)}, u32[]{:S(2)}, u32[]{:S(2)}) %collective-permute-start.3) | collective-permute-done | bytes 524320 | tf_op jit(solution)/shard_map/ppermute | solution.py:62
  75.3 1.9 bitcast_dynamic-update-slice_fusion.7
  77.2 1.9 bitcast_dynamic-update-slice_fusion.6
  79.1 0.8 bitcast_dynamic-update-slice_fusion.5
  80.0 0.9 bitcast_dynamic-update-slice_fusion.4
  80.8 1.0 bitcast_dynamic-update-slice_fusion.3
  81.9 0.8 bitcast_dynamic-update-slice_fusion.2
  82.7 1.9 bitcast_dynamic-update-slice_fusion.1
  84.6 0.9 bitcast_dynamic-update-slice_fusion
  85.4 0.1 copy.18
  85.6 0.6 collective-permute-start.10
  86.4 0.1 copy.15
  86.5 0.1 reduce-window.9
  86.6 0.1 reduce
  86.8 0.1 select_reduce_fusion
  87.2 0.1 broadcast_in_dim.462
  87.3 5.7 %collective-permute-done.10 = bf16[128,512]{0,1:T(8,128)(2,1)S(1)} collective-permute-done((bf16[128,512]{0,1:T(8,128)(2,1)S(1)}, bf16[128,512]{0,1:T(8,128)(2,1)S(1)}, u32[]{:S(2)}, u32[]{:S(2)}) %collective-permute-start.10) | collective-permute-done | bytes 131104 | tf_op jit(solution)/shard_map/ppermute | solution.py:89
  93.0 4.4 %collective-permute-start.11 = (bf16[128,2,256]{0,2,1:T(8,128)(2,1)S(1)}, bf16[128,2,256]{0,2,1:T(8,128)(2,1)S(1)}, u32[]{:S(2)}, u32[]{:S(2)}) collective-permute-start(bf16[128,2,256]{0,2,1:T(8,128)(2,1)S(1)} %broadcast_select_fusion.6), channel_id=1, source_target_pairs={{0,8},{8,0},{1,9},{9,1},{2,10},{10,2},{3,11},{11,3},{4,12},{12,4},... | collective-permute-start | bytes 393224 | tf_op jit(solution)/shard_map/ppermute | solution.py:48
  97.4 40.3 %all-gather.3.cloned.1.call-done = bf16[4096,3,256]{0,2,1:T(8,128)(2,1)} async-done(((bf16[256,3,256]{0,2,1:T(8,128)(2,1)}), bf16[4096,3,256]{0,2,1:T(8,128)(2,1)}) %all-gather.3.cloned.1.call-update) | async-done | bytes 6291472 | tf_op jit(solution)/shard_map/all_gather | solution.py:86
  137.7 7.6 %convolution_convert_fusion.1 = bf16[512,768]{1,0:T(8,128)(2,1)S(1)} fusion(bf16[512,4096]{1,0:T(8,128)(2,1)} %bitcast.13, bf16[4096,768]{0,1:T(8,128)(2,1)} %bitcast.114), kind=kOutput, calls=%fused_computation.61 | convolution fusion | flops 3221618688 | bytes 11272192 | tf_op jit(solution)/shard_map/dot_general | solution.py:99
  145.4 5.7 %convolution_convert_fusion.2 = bf16[512,768]{1,0:T(8,128)(2,1)S(1)} fusion(bf16[512,4096]{1,0:T(8,128)(2,1)} %bitcast.10, bf16[4096,768]{0,1:T(8,128)(2,1)S(1)} %bitcast.115), kind=kOutput, calls=%fused_computation.62 | convolution fusion | flops 3221618688 | bytes 11272192 | tf_op jit(solution)/shard_map/dot_general | solution.py:99
  151.0 1.3 pad_maximum_fusion.1
  152.4 3.2 %gather_fusion = bf16[16,64,768]{2,1,0:T(8,128)(2,1)} fusion(bf16[16,64,768]{2,1,0:T(8,128)(2,1)} %pad_maximum_fusion.1, s32[1024]{0:T(1024)S(1)} %pad_clamp_fusion), kind=kCustom, calls=%fused_computation | custom fusion | bytes 3145792 | tf_op jit(solution)/shard_map/jit(_take)/gather | solution.py:109
  155.6 1.6 bitcast_select_fusion
  157.2 1.2 copy-done.2
  158.4 2.2 collective-permute-start.9
  160.7 0.7 pad_maximum_fusion.3
  161.5 4.6 %collective-permute-done.9 = bf16[130,768]{1,0:T(8,128)(2,1)S(1)} collective-permute-done((bf16[130,768]{1,0:T(8,128)(2,1)S(1)}, bf16[130,768]{1,0:T(8,128)(2,1)S(1)}, u32[]{:S(2)}, u32[]{:S(2)}) %collective-permute-start.9) | collective-permute-done | bytes 199712 | tf_op jit(solution)/shard_map/ppermute | solution.py:123
  166.1 5.5 %select_add_fusion.1 = f32[1152,768]{1,0:T(8,128)S(1)} fusion(bf16[130,768]{1,0:T(8,128)(2,1)S(1)} %collective-permute-done.9, bf16[1024,768]{1,0:T(8,128)(2,1)} %copy-done.2, f32[768]{0:T(1024)S(1)} %mul.692, f32[768]{0:T(1024)S(1)} %mul.689, f32[768]{0:T(1024)S(1)} %mul.681, pred[1152]{0:T(1024)(128)(4,1)S(1)} %get-tuple-element.291, ...), kind=kLoop, calls=%fused_computation.50 | loop fusion | flops 17694720 | bytes 5324160 | tf_op jit(solution)/shard_map/add | solution.py:19
  171.7 1.7 copy-done
  173.4 0.1 fusion.17
  173.5 54.6 %while.17 = (s32[]{:T(128)}, f32[1024,256]{1,0:T(8,128)S(1)}, s32[1024]{0:T(1024)S(1)}, f32[128,256]{1,0:T(8,128)S(1)}, bf16[1152,256]{1,0:T(8,128)(2,1)S(1)}, /...) while((s32[]{:T(128)}, f32[1024,256]{1,0:T(8,128)S(1)}, ...), condition=%wide.region_4.5_spmd.clone, body=%wide.region_3.4_spmd.clone.sunk | while | flops 17055876 | bytes 10573791 | solution.py:39
  173.7 0.1 constant_dynamic-slice_fusion.21
  173.9 6.4 %fusion.39 = f32[1024,256]{1,0:T(8,128)S(1)} fusion(f32[1024,256]{1,0:T(8,128)S(1)} %get-tuple-element.427, bf16[1152,256]{1,0:T(8,128)(2,1)S(1)} %get-tuple-element.469, s32[]{:T(128)S(6)} %select_n.820, f32[256]{0:T(256)S(1)} %bitcast.98, s32[]{:T(128)S(6)} %select_n.837, f32[256]{0:T(256)S(1)} %bitcast.99, s32[]{:T(128)S(6)} %select_n.838, ...), kind=kLoop, calls=%fused_computation.16.clone.1 | loop fusion | flops 17039360 | bytes 10518593 | tf_op jit(solution)/shard_map/while/body/eval_jaxpr/add | solution.py:33
  180.5 0.1 constant_dynamic-slice_fusion.21
  180.8 6.4 %fusion.39 = f32[1024,256]{1,0:T(8,128)S(1)} fusion(f32[1024,256]{1,0:T(8,128)S(1)} %get-tuple-element.427, bf16[1152,256]{1,0:T(8,128)(2,1)S(1)} %get-tuple-element.469, s32[]{:T(128)S(6)} %select_n.820, f32[256]{0:T(256)S(1)} %bitcast.98, s32[]{:T(128)S(6)} %select_n.837, f32[256]{0:T(256)S(1)} %bitcast.99, s32[]{:T(128)S(6)} %select_n.838, ...), kind=kLoop, calls=%fused_computation.16.clone.1 | loop fusion | flops 17039360 | bytes 10518593 | tf_op jit(solution)/shard_map/while/body/eval_jaxpr/add | solution.py:33
  187.3 0.1 constant_dynamic-slice_fusion.21
  187.6 6.4 %fusion.39 = f32[1024,256]{1,0:T(8,128)S(1)} fusion(f32[1024,256]{1,0:T(8,128)S(1)} %get-tuple-element.427, bf16[1152,256]{1,0:T(8,128)(2,1)S(1)} %get-tuple-element.469, s32[]{:T(128)S(6)} %select_n.820, f32[256]{0:T(256)S(1)} %bitcast.98, s32[]{:T(128)S(6)} %select_n.837, f32[256]{0:T(256)S(1)} %bitcast.99, s32[]{:T(128)S(6)} %select_n.838, ...), kind=kLoop, calls=%fused_computation.16.clone.1 | loop fusion | flops 17039360 | bytes 10518593 | tf_op jit(solution)/shard_map/while/body/eval_jaxpr/add | solution.py:33
  194.4 6.4 %fusion.39 = f32[1024,256]{1,0:T(8,128)S(1)} fusion(f32[1024,256]{1,0:T(8,128)S(1)} %get-tuple-element.427, bf16[1152,256]{1,0:T(8,128)(2,1)S(1)} %get-tuple-element.469, s32[]{:T(128)S(6)} %select_n.820, f32[256]{0:T(256)S(1)} %bitcast.98, s32[]{:T(128)S(6)} %select_n.837, f32[256]{0:T(256)S(1)} %bitcast.99, s32[]{:T(128)S(6)} %select_n.838, ...), kind=kLoop, calls=%fused_computation.16.clone.1 | loop fusion | flops 17039360 | bytes 10518593 | tf_op jit(solution)/shard_map/while/body/eval_jaxpr/add | solution.py:33
  201.2 6.4 %fusion.39 = f32[1024,256]{1,0:T(8,128)S(1)} fusion(f32[1024,256]{1,0:T(8,128)S(1)} %get-tuple-element.427, bf16[1152,256]{1,0:T(8,128)(2,1)S(1)} %get-tuple-element.469, s32[]{:T(128)S(6)} %select_n.820, f32[256]{0:T(256)S(1)} %bitcast.98, s32[]{:T(128)S(6)} %select_n.837, f32[256]{0:T(256)S(1)} %bitcast.99, s32[]{:T(128)S(6)} %select_n.838, ...), kind=kLoop, calls=%fused_computation.16.clone.1 | loop fusion | flops 17039360 | bytes 10518593 | tf_op jit(solution)/shard_map/while/body/eval_jaxpr/add | solution.py:33
  208.1 6.4 %fusion.39 = f32[1024,256]{1,0:T(8,128)S(1)} fusion(f32[1024,256]{1,0:T(8,128)S(1)} %get-tuple-element.427, bf16[1152,256]{1,0:T(8,128)(2,1)S(1)} %get-tuple-element.469, s32[]{:T(128)S(6)} %select_n.820, f32[256]{0:T(256)S(1)} %bitcast.98, s32[]{:T(128)S(6)} %select_n.837, f32[256]{0:T(256)S(1)} %bitcast.99, s32[]{:T(128)S(6)} %select_n.838, ...), kind=kLoop, calls=%fused_computation.16.clone.1 | loop fusion | flops 17039360 | bytes 10518593 | tf_op jit(solution)/shard_map/while/body/eval_jaxpr/add | solution.py:33
  214.9 6.4 %fusion.39 = f32[1024,256]{1,0:T(8,128)S(1)} fusion(f32[1024,256]{1,0:T(8,128)S(1)} %get-tuple-element.427, bf16[1152,256]{1,0:T(8,128)(2,1)S(1)} %get-tuple-element.469, s32[]{:T(128)S(6)} %select_n.820, f32[256]{0:T(256)S(1)} %bitcast.98, s32[]{:T(128)S(6)} %select_n.837, f32[256]{0:T(256)S(1)} %bitcast.99, s32[]{:T(128)S(6)} %select_n.838, ...), kind=kLoop, calls=%fused_computation.16.clone.1 | loop fusion | flops 17039360 | bytes 10518593 | tf_op jit(solution)/shard_map/while/body/eval_jaxpr/add | solution.py:33
  221.8 6.4 %fusion.39 = f32[1024,256]{1,0:T(8,128)S(1)} fusion(f32[1024,256]{1,0:T(8,128)S(1)} %get-tuple-element.427, bf16[1152,256]{1,0:T(8,128)(2,1)S(1)} %get-tuple-element.469, s32[]{:T(128)S(6)} %select_n.820, f32[256]{0:T(256)S(1)} %bitcast.98, s32[]{:T(128)S(6)} %select_n.837, f32[256]{0:T(256)S(1)} %bitcast.99, s32[]{:T(128)S(6)} %select_n.838, ...), kind=kLoop, calls=%fused_computation.16.clone.1 | loop fusion | flops 17039360 | bytes 10518593 | tf_op jit(solution)/shard_map/while/body/eval_jaxpr/add | solution.py:33
  228.2 1.3 fusion.21
  229.6 0.1 collective-permute-start.12
  229.7 1.5 collective-permute-done.12
  231.2 6.6 %convolution_convert_fusion = bf16[512,4096]{1,0:T(8,128)(2,1)} fusion(bf16[4096,512]{0,1:T(8,128)(2,1)} %bitcast.116, bf16[512,256]{1,0:T(8,128)(2,1)S(1)} %bitcast.117, bf16[512,256]{1,0:T(8,128)(2,1)S(1)} %bitcast.96), kind=kOutput, calls=%fused_computation.49 | convolution fusion | flops 2150629376 | bytes 8912896 | tf_op jit(solution)/shard_map/dot_general | solution.py:144
  237.8 56.1 %reduce-scatter.2.cloned.1.call-done = bf16[64,4096]{1,0:T(8,128)(2,1)} async-done(((bf16[512,4096]{1,0:T(8,128)(2,1)}), bf16[64,4096]{1,0:T(8,128)(2,1)}) %reduce-scatter.2.cloned.1.call-update) | async-done | bytes 524304 | tf_op jit(solution)/shard_map/reduce_scatter | solution.py:143
  293.9 2.0 fusion.20
  (75 shorter events, 1.8 us)
Async XLA Ops:
  6.5 131.2 %all-gather.3.cloned.1.call-start = ((), (), s32[]{:S(2)}) async-start(), calls=%async_computation.1 | async-start | bytes 6684672 | tf_op jit(solution)/shard_map/all_gather | solution.py:86
  9.8 18.0 %collective-permute-start = (bf16[64,4096]{1,0:T(8,128)(2,1)}, bf16[64,4096]{1,0:T(8,128)(2,1)S(1)}, u32[]{:S(2)}, u32[]{:S(2)}) collective-permute-start(bf16[64,4096]{1,0:T(8,128)(2,1)} %fusion.19), channel_id=1, source_target_pairs={{0,2},{2,4},{4,6},{6,8},{8,10},{10,12},{12,14},{14,0},{1,3},{3,5},... | collective-permute-start | bytes 1572872 | tf_op jit(solution)/shard_map/ppermute | solution.py:62
  27.8 14.3 %collective-permute-start.1 = (bf16[64,4096]{1,0:T(8,128)(2,1)S(1)}, bf16[64,4096]{1,0:T(8,128)(2,1)S(1)}, u32[]{:S(2)}, u32[]{:S(2)}) collective-permute-start(bf16[64,4096]{1,0:T(8,128)(2,1)S(1)} %collective-permute-done), channel_id=1, source_target_pairs={{0,2},{2,4},{4,6},{6,8},{8,10},{10,12},{12,14},{14,0},{1,3},{3,5},... | collective-permute-start | bytes 1572872 | tf_op jit(solution)/shard_map/ppermute | solution.py:62
  27.8 19.8 %collective-permute-start.4 = (bf16[64,4096]{1,0:T(8,128)(2,1)}, bf16[64,4096]{1,0:T(8,128)(2,1)S(1)}, u32[]{:S(2)}, u32[]{:S(2)}) collective-permute-start(bf16[64,4096]{1,0:T(8,128)(2,1)} %fusion.19), channel_id=1, source_target_pairs={{0,14},{2,0},{4,2},{6,4},{8,6},{10,8},{12,10},{14,12},{1,15},{3,1}... | collective-permute-start | bytes 1572872 | tf_op jit(solution)/shard_map/ppermute | solution.py:65
  42.1 21.2 %collective-permute-start.2 = (bf16[64,4096]{1,0:T(8,128)(2,1)S(1)}, bf16[64,4096]{1,0:T(8,128)(2,1)}, u32[]{:S(2)}, u32[]{:S(2)}) collective-permute-start(bf16[64,4096]{1,0:T(8,128)(2,1)S(1)} %collective-permute-done.1), channel_id=1, source_target_pairs={{0,2},{2,4},{4,6},{6,8},{8,10},{10,12},{12,14},{14,0},{1,3},{3,5},... | collective-permute-start | bytes 1572872 | tf_op jit(solution)/shard_map/ppermute | solution.py:62
  43.5 37.4 %copy-start.1 = (bf16[64,4096]{1,0:T(8,128)(2,1)S(1)}, bf16[64,4096]{1,0:T(8,128)(2,1)}, u32[]{:S(2)}) copy-start(bf16[64,4096]{1,0:T(8,128)(2,1)} %param.10) | copy-start | bytes 1572868
  43.5 23.7 %collective-permute-start.7 = (bf16[128,3,256]{0,2,1:T(8,128)(2,1)S(1)}, bf16[128,3,256]{0,2,1:T(8,128)(2,1)S(1)}, u32[]{:S(2)}, u32[]{:S(2)}) collective-permute-start(bf16[128,3,256]{0,2,1:T(8,128)(2,1)S(1)} %broadcast_select_fusion.2), channel_id=1, source_target_pairs={{0,8},{8,0},{1,9},{9,1},{2,10},{10,2},{3,11},{11,3},{4,12},{12,4},... | collective-permute-start | bytes 589832 | tf_op jit(solution)/shard_map/ppermute | solution.py:48
  47.6 20.5 %collective-permute-start.5 = (bf16[64,4096]{1,0:T(8,128)(2,1)S(1)}, bf16[64,4096]{1,0:T(8,128)(2,1)}, u32[]{:S(2)}, u32[]{:S(2)}) collective-permute-start(bf16[64,4096]{1,0:T(8,128)(2,1)S(1)} %collective-permute-done.4), channel_id=1, source_target_pairs={{0,14},{2,0},{4,2},{6,4},{8,6},{10,8},{12,10},{14,12},{1,15},{3,1}... | collective-permute-start | bytes 1572872 | tf_op jit(solution)/shard_map/ppermute | solution.py:65
  63.3 12.0 %collective-permute-start.3 = (bf16[64,4096]{1,0:T(8,128)(2,1)}, bf16[64,4096]{1,0:T(8,128)(2,1)}, u32[]{:S(2)}, u32[]{:S(2)}) collective-permute-start(bf16[64,4096]{1,0:T(8,128)(2,1)} %collective-permute-done.2), channel_id=1, source_target_pairs={{0,2},{2,4},{4,6},{6,8},{8,10},{10,12},{12,14},{14,0},{1,3},{3,5},... | collective-permute-start | bytes 1572872 | tf_op jit(solution)/shard_map/ppermute | solution.py:62
  68.1 161.5 %all-gather.5.cloned.1.call-start = ((), (), s32[]{:S(2)}) async-start(), calls=%async_computation.2 | async-start | bytes 4456448 | tf_op jit(solution)/shard_map/all_gather | solution.py:91
  68.1 16.4 %collective-permute-start.6 = (bf16[64,4096]{1,0:T(8,128)(2,1)}, bf16[64,4096]{1,0:T(8,128)(2,1)S(1)}, u32[]{:S(2)}, u32[]{:S(2)}) collective-permute-start(bf16[64,4096]{1,0:T(8,128)(2,1)} %collective-permute-done.5), channel_id=1, source_target_pairs={{0,14},{2,0},{4,2},{6,4},{8,6},{10,8},{12,10},{14,12},{1,15},{3,1}... | collective-permute-start | bytes 1572872 | tf_op jit(solution)/shard_map/ppermute | solution.py:65
  77.2 8.3 %copy-start.3 = (bf16[128,512]{1,0:T(8,128)(2,1)S(1)}, bf16[128,512]{1,0:T(8,128)(2,1)}, u32[]{:S(2)}) copy-start(bf16[128,512]{1,0:T(8,128)(2,1)} %param.12) | copy-start | bytes 393220
  79.1 7.1 %copy-start.9 = (s32[1,2]{1,0:T(1,128)S(1)}, s32[1,2]{1,0:T(1,128)}, u32[]{:S(2)}) copy-start(s32[1,2]{1,0:T(1,128)} %constant.356.clone) | copy-start | bytes 28
  79.1 7.3 %copy-start.6 = (s32[64]{0:T(128)S(1)}, s32[64]{0:T(128)}, u32[]{:S(2)}) copy-start(s32[64]{0:T(128)} %param.16) | copy-start | bytes 772
  79.1 7.6 %copy-start.7 = (f32[512]{0:T(512)S(1)}, f32[512]{0:T(512)}, u32[]{:S(2)}) copy-start(f32[512]{0:T(512)} %param.15) | copy-start | bytes 6148
  79.1 7.9 %copy-start.4 = (f32[128,512]{1,0:T(8,128)S(1)}, f32[128,512]{1,0:T(8,128)}, u32[]{:S(2)}) copy-start(f32[128,512]{1,0:T(8,128)} %param.14) | copy-start | bytes 786436
  79.1 8.0 %copy-start.5 = (f32[3,3,512]{2,1,0:T(4,128)S(1)}, f32[3,3,512]{2,1,0:T(4,128)}, u32[]{:S(2)}) copy-start(f32[3,3,512]{2,1,0:T(4,128)} %param.13) | copy-start | bytes 55300
  85.4 12.0 %collective-permute-start.8 = (bf16[8,64,4096]{2,1,0:T(8,128)(2,1)}, bf16[8,64,4096]{2,1,0:T(8,128)(2,1)}, u32[]{:S(2)}, u32[]{:S(2)}) collective-permute-start(bf16[8,64,4096]{2,1,0:T(8,128)(2,1)} %bitcast_dynamic-update-slice_fusion), channel_id=1, source_target_pairs={{0,1},{1,0},{2,3},{3,2},{4,5},{5,4},{6,7},{7,6},{8,9},{9,8},{10,11... | collective-permute-start | bytes 12582920 | tf_op jit(solution)/shard_map/ppermute | solution.py:102
  85.6 7.4 %collective-permute-start.10 = (bf16[128,512]{0,1:T(8,128)(2,1)S(1)}, bf16[128,512]{0,1:T(8,128)(2,1)S(1)}, u32[]{:S(2)}, u32[]{:S(2)}) collective-permute-start(bf16[128,512]{0,1:T(8,128)(2,1)S(1)} %copy.18), channel_id=1, source_target_pairs={{0,1},{1,0},{2,3},{3,2},{4,5},{5,4},{6,7},{7,6},{8,9},{9,8},{10,11... | collective-permute-start | bytes 393224 | tf_op jit(solution)/shard_map/ppermute | solution.py:89
  93.0 67.6 %collective-permute-start.11 = (bf16[128,2,256]{0,2,1:T(8,128)(2,1)S(1)}, bf16[128,2,256]{0,2,1:T(8,128)(2,1)S(1)}, u32[]{:S(2)}, u32[]{:S(2)}) collective-permute-start(bf16[128,2,256]{0,2,1:T(8,128)(2,1)S(1)} %broadcast_select_fusion.6), channel_id=1, source_target_pairs={{0,8},{8,0},{1,9},{9,1},{2,10},{10,2},{3,11},{11,3},{4,12},{12,4},... | collective-permute-start | bytes 393224 | tf_op jit(solution)/shard_map/ppermute | solution.py:48
  137.7 7.7 %copy-start.8 = (bf16[4096,3,256]{0,2,1:T(8,128)(2,1)S(1)}, bf16[4096,3,256]{0,2,1:T(8,128)(2,1)}, u32[]{:S(2)}) copy-start(bf16[4096,3,256]{0,2,1:T(8,128)(2,1)} %all-gather.3.cloned.1.call-done) | copy-start | bytes 18874372
  157.2 1.2 copy-start.2
  158.4 7.7 %collective-permute-start.9 = (bf16[130,768]{1,0:T(8,128)(2,1)S(1)}, bf16[130,768]{1,0:T(8,128)(2,1)S(1)}, u32[]{:S(2)}, u32[]{:S(2)}) collective-permute-start(bf16[130,768]{1,0:T(8,128)(2,1)S(1)} %slice.65), channel_id=1, source_target_pairs={{0,16},{16,32},{32,48},{48,64},{64,80},{80,96},{96,112},{112,128},... | collective-permute-start | bytes 599048 | tf_op jit(solution)/shard_map/ppermute | solution.py:123
  161.5 132.5 %reduce-scatter.2.cloned.1.call-start = ((), (), s32[]{:S(2)}) async-start(), calls=%async_computation.3 | async-start | bytes 4718592 | tf_op jit(solution)/shard_map/reduce_scatter | solution.py:143
  171.7 1.7 copy-start
  229.6 1.6 collective-permute-start.12
Sparse Core Ops, SparseCore 0:
  68.2 69.4 all-gather.2
  161.6 63.3 all-gather.4
  237.9 55.9 reduce-scatter.1

commit v9 on v8

--- a/solution.py
+++ b/solution.py
@@ -36,7 +36,7 @@
         return running
 
     zero_sum = jnp.zeros((out_count, shaped.shape[1]), jnp.float32)
-    return lax.fori_loop(0, tap_count // 16, tap_group, zero_sum)
+    return lax.fori_loop(0, tap_count // 16, tap_group, zero_sum, unroll=True)
 
 
 def swap_half(piece, zh, axis):
@@ -124,7 +124,9 @@
     short_all = short_filter(
         jnp.concatenate([before, projected], 0), my_taps, wide_position, wide_rows
     )
-    extended = (short_all[:, half : 2 * half] * short_all[:, 2 * half :]).astype(jnp.bfloat16)
+    extended = lax.reduce_precision(
+        short_all[:, half : 2 * half] * short_all[:, 2 * half :], exponent_bits=8, mantissa_bits=7
+    )
     query = short_all[tap_count:, :half]
     shaped = my_filter * jnp.exp(
         -my_decay[None, :] * jnp.arange(tap_count, dtype=jnp.float32)[:, None]

time: 304 us -> 293 us (0.964)
  other arithmetic: 70.1 us -> 55.1 us
  waiting for transfers between devices: 158 us -> 162 us
    add x8 -> x1, other arithmetic: 51.4 us -> 10.2 us  [tap_group(): running + jnp.where(inside, weight_row * window.astype(jnp.float32), jnp....]
    convert_element_type x1, other arithmetic: 1.33 us -> 26.2 us  [block_body(): gated_mix = (query * long_mix).astype(jnp.bfloat16)]
    all_gather x1, waiting for transfers between devices: 0.02 us -> 17.1 us  [block_body(): out_full = lax.all_gather(out_piece, 'p', axis=0, tiled=True)]
    ppermute x1, waiting for transfers between devices: 5.66 us -> 0.01 us  [block_body(): lax.ppermute(out_weight, 'c', [(0, 1), (1, 0)])]
    ppermute x2, waiting for transfers between devices: 3.95 us -> 0.01 us  [swap_half(): got = lax.ppermute(give, 'zh', [(0, 1), (1, 0)])]
    dynamic_slice x8 -> x7, local copies, waits for them, and re-layouts: 0.7 us -> 4.6 us  [tap_group(): weight_row = lax.dynamic_slice_in_dim(shaped, tap_index, 1, 0)]
    ge x8 -> x7, other arithmetic: 0.31 us -> 3.92 us  [tap_group(): inside = (positions >= tap_index)[:, None]]
    unnamed x29 -> x111, local copies, waits for them, and re-layouts: 11.6 us -> 9.61 us
  transfers between devices with their start and end apart: 16 -> 16, of which waited for: 10 -> 9; matrix products, arithmetic and copies ran while one was open for 31% -> 27% of each run, Pallas kernels for 0% -> 0%
where the time goes in v9:
time: 293 us; the launch traced here: 292 us
  waiting for transfers between devices  162 us (55%)
  other arithmetic  55.1 us (19%)
  starting transfers between devices  21.9 us (7%)
  matrix products  19.9 us (7%)
  local copies, waits for them, and re-layouts  18.5 us (6%)
  between operations  14.1 us (5%)
    reduce_scatter x1, waiting for transfers between devices, block_body(): lax.psum_scatter(lax.dot_general(lhs, rhs, (((1,), (1,)), ((), ())), pref...  55.2 us
    ppermute x4, waiting for transfers between devices, z_ring_gather(): going_right = lax.ppermute(going_right, ('zh', 'zl'), right)  44 us
    all_gather x1, waiting for transfers between devices, block_body(): in_full = lax.all_gather(in_piece, 'p', axis=0, tiled=True)  40.2 us
    convert_element_type x1, other arithmetic, block_body(): gated_mix = (query * long_mix).astype(jnp.bfloat16)  26.2 us
    all_gather x1, waiting for transfers between devices, block_body(): out_full = lax.all_gather(out_piece, 'p', axis=0, tiled=True)  17.1 us
    dot_general x2, matrix products, project(): out = jnp.dot(flat, flat_in, preferred_element_type=jnp.float32)  13.3 us
    ppermute x3, starting transfers between devices, z_ring_gather(): going_left = lax.ppermute(going_left, ('zh', 'zl'), left)  10.5 us
    add x1, other arithmetic, tap_group(): running + jnp.where(inside, weight_row * window.astype(jnp.float32), jnp....  10.2 us
  transfers between devices with their start and end apart: 16, of which 9 were waited for; matrix products, arithmetic and copies ran while one was open for 27% of the time, Pallas kernels for 0%

profile of v9, /device:TPU:2, one launch (start us, length us, event | category | flops | bytes accessed | tf_op | source)
XLA Modules:
  0.0 291.9 jit_solution(9868693434027736691)
XLA Ops:
  6.5 1.3 fusion.3
  7.8 2.0 fusion.4
  9.8 1.9 collective-permute-start
  11.8 3.9 %collective-permute-start.4 = (bf16[64,4096]{1,0:T(8,128)(2,1)}, bf16[64,4096]{1,0:T(8,128)(2,1)S(1)}, u32[]{:S(2)}, u32[]{:S(2)}) collective-permute-start(bf16[64,4096]{1,0:T(8,128)(2,1)} %fusion.4), channel_id=1, source_target_pairs={{0,14},{2,0},{4,2},{6,4},{8,6},{10,8},{12,10},{14,12},{1,15},{3,1}... | collective-permute-start | bytes 1572872 | tf_op jit(solution)/shard_map/ppermute | solution.py:65
  15.7 1.0 fusion.273
  16.7 0.2 copy.21
  16.9 0.2 copy.20
  17.1 10.7 %collective-permute-done = bf16[64,4096]{1,0:T(8,128)(2,1)S(1)} collective-permute-done((bf16[64,4096]{1,0:T(8,128)(2,1)}, bf16[64,4096]{1,0:T(8,128)(2,1)S(1)}, u32[]{:S(2)}, u32[]{:S(2)}) %collective-permute-start) | collective-permute-done | bytes 524320 | tf_op jit(solution)/shard_map/ppermute | solution.py:62
  27.8 0.7 broadcast_select_fusion.2
  28.5 4.3 %collective-permute-start.7 = (bf16[128,3,256]{0,2,1:T(8,128)(2,1)}, bf16[128,3,256]{0,2,1:T(8,128)(2,1)S(1)}, u32[]{:S(2)}, u32[]{:S(2)}) collective-permute-start(bf16[128,3,256]{0,2,1:T(8,128)(2,1)} %broadcast_select_fusion.2), channel_id=1, source_target_pairs={{0,8},{8,0},{1,9},{9,1},{2,10},{10,2},{3,11},{11,3},{4,12},{12,4},... | collective-permute-start | bytes 589832 | tf_op jit(solution)/shard_map/ppermute | solution.py:48
  32.8 0.1 copy.18
  33.1 13.9 %collective-permute-done.1 = bf16[64,4096]{1,0:T(8,128)(2,1)S(1)} collective-permute-done((bf16[64,4096]{1,0:T(8,128)(2,1)S(1)}, bf16[64,4096]{1,0:T(8,128)(2,1)S(1)}, u32[]{:S(2)}, u32[]{:S(2)}) %collective-permute-start.1) | collective-permute-done | bytes 524320 | tf_op jit(solution)/shard_map/ppermute | solution.py:62
  47.2 0.6 fusion.270
  47.8 0.5 compare_and_fusion
  48.3 3.2 %collective-permute-start.5 = (bf16[64,4096]{1,0:T(8,128)(2,1)S(1)}, bf16[64,4096]{1,0:T(8,128)(2,1)}, u32[]{:S(2)}, u32[]{:S(2)}) collective-permute-start(bf16[64,4096]{1,0:T(8,128)(2,1)S(1)} %collective-permute-done.4), channel_id=1, source_target_pairs={{0,14},{2,0},{4,2},{6,4},{8,6},{10,8},{12,10},{14,12},{1,15},{3,1}... | collective-permute-start | bytes 1572872 | tf_op jit(solution)/shard_map/ppermute | solution.py:65
  51.5 10.2 %collective-permute-done.2 = bf16[64,4096]{1,0:T(8,128)(2,1)S(1)} collective-permute-done((bf16[64,4096]{1,0:T(8,128)(2,1)S(1)}, bf16[64,4096]{1,0:T(8,128)(2,1)S(1)}, u32[]{:S(2)}, u32[]{:S(2)}) %collective-permute-start.2) | collective-permute-done | bytes 524320 | tf_op jit(solution)/shard_map/ppermute | solution.py:62
  61.8 0.8 pad_maximum_fusion.2
  62.7 0.1 copy.15
  62.9 0.1 reduce
  63.0 0.1 select_reduce_fusion
  63.2 3.3 %collective-permute-start.6 = (bf16[64,4096]{1,0:T(8,128)(2,1)}, bf16[64,4096]{1,0:T(8,128)(2,1)S(1)}, u32[]{:S(2)}, u32[]{:S(2)}) collective-permute-start(bf16[64,4096]{1,0:T(8,128)(2,1)} %collective-permute-done.5), channel_id=1, source_target_pairs={{0,14},{2,0},{4,2},{6,4},{8,6},{10,8},{12,10},{14,12},{1,15},{3,1}... | collective-permute-start | bytes 1572872 | tf_op jit(solution)/shard_map/ppermute | solution.py:65
  66.5 9.1 %collective-permute-done.3 = bf16[64,4096]{1,0:T(8,128)(2,1)} collective-permute-done((bf16[64,4096]{1,0:T(8,128)(2,1)S(1)}, bf16[64,4096]{1,0:T(8,128)(2,1)}, u32[]{:S(2)}, u32[]{:S(2)}) %collective-permute-start.3) | collective-permute-done | bytes 524320 | tf_op jit(solution)/shard_map/ppermute | solution.py:62
  75.6 1.9 bitcast_dynamic-update-slice_fusion.7
  77.5 0.8 bitcast_dynamic-update-slice_fusion.6
  78.4 0.9 bitcast_dynamic-update-slice_fusion.5
  79.2 0.8 bitcast_dynamic-update-slice_fusion.4
  80.1 1.0 bitcast_dynamic-update-slice_fusion.3
  81.0 0.8 bitcast_dynamic-update-slice_fusion.2
  81.9 1.9 bitcast_dynamic-update-slice_fusion.1
  83.7 0.9 bitcast_dynamic-update-slice_fusion
  84.8 0.6 fusion.280
  85.4 0.6 broadcast_compare_fusion.97
  86.0 0.7 broadcast_compare_fusion.98
  86.7 0.6 broadcast_compare_fusion.31
  87.3 0.7 broadcast_compare_fusion.50
  87.9 0.7 broadcast_compare_fusion.69
  88.6 0.7 broadcast_compare_fusion.88
  89.3 0.7 fusion.279
  90.0 0.7 fusion.274
  90.6 0.7 fusion.275
  91.3 0.7 fusion.276
  92.0 0.7 fusion.277
  92.6 0.7 fusion.278
  93.6 2.5 collective-permute-start.11
  96.1 40.2 %all-gather.3.cloned.1.call-done = bf16[4096,3,256]{0,2,1:T(8,128)(2,1)} async-done(((bf16[256,3,256]{0,2,1:T(8,128)(2,1)}), bf16[4096,3,256]{0,2,1:T(8,128)(2,1)}) %all-gather.3.cloned.1.call-update) | async-done | bytes 6291472 | tf_op jit(solution)/shard_map/all_gather | solution.py:86
  136.4 7.6 %convolution_convert_fusion.1 = bf16[512,768]{1,0:T(8,128)(2,1)S(1)} fusion(bf16[512,4096]{1,0:T(8,128)(2,1)} %bitcast.13, bf16[4096,768]{0,1:T(8,128)(2,1)} %bitcast.306), kind=kOutput, calls=%fused_computation.13 | convolution fusion | flops 3221618688 | bytes 11272192 | tf_op jit(solution)/shard_map/dot_general | solution.py:99
  144.0 5.7 %convolution_convert_fusion.2 = bf16[512,768]{1,0:T(8,128)(2,1)S(1)} fusion(bf16[512,4096]{1,0:T(8,128)(2,1)} %bitcast.10, bf16[4096,768]{0,1:T(8,128)(2,1)S(1)} %bitcast.307), kind=kOutput, calls=%fused_computation.14 | convolution fusion | flops 3221618688 | bytes 11272192 | tf_op jit(solution)/shard_map/dot_general | solution.py:99
  149.7 0.1 pad_maximum_fusion.1
  149.8 1.8 gather_fusion
  151.6 1.6 bitcast_select_fusion
  153.3 2.2 collective-permute-start.9
  155.6 0.7 pad_maximum_fusion.3
  156.3 0.3 reduce-scatter.2.cloned.1.call-start
  156.6 4.4 %collective-permute-done.9 = bf16[130,768]{1,0:T(8,128)(2,1)S(1)} collective-permute-done((bf16[130,768]{1,0:T(8,128)(2,1)S(1)}, bf16[130,768]{1,0:T(8,128)(2,1)S(1)}, u32[]{:S(2)}, u32[]{:S(2)}) %collective-permute-start.9) | collective-permute-done | bytes 199712 | tf_op jit(solution)/shard_map/ppermute | solution.py:123
  161.1 2.5 select_add_fusion
  163.6 1.8 copy-done
  165.4 0.2 fusion.2
  166.0 10.2 %fusion.201 = f32[1024,256]{1,0:T(8,128)S(1)} fusion(f32[1152,256]{1,0:T(8,128)S(1)} %fusion.2, f32[256]{0:T(256)} %bitcast.287, f32[256]{0:T(256)} %bitcast.288, f32[256]{0:T(256)} %bitcast.289, f32[256]{0:T(256)} %bitcast.290, f32[256]{0:T(256)} %bitcast.291, f32[256]{0:T(256)} %bitcast.292, f32[256]{0:T(256)} %bitcast.293, f32[256]{0:T(256)} %bitcast.294, ...), kind=kLoop, calls=%fused_computation.312 | loop fusion | flops 24903680 | bytes 34668544 | tf_op jit(solution)/shard_map/eval_jaxpr/add | solution.py:33
  176.6 26.2 %fusion.9 = bf16[1024,256]{1,0:T(8,128)(2,1)S(1)} fusion(f32[1152,256]{1,0:T(8,128)S(1)} %fusion.2, f32[1024,256]{1,0:T(8,128)S(1)} %fusion.201, f32[256]{0:T(256)} %bitcast.179, f32[256]{0:T(256)} %bitcast.180, f32[256]{0:T(256)} %bitcast.181, f32[256]{0:T(256)} %bitcast.182, f32[256]{0:T(256)} %bitcast.183, f32[256]{0:T(256)} %bitcast.184, ...), kind=kLoop, calls=%fused_computation.24 | loop fusion | flops 76021760 | bytes 103481344 | tf_op jit(solution)/shard_map/convert_element_type | solution.py:135
  202.8 17.1 %all-gather.5.cloned.1.call-done = bf16[4096,2,256]{0,2,1:T(8,128)(2,1)} async-done(((bf16[256,2,256]{0,2,1:T(8,128)(2,1)}), bf16[4096,2,256]{0,2,1:T(8,128)(2,1)}) %all-gather.5.cloned.1.call-update) | async-done | bytes 4194320 | tf_op jit(solution)/shard_map/all_gather | solution.py:91
  220.0 1.5 collective-permute-done.12
  221.5 6.6 %convolution_convert_fusion = bf16[512,4096]{1,0:T(8,128)(2,1)} fusion(bf16[4096,512]{0,1:T(8,128)(2,1)} %bitcast.308, bf16[512,256]{1,0:T(8,128)(2,1)S(1)} %bitcast.309, bf16[512,256]{1,0:T(8,128)(2,1)S(1)} %bitcast.176), kind=kOutput, calls=%fused_computation.1 | convolution fusion | flops 2150629376 | bytes 8912896 | tf_op jit(solution)/shard_map/dot_general | solution.py:146
  228.2 55.2 %reduce-scatter.2.cloned.1.call-done = bf16[64,4096]{1,0:T(8,128)(2,1)} async-done(((bf16[512,4096]{1,0:T(8,128)(2,1)}), bf16[64,4096]{1,0:T(8,128)(2,1)}) %reduce-scatter.2.cloned.1.call-update) | async-done | bytes 524304 | tf_op jit(solution)/shard_map/reduce_scatter | solution.py:145
  283.4 2.0 fusion.5
  (145 shorter events, 1.5 us)
Async XLA Ops:
  6.5 26.5 %copy-start.50 = (s32[1,2]{1,0:T(1,128)S(1)}, s32[1,2]{1,0:T(1,128)}, u32[]{:S(2)}) copy-start(s32[1,2]{1,0:T(1,128)} %constant.337.clone) | copy-start | bytes 28
  6.5 26.3 %copy-start.2 = (bf16[128,512]{1,0:T(8,128)(2,1)S(1)}, bf16[128,512]{1,0:T(8,128)(2,1)}, u32[]{:S(2)}) copy-start(bf16[128,512]{1,0:T(8,128)(2,1)} %param.10) | copy-start | bytes 393220
  6.5 56.2 %copy-start.45 = (s32[64]{0:T(128)S(1)}, s32[64]{0:T(128)}, u32[]{:S(2)}) copy-start(s32[64]{0:T(128)} %param.14) | copy-start | bytes 772
  6.5 129.8 %all-gather.3.cloned.1.call-start = ((), (), s32[]{:S(2)}) async-start(), calls=%async_computation.1 | async-start | bytes 6684672 | tf_op jit(solution)/shard_map/all_gather | solution.py:86
  9.8 18.0 %collective-permute-start = (bf16[64,4096]{1,0:T(8,128)(2,1)}, bf16[64,4096]{1,0:T(8,128)(2,1)S(1)}, u32[]{:S(2)}, u32[]{:S(2)}) collective-permute-start(bf16[64,4096]{1,0:T(8,128)(2,1)} %fusion.4), channel_id=1, source_target_pairs={{0,2},{2,4},{4,6},{6,8},{8,10},{10,12},{12,14},{14,0},{1,3},{3,5},... | collective-permute-start | bytes 1572872 | tf_op jit(solution)/shard_map/ppermute | solution.py:62
  11.8 36.6 %collective-permute-start.4 = (bf16[64,4096]{1,0:T(8,128)(2,1)}, bf16[64,4096]{1,0:T(8,128)(2,1)S(1)}, u32[]{:S(2)}, u32[]{:S(2)}) collective-permute-start(bf16[64,4096]{1,0:T(8,128)(2,1)} %fusion.4), channel_id=1, source_target_pairs={{0,14},{2,0},{4,2},{6,4},{8,6},{10,8},{12,10},{14,12},{1,15},{3,1}... | collective-permute-start | bytes 1572872 | tf_op jit(solution)/shard_map/ppermute | solution.py:65
  27.8 19.1 %collective-permute-start.1 = (bf16[64,4096]{1,0:T(8,128)(2,1)S(1)}, bf16[64,4096]{1,0:T(8,128)(2,1)S(1)}, u32[]{:S(2)}, u32[]{:S(2)}) collective-permute-start(bf16[64,4096]{1,0:T(8,128)(2,1)S(1)} %collective-permute-done), channel_id=1, source_target_pairs={{0,2},{2,4},{4,6},{6,8},{8,10},{10,12},{12,14},{14,0},{1,3},{3,5},... | collective-permute-start | bytes 1572872 | tf_op jit(solution)/shard_map/ppermute | solution.py:62
  28.5 51.5 %copy-start.1 = (bf16[64,4096]{1,0:T(8,128)(2,1)S(1)}, bf16[64,4096]{1,0:T(8,128)(2,1)}, u32[]{:S(2)}) copy-start(bf16[64,4096]{1,0:T(8,128)(2,1)} %param.8) | copy-start | bytes 1572868
  28.5 33.3 %collective-permute-start.7 = (bf16[128,3,256]{0,2,1:T(8,128)(2,1)}, bf16[128,3,256]{0,2,1:T(8,128)(2,1)S(1)}, u32[]{:S(2)}, u32[]{:S(2)}) collective-permute-start(bf16[128,3,256]{0,2,1:T(8,128)(2,1)} %broadcast_select_fusion.2), channel_id=1, source_target_pairs={{0,8},{8,0},{1,9},{9,1},{2,10},{10,2},{3,11},{11,3},{4,12},{12,4},... | collective-permute-start | bytes 589832 | tf_op jit(solution)/shard_map/ppermute | solution.py:48
  32.9 60.6 %collective-permute-start.10 = (bf16[128,512]{0,1:T(8,128)(2,1)S(1)}, bf16[128,512]{0,1:T(8,128)(2,1)S(1)}, u32[]{:S(2)}, u32[]{:S(2)}) collective-permute-start(bf16[128,512]{0,1:T(8,128)(2,1)S(1)} %copy.18), channel_id=1, source_target_pairs={{0,1},{1,0},{2,3},{3,2},{4,5},{5,4},{6,7},{7,6},{8,9},{9,8},{10,11... | collective-permute-start | bytes 393224 | tf_op jit(solution)/shard_map/ppermute | solution.py:89
  47.0 14.8 %collective-permute-start.2 = (bf16[64,4096]{1,0:T(8,128)(2,1)S(1)}, bf16[64,4096]{1,0:T(8,128)(2,1)S(1)}, u32[]{:S(2)}, u32[]{:S(2)}) collective-permute-start(bf16[64,4096]{1,0:T(8,128)(2,1)S(1)} %collective-permute-done.1), channel_id=1, source_target_pairs={{0,2},{2,4},{4,6},{6,8},{8,10},{10,12},{12,14},{14,0},{1,3},{3,5},... | collective-permute-start | bytes 1572872 | tf_op jit(solution)/shard_map/ppermute | solution.py:62
  48.3 14.9 %collective-permute-start.5 = (bf16[64,4096]{1,0:T(8,128)(2,1)S(1)}, bf16[64,4096]{1,0:T(8,128)(2,1)}, u32[]{:S(2)}, u32[]{:S(2)}) collective-permute-start(bf16[64,4096]{1,0:T(8,128)(2,1)S(1)} %collective-permute-done.4), channel_id=1, source_target_pairs={{0,14},{2,0},{4,2},{6,4},{8,6},{10,8},{12,10},{14,12},{1,15},{3,1}... | collective-permute-start | bytes 1572872 | tf_op jit(solution)/shard_map/ppermute | solution.py:65
  61.8 13.8 %collective-permute-start.3 = (bf16[64,4096]{1,0:T(8,128)(2,1)S(1)}, bf16[64,4096]{1,0:T(8,128)(2,1)}, u32[]{:S(2)}, u32[]{:S(2)}) collective-permute-start(bf16[64,4096]{1,0:T(8,128)(2,1)S(1)} %collective-permute-done.2), channel_id=1, source_target_pairs={{0,2},{2,4},{4,6},{6,8},{8,10},{10,12},{12,14},{14,0},{1,3},{3,5},... | collective-permute-start | bytes 1572872 | tf_op jit(solution)/shard_map/ppermute | solution.py:62
  62.7 157.2 %all-gather.5.cloned.1.call-start = ((), (), s32[]{:S(2)}) async-start(), calls=%async_computation.2 | async-start | bytes 4456448 | tf_op jit(solution)/shard_map/all_gather | solution.py:91
  63.2 20.5 %collective-permute-start.6 = (bf16[64,4096]{1,0:T(8,128)(2,1)}, bf16[64,4096]{1,0:T(8,128)(2,1)S(1)}, u32[]{:S(2)}, u32[]{:S(2)}) collective-permute-start(bf16[64,4096]{1,0:T(8,128)(2,1)} %collective-permute-done.5), channel_id=1, source_target_pairs={{0,14},{2,0},{4,2},{6,4},{8,6},{10,8},{12,10},{14,12},{1,15},{3,1}... | collective-permute-start | bytes 1572872 | tf_op jit(solution)/shard_map/ppermute | solution.py:65
  77.5 7.1 %copy-start.48 = (f32[512]{0:T(512)S(1)}, f32[512]{0:T(512)}, u32[]{:S(2)}) copy-start(f32[512]{0:T(512)} %param.13) | copy-start | bytes 6148
  77.5 7.2 %copy-start.3 = (f32[128,512]{1,0:T(8,128)S(1)}, f32[128,512]{1,0:T(8,128)}, u32[]{:S(2)}) copy-start(f32[128,512]{1,0:T(8,128)} %param.12) | copy-start | bytes 786436
  78.3 15.0 %copy-start.4 = (f32[3,3,512]{2,1,0:T(4,128)S(1)}, f32[3,3,512]{2,1,0:T(4,128)}, u32[]{:S(2)}) copy-start(f32[3,3,512]{2,1,0:T(4,128)} %param.11) | copy-start | bytes 55300
  78.3 15.0 %copy-start.47 = (pred[16]{0:T(512)(128)(4,1)S(1)}, pred[16]{0:T(512)(128)(4,1)}, u32[]{:S(2)}) copy-start(pred[16]{0:T(512)(128)(4,1)} %compare_and_fusion) | copy-start | bytes 52
  78.3 15.2 %copy-start.46 = (s32[16]{0:T(128)S(1)}, s32[16]{0:T(128)}, u32[]{:S(2)}) copy-start(s32[16]{0:T(128)} %fusion.270) | copy-start | bytes 196
  84.6 11.5 %collective-permute-start.8 = (bf16[8,64,4096]{2,1,0:T(8,128)(2,1)}, bf16[8,64,4096]{2,1,0:T(8,128)(2,1)}, u32[]{:S(2)}, u32[]{:S(2)}) collective-permute-start(bf16[8,64,4096]{2,1,0:T(8,128)(2,1)} %bitcast_dynamic-update-slice_fusion), channel_id=1, source_target_pairs={{0,1},{1,0},{2,3},{3,2},{4,5},{5,4},{6,7},{7,6},{8,9},{9,8},{10,11... | collective-permute-start | bytes 12582920 | tf_op jit(solution)/shard_map/ppermute | solution.py:102
  93.6 61.9 %collective-permute-start.11 = (bf16[128,2,256]{0,2,1:T(8,128)(2,1)S(1)}, bf16[128,2,256]{0,2,1:T(8,128)(2,1)S(1)}, u32[]{:S(2)}, u32[]{:S(2)}) collective-permute-start(bf16[128,2,256]{0,2,1:T(8,128)(2,1)S(1)} %broadcast_select_fusion.6), channel_id=1, source_target_pairs={{0,8},{8,0},{1,9},{9,1},{2,10},{10,2},{3,11},{11,3},{4,12},{12,4},... | collective-permute-start | bytes 393224 | tf_op jit(solution)/shard_map/ppermute | solution.py:48
  136.4 7.7 %copy-start.49 = (bf16[4096,3,256]{0,2,1:T(8,128)(2,1)S(1)}, bf16[4096,3,256]{0,2,1:T(8,128)(2,1)}, u32[]{:S(2)}) copy-start(bf16[4096,3,256]{0,2,1:T(8,128)(2,1)} %all-gather.3.cloned.1.call-done) | copy-start | bytes 18874372
  153.3 7.7 %collective-permute-start.9 = (bf16[130,768]{1,0:T(8,128)(2,1)S(1)}, bf16[130,768]{1,0:T(8,128)(2,1)S(1)}, u32[]{:S(2)}, u32[]{:S(2)}) collective-permute-start(bf16[130,768]{1,0:T(8,128)(2,1)S(1)} %slice.65), channel_id=1, source_target_pairs={{0,16},{16,32},{32,48},{48,64},{64,80},{80,96},{96,112},{112,128},... | collective-permute-start | bytes 599048 | tf_op jit(solution)/shard_map/ppermute | solution.py:123
  156.3 127.0 %reduce-scatter.2.cloned.1.call-start = ((), (), s32[]{:S(2)}) async-start(), calls=%async_computation.3 | async-start | bytes 4718592 | tf_op jit(solution)/shard_map/reduce_scatter | solution.py:145
  161.0 4.6 %copy-start.39 = (f32[1,256]{1,0:T(1,128)S(1)}, f32[1,256]{1,0:T(1,128)}, u32[]{:S(2)}) copy-start(f32[1,256]{1,0:T(1,128)} %get-tuple-element.145) | copy-start | bytes 3076
  161.0 4.6 %copy-start.40 = (f32[1,256]{1,0:T(1,128)S(1)}, f32[1,256]{1,0:T(1,128)}, u32[]{:S(2)}) copy-start(f32[1,256]{1,0:T(1,128)} %get-tuple-element.146) | copy-start | bytes 3076
  161.0 4.6 %copy-start.41 = (pred[1024]{0:T(1024)(128)(4,1)S(1)}, pred[1024]{0:T(1024)(128)(4,1)}, u32[]{:S(2)}) copy-start(pred[1024]{0:T(1024)(128)(4,1)} %get-tuple-element.170) | copy-start | bytes 3076
  161.0 4.6 %copy-start.42 = (pred[1024]{0:T(1024)(128)(4,1)S(1)}, pred[1024]{0:T(1024)(128)(4,1)}, u32[]{:S(2)}) copy-start(pred[1024]{0:T(1024)(128)(4,1)} %get-tuple-element.171) | copy-start | bytes 3076
  161.1 4.6 %copy-start.43 = (pred[1024]{0:T(1024)(128)(4,1)S(1)}, pred[1024]{0:T(1024)(128)(4,1)}, u32[]{:S(2)}) copy-start(pred[1024]{0:T(1024)(128)(4,1)} %get-tuple-element.172) | copy-start | bytes 3076
  161.1 4.6 %copy-start.44 = (pred[1024]{0:T(1024)(128)(4,1)S(1)}, pred[1024]{0:T(1024)(128)(4,1)}, u32[]{:S(2)}) copy-start(pred[1024]{0:T(1024)(128)(4,1)} %get-tuple-element.173) | copy-start | bytes 3076
  165.7 10.6 %copy-start.5 = (pred[1024]{0:T(1024)(128)(4,1)S(1)}, pred[1024]{0:T(1024)(128)(4,1)}, u32[]{:S(2)}) copy-start(pred[1024]{0:T(1024)(128)(4,1)} %get-tuple-element.261) | copy-start | bytes 3076
  165.7 10.6 %copy-start.6 = (pred[1024]{0:T(1024)(128)(4,1)S(1)}, pred[1024]{0:T(1024)(128)(4,1)}, u32[]{:S(2)}) copy-start(pred[1024]{0:T(1024)(128)(4,1)} %get-tuple-element.262) | copy-start | bytes 3076
  165.7 10.6 %copy-start.7 = (pred[1024]{0:T(1024)(128)(4,1)S(1)}, pred[1024]{0:T(1024)(128)(4,1)}, u32[]{:S(2)}) copy-start(pred[1024]{0:T(1024)(128)(4,1)} %get-tuple-element.263) | copy-start | bytes 3076
  165.7 10.6 %copy-start.8 = (pred[1024]{0:T(1024)(128)(4,1)S(1)}, pred[1024]{0:T(1024)(128)(4,1)}, u32[]{:S(2)}) copy-start(pred[1024]{0:T(1024)(128)(4,1)} %get-tuple-element.226) | copy-start | bytes 3076
  165.7 10.6 %copy-start.9 = (pred[1024]{0:T(1024)(128)(4,1)S(1)}, pred[1024]{0:T(1024)(128)(4,1)}, u32[]{:S(2)}) copy-start(pred[1024]{0:T(1024)(128)(4,1)} %get-tuple-element.227) | copy-start | bytes 3076
  165.7 10.6 %copy-start.10 = (pred[1024]{0:T(1024)(128)(4,1)S(1)}, pred[1024]{0:T(1024)(128)(4,1)}, u32[]{:S(2)}) copy-start(pred[1024]{0:T(1024)(128)(4,1)} %get-tuple-element.228) | copy-start | bytes 3076
  165.7 10.6 %copy-start.11 = (pred[1024]{0:T(1024)(128)(4,1)S(1)}, pred[1024]{0:T(1024)(128)(4,1)}, u32[]{:S(2)}) copy-start(pred[1024]{0:T(1024)(128)(4,1)} %get-tuple-element.229) | copy-start | bytes 3076
  165.7 10.6 %copy-start.12 = (pred[1024]{0:T(1024)(128)(4,1)S(1)}, pred[1024]{0:T(1024)(128)(4,1)}, u32[]{:S(2)}) copy-start(pred[1024]{0:T(1024)(128)(4,1)} %get-tuple-element.230) | copy-start | bytes 3076
  165.8 10.6 %copy-start.13 = (pred[1024]{0:T(1024)(128)(4,1)S(1)}, pred[1024]{0:T(1024)(128)(4,1)}, u32[]{:S(2)}) copy-start(pred[1024]{0:T(1024)(128)(4,1)} %get-tuple-element.231) | copy-start | bytes 3076
  165.8 10.6 %copy-start.14 = (pred[1024]{0:T(1024)(128)(4,1)S(1)}, pred[1024]{0:T(1024)(128)(4,1)}, u32[]{:S(2)}) copy-start(pred[1024]{0:T(1024)(128)(4,1)} %get-tuple-element.232) | copy-start | bytes 3076
  165.8 10.6 %copy-start.15 = (pred[1024]{0:T(1024)(128)(4,1)S(1)}, pred[1024]{0:T(1024)(128)(4,1)}, u32[]{:S(2)}) copy-start(pred[1024]{0:T(1024)(128)(4,1)} %get-tuple-element.233) | copy-start | bytes 3076
  165.8 10.6 %copy-start.16 = (pred[1024]{0:T(1024)(128)(4,1)S(1)}, pred[1024]{0:T(1024)(128)(4,1)}, u32[]{:S(2)}) copy-start(pred[1024]{0:T(1024)(128)(4,1)} %get-tuple-element.234) | copy-start | bytes 3076
  165.8 10.6 %copy-start.17 = (pred[1024]{0:T(1024)(128)(4,1)S(1)}, pred[1024]{0:T(1024)(128)(4,1)}, u32[]{:S(2)}) copy-start(pred[1024]{0:T(1024)(128)(4,1)} %get-tuple-element.235) | copy-start | bytes 3076
  165.8 10.6 %copy-start.18 = (pred[1024]{0:T(1024)(128)(4,1)S(1)}, pred[1024]{0:T(1024)(128)(4,1)}, u32[]{:S(2)}) copy-start(pred[1024]{0:T(1024)(128)(4,1)} %get-tuple-element.236) | copy-start | bytes 3076
  165.8 10.6 %copy-start.19 = (pred[1024]{0:T(1024)(128)(4,1)S(1)}, pred[1024]{0:T(1024)(128)(4,1)}, u32[]{:S(2)}) copy-start(pred[1024]{0:T(1024)(128)(4,1)} %get-tuple-element.237) | copy-start | bytes 3076
  165.8 10.6 %copy-start.20 = (pred[1024]{0:T(1024)(128)(4,1)S(1)}, pred[1024]{0:T(1024)(128)(4,1)}, u32[]{:S(2)}) copy-start(pred[1024]{0:T(1024)(128)(4,1)} %get-tuple-element.238) | copy-start | bytes 3076
  165.8 10.6 %copy-start.21 = (pred[1024]{0:T(1024)(128)(4,1)S(1)}, pred[1024]{0:T(1024)(128)(4,1)}, u32[]{:S(2)}) copy-start(pred[1024]{0:T(1024)(128)(4,1)} %get-tuple-element.239) | copy-start | bytes 3076
  165.8 10.6 %copy-start.22 = (pred[1024]{0:T(1024)(128)(4,1)S(1)}, pred[1024]{0:T(1024)(128)(4,1)}, u32[]{:S(2)}) copy-start(pred[1024]{0:T(1024)(128)(4,1)} %get-tuple-element.240) | copy-start | bytes 3076
  165.9 10.6 %copy-start.23 = (pred[1024]{0:T(1024)(128)(4,1)S(1)}, pred[1024]{0:T(1024)(128)(4,1)}, u32[]{:S(2)}) copy-start(pred[1024]{0:T(1024)(128)(4,1)} %get-tuple-element.241) | copy-start | bytes 3076
  165.9 10.6 %copy-start.24 = (pred[1024]{0:T(1024)(128)(4,1)S(1)}, pred[1024]{0:T(1024)(128)(4,1)}, u32[]{:S(2)}) copy-start(pred[1024]{0:T(1024)(128)(4,1)} %get-tuple-element.242) | copy-start | bytes 3076
  165.9 10.6 %copy-start.25 = (pred[1024]{0:T(1024)(128)(4,1)S(1)}, pred[1024]{0:T(1024)(128)(4,1)}, u32[]{:S(2)}) copy-start(pred[1024]{0:T(1024)(128)(4,1)} %get-tuple-element.243) | copy-start | bytes 3076
  165.9 10.6 %copy-start.26 = (pred[1024]{0:T(1024)(128)(4,1)S(1)}, pred[1024]{0:T(1024)(128)(4,1)}, u32[]{:S(2)}) copy-start(pred[1024]{0:T(1024)(128)(4,1)} %get-tuple-element.244) | copy-start | bytes 3076
  165.9 10.6 %copy-start.27 = (pred[1024]{0:T(1024)(128)(4,1)S(1)}, pred[1024]{0:T(1024)(128)(4,1)}, u32[]{:S(2)}) copy-start(pred[1024]{0:T(1024)(128)(4,1)} %get-tuple-element.207) | copy-start | bytes 3076
  165.9 10.6 %copy-start.28 = (pred[1024]{0:T(1024)(128)(4,1)S(1)}, pred[1024]{0:T(1024)(128)(4,1)}, u32[]{:S(2)}) copy-start(pred[1024]{0:T(1024)(128)(4,1)} %get-tuple-element.208) | copy-start | bytes 3076
  165.9 10.6 %copy-start.29 = (pred[1024]{0:T(1024)(128)(4,1)S(1)}, pred[1024]{0:T(1024)(128)(4,1)}, u32[]{:S(2)}) copy-start(pred[1024]{0:T(1024)(128)(4,1)} %get-tuple-element.209) | copy-start | bytes 3076
  165.9 10.6 %copy-start.30 = (pred[1024]{0:T(1024)(128)(4,1)S(1)}, pred[1024]{0:T(1024)(128)(4,1)}, u32[]{:S(2)}) copy-start(pred[1024]{0:T(1024)(128)(4,1)} %get-tuple-element.210) | copy-start | bytes 3076
  165.9 10.6 %copy-start.31 = (pred[1024]{0:T(1024)(128)(4,1)S(1)}, pred[1024]{0:T(1024)(128)(4,1)}, u32[]{:S(2)}) copy-start(pred[1024]{0:T(1024)(128)(4,1)} %get-tuple-element.211) | copy-start | bytes 3076
  165.9 10.6 %copy-start.32 = (pred[1024]{0:T(1024)(128)(4,1)S(1)}, pred[1024]{0:T(1024)(128)(4,1)}, u32[]{:S(2)}) copy-start(pred[1024]{0:T(1024)(128)(4,1)} %get-tuple-element.212) | copy-start | bytes 3076
  166.0 10.6 %copy-start.33 = (pred[1024]{0:T(1024)(128)(4,1)S(1)}, pred[1024]{0:T(1024)(128)(4,1)}, u32[]{:S(2)}) copy-start(pred[1024]{0:T(1024)(128)(4,1)} %get-tuple-element.213) | copy-start | bytes 3076
  166.0 10.6 %copy-start.34 = (pred[1024]{0:T(1024)(128)(4,1)S(1)}, pred[1024]{0:T(1024)(128)(4,1)}, u32[]{:S(2)}) copy-start(pred[1024]{0:T(1024)(128)(4,1)} %get-tuple-element.214) | copy-start | bytes 3076
  166.0 10.6 %copy-start.35 = (pred[1024]{0:T(1024)(128)(4,1)S(1)}, pred[1024]{0:T(1024)(128)(4,1)}, u32[]{:S(2)}) copy-start(pred[1024]{0:T(1024)(128)(4,1)} %get-tuple-element.215) | copy-start | bytes 3076
  166.0 10.6 %copy-start.36 = (pred[1024]{0:T(1024)(128)(4,1)S(1)}, pred[1024]{0:T(1024)(128)(4,1)}, u32[]{:S(2)}) copy-start(pred[1024]{0:T(1024)(128)(4,1)} %get-tuple-element.216) | copy-start | bytes 3076
  219.9 1.6 collective-permute-start.12
  (3 other events, 11.0 us)
Sparse Core Ops, SparseCore 0:
  62.8 73.5 all-gather.2
  156.5 63.3 all-gather.4
  228.3 55.0 reduce-scatter.1

commit v10 on v8

--- a/solution.py
+++ b/solution.py
@@ -22,7 +22,7 @@
     return running
 
 
-def long_filter(extended, shaped, positions, out_count, tap_count):
+def long_filter(extended, shaped, positions, out_count, tap_count, unroll=True):
 
     def tap_group(group_index, running):
         for inner in range(16):
@@ -36,7 +36,7 @@
         return running
 
     zero_sum = jnp.zeros((out_count, shaped.shape[1]), jnp.float32)
-    return lax.fori_loop(0, tap_count // 16, tap_group, zero_sum)
+    return lax.fori_loop(0, tap_count // 16, tap_group, zero_sum, unroll=unroll)
 
 
 def swap_half(piece, zh, axis):
@@ -120,17 +120,38 @@
     my_filter = lax.dynamic_slice_in_dim(filter_taps, zh * half, half, 1)
     my_decay = lax.dynamic_slice_in_dim(decay_rate, zh * half, half, 0)
 
-    before = lax.ppermute(projected[col_rows - tap_count - 2 :], "p", ahead)
-    short_all = short_filter(
-        jnp.concatenate([before, projected], 0), my_taps, wide_position, wide_rows
-    )
-    extended = (short_all[:, half : 2 * half] * short_all[:, 2 * half :]).astype(jnp.bfloat16)
-    query = short_all[tap_count:, :half]
     shaped = my_filter * jnp.exp(
         -my_decay[None, :] * jnp.arange(tap_count, dtype=jnp.float32)[:, None]
     )
-    long_mix = long_filter(extended, shaped, own_position, col_rows, tap_count)
-    gated_mix = (query * long_mix).astype(jnp.bfloat16)
+
+    def kv_of(short_out):
+        return lax.reduce_precision(
+            short_out[:, half : 2 * half] * short_out[:, 2 * half :], exponent_bits=8, mantissa_bits=7
+        )
+
+    split = tap_count + 8
+    before = lax.ppermute(projected[col_rows - tap_count - 2 :], "p", ahead)
+    start = split - tap_count
+    short_big = short_filter(
+        projected[start - 2 :], my_taps, own_position[start:], col_rows - start
+    )
+    long_big = long_filter(
+        kv_of(short_big), shaped, own_position[split:], col_rows - split, tap_count
+    )
+    query_big = short_big[tap_count:, :half]
+    short_small = short_filter(
+        jnp.concatenate([before, projected[:split]], 0),
+        my_taps,
+        wide_position[: tap_count + split],
+        tap_count + split,
+    )
+    long_small = long_filter(
+        kv_of(short_small), shaped, own_position[:split], split, tap_count, unroll=False
+    )
+    query_small = short_small[tap_count:, :half]
+    gated_mix = jnp.concatenate(
+        [query_small * long_small, query_big * long_big], 0
+    ).astype(jnp.bfloat16)
     gated_mix, out_full = lax.optimization_barrier((gated_mix, out_full))
     core = lax.axis_index("c")
     swap = [(0, 1), (1, 0)]

time: 304 us -> 282 us (0.928)
  waiting for transfers between devices: 158 us -> 135 us
  other arithmetic: 70.1 us -> 61.3 us
  local copies, waits for them, and re-layouts: 18 us -> 23.4 us
  starting transfers between devices: 21.1 us -> 24.7 us
    add x8 -> x9, other arithmetic: 51.4 us -> 13.1 us  [tap_group(): running + jnp.where(inside, weight_row * window.astype(jnp.float32), jnp....]
    another operation x2 -> x4, other arithmetic: 0.21 us -> 26.9 us
    all_gather x1, waiting for transfers between devices: 40.3 us -> 27.6 us  [block_body(): in_full = lax.all_gather(in_piece, 'p', axis=0, tiled=True)]
    ppermute x1, waiting for transfers between devices: 5.66 us -> 0.01 us  [block_body(): lax.ppermute(out_weight, 'c', [(0, 1), (1, 0)])]
    dynamic_slice x8 -> x16, local copies, waits for them, and re-layouts: 0.7 us -> 5.91 us  [tap_group(): weight_row = lax.dynamic_slice_in_dim(shaped, tap_index, 1, 0)]
    ge x8 -> x15, other arithmetic: 0.31 us -> 5.37 us  [tap_group(): inside = (positions >= tap_index)[:, None]]
    ppermute x1, waiting for transfers between devices: 4.63 us -> 0.01 us  [block_body(): before = lax.ppermute(projected[col_rows - tap_count - 2:], 'p', ahead)]
    ppermute x4, waiting for transfers between devices: 45.4 us -> 41.5 us  [z_ring_gather(): going_right = lax.ppermute(going_right, ('zh', 'zl'), right)]
  transfers between devices with their start and end apart: 16 -> 16, of which waited for: 10 -> 8; matrix products, arithmetic and copies ran while one was open for 31% -> 32% of each run, Pallas kernels for 0% -> 0%
where the time goes in v10:
time: 282 us; the launch traced here: 280 us
  waiting for transfers between devices  135 us (48%)
  other arithmetic  61.3 us (22%)
  starting transfers between devices  24.7 us (9%)
  local copies, waits for them, and re-layouts  23.4 us (8%)
  matrix products  19.8 us (7%)
  between operations  14 us (5%)
    reduce_scatter x1, waiting for transfers between devices, block_body(): lax.psum_scatter(lax.dot_general(lhs, rhs, (((1,), (1,)), ((), ())), pref...  57.3 us
    ppermute x4, waiting for transfers between devices, z_ring_gather(): going_right = lax.ppermute(going_right, ('zh', 'zl'), right)  41.5 us
    all_gather x1, waiting for transfers between devices, block_body(): in_full = lax.all_gather(in_piece, 'p', axis=0, tiled=True)  27.6 us
    another operation x4, other arithmetic  26.9 us
    dot_general x2, matrix products, project(): out = jnp.dot(flat, flat_in, preferred_element_type=jnp.float32)  13.3 us
    add x9, other arithmetic, tap_group(): running + jnp.where(inside, weight_row * window.astype(jnp.float32), jnp....  13.1 us
    unnamed x105, local copies, waits for them, and re-layouts  11.4 us
    ppermute x3, starting transfers between devices, z_ring_gather(): going_left = lax.ppermute(going_left, ('zh', 'zl'), left)  10.6 us
  transfers between devices with their start and end apart: 16, of which 8 were waited for; matrix products, arithmetic and copies ran while one was open for 32% of the time, Pallas kernels for 0%

profile of v10, /device:TPU:2, one launch (start us, length us, event | category | flops | bytes accessed | tf_op | source)
XLA Modules:
  0.0 280.5 jit_solution(635205035865662391)
XLA Ops:
  6.5 1.3 fusion.15
  7.8 2.0 fusion.16
  9.8 1.9 collective-permute-start
  11.7 3.9 %collective-permute-start.4 = (bf16[64,4096]{1,0:T(8,128)(2,1)}, bf16[64,4096]{1,0:T(8,128)(2,1)S(1)}, u32[]{:S(2)}, u32[]{:S(2)}) collective-permute-start(bf16[64,4096]{1,0:T(8,128)(2,1)} %fusion.16), channel_id=1, source_target_pairs={{0,14},{2,0},{4,2},{6,4},{8,6},{10,8},{12,10},{14,12},{1,15},{3,1}... | collective-permute-start | bytes 1572872 | tf_op jit(solution)/shard_map/ppermute | solution.py:65
  15.7 1.0 fusion.289
  17.1 4.7 %collective-permute-start.7 = (bf16[128,3,256]{0,2,1:T(8,128)(2,1)S(1)}, bf16[128,3,256]{0,2,1:T(8,128)(2,1)S(1)}, u32[]{:S(2)}, u32[]{:S(2)}) collective-permute-start(bf16[128,3,256]{0,2,1:T(8,128)(2,1)S(1)} %broadcast_select_fusion.2), channel_id=1, source_target_pairs={{0,8},{8,0},{1,9},{9,1},{2,10},{10,2},{3,11},{11,3},{4,12},{12,4},... | collective-permute-start | bytes 589832 | tf_op jit(solution)/shard_map/ppermute | solution.py:48
  21.8 1.0 copy.18
  22.9 0.7 copy.15
  23.8 0.7 sub.202
  24.6 3.2 %collective-permute-done = bf16[64,4096]{1,0:T(8,128)(2,1)S(1)} collective-permute-done((bf16[64,4096]{1,0:T(8,128)(2,1)}, bf16[64,4096]{1,0:T(8,128)(2,1)S(1)}, u32[]{:S(2)}, u32[]{:S(2)}) %collective-permute-start) | collective-permute-done | bytes 524320 | tf_op jit(solution)/shard_map/ppermute | solution.py:62
  27.8 2.4 collective-permute-start.1
  31.4 17.1 %collective-permute-done.1 = bf16[64,4096]{1,0:T(8,128)(2,1)S(1)} collective-permute-done((bf16[64,4096]{1,0:T(8,128)(2,1)S(1)}, bf16[64,4096]{1,0:T(8,128)(2,1)S(1)}, u32[]{:S(2)}, u32[]{:S(2)}) %collective-permute-start.1) | collective-permute-done | bytes 524320 | tf_op jit(solution)/shard_map/ppermute | solution.py:62
  48.5 0.7 broadcast_compare_fusion.21
  49.2 3.3 %collective-permute-start.5 = (bf16[64,4096]{1,0:T(8,128)(2,1)S(1)}, bf16[64,4096]{1,0:T(8,128)(2,1)}, u32[]{:S(2)}, u32[]{:S(2)}) collective-permute-start(bf16[64,4096]{1,0:T(8,128)(2,1)S(1)} %collective-permute-done.4), channel_id=1, source_target_pairs={{0,14},{2,0},{4,2},{6,4},{8,6},{10,8},{12,10},{14,12},{1,15},{3,1}... | collective-permute-start | bytes 1572872 | tf_op jit(solution)/shard_map/ppermute | solution.py:65
  52.6 11.1 %collective-permute-done.2 = bf16[64,4096]{1,0:T(8,128)(2,1)} collective-permute-done((bf16[64,4096]{1,0:T(8,128)(2,1)S(1)}, bf16[64,4096]{1,0:T(8,128)(2,1)}, u32[]{:S(2)}, u32[]{:S(2)}) %collective-permute-start.2) | collective-permute-done | bytes 524320 | tf_op jit(solution)/shard_map/ppermute | solution.py:62
  63.7 0.8 pad_maximum_fusion.3
  64.8 3.3 %collective-permute-start.6 = (bf16[64,4096]{1,0:T(8,128)(2,1)}, bf16[64,4096]{1,0:T(8,128)(2,1)S(1)}, u32[]{:S(2)}, u32[]{:S(2)}) collective-permute-start(bf16[64,4096]{1,0:T(8,128)(2,1)} %collective-permute-done.5), channel_id=1, source_target_pairs={{0,14},{2,0},{4,2},{6,4},{8,6},{10,8},{12,10},{14,12},{1,15},{3,1}... | collective-permute-start | bytes 1572872 | tf_op jit(solution)/shard_map/ppermute | solution.py:65
  68.1 10.1 %collective-permute-done.3 = bf16[64,4096]{1,0:T(8,128)(2,1)} collective-permute-done((bf16[64,4096]{1,0:T(8,128)(2,1)}, bf16[64,4096]{1,0:T(8,128)(2,1)}, u32[]{:S(2)}, u32[]{:S(2)}) %collective-permute-start.3) | collective-permute-done | bytes 524320 | tf_op jit(solution)/shard_map/ppermute | solution.py:62
  78.2 1.9 bitcast_dynamic-update-slice_fusion.7
  80.1 1.9 bitcast_dynamic-update-slice_fusion.6
  82.0 0.8 bitcast_dynamic-update-slice_fusion.5
  82.8 0.8 bitcast_dynamic-update-slice_fusion.4
  83.6 1.0 bitcast_dynamic-update-slice_fusion.3
  84.6 0.8 bitcast_dynamic-update-slice_fusion.2
  85.5 1.9 bitcast_dynamic-update-slice_fusion.1
  87.4 0.8 bitcast_dynamic-update-slice_fusion
  89.1 0.7 broadcast_compare_fusion.110
  89.8 0.7 broadcast_compare_fusion.111
  90.4 0.7 broadcast_compare_fusion.40
  91.2 0.7 broadcast_compare_fusion.59
  91.9 0.7 broadcast_compare_fusion.78
  92.7 0.7 broadcast_compare_fusion.97
  93.4 0.7 fusion.295
  94.1 0.7 fusion.290
  94.7 0.7 fusion.291
  96.1 0.7 fusion.293
  97.5 2.3 collective-permute-start.11
  101.2 6.9 %collective-permute-done.11 = bf16[128,2,256]{0,2,1:T(8,128)(2,1)S(1)} collective-permute-done((bf16[128,2,256]{0,2,1:T(8,128)(2,1)S(1)}, bf16[128,2,256]{0,2,1:T(8,128)(2,1)S(1)}, u32[]{:S(2)}, u32[]{:S(2)}) %collective-permute-start.11) | collective-permute-done | bytes 131104 | tf_op jit(solution)/shard_map/ppermute | solution.py:48
  108.1 0.7 pad_maximum_fusion.4
  109.1 27.6 %all-gather.3.cloned.1.call-done = bf16[4096,3,256]{0,2,1:T(8,128)(2,1)} async-done(((bf16[256,3,256]{0,2,1:T(8,128)(2,1)}), bf16[4096,3,256]{0,2,1:T(8,128)(2,1)}) %all-gather.3.cloned.1.call-update) | async-done | bytes 6291472 | tf_op jit(solution)/shard_map/all_gather | solution.py:86
  136.8 7.6 %convolution_convert_fusion.1 = bf16[512,768]{1,0:T(8,128)(2,1)S(1)} fusion(bf16[512,4096]{1,0:T(8,128)(2,1)} %bitcast.13, bf16[4096,768]{0,1:T(8,128)(2,1)} %bitcast.370), kind=kOutput, calls=%fused_computation.56 | convolution fusion | flops 3221618688 | bytes 11272192 | tf_op jit(solution)/shard_map/dot_general | solution.py:99
  144.4 5.7 %convolution_convert_fusion.2 = bf16[512,768]{1,0:T(8,128)(2,1)S(1)} fusion(bf16[512,4096]{1,0:T(8,128)(2,1)} %bitcast.10, bf16[4096,768]{0,1:T(8,128)(2,1)S(1)} %bitcast.371), kind=kOutput, calls=%fused_computation.57 | convolution fusion | flops 3221618688 | bytes 11272192 | tf_op jit(solution)/shard_map/dot_general | solution.py:99
  150.3 1.8 gather_fusion
  152.1 1.7 bitcast_select_fusion
  153.8 0.7 slice.117
  154.8 2.2 select_add_fusion.1
  157.0 1.6 copy-done
  158.8 2.4 collective-permute-start.9
  161.5 7.4 %fusion.214 = f32[888,256]{1,0:T(8,128)} fusion(f32[1016,256]{1,0:T(8,128)S(1)} %fusion.18, f32[256]{0:T(256)S(1)} %bitcast.242, f32[256]{0:T(256)S(1)} %bitcast.243, f32[256]{0:T(256)S(1)} %bitcast.244, f32[256]{0:T(256)S(1)} %bitcast.245, f32[256]{0:T(256)S(1)} %bitcast.246, f32[256]{0:T(256)S(1)} %bitcast.247, f32[256]{0:T(256)S(1)} %bitcast.248, ...), kind=kLoop, calls=%fused_computation.355 | loop fusion | flops 21596160 | bytes 30068480 | tf_op jit(solution)/shard_map/eval_jaxpr/add | solution.py:33
  168.9 26.7 %fusion.22 = bf16[888,256]{1,0:T(8,128)(2,1)} fusion(f32[1016,256]{1,0:T(8,128)S(1)} %fusion.18, f32[888,256]{1,0:T(8,128)} %fusion.214, f32[256]{0:T(256)} %bitcast.368, f32[256]{0:T(256)} %bitcast.274, f32[256]{0:T(256)} %bitcast.275, f32[256]{0:T(256)} %bitcast.276, f32[256]{0:T(256)} %bitcast.277, f32[256]{0:T(256)} %bitcast.278, f32[256]{0:T(256)} %bitcast.279, ...), kind=kLoop, calls=%fused_computation.67 | loop fusion | flops 65925120 | bytes 89750784 | tf_op jit(solution)/shard_map/convert.1
  195.6 1.6 select_add_fusion.2
  197.3 9.0 %while.17 = (s32[]{:T(128)}, f32[136,256]{1,0:T(8,128)S(1)}, s32[136]{0:T(256)S(1)}, f32[128,256]{1,0:T(8,128)S(1)}, f32[264,256]{1,0:T(8,128)S(1)}, /*index=5*/...) while((s32[]{:T(128)}, f32[136,256]{1,0:T(8,128)S(1)}, ...), condition=%wide.region_4.5_spmd.clone, body=%wide.region_3.4_spmd.clone.sunk | while | flops 1708291 | bytes 2562815 | solution.py:39
  197.7 0.7 fusion.303
  198.8 0.7 fusion.303
  200.0 0.7 fusion.303
  201.1 0.7 fusion.303
  202.2 0.7 fusion.303
  203.4 0.7 fusion.303
  204.5 0.7 fusion.303
  205.6 0.7 fusion.303
  206.6 1.5 collective-permute-done.12
  208.1 6.5 %convolution_convert_fusion = bf16[512,4096]{1,0:T(8,128)(2,1)} fusion(bf16[4096,512]{0,1:T(8,128)(2,1)} %bitcast.372, bf16[512,256]{1,0:T(8,128)(2,1)S(1)} %bitcast.373, bf16[512,256]{1,0:T(8,128)(2,1)S(1)} %bitcast.224), kind=kOutput, calls=%fused_computation.49 | convolution fusion | flops 2150629376 | bytes 8912896 | tf_op jit(solution)/shard_map/dot_general | solution.py:165
  214.7 57.3 %reduce-scatter.2.cloned.1.call-done = bf16[64,4096]{1,0:T(8,128)(2,1)} async-done(((bf16[512,4096]{1,0:T(8,128)(2,1)}), bf16[64,4096]{1,0:T(8,128)(2,1)}) %reduce-scatter.2.cloned.1.call-update) | async-done | bytes 524304 | tf_op jit(solution)/shard_map/reduce_scatter | solution.py:164
  272.0 2.0 fusion.17
  (173 shorter events, 7.9 us)
Async XLA Ops:
  6.5 42.7 %copy-start.47 = (s32[1,2]{1,0:T(1,128)S(1)}, s32[1,2]{1,0:T(1,128)}, u32[]{:S(2)}) copy-start(s32[1,2]{1,0:T(1,128)} %constant.606.clone) | copy-start | bytes 28
  6.5 130.2 %all-gather.3.cloned.1.call-start = ((), (), s32[]{:S(2)}) async-start(), calls=%async_computation.1 | async-start | bytes 6684672 | tf_op jit(solution)/shard_map/all_gather | solution.py:86
  9.8 18.0 %collective-permute-start = (bf16[64,4096]{1,0:T(8,128)(2,1)}, bf16[64,4096]{1,0:T(8,128)(2,1)S(1)}, u32[]{:S(2)}, u32[]{:S(2)}) collective-permute-start(bf16[64,4096]{1,0:T(8,128)(2,1)} %fusion.16), channel_id=1, source_target_pairs={{0,2},{2,4},{4,6},{6,8},{8,10},{10,12},{12,14},{14,0},{1,3},{3,5},... | collective-permute-start | bytes 1572872 | tf_op jit(solution)/shard_map/ppermute | solution.py:62
  11.7 37.5 %collective-permute-start.4 = (bf16[64,4096]{1,0:T(8,128)(2,1)}, bf16[64,4096]{1,0:T(8,128)(2,1)S(1)}, u32[]{:S(2)}, u32[]{:S(2)}) collective-permute-start(bf16[64,4096]{1,0:T(8,128)(2,1)} %fusion.16), channel_id=1, source_target_pairs={{0,14},{2,0},{4,2},{6,4},{8,6},{10,8},{12,10},{14,12},{1,15},{3,1}... | collective-permute-start | bytes 1572872 | tf_op jit(solution)/shard_map/ppermute | solution.py:65
  16.7 66.9 %copy-start.1 = (bf16[64,4096]{1,0:T(8,128)(2,1)S(1)}, bf16[64,4096]{1,0:T(8,128)(2,1)}, u32[]{:S(2)}) copy-start(bf16[64,4096]{1,0:T(8,128)(2,1)} %param.10) | copy-start | bytes 1572868
  17.1 46.6 %collective-permute-start.7 = (bf16[128,3,256]{0,2,1:T(8,128)(2,1)S(1)}, bf16[128,3,256]{0,2,1:T(8,128)(2,1)S(1)}, u32[]{:S(2)}, u32[]{:S(2)}) collective-permute-start(bf16[128,3,256]{0,2,1:T(8,128)(2,1)S(1)} %broadcast_select_fusion.2), channel_id=1, source_target_pairs={{0,8},{8,0},{1,9},{9,1},{2,10},{10,2},{3,11},{11,3},{4,12},{12,4},... | collective-permute-start | bytes 589832 | tf_op jit(solution)/shard_map/ppermute | solution.py:48
  22.8 74.6 %collective-permute-start.10 = (bf16[128,512]{0,1:T(8,128)(2,1)S(1)}, bf16[128,512]{0,1:T(8,128)(2,1)S(1)}, u32[]{:S(2)}, u32[]{:S(2)}) collective-permute-start(bf16[128,512]{0,1:T(8,128)(2,1)S(1)} %copy.18), channel_id=1, source_target_pairs={{0,1},{1,0},{2,3},{3,2},{4,5},{5,4},{6,7},{7,6},{8,9},{9,8},{10,11... | collective-permute-start | bytes 393224 | tf_op jit(solution)/shard_map/ppermute | solution.py:89
  27.8 20.7 %collective-permute-start.1 = (bf16[64,4096]{1,0:T(8,128)(2,1)S(1)}, bf16[64,4096]{1,0:T(8,128)(2,1)S(1)}, u32[]{:S(2)}, u32[]{:S(2)}) collective-permute-start(bf16[64,4096]{1,0:T(8,128)(2,1)S(1)} %collective-permute-done), channel_id=1, source_target_pairs={{0,2},{2,4},{4,6},{6,8},{8,10},{10,12},{12,14},{14,0},{1,3},{3,5},... | collective-permute-start | bytes 1572872 | tf_op jit(solution)/shard_map/ppermute | solution.py:62
  48.5 15.1 %collective-permute-start.2 = (bf16[64,4096]{1,0:T(8,128)(2,1)S(1)}, bf16[64,4096]{1,0:T(8,128)(2,1)}, u32[]{:S(2)}, u32[]{:S(2)}) collective-permute-start(bf16[64,4096]{1,0:T(8,128)(2,1)S(1)} %collective-permute-done.1), channel_id=1, source_target_pairs={{0,2},{2,4},{4,6},{6,8},{8,10},{10,12},{12,14},{14,0},{1,3},{3,5},... | collective-permute-start | bytes 1572872 | tf_op jit(solution)/shard_map/ppermute | solution.py:62
  49.2 15.5 %collective-permute-start.5 = (bf16[64,4096]{1,0:T(8,128)(2,1)S(1)}, bf16[64,4096]{1,0:T(8,128)(2,1)}, u32[]{:S(2)}, u32[]{:S(2)}) collective-permute-start(bf16[64,4096]{1,0:T(8,128)(2,1)S(1)} %collective-permute-done.4), channel_id=1, source_target_pairs={{0,14},{2,0},{4,2},{6,4},{8,6},{10,8},{12,10},{14,12},{1,15},{3,1}... | collective-permute-start | bytes 1572872 | tf_op jit(solution)/shard_map/ppermute | solution.py:65
  63.7 14.5 %collective-permute-start.3 = (bf16[64,4096]{1,0:T(8,128)(2,1)}, bf16[64,4096]{1,0:T(8,128)(2,1)}, u32[]{:S(2)}, u32[]{:S(2)}) collective-permute-start(bf16[64,4096]{1,0:T(8,128)(2,1)} %collective-permute-done.2), channel_id=1, source_target_pairs={{0,2},{2,4},{4,6},{6,8},{8,10},{10,12},{12,14},{14,0},{1,3},{3,5},... | collective-permute-start | bytes 1572872 | tf_op jit(solution)/shard_map/ppermute | solution.py:62
  64.5 141.9 %all-gather.5.cloned.1.call-start = ((), (), s32[]{:S(2)}) async-start(), calls=%async_computation.2 | async-start | bytes 4456448 | tf_op jit(solution)/shard_map/all_gather | solution.py:91
  64.7 23.6 %copy-start.45 = (f32[512]{0:T(512)S(1)}, f32[512]{0:T(512)}, u32[]{:S(2)}) copy-start(f32[512]{0:T(512)} %param.15) | copy-start | bytes 6148
  64.7 23.6 %copy-start.3 = (f32[128,512]{1,0:T(8,128)S(1)}, f32[128,512]{1,0:T(8,128)}, u32[]{:S(2)}) copy-start(f32[128,512]{1,0:T(8,128)} %param.14) | copy-start | bytes 786436
  64.8 22.6 %collective-permute-start.6 = (bf16[64,4096]{1,0:T(8,128)(2,1)}, bf16[64,4096]{1,0:T(8,128)(2,1)S(1)}, u32[]{:S(2)}, u32[]{:S(2)}) collective-permute-start(bf16[64,4096]{1,0:T(8,128)(2,1)} %collective-permute-done.5), channel_id=1, source_target_pairs={{0,14},{2,0},{4,2},{6,4},{8,6},{10,8},{12,10},{14,12},{1,15},{3,1}... | collective-permute-start | bytes 1572872 | tf_op jit(solution)/shard_map/ppermute | solution.py:65
  80.1 19.7 %copy-start.4 = (f32[3,3,512]{2,1,0:T(4,128)S(1)}, f32[3,3,512]{2,1,0:T(4,128)}, u32[]{:S(2)}) copy-start(f32[3,3,512]{2,1,0:T(4,128)} %param.13) | copy-start | bytes 55300
  88.2 20.9 %collective-permute-start.8 = (bf16[8,64,4096]{2,1,0:T(8,128)(2,1)}, bf16[8,64,4096]{2,1,0:T(8,128)(2,1)}, u32[]{:S(2)}, u32[]{:S(2)}) collective-permute-start(bf16[8,64,4096]{2,1,0:T(8,128)(2,1)} %bitcast_dynamic-update-slice_fusion), channel_id=1, source_target_pairs={{0,1},{1,0},{2,3},{3,2},{4,5},{5,4},{6,7},{7,6},{8,9},{9,8},{10,11... | collective-permute-start | bytes 12582920 | tf_op jit(solution)/shard_map/ppermute | solution.py:102
  97.5 10.6 %collective-permute-start.11 = (bf16[128,2,256]{0,2,1:T(8,128)(2,1)S(1)}, bf16[128,2,256]{0,2,1:T(8,128)(2,1)S(1)}, u32[]{:S(2)}, u32[]{:S(2)}) collective-permute-start(bf16[128,2,256]{0,2,1:T(8,128)(2,1)S(1)} %broadcast_select_fusion.6), channel_id=1, source_target_pairs={{0,8},{8,0},{1,9},{9,1},{2,10},{10,2},{3,11},{11,3},{4,12},{12,4},... | collective-permute-start | bytes 393224 | tf_op jit(solution)/shard_map/ppermute | solution.py:48
  108.9 163.1 %reduce-scatter.2.cloned.1.call-start = ((), (), s32[]{:S(2)}) async-start(), calls=%async_computation.3 | async-start | bytes 4718592 | tf_op jit(solution)/shard_map/reduce_scatter | solution.py:164
  136.8 7.7 %copy-start.46 = (bf16[4096,3,256]{0,2,1:T(8,128)(2,1)S(1)}, bf16[4096,3,256]{0,2,1:T(8,128)(2,1)}, u32[]{:S(2)}) copy-start(bf16[4096,3,256]{0,2,1:T(8,128)(2,1)} %all-gather.3.cloned.1.call-done) | copy-start | bytes 18874372
  150.1 2.0 copy-start.41
  150.1 4.4 %copy-start.38 = (pred[1016]{0:T(1024)(128)(4,1)S(1)}, pred[1016]{0:T(1024)(128)(4,1)}, u32[]{:S(2)}) copy-start(pred[1016]{0:T(1024)(128)(4,1)} %get-tuple-element.546) | copy-start | bytes 3052
  150.1 4.4 %copy-start.39 = (pred[1016]{0:T(1024)(128)(4,1)S(1)}, pred[1016]{0:T(1024)(128)(4,1)}, u32[]{:S(2)}) copy-start(pred[1016]{0:T(1024)(128)(4,1)} %get-tuple-element.547) | copy-start | bytes 3052
  150.1 4.4 %copy-start.40 = (pred[1016]{0:T(1024)(128)(4,1)S(1)}, pred[1016]{0:T(1024)(128)(4,1)}, u32[]{:S(2)}) copy-start(pred[1016]{0:T(1024)(128)(4,1)} %get-tuple-element.548) | copy-start | bytes 3052
  154.5 6.7 %copy-start.5 = (pred[888]{0:T(1024)(128)(4,1)S(1)}, pred[888]{0:T(1024)(128)(4,1)}, u32[]{:S(2)}) copy-start(pred[888]{0:T(1024)(128)(4,1)} %get-tuple-element.436) | copy-start | bytes 2668
  154.5 6.7 %copy-start.6 = (f32[1,256]{1,0:T(1,128)S(1)}, f32[1,256]{1,0:T(1,128)}, u32[]{:S(2)}) copy-start(f32[1,256]{1,0:T(1,128)} %get-tuple-element.380) | copy-start | bytes 3076
  154.5 6.7 %copy-start.7 = (f32[1,256]{1,0:T(1,128)S(1)}, f32[1,256]{1,0:T(1,128)}, u32[]{:S(2)}) copy-start(f32[1,256]{1,0:T(1,128)} %get-tuple-element.381) | copy-start | bytes 3076
  154.5 6.7 %copy-start.8 = (f32[1,256]{1,0:T(1,128)S(1)}, f32[1,256]{1,0:T(1,128)}, u32[]{:S(2)}) copy-start(f32[1,256]{1,0:T(1,128)} %get-tuple-element.382) | copy-start | bytes 3076
  154.5 6.7 %copy-start.9 = (f32[1,256]{1,0:T(1,128)S(1)}, f32[1,256]{1,0:T(1,128)}, u32[]{:S(2)}) copy-start(f32[1,256]{1,0:T(1,128)} %get-tuple-element.383) | copy-start | bytes 3076
  154.5 6.7 %copy-start.10 = (f32[1,256]{1,0:T(1,128)S(1)}, f32[1,256]{1,0:T(1,128)}, u32[]{:S(2)}) copy-start(f32[1,256]{1,0:T(1,128)} %get-tuple-element.384) | copy-start | bytes 3076
  154.5 6.7 %copy-start.11 = (f32[1,256]{1,0:T(1,128)S(1)}, f32[1,256]{1,0:T(1,128)}, u32[]{:S(2)}) copy-start(f32[1,256]{1,0:T(1,128)} %get-tuple-element.385) | copy-start | bytes 3076
  154.6 6.7 %copy-start.12 = (f32[1,256]{1,0:T(1,128)S(1)}, f32[1,256]{1,0:T(1,128)}, u32[]{:S(2)}) copy-start(f32[1,256]{1,0:T(1,128)} %get-tuple-element.386) | copy-start | bytes 3076
  154.6 6.7 %copy-start.13 = (f32[1,256]{1,0:T(1,128)S(1)}, f32[1,256]{1,0:T(1,128)}, u32[]{:S(2)}) copy-start(f32[1,256]{1,0:T(1,128)} %get-tuple-element.387) | copy-start | bytes 3076
  154.6 6.7 %copy-start.14 = (f32[1,256]{1,0:T(1,128)S(1)}, f32[1,256]{1,0:T(1,128)}, u32[]{:S(2)}) copy-start(f32[1,256]{1,0:T(1,128)} %get-tuple-element.388) | copy-start | bytes 3076
  154.6 6.7 %copy-start.15 = (f32[1,256]{1,0:T(1,128)S(1)}, f32[1,256]{1,0:T(1,128)}, u32[]{:S(2)}) copy-start(f32[1,256]{1,0:T(1,128)} %get-tuple-element.389) | copy-start | bytes 3076
  154.6 6.7 %copy-start.16 = (f32[1,256]{1,0:T(1,128)S(1)}, f32[1,256]{1,0:T(1,128)}, u32[]{:S(2)}) copy-start(f32[1,256]{1,0:T(1,128)} %get-tuple-element.390) | copy-start | bytes 3076
  154.6 6.7 %copy-start.17 = (f32[1,256]{1,0:T(1,128)S(1)}, f32[1,256]{1,0:T(1,128)}, u32[]{:S(2)}) copy-start(f32[1,256]{1,0:T(1,128)} %get-tuple-element.391) | copy-start | bytes 3076
  154.6 6.7 %copy-start.18 = (f32[1,256]{1,0:T(1,128)S(1)}, f32[1,256]{1,0:T(1,128)}, u32[]{:S(2)}) copy-start(f32[1,256]{1,0:T(1,128)} %get-tuple-element.392) | copy-start | bytes 3076
  154.6 6.7 %copy-start.19 = (f32[1,256]{1,0:T(1,128)S(1)}, f32[1,256]{1,0:T(1,128)}, u32[]{:S(2)}) copy-start(f32[1,256]{1,0:T(1,128)} %get-tuple-element.393) | copy-start | bytes 3076
  154.6 6.7 %copy-start.20 = (f32[1,256]{1,0:T(1,128)S(1)}, f32[1,256]{1,0:T(1,128)}, u32[]{:S(2)}) copy-start(f32[1,256]{1,0:T(1,128)} %get-tuple-element.394) | copy-start | bytes 3076
  154.6 6.7 %copy-start.21 = (f32[1,256]{1,0:T(1,128)S(1)}, f32[1,256]{1,0:T(1,128)}, u32[]{:S(2)}) copy-start(f32[1,256]{1,0:T(1,128)} %get-tuple-element.395) | copy-start | bytes 3076
  154.7 6.7 %copy-start.22 = (f32[1,256]{1,0:T(1,128)S(1)}, f32[1,256]{1,0:T(1,128)}, u32[]{:S(2)}) copy-start(f32[1,256]{1,0:T(1,128)} %get-tuple-element.396) | copy-start | bytes 3076
  154.7 6.7 %copy-start.23 = (f32[1,256]{1,0:T(1,128)S(1)}, f32[1,256]{1,0:T(1,128)}, u32[]{:S(2)}) copy-start(f32[1,256]{1,0:T(1,128)} %get-tuple-element.397) | copy-start | bytes 3076
  154.7 6.7 %copy-start.24 = (f32[1,256]{1,0:T(1,128)S(1)}, f32[1,256]{1,0:T(1,128)}, u32[]{:S(2)}) copy-start(f32[1,256]{1,0:T(1,128)} %get-tuple-element.398) | copy-start | bytes 3076
  154.7 6.7 %copy-start.25 = (f32[1,256]{1,0:T(1,128)S(1)}, f32[1,256]{1,0:T(1,128)}, u32[]{:S(2)}) copy-start(f32[1,256]{1,0:T(1,128)} %get-tuple-element.399) | copy-start | bytes 3076
  154.7 6.7 %copy-start.26 = (f32[1,256]{1,0:T(1,128)S(1)}, f32[1,256]{1,0:T(1,128)}, u32[]{:S(2)}) copy-start(f32[1,256]{1,0:T(1,128)} %get-tuple-element.400) | copy-start | bytes 3076
  154.7 6.7 %copy-start.27 = (f32[1,256]{1,0:T(1,128)S(1)}, f32[1,256]{1,0:T(1,128)}, u32[]{:S(2)}) copy-start(f32[1,256]{1,0:T(1,128)} %get-tuple-element.401) | copy-start | bytes 3076
  154.7 6.7 %copy-start.28 = (f32[1,256]{1,0:T(1,128)S(1)}, f32[1,256]{1,0:T(1,128)}, u32[]{:S(2)}) copy-start(f32[1,256]{1,0:T(1,128)} %get-tuple-element.402) | copy-start | bytes 3076
  154.7 6.7 %copy-start.29 = (f32[1,256]{1,0:T(1,128)S(1)}, f32[1,256]{1,0:T(1,128)}, u32[]{:S(2)}) copy-start(f32[1,256]{1,0:T(1,128)} %get-tuple-element.403) | copy-start | bytes 3076
  154.7 6.7 %copy-start.30 = (f32[1,256]{1,0:T(1,128)S(1)}, f32[1,256]{1,0:T(1,128)}, u32[]{:S(2)}) copy-start(f32[1,256]{1,0:T(1,128)} %get-tuple-element.404) | copy-start | bytes 3076
  154.7 6.7 %copy-start.31 = (f32[1,256]{1,0:T(1,128)S(1)}, f32[1,256]{1,0:T(1,128)}, u32[]{:S(2)}) copy-start(f32[1,256]{1,0:T(1,128)} %get-tuple-element.405) | copy-start | bytes 3076
  154.8 6.7 %copy-start.32 = (f32[1,256]{1,0:T(1,128)S(1)}, f32[1,256]{1,0:T(1,128)}, u32[]{:S(2)}) copy-start(f32[1,256]{1,0:T(1,128)} %get-tuple-element.406) | copy-start | bytes 3076
  154.8 6.7 %copy-start.33 = (f32[1,256]{1,0:T(1,128)S(1)}, f32[1,256]{1,0:T(1,128)}, u32[]{:S(2)}) copy-start(f32[1,256]{1,0:T(1,128)} %get-tuple-element.407) | copy-start | bytes 3076
  154.8 6.7 %copy-start.34 = (f32[1,256]{1,0:T(1,128)S(1)}, f32[1,256]{1,0:T(1,128)}, u32[]{:S(2)}) copy-start(f32[1,256]{1,0:T(1,128)} %get-tuple-element.408) | copy-start | bytes 3076
  154.8 6.7 %copy-start.35 = (f32[1,256]{1,0:T(1,128)S(1)}, f32[1,256]{1,0:T(1,128)}, u32[]{:S(2)}) copy-start(f32[1,256]{1,0:T(1,128)} %get-tuple-element.409) | copy-start | bytes 3076
  154.8 6.7 %copy-start.36 = (f32[1,256]{1,0:T(1,128)S(1)}, f32[1,256]{1,0:T(1,128)}, u32[]{:S(2)}) copy-start(f32[1,256]{1,0:T(1,128)} %get-tuple-element.410) | copy-start | bytes 3076
  154.8 6.7 %copy-start.37 = (f32[1,256]{1,0:T(1,128)S(1)}, f32[1,256]{1,0:T(1,128)}, u32[]{:S(2)}) copy-start(f32[1,256]{1,0:T(1,128)} %get-tuple-element.411) | copy-start | bytes 3076
  157.0 1.6 copy-start
  158.8 36.8 %collective-permute-start.9 = (bf16[130,768]{1,0:T(8,128)(2,1)}, bf16[130,768]{1,0:T(8,128)(2,1)}, u32[]{:S(2)}, u32[]{:S(2)}) collective-permute-start(bf16[130,768]{1,0:T(8,128)(2,1)} %slice.117), channel_id=1, source_target_pairs={{0,16},{16,32},{32,48},{48,64},{64,80},{80,96},{96,112},{112,128},... | collective-permute-start | bytes 599048 | tf_op jit(solution)/shard_map/ppermute | solution.py:133
  168.9 26.7 %copy-start.42 = (pred[264]{0:T(512)(128)(4,1)S(1)}, pred[264]{0:T(512)(128)(4,1)}, u32[]{:S(2)}) copy-start(pred[264]{0:T(512)(128)(4,1)} %get-tuple-element.415) | copy-start | bytes 796
  168.9 26.7 %copy-start.43 = (pred[264]{0:T(512)(128)(4,1)S(1)}, pred[264]{0:T(512)(128)(4,1)}, u32[]{:S(2)}) copy-start(pred[264]{0:T(512)(128)(4,1)} %get-tuple-element.416) | copy-start | bytes 796
  168.9 26.7 %copy-start.44 = (pred[264]{0:T(512)(128)(4,1)S(1)}, pred[264]{0:T(512)(128)(4,1)}, u32[]{:S(2)}) copy-start(pred[264]{0:T(512)(128)(4,1)} %get-tuple-element.417) | copy-start | bytes 796
  197.3 9.1 %copy-start.2 = (bf16[888,256]{1,0:T(8,128)(2,1)S(1)}, bf16[888,256]{1,0:T(8,128)(2,1)}, u32[]{:S(2)}) copy-start(bf16[888,256]{1,0:T(8,128)(2,1)} %fusion.22) | copy-start | bytes 1363972
  206.5 1.6 collective-permute-start.12
Sparse Core Ops, SparseCore 0:
  64.7 72.0 all-gather.2
  139.2 63.5 all-gather.4
  214.8 57.1 reduce-scatter.1

commit v11 on v9

--- a/solution.py
+++ b/solution.py
@@ -59,11 +59,16 @@
     by_offset = {0: block}
     going_right, going_left = block, block
     for step in range(1, nz // 2 + 1):
-        going_right = lax.ppermute(going_right, ("zh", "zl"), right)
-        by_offset[-step] = going_right
         if step < nz - step:
+            going_right = lax.ppermute(going_right, ("zh", "zl"), right)
+            by_offset[-step] = going_right
             going_left = lax.ppermute(going_left, ("zh", "zl"), left)
             by_offset[step] = going_left
+        else:
+            cut = block.shape[0] // 2
+            first = lax.ppermute(going_right[:cut], ("zh", "zl"), right)
+            second = lax.ppermute(going_left[cut:], ("zh", "zl"), left)
+            by_offset[-step] = jnp.concatenate([first, second], 0)
     lowest = -(nz // 2)
     relative = jnp.stack([by_offset[lowest + i] for i in range(nz)], 0)
     pick = (jnp.arange(nz, dtype=jnp.int32) - z - lowest) % nz

time: 293 us -> 282 us (0.962)
  waiting for transfers between devices: 162 us -> 149 us
  starting transfers between devices: 21.9 us -> 25.7 us
    ppermute x4 -> x3, waiting for transfers between devices: 44 us -> 0.01 us  [z_ring_gather(): going_right = lax.ppermute(going_right, ('zh', 'zl'), right)]
    ppermute x3, waiting for transfers between devices: 0.01 us -> 31 us  [z_ring_gather(): going_left = lax.ppermute(going_left, ('zh', 'zl'), left)]
    all_gather x1, waiting for transfers between devices: 40.2 us -> 31.1 us  [block_body(): in_full = lax.all_gather(in_piece, 'p', axis=0, tiled=True)]
    ppermute x0 -> x2, waiting for transfers between devices: none -> 7.09 us  [the longest x1 4.43 us: z_ring_gather(): first = lax.ppermute(going_right[:cut], ('zh', 'zl'), right)]
    ppermute x0 -> x2, starting transfers between devices: none -> 3.69 us  [the longest x1 3.69 us: z_ring_gather(): second = lax.ppermute(going_left[cut:], ('zh', 'zl'), left)]
    unnamed x111 -> x110, local copies, waits for them, and re-layouts: 9.61 us -> 7.78 us
  transfers between devices with their start and end apart: 16 -> 17, of which waited for: 9 -> 10; matrix products, arithmetic and copies ran while one was open for 27% -> 28% of each run, Pallas kernels for 0% -> 0%
where the time goes in v11:
time: 282 us; the launch traced here: 280 us
  waiting for transfers between devices  149 us (53%)
  other arithmetic  54.5 us (19%)
  starting transfers between devices  25.7 us (9%)
  matrix products  19.9 us (7%)
  local copies, waits for them, and re-layouts  17.5 us (6%)
  between operations  14.1 us (5%)
    reduce_scatter x1, waiting for transfers between devices, block_body(): lax.psum_scatter(lax.dot_general(lhs, rhs, (((1,), (1,)), ((), ())), pref...  55.2 us
    all_gather x1, waiting for transfers between devices, block_body(): in_full = lax.all_gather(in_piece, 'p', axis=0, tiled=True)  31.1 us
    ppermute x3, waiting for transfers between devices, z_ring_gather(): going_left = lax.ppermute(going_left, ('zh', 'zl'), left)  31 us
    convert_element_type x1, other arithmetic, block_body(): gated_mix = (query * long_mix).astype(jnp.bfloat16)  26.2 us
    all_gather x1, waiting for transfers between devices, block_body(): out_full = lax.all_gather(out_piece, 'p', axis=0, tiled=True)  18.6 us
    dot_general x2, matrix products, project(): out = jnp.dot(flat, flat_in, preferred_element_type=jnp.float32)  13.3 us
    ppermute x3, starting transfers between devices, z_ring_gather(): going_left = lax.ppermute(going_left, ('zh', 'zl'), left)  13.3 us
    add x1, other arithmetic, tap_group(): running + jnp.where(inside, weight_row * window.astype(jnp.float32), jnp....  8.77 us
  transfers between devices with their start and end apart: 17, of which 10 were waited for; matrix products, arithmetic and copies ran while one was open for 28% of the time, Pallas kernels for 0%

profile of v11, /device:TPU:2, one launch (start us, length us, event | category | flops | bytes accessed | tf_op | source)
XLA Modules:
  0.0 280.5 jit_solution(15320917121550696671)
XLA Ops:
  6.5 1.3 fusion.3
  7.8 1.2 fusion.4
  9.0 5.9 %collective-permute-start.4 = (bf16[64,4096]{1,0:T(8,128)(2,1)S(1)}, bf16[64,4096]{1,0:T(8,128)(2,1)S(1)}, u32[]{:S(2)}, u32[]{:S(2)}) collective-permute-start(bf16[64,4096]{1,0:T(8,128)(2,1)S(1)} %fusion.4), channel_id=1, source_target_pairs={{0,14},{2,0},{4,2},{6,4},{8,6},{10,8},{12,10},{14,12},{1,15},{3,1}... | collective-permute-start | bytes 1572872 | tf_op jit(solution)/shard_map/ppermute | solution.py:65
  15.0 1.0 fusion.274
  16.0 0.2 copy.21
  16.2 0.2 copy.20
  16.4 0.7 broadcast_select_fusion.2
  17.1 3.4 %collective-permute-start.8 = (bf16[128,3,256]{0,2,1:T(8,128)(2,1)}, bf16[128,3,256]{0,2,1:T(8,128)(2,1)}, u32[]{:S(2)}, u32[]{:S(2)}) collective-permute-start(bf16[128,3,256]{0,2,1:T(8,128)(2,1)} %broadcast_select_fusion.2), channel_id=1, source_target_pairs={{0,8},{8,0},{1,9},{9,1},{2,10},{10,2},{3,11},{11,3},{4,12},{12,4},... | collective-permute-start | bytes 589832 | tf_op jit(solution)/shard_map/ppermute | solution.py:48
  20.4 0.1 copy.18
  20.7 14.0 %collective-permute-done.4 = bf16[64,4096]{1,0:T(8,128)(2,1)S(1)} collective-permute-done((bf16[64,4096]{1,0:T(8,128)(2,1)S(1)}, bf16[64,4096]{1,0:T(8,128)(2,1)S(1)}, u32[]{:S(2)}, u32[]{:S(2)}) %collective-permute-start.4) | collective-permute-done | bytes 524320 | tf_op jit(solution)/shard_map/ppermute | solution.py:65
  34.6 3.7 %collective-permute-start.5 = (bf16[64,4096]{1,0:T(8,128)(2,1)S(1)}, bf16[64,4096]{1,0:T(8,128)(2,1)S(1)}, u32[]{:S(2)}, u32[]{:S(2)}) collective-permute-start(bf16[64,4096]{1,0:T(8,128)(2,1)S(1)} %collective-permute-done.4), channel_id=1, source_target_pairs={{0,14},{2,0},{4,2},{6,4},{8,6},{10,8},{12,10},{14,12},{1,15},{3,1}... | collective-permute-start | bytes 1572872 | tf_op jit(solution)/shard_map/ppermute | solution.py:65
  38.4 10.3 %collective-permute-done.5 = bf16[64,4096]{1,0:T(8,128)(2,1)S(1)} collective-permute-done((bf16[64,4096]{1,0:T(8,128)(2,1)S(1)}, bf16[64,4096]{1,0:T(8,128)(2,1)S(1)}, u32[]{:S(2)}, u32[]{:S(2)}) %collective-permute-start.5) | collective-permute-done | bytes 524320 | tf_op jit(solution)/shard_map/ppermute | solution.py:65
  48.7 3.7 %collective-permute-start.6 = (bf16[64,4096]{1,0:T(8,128)(2,1)S(1)}, bf16[64,4096]{1,0:T(8,128)(2,1)S(1)}, u32[]{:S(2)}, u32[]{:S(2)}) collective-permute-start(bf16[64,4096]{1,0:T(8,128)(2,1)S(1)} %collective-permute-done.5), channel_id=1, source_target_pairs={{0,14},{2,0},{4,2},{6,4},{8,6},{10,8},{12,10},{14,12},{1,15},{3,1}... | collective-permute-start | bytes 1572872 | tf_op jit(solution)/shard_map/ppermute | solution.py:65
  52.4 1.0 broadcast_select_fusion.1
  53.4 0.8 pad_maximum_fusion.2
  54.5 0.1 reduce
  54.7 0.6 fusion.271
  55.3 6.7 %collective-permute-done.6 = bf16[64,4096]{1,0:T(8,128)(2,1)S(1)} collective-permute-done((bf16[64,4096]{1,0:T(8,128)(2,1)S(1)}, bf16[64,4096]{1,0:T(8,128)(2,1)S(1)}, u32[]{:S(2)}, u32[]{:S(2)}) %collective-permute-start.6) | collective-permute-done | bytes 524320 | tf_op jit(solution)/shard_map/ppermute | solution.py:65
  62.0 0.7 slice.74
  62.7 3.7 %collective-permute-start.7 = (bf16[32,4096]{1,0:T(8,128)(2,1)}, bf16[32,4096]{1,0:T(8,128)(2,1)}, u32[]{:S(2)}, u32[]{:S(2)}) collective-permute-start(bf16[32,4096]{1,0:T(8,128)(2,1)} %slice.74), channel_id=1, source_target_pairs={{0,14},{2,0},{4,2},{6,4},{8,6},{10,8},{12,10},{14,12},{1,15},{3,1}... | collective-permute-start | bytes 786440 | tf_op jit(solution)/shard_map/ppermute | solution.py:70
  66.4 0.7 slice.73
  67.1 0.1 select_reduce_fusion
  67.3 0.6 compare_and_fusion
  67.9 2.7 collective-permute-done.7
  70.6 4.4 %collective-permute-done.3 = bf16[32,4096]{1,0:T(8,128)(2,1)} collective-permute-done((bf16[32,4096]{1,0:T(8,128)(2,1)}, bf16[32,4096]{1,0:T(8,128)(2,1)}, u32[]{:S(2)}, u32[]{:S(2)}) %collective-permute-start.3) | collective-permute-done | bytes 262176 | tf_op jit(solution)/shard_map/ppermute | solution.py:69
  75.0 1.9 fusion.263
  76.9 0.8 bitcast_dynamic-update-slice_fusion.6
  77.7 2.0 bitcast_dynamic-update-slice_fusion.5
  79.7 0.8 bitcast_dynamic-update-slice_fusion.4
  80.6 1.0 bitcast_dynamic-update-slice_fusion.3
  81.5 0.8 bitcast_dynamic-update-slice_fusion.2
  82.3 0.8 bitcast_dynamic-update-slice_fusion.1
  83.2 0.9 bitcast_dynamic-update-slice_fusion
  84.3 0.6 broadcast_compare_fusion.31
  84.9 0.7 broadcast_compare_fusion.50
  85.6 0.7 broadcast_compare_fusion.69
  86.2 0.7 broadcast_compare_fusion.88
  86.9 0.6 fusion.280
  87.6 0.7 fusion.275
  88.2 0.7 fusion.276
  88.9 0.7 fusion.277
  89.6 0.7 fusion.278
  90.2 0.7 fusion.279
  91.2 2.7 collective-permute-start.12
  93.9 31.1 %all-gather.3.cloned.1.call-done = bf16[4096,3,256]{0,2,1:T(8,128)(2,1)} async-done(((bf16[256,3,256]{0,2,1:T(8,128)(2,1)}), bf16[4096,3,256]{0,2,1:T(8,128)(2,1)}) %all-gather.3.cloned.1.call-update) | async-done | bytes 6291472 | tf_op jit(solution)/shard_map/all_gather | solution.py:91
  125.0 7.6 %convolution_convert_fusion.1 = bf16[512,768]{1,0:T(8,128)(2,1)S(1)} fusion(bf16[512,4096]{1,0:T(8,128)(2,1)} %bitcast.13, bf16[4096,768]{0,1:T(8,128)(2,1)} %bitcast.308), kind=kOutput, calls=%fused_computation.13 | convolution fusion | flops 3221618688 | bytes 11272192 | tf_op jit(solution)/shard_map/dot_general | solution.py:104
  132.6 5.7 %convolution_convert_fusion.2 = bf16[512,768]{1,0:T(8,128)(2,1)S(1)} fusion(bf16[512,4096]{1,0:T(8,128)(2,1)} %bitcast.10, bf16[4096,768]{0,1:T(8,128)(2,1)S(1)} %bitcast.309), kind=kOutput, calls=%fused_computation.14 | convolution fusion | flops 3221618688 | bytes 11272192 | tf_op jit(solution)/shard_map/dot_general | solution.py:104
  138.3 0.1 pad_maximum_fusion.1
  138.5 1.8 gather_fusion
  140.3 1.6 bitcast_select_fusion
  142.0 2.2 collective-permute-start.10
  144.2 0.7 pad_maximum_fusion.3
  145.0 0.3 reduce-scatter.2.cloned.1.call-start
  145.2 4.4 %collective-permute-done.10 = bf16[130,768]{1,0:T(8,128)(2,1)S(1)} collective-permute-done((bf16[130,768]{1,0:T(8,128)(2,1)S(1)}, bf16[130,768]{1,0:T(8,128)(2,1)S(1)}, u32[]{:S(2)}, u32[]{:S(2)}) %collective-permute-start.10) | collective-permute-done | bytes 199712 | tf_op jit(solution)/shard_map/ppermute | solution.py:128
  149.7 2.5 select_add_fusion
  152.2 1.8 copy-done
  154.1 0.2 fusion.2
  154.6 8.8 %fusion.201 = f32[1024,256]{1,0:T(8,128)S(1)} fusion(f32[1152,256]{1,0:T(8,128)S(1)} %fusion.2, f32[256]{0:T(256)S(1)} %bitcast.289, f32[256]{0:T(256)S(1)} %bitcast.290, f32[256]{0:T(256)S(1)} %bitcast.291, f32[256]{0:T(256)S(1)} %bitcast.292, f32[256]{0:T(256)S(1)} %bitcast.293, f32[256]{0:T(256)S(1)} %bitcast.294, f32[256]{0:T(256)S(1)} %bitcast.295, ...), kind=kLoop, calls=%fused_computation.312 | loop fusion | flops 24903680 | bytes 34668544 | tf_op jit(solution)/shard_map/eval_jaxpr/add | solution.py:33
  163.7 26.2 %fusion.9 = bf16[1024,256]{1,0:T(8,128)(2,1)S(1)} fusion(f32[1152,256]{1,0:T(8,128)S(1)} %fusion.2, f32[1024,256]{1,0:T(8,128)S(1)} %fusion.201, f32[256]{0:T(256)} %bitcast.181, f32[256]{0:T(256)} %bitcast.182, f32[256]{0:T(256)} %bitcast.183, f32[256]{0:T(256)} %bitcast.184, f32[256]{0:T(256)} %bitcast.185, f32[256]{0:T(256)} %bitcast.186, ...), kind=kLoop, calls=%fused_computation.24 | loop fusion | flops 76021760 | bytes 103481344 | tf_op jit(solution)/shard_map/convert_element_type | solution.py:140
  190.0 18.6 %all-gather.5.cloned.1.call-done = bf16[4096,2,256]{0,2,1:T(8,128)(2,1)} async-done(((bf16[256,2,256]{0,2,1:T(8,128)(2,1)}), bf16[4096,2,256]{0,2,1:T(8,128)(2,1)}) %all-gather.5.cloned.1.call-update) | async-done | bytes 4194320 | tf_op jit(solution)/shard_map/all_gather | solution.py:96
  208.7 1.5 collective-permute-done.13
  210.2 6.6 %convolution_convert_fusion = bf16[512,4096]{1,0:T(8,128)(2,1)} fusion(bf16[4096,512]{0,1:T(8,128)(2,1)} %bitcast.310, bf16[512,256]{1,0:T(8,128)(2,1)S(1)} %bitcast.311, bf16[512,256]{1,0:T(8,128)(2,1)S(1)} %bitcast.178), kind=kOutput, calls=%fused_computation.1 | convolution fusion | flops 2150629376 | bytes 8912896 | tf_op jit(solution)/shard_map/dot_general | solution.py:151
  216.8 55.2 %reduce-scatter.2.cloned.1.call-done = bf16[64,4096]{1,0:T(8,128)(2,1)} async-done(((bf16[512,4096]{1,0:T(8,128)(2,1)}), bf16[64,4096]{1,0:T(8,128)(2,1)}) %reduce-scatter.2.cloned.1.call-update) | async-done | bytes 524304 | tf_op jit(solution)/shard_map/reduce_scatter | solution.py:150
  272.0 2.0 fusion.5
  (149 shorter events, 1.6 us)
Async XLA Ops:
  6.5 31.8 %copy-start.50 = (s32[1,2]{1,0:T(1,128)S(1)}, s32[1,2]{1,0:T(1,128)}, u32[]{:S(2)}) copy-start(s32[1,2]{1,0:T(1,128)} %constant.337.clone) | copy-start | bytes 28
  6.5 13.9 %copy-start.2 = (bf16[128,512]{1,0:T(8,128)(2,1)S(1)}, bf16[128,512]{1,0:T(8,128)(2,1)}, u32[]{:S(2)}) copy-start(bf16[128,512]{1,0:T(8,128)(2,1)} %param.10) | copy-start | bytes 393220
  6.5 47.8 %copy-start.45 = (s32[64]{0:T(128)S(1)}, s32[64]{0:T(128)}, u32[]{:S(2)}) copy-start(s32[64]{0:T(128)} %param.14) | copy-start | bytes 772
  6.5 118.4 %all-gather.3.cloned.1.call-start = ((), (), s32[]{:S(2)}) async-start(), calls=%async_computation.1 | async-start | bytes 6684672 | tf_op jit(solution)/shard_map/all_gather | solution.py:91
  9.0 25.6 %collective-permute-start.4 = (bf16[64,4096]{1,0:T(8,128)(2,1)S(1)}, bf16[64,4096]{1,0:T(8,128)(2,1)S(1)}, u32[]{:S(2)}, u32[]{:S(2)}) collective-permute-start(bf16[64,4096]{1,0:T(8,128)(2,1)S(1)} %fusion.4), channel_id=1, source_target_pairs={{0,14},{2,0},{4,2},{6,4},{8,6},{10,8},{12,10},{14,12},{1,15},{3,1}... | collective-permute-start | bytes 1572872 | tf_op jit(solution)/shard_map/ppermute | solution.py:65
  15.0 23.3 %collective-permute-start = (bf16[64,4096]{1,0:T(8,128)(2,1)S(1)}, bf16[64,4096]{1,0:T(8,128)(2,1)S(1)}, u32[]{:S(2)}, u32[]{:S(2)}) collective-permute-start(bf16[64,4096]{1,0:T(8,128)(2,1)S(1)} %fusion.4), channel_id=1, source_target_pairs={{0,2},{2,4},{4,6},{6,8},{8,10},{10,12},{12,14},{14,0},{1,3},{3,5},... | collective-permute-start | bytes 1572872 | tf_op jit(solution)/shard_map/ppermute | solution.py:63
  17.1 35.3 %collective-permute-start.8 = (bf16[128,3,256]{0,2,1:T(8,128)(2,1)}, bf16[128,3,256]{0,2,1:T(8,128)(2,1)}, u32[]{:S(2)}, u32[]{:S(2)}) collective-permute-start(bf16[128,3,256]{0,2,1:T(8,128)(2,1)} %broadcast_select_fusion.2), channel_id=1, source_target_pairs={{0,8},{8,0},{1,9},{9,1},{2,10},{10,2},{3,11},{11,3},{4,12},{12,4},... | collective-permute-start | bytes 589832 | tf_op jit(solution)/shard_map/ppermute | solution.py:48
  20.6 70.6 %collective-permute-start.11 = (bf16[128,512]{0,1:T(8,128)(2,1)S(1)}, bf16[128,512]{0,1:T(8,128)(2,1)S(1)}, u32[]{:S(2)}, u32[]{:S(2)}) collective-permute-start(bf16[128,512]{0,1:T(8,128)(2,1)S(1)} %copy.18), channel_id=1, source_target_pairs={{0,1},{1,0},{2,3},{3,2},{4,5},{5,4},{6,7},{7,6},{8,9},{9,8},{10,11... | collective-permute-start | bytes 393224 | tf_op jit(solution)/shard_map/ppermute | solution.py:94
  34.6 14.1 %collective-permute-start.5 = (bf16[64,4096]{1,0:T(8,128)(2,1)S(1)}, bf16[64,4096]{1,0:T(8,128)(2,1)S(1)}, u32[]{:S(2)}, u32[]{:S(2)}) collective-permute-start(bf16[64,4096]{1,0:T(8,128)(2,1)S(1)} %collective-permute-done.4), channel_id=1, source_target_pairs={{0,14},{2,0},{4,2},{6,4},{8,6},{10,8},{12,10},{14,12},{1,15},{3,1}... | collective-permute-start | bytes 1572872 | tf_op jit(solution)/shard_map/ppermute | solution.py:65
  38.3 14.1 %collective-permute-start.1 = (bf16[64,4096]{1,0:T(8,128)(2,1)S(1)}, bf16[64,4096]{1,0:T(8,128)(2,1)}, u32[]{:S(2)}, u32[]{:S(2)}) collective-permute-start(bf16[64,4096]{1,0:T(8,128)(2,1)S(1)} %collective-permute-done), channel_id=1, source_target_pairs={{0,2},{2,4},{4,6},{6,8},{8,10},{10,12},{12,14},{14,0},{1,3},{3,5},... | collective-permute-start | bytes 1572872 | tf_op jit(solution)/shard_map/ppermute | solution.py:63
  48.7 13.3 %collective-permute-start.6 = (bf16[64,4096]{1,0:T(8,128)(2,1)S(1)}, bf16[64,4096]{1,0:T(8,128)(2,1)S(1)}, u32[]{:S(2)}, u32[]{:S(2)}) collective-permute-start(bf16[64,4096]{1,0:T(8,128)(2,1)S(1)} %collective-permute-done.5), channel_id=1, source_target_pairs={{0,14},{2,0},{4,2},{6,4},{8,6},{10,8},{12,10},{14,12},{1,15},{3,1}... | collective-permute-start | bytes 1572872 | tf_op jit(solution)/shard_map/ppermute | solution.py:65
  52.4 14.0 %collective-permute-start.2 = (bf16[64,4096]{1,0:T(8,128)(2,1)}, bf16[64,4096]{1,0:T(8,128)(2,1)S(1)}, u32[]{:S(2)}, u32[]{:S(2)}) collective-permute-start(bf16[64,4096]{1,0:T(8,128)(2,1)} %collective-permute-done.1), channel_id=1, source_target_pairs={{0,2},{2,4},{4,6},{6,8},{8,10},{10,12},{12,14},{14,0},{1,3},{3,5},... | collective-permute-start | bytes 1572872 | tf_op jit(solution)/shard_map/ppermute | solution.py:63
  53.4 27.2 %copy-start.1 = (bf16[64,4096]{1,0:T(8,128)(2,1)S(1)}, bf16[64,4096]{1,0:T(8,128)(2,1)}, u32[]{:S(2)}) copy-start(bf16[64,4096]{1,0:T(8,128)(2,1)} %param.8) | copy-start | bytes 1572868
  54.2 154.3 %all-gather.5.cloned.1.call-start = ((), (), s32[]{:S(2)}) async-start(), calls=%async_computation.2 | async-start | bytes 4456448 | tf_op jit(solution)/shard_map/all_gather | solution.py:96
  62.7 7.9 %collective-permute-start.7 = (bf16[32,4096]{1,0:T(8,128)(2,1)}, bf16[32,4096]{1,0:T(8,128)(2,1)}, u32[]{:S(2)}, u32[]{:S(2)}) collective-permute-start(bf16[32,4096]{1,0:T(8,128)(2,1)} %slice.74), channel_id=1, source_target_pairs={{0,14},{2,0},{4,2},{6,4},{8,6},{10,8},{12,10},{14,12},{1,15},{3,1}... | collective-permute-start | bytes 786440 | tf_op jit(solution)/shard_map/ppermute | solution.py:70
  67.1 7.9 %collective-permute-start.3 = (bf16[32,4096]{1,0:T(8,128)(2,1)}, bf16[32,4096]{1,0:T(8,128)(2,1)}, u32[]{:S(2)}, u32[]{:S(2)}) collective-permute-start(bf16[32,4096]{1,0:T(8,128)(2,1)} %slice.73), channel_id=1, source_target_pairs={{0,2},{2,4},{4,6},{6,8},{8,10},{10,12},{12,14},{14,0},{1,3},{3,5},... | collective-permute-start | bytes 786440 | tf_op jit(solution)/shard_map/ppermute | solution.py:69
  76.9 7.1 %copy-start.48 = (f32[512]{0:T(512)S(1)}, f32[512]{0:T(512)}, u32[]{:S(2)}) copy-start(f32[512]{0:T(512)} %param.13) | copy-start | bytes 6148
  77.7 6.4 %copy-start.3 = (f32[128,512]{1,0:T(8,128)S(1)}, f32[128,512]{1,0:T(8,128)}, u32[]{:S(2)}) copy-start(f32[128,512]{1,0:T(8,128)} %param.12) | copy-start | bytes 786436
  77.7 13.2 %copy-start.4 = (f32[3,3,512]{2,1,0:T(4,128)S(1)}, f32[3,3,512]{2,1,0:T(4,128)}, u32[]{:S(2)}) copy-start(f32[3,3,512]{2,1,0:T(4,128)} %param.11) | copy-start | bytes 55300
  77.7 13.2 %copy-start.47 = (pred[16]{0:T(512)(128)(4,1)S(1)}, pred[16]{0:T(512)(128)(4,1)}, u32[]{:S(2)}) copy-start(pred[16]{0:T(512)(128)(4,1)} %compare_and_fusion) | copy-start | bytes 52
  77.7 13.4 %copy-start.46 = (s32[16]{0:T(128)S(1)}, s32[16]{0:T(128)}, u32[]{:S(2)}) copy-start(s32[16]{0:T(128)} %fusion.271) | copy-start | bytes 196
  84.0 9.9 %collective-permute-start.9 = (bf16[8,64,4096]{2,1,0:T(8,128)(2,1)}, bf16[8,64,4096]{2,1,0:T(8,128)(2,1)}, u32[]{:S(2)}, u32[]{:S(2)}) collective-permute-start(bf16[8,64,4096]{2,1,0:T(8,128)(2,1)} %bitcast_dynamic-update-slice_fusion), channel_id=1, source_target_pairs={{0,1},{1,0},{2,3},{3,2},{4,5},{5,4},{6,7},{7,6},{8,9},{9,8},{10,11... | collective-permute-start | bytes 12582920 | tf_op jit(solution)/shard_map/ppermute | solution.py:107
  91.2 52.9 %collective-permute-start.12 = (bf16[128,2,256]{0,2,1:T(8,128)(2,1)S(1)}, bf16[128,2,256]{0,2,1:T(8,128)(2,1)S(1)}, u32[]{:S(2)}, u32[]{:S(2)}) collective-permute-start(bf16[128,2,256]{0,2,1:T(8,128)(2,1)S(1)} %broadcast_select_fusion.6), channel_id=1, source_target_pairs={{0,8},{8,0},{1,9},{9,1},{2,10},{10,2},{3,11},{11,3},{4,12},{12,4},... | collective-permute-start | bytes 393224 | tf_op jit(solution)/shard_map/ppermute | solution.py:48
  125.0 7.6 %copy-start.49 = (bf16[4096,3,256]{0,2,1:T(8,128)(2,1)S(1)}, bf16[4096,3,256]{0,2,1:T(8,128)(2,1)}, u32[]{:S(2)}) copy-start(bf16[4096,3,256]{0,2,1:T(8,128)(2,1)} %all-gather.3.cloned.1.call-done) | copy-start | bytes 18874372
  142.0 7.7 %collective-permute-start.10 = (bf16[130,768]{1,0:T(8,128)(2,1)S(1)}, bf16[130,768]{1,0:T(8,128)(2,1)S(1)}, u32[]{:S(2)}, u32[]{:S(2)}) collective-permute-start(bf16[130,768]{1,0:T(8,128)(2,1)S(1)} %slice.75), channel_id=1, source_target_pairs={{0,16},{16,32},{32,48},{48,64},{64,80},{80,96},{96,112},{112,128},... | collective-permute-start | bytes 599048 | tf_op jit(solution)/shard_map/ppermute | solution.py:128
  145.0 127.0 %reduce-scatter.2.cloned.1.call-start = ((), (), s32[]{:S(2)}) async-start(), calls=%async_computation.3 | async-start | bytes 4718592 | tf_op jit(solution)/shard_map/reduce_scatter | solution.py:150
  149.7 4.6 %copy-start.40 = (f32[1,256]{1,0:T(1,128)S(1)}, f32[1,256]{1,0:T(1,128)}, u32[]{:S(2)}) copy-start(f32[1,256]{1,0:T(1,128)} %get-tuple-element.123) | copy-start | bytes 3076
  149.7 4.6 %copy-start.41 = (f32[1,256]{1,0:T(1,128)S(1)}, f32[1,256]{1,0:T(1,128)}, u32[]{:S(2)}) copy-start(f32[1,256]{1,0:T(1,128)} %get-tuple-element.124) | copy-start | bytes 3076
  149.7 4.6 %copy-start.42 = (f32[1,256]{1,0:T(1,128)S(1)}, f32[1,256]{1,0:T(1,128)}, u32[]{:S(2)}) copy-start(f32[1,256]{1,0:T(1,128)} %get-tuple-element.125) | copy-start | bytes 3076
  149.7 4.6 %copy-start.43 = (f32[1,256]{1,0:T(1,128)S(1)}, f32[1,256]{1,0:T(1,128)}, u32[]{:S(2)}) copy-start(f32[1,256]{1,0:T(1,128)} %get-tuple-element.126) | copy-start | bytes 3076
  149.7 4.6 %copy-start.44 = (f32[1,256]{1,0:T(1,128)S(1)}, f32[1,256]{1,0:T(1,128)}, u32[]{:S(2)}) copy-start(f32[1,256]{1,0:T(1,128)} %get-tuple-element.127) | copy-start | bytes 3076
  154.3 9.1 %copy-start.5 = (pred[1024]{0:T(1024)(128)(4,1)S(1)}, pred[1024]{0:T(1024)(128)(4,1)}, u32[]{:S(2)}) copy-start(pred[1024]{0:T(1024)(128)(4,1)} %get-tuple-element.261) | copy-start | bytes 3076
  154.3 9.1 %copy-start.6 = (pred[1024]{0:T(1024)(128)(4,1)S(1)}, pred[1024]{0:T(1024)(128)(4,1)}, u32[]{:S(2)}) copy-start(pred[1024]{0:T(1024)(128)(4,1)} %get-tuple-element.262) | copy-start | bytes 3076
  154.3 9.1 %copy-start.7 = (pred[1024]{0:T(1024)(128)(4,1)S(1)}, pred[1024]{0:T(1024)(128)(4,1)}, u32[]{:S(2)}) copy-start(pred[1024]{0:T(1024)(128)(4,1)} %get-tuple-element.263) | copy-start | bytes 3076
  154.3 9.1 %copy-start.8 = (pred[1024]{0:T(1024)(128)(4,1)S(1)}, pred[1024]{0:T(1024)(128)(4,1)}, u32[]{:S(2)}) copy-start(pred[1024]{0:T(1024)(128)(4,1)} %get-tuple-element.226) | copy-start | bytes 3076
  154.3 9.1 %copy-start.9 = (pred[1024]{0:T(1024)(128)(4,1)S(1)}, pred[1024]{0:T(1024)(128)(4,1)}, u32[]{:S(2)}) copy-start(pred[1024]{0:T(1024)(128)(4,1)} %get-tuple-element.227) | copy-start | bytes 3076
  154.3 9.1 %copy-start.10 = (pred[1024]{0:T(1024)(128)(4,1)S(1)}, pred[1024]{0:T(1024)(128)(4,1)}, u32[]{:S(2)}) copy-start(pred[1024]{0:T(1024)(128)(4,1)} %get-tuple-element.228) | copy-start | bytes 3076
  154.4 9.1 %copy-start.11 = (pred[1024]{0:T(1024)(128)(4,1)S(1)}, pred[1024]{0:T(1024)(128)(4,1)}, u32[]{:S(2)}) copy-start(pred[1024]{0:T(1024)(128)(4,1)} %get-tuple-element.229) | copy-start | bytes 3076
  154.4 9.1 %copy-start.12 = (pred[1024]{0:T(1024)(128)(4,1)S(1)}, pred[1024]{0:T(1024)(128)(4,1)}, u32[]{:S(2)}) copy-start(pred[1024]{0:T(1024)(128)(4,1)} %get-tuple-element.230) | copy-start | bytes 3076
  154.4 9.1 %copy-start.13 = (pred[1024]{0:T(1024)(128)(4,1)S(1)}, pred[1024]{0:T(1024)(128)(4,1)}, u32[]{:S(2)}) copy-start(pred[1024]{0:T(1024)(128)(4,1)} %get-tuple-element.231) | copy-start | bytes 3076
  154.4 9.1 %copy-start.14 = (pred[1024]{0:T(1024)(128)(4,1)S(1)}, pred[1024]{0:T(1024)(128)(4,1)}, u32[]{:S(2)}) copy-start(pred[1024]{0:T(1024)(128)(4,1)} %get-tuple-element.232) | copy-start | bytes 3076
  154.4 9.1 %copy-start.15 = (pred[1024]{0:T(1024)(128)(4,1)S(1)}, pred[1024]{0:T(1024)(128)(4,1)}, u32[]{:S(2)}) copy-start(pred[1024]{0:T(1024)(128)(4,1)} %get-tuple-element.233) | copy-start | bytes 3076
  154.4 9.1 %copy-start.16 = (pred[1024]{0:T(1024)(128)(4,1)S(1)}, pred[1024]{0:T(1024)(128)(4,1)}, u32[]{:S(2)}) copy-start(pred[1024]{0:T(1024)(128)(4,1)} %get-tuple-element.234) | copy-start | bytes 3076
  154.4 9.1 %copy-start.17 = (pred[1024]{0:T(1024)(128)(4,1)S(1)}, pred[1024]{0:T(1024)(128)(4,1)}, u32[]{:S(2)}) copy-start(pred[1024]{0:T(1024)(128)(4,1)} %get-tuple-element.235) | copy-start | bytes 3076
  154.4 9.1 %copy-start.18 = (pred[1024]{0:T(1024)(128)(4,1)S(1)}, pred[1024]{0:T(1024)(128)(4,1)}, u32[]{:S(2)}) copy-start(pred[1024]{0:T(1024)(128)(4,1)} %get-tuple-element.236) | copy-start | bytes 3076
  154.4 9.1 %copy-start.19 = (pred[1024]{0:T(1024)(128)(4,1)S(1)}, pred[1024]{0:T(1024)(128)(4,1)}, u32[]{:S(2)}) copy-start(pred[1024]{0:T(1024)(128)(4,1)} %get-tuple-element.237) | copy-start | bytes 3076
  154.4 9.1 %copy-start.20 = (pred[1024]{0:T(1024)(128)(4,1)S(1)}, pred[1024]{0:T(1024)(128)(4,1)}, u32[]{:S(2)}) copy-start(pred[1024]{0:T(1024)(128)(4,1)} %get-tuple-element.238) | copy-start | bytes 3076
  154.5 9.1 %copy-start.21 = (pred[1024]{0:T(1024)(128)(4,1)S(1)}, pred[1024]{0:T(1024)(128)(4,1)}, u32[]{:S(2)}) copy-start(pred[1024]{0:T(1024)(128)(4,1)} %get-tuple-element.239) | copy-start | bytes 3076
  154.5 9.1 %copy-start.22 = (pred[1024]{0:T(1024)(128)(4,1)S(1)}, pred[1024]{0:T(1024)(128)(4,1)}, u32[]{:S(2)}) copy-start(pred[1024]{0:T(1024)(128)(4,1)} %get-tuple-element.240) | copy-start | bytes 3076
  154.5 9.1 %copy-start.23 = (pred[1024]{0:T(1024)(128)(4,1)S(1)}, pred[1024]{0:T(1024)(128)(4,1)}, u32[]{:S(2)}) copy-start(pred[1024]{0:T(1024)(128)(4,1)} %get-tuple-element.241) | copy-start | bytes 3076
  154.5 9.1 %copy-start.24 = (pred[1024]{0:T(1024)(128)(4,1)S(1)}, pred[1024]{0:T(1024)(128)(4,1)}, u32[]{:S(2)}) copy-start(pred[1024]{0:T(1024)(128)(4,1)} %get-tuple-element.242) | copy-start | bytes 3076
  154.5 9.1 %copy-start.25 = (pred[1024]{0:T(1024)(128)(4,1)S(1)}, pred[1024]{0:T(1024)(128)(4,1)}, u32[]{:S(2)}) copy-start(pred[1024]{0:T(1024)(128)(4,1)} %get-tuple-element.243) | copy-start | bytes 3076
  154.5 9.1 %copy-start.26 = (pred[1024]{0:T(1024)(128)(4,1)S(1)}, pred[1024]{0:T(1024)(128)(4,1)}, u32[]{:S(2)}) copy-start(pred[1024]{0:T(1024)(128)(4,1)} %get-tuple-element.244) | copy-start | bytes 3076
  154.5 9.1 %copy-start.27 = (pred[1024]{0:T(1024)(128)(4,1)S(1)}, pred[1024]{0:T(1024)(128)(4,1)}, u32[]{:S(2)}) copy-start(pred[1024]{0:T(1024)(128)(4,1)} %get-tuple-element.207) | copy-start | bytes 3076
  154.5 9.1 %copy-start.28 = (pred[1024]{0:T(1024)(128)(4,1)S(1)}, pred[1024]{0:T(1024)(128)(4,1)}, u32[]{:S(2)}) copy-start(pred[1024]{0:T(1024)(128)(4,1)} %get-tuple-element.208) | copy-start | bytes 3076
  154.5 9.1 %copy-start.29 = (pred[1024]{0:T(1024)(128)(4,1)S(1)}, pred[1024]{0:T(1024)(128)(4,1)}, u32[]{:S(2)}) copy-start(pred[1024]{0:T(1024)(128)(4,1)} %get-tuple-element.209) | copy-start | bytes 3076
  154.5 9.1 %copy-start.30 = (pred[1024]{0:T(1024)(128)(4,1)S(1)}, pred[1024]{0:T(1024)(128)(4,1)}, u32[]{:S(2)}) copy-start(pred[1024]{0:T(1024)(128)(4,1)} %get-tuple-element.210) | copy-start | bytes 3076
  154.6 9.1 %copy-start.31 = (pred[1024]{0:T(1024)(128)(4,1)S(1)}, pred[1024]{0:T(1024)(128)(4,1)}, u32[]{:S(2)}) copy-start(pred[1024]{0:T(1024)(128)(4,1)} %get-tuple-element.211) | copy-start | bytes 3076
  154.6 9.1 %copy-start.32 = (pred[1024]{0:T(1024)(128)(4,1)S(1)}, pred[1024]{0:T(1024)(128)(4,1)}, u32[]{:S(2)}) copy-start(pred[1024]{0:T(1024)(128)(4,1)} %get-tuple-element.212) | copy-start | bytes 3076
  154.6 9.1 %copy-start.33 = (pred[1024]{0:T(1024)(128)(4,1)S(1)}, pred[1024]{0:T(1024)(128)(4,1)}, u32[]{:S(2)}) copy-start(pred[1024]{0:T(1024)(128)(4,1)} %get-tuple-element.213) | copy-start | bytes 3076
  154.6 9.1 %copy-start.34 = (pred[1024]{0:T(1024)(128)(4,1)S(1)}, pred[1024]{0:T(1024)(128)(4,1)}, u32[]{:S(2)}) copy-start(pred[1024]{0:T(1024)(128)(4,1)} %get-tuple-element.214) | copy-start | bytes 3076
  154.6 9.1 %copy-start.35 = (pred[1024]{0:T(1024)(128)(4,1)S(1)}, pred[1024]{0:T(1024)(128)(4,1)}, u32[]{:S(2)}) copy-start(pred[1024]{0:T(1024)(128)(4,1)} %get-tuple-element.215) | copy-start | bytes 3076
  154.6 9.1 %copy-start.36 = (pred[1024]{0:T(1024)(128)(4,1)S(1)}, pred[1024]{0:T(1024)(128)(4,1)}, u32[]{:S(2)}) copy-start(pred[1024]{0:T(1024)(128)(4,1)} %get-tuple-element.216) | copy-start | bytes 3076
  208.6 1.6 collective-permute-start.13
  (4 other events, 15.6 us)
Sparse Core Ops, SparseCore 0:
  54.3 70.6 all-gather.2
  145.1 63.3 all-gather.4
  216.9 55.0 reduce-scatter.1
